TPU v7x, 32 devices: a whole 2x2x4 slice. The times are simulated.
32 devices in a mesh: sec: 2 (over x), ta: 4 (over z), sa: 4 (over y, core).
Axes of the slice: x: 2, y: 2, z: 4, core: 2. Of those that a mesh axis runs over, the one named last changes fastest.
Arguments:
- gauge_links: float32 [4, 3, 3, 2, 16, 16, 256], P(None, None, None, None, 'ta', 'sa'), may hold values from -2.5 to 2.5
- noise_slabs: float32 [8, 3, 2, 4, 16, 256], P('sec', None, None, 'ta', 'sa'), may hold values from -6 to 6
- offsets: int32 [8], replicated, may hold values from 0 to 3, as said below
- vectors: bfloat16 [16, 32, 3, 2, 16, 256], P('ta', 'sec', None, None, 'sa'), may hold values from -0.0390625 to 0.0390625
Outputs:
- perambulator: float32 [8, 4, 2, 16, 32], P('sec', None, None, 'ta', 'sa')
Inputs may be any that keep to these rules, and one draw needn't show every extreme that they name: `offsets`: each value from 0 to 3 is the offset of exactly 2 right-hand sides.
All inputs are finite; a program needn't handle non-finite values.
Results may differ from a plain program's by a relative error of at most 0.003.
Values may be sent and summed in bfloat16 or wider, within the bound.
No kernel may reach another device: no remote copies, remote signals or barrier semaphores. Data moves between devices by JAX's collectives and lax.ppermute only.
A program may use at most 128 MiB of HBM per device.

v0:
```python
import functools

import jax
import jax.numpy as jnp
from jax import lax
from jax.experimental import pallas as pl
from jax.experimental.pallas import tpu as pltpu
from jax.sharding import PartitionSpec as P

NX = 32
TDIL = 4
ITERS = 2
INTERPRET = False


kappa_hop = 0.12
GAMMA_PERM = ((3, 2, 1, 0), (3, 2, 1, 0), (2, 3, 0, 1), (2, 3, 0, 1))
GAMMA_REAL = ((0, 0, 0, 0), (-1, 1, 1, -1), (0, 0, 0, 0), (1, 1, 1, 1))
GAMMA_IMAG = ((1, 1, -1, -1), (0, 0, 0, 0), (1, -1, -1, 1), (0, 0, 0, 0))


def passed_along(value, axis, steps):
    count = lax.axis_size(axis)
    pairs = [(source, (source + steps) % count) for source in range(count)]
    return lax.ppermute(value, axis, pairs)


def from_partner(x, axis, stride):
    return lax.ppermute(x, axis, [(i, i ^ 1 << stride) for i in range(lax.axis_size(axis))])


def times_phase(re, im, cr, ci):
    if ci == 0:
        if cr == 1:
            return re, im
        return -re, -im
    if ci == 1:
        return -im, re
    return im, -re


def move_first(operand, stride):
    positions = jnp.arange(operand.shape[-1]) % NX
    if stride == 1:
        return jnp.where(
            positions == NX - 1, jnp.roll(operand, NX - 1, axis=-1), jnp.roll(operand, -1, axis=-1)
        )
    return jnp.where(
        positions == 0, jnp.roll(operand, 1 - NX, axis=-1), jnp.roll(operand, 1, axis=-1)
    )


def move_second(operand, stride):
    return jnp.roll(operand, -stride * NX, axis=-1)


def hop_kernel(p_ref, u_ref, b_ref, src_ref, out_ref):
    T = out_ref.shape[3]
    Z = out_ref.shape[4]
    L = out_ref.shape[5]
    rows = p_ref.shape[4]
    xpos = lax.broadcasted_iota(jnp.int32, (Z, L), 1) % NX
    x_last = xpos == NX - 1
    x_first = xpos == 0

    def body(t, carry):
        acc = [[[None, None] for _ in range(3)] for _ in range(4)]

        def shifted(s, c, ri, mu, stride):
            if mu == 3:
                return p_ref[s, c, ri, t + 1 + stride, pl.ds(0, Z), :]
            if mu == 2:
                full = p_ref[s, c, ri, t + 1, :, :]
                full = pltpu.roll(full, rows - 1 if stride == 1 else 1, axis=0)
                return full[:Z]
            v = p_ref[s, c, ri, t + 1, pl.ds(0, Z), :]
            if mu == 1:
                return pltpu.roll(v, (L - NX) if stride == 1 else NX, axis=1)
            if stride == 1:
                return jnp.where(x_last, pltpu.roll(v, NX - 1, axis=1), pltpu.roll(v, L - 1, axis=1))
            return jnp.where(x_first, pltpu.roll(v, L - NX + 1, axis=1), pltpu.roll(v, 1, axis=1))

        for mu in range(4):
            perm = GAMMA_PERM[mu]
            heads = [0, 1]
            for stride in (1, -1):
                orient = -1 if stride == 1 else 1
                half = []
                for s in heads:
                    p = perm[s]
                    cr, ci = orient * GAMMA_REAL[mu][s], orient * GAMMA_IMAG[mu][s]
                    colours = []
                    for c in range(3):
                        sre = shifted(s, c, 0, mu, stride)
                        sim = shifted(s, c, 1, mu, stride)
                        pre, pim = times_phase(shifted(p, c, 0, mu, stride), shifted(p, c, 1, mu, stride), cr, ci)
                        colours.append((sre + pre, sim + pim))
                    half.append(colours)
                links = u_ref if stride == 1 else b_ref
                for k, s in enumerate(heads):
                    p = perm[s]
                    cpr, cpi = orient * GAMMA_REAL[mu][p], orient * GAMMA_IMAG[mu][p]
                    for a in range(3):
                        sum_re = None
                        sum_im = None
                        for b in range(3):
                            if stride == 1:
                                lre = links[mu, a, b, 0, t]
                                lim = links[mu, a, b, 1, t]
                                hre, him = half[k][b]
                                tre = lre * hre - lim * him
                                tim = lre * him + lim * hre
                            else:
                                lre = links[mu, b, a, 0, t]
                                lim = links[mu, b, a, 1, t]
                                hre, him = half[k][b]
                                tre = lre * hre + lim * him
                                tim = lre * him - lim * hre
                            sum_re = tre if sum_re is None else sum_re + tre
                            sum_im = tim if sum_im is None else sum_im + tim
                        for row, (vre, vim) in ((s, (sum_re, sum_im)), (p, times_phase(sum_re, sum_im, cpr, cpi))):
                            if acc[row][a][0] is None:
                                acc[row][a] = [vre, vim]
                            else:
                                acc[row][a] = [acc[row][a][0] + vre, acc[row][a][1] + vim]
        for s in range(4):
            for c in range(3):
                for ri in range(2):
                    psi = p_ref[s, c, ri, t + 1, pl.ds(0, Z), :]
                    src = src_ref[s, c, ri, t]
                    residual = src - (psi - kappa_hop * acc[s][c][ri])
                    out_ref[s, c, ri, t] = psi + residual
        return carry

    lax.fori_loop(0, T, body, 0)


def hopping_step(padded, links, back_links, source):
    R, S, C, RI, T, Z, L = source.shape
    rows = padded.shape[5]
    spinor_block = pl.BlockSpec((None, S, C, RI, T + 2, rows, L), lambda r: (r, 0, 0, 0, 0, 0, 0))
    link_block = pl.BlockSpec(links.shape, lambda r: (0,) * 7)
    site_block = pl.BlockSpec((None, S, C, RI, T, Z, L), lambda r: (r, 0, 0, 0, 0, 0, 0))
    return pl.pallas_call(
        hop_kernel,
        grid=(R,),
        in_specs=[spinor_block, link_block, link_block, site_block],
        out_specs=site_block,
        out_shape=jax.ShapeDtypeStruct(source.shape, jnp.float32),
        compiler_params=pltpu.CompilerParams(dimension_semantics=("arbitrary",)),
        interpret=INTERPRET,
    )(padded, links, back_links, source)


def padded_spinor(spinor, lower_sign, upper_sign):
    R, S, C, RI, T, Z, L = spinor.shape
    rows = -(-(Z + 2) // 8) * 8
    t_lo = passed_along(spinor[:, :, :, :, T - 1:, :, :], "ta", 1) * lower_sign
    t_hi = passed_along(spinor[:, :, :, :, :1, :, :], "ta", -1) * upper_sign
    z_lo = passed_along(spinor[:, :, :, :, :, Z - 1:, :], "sa", 1)
    z_hi = passed_along(spinor[:, :, :, :, :, :1, :], "sa", -1)
    gap = jnp.zeros((R, S, C, RI, T, rows - Z - 2, L), jnp.float32)
    middle = jnp.concatenate([spinor, z_hi, gap, z_lo], axis=5)
    t_pad = ((0, 0),) * 5 + ((0, rows - Z), (0, 0))
    return jnp.concatenate([jnp.pad(t_lo, t_pad), middle, jnp.pad(t_hi, t_pad)], axis=4)


def intersection_part(rounded, vector_piece):
    products = jnp.einsum(
        "tvcazs,rqcbtzs->rqabtv", vector_piece, rounded, preferred_element_type=jnp.float32
    )
    real_part = products[:, :, 0, 0] + products[:, :, 1, 1]
    imag_part = products[:, :, 0, 1] - products[:, :, 1, 0]
    return jnp.stack([real_part, imag_part], axis=2)


def local(gauge_links, noise_slabs, offsets, vectors):
    partner_vectors = from_partner(vectors, "sec", 0)
    batch_rows = noise_slabs.shape[0]
    slab_length = gauge_links.shape[4]
    section_index = lax.axis_index("sec")
    slab_index = lax.axis_index("ta")
    slab_count = lax.axis_size("ta")
    lower_sign = jnp.where(slab_index == 0, -1.0, 1.0).astype(jnp.float32)
    upper_sign = jnp.where(slab_index == slab_count - 1, -1.0, 1.0).astype(jnp.float32)
    filled = jnp.repeat(noise_slabs, TDIL, axis=3)
    global_time = slab_index * slab_length + jnp.arange(slab_length)
    own_offsets = lax.dynamic_slice_in_dim(offsets, section_index * batch_rows, batch_rows)
    time_mask = (global_time[None, :] % TDIL == own_offsets[:, None]).astype(jnp.float32)
    rhs_index = section_index * batch_rows + jnp.arange(batch_rows)
    spin_mask = (jnp.arange(4)[None, :] == rhs_index[:, None] % 4).astype(jnp.float32)
    source = (
        spin_mask[:, :, None, None, None, None, None]
        * (filled * time_mask[:, None, None, :, None, None])[:, None]
    )
    time_edge = passed_along(gauge_links[3, :, :, :, -1:, :, :], "ta", 1)
    space_edge = passed_along(gauge_links[2, :, :, :, :, -1:, :], "sa", 1)
    back_links = jnp.stack(
        [
            move_first(gauge_links[0], -1),
            move_second(gauge_links[1], -1),
            jnp.concatenate([space_edge, gauge_links[2, :, :, :, :, :-1, :]], axis=4),
            jnp.concatenate([time_edge, gauge_links[3, :, :, :, :-1, :, :]], axis=3),
        ]
    )
    spinor = source
    for _ in range(ITERS):
        padded = padded_spinor(spinor, lower_sign, upper_sign)
        spinor = hopping_step(padded, gauge_links, back_links, source)
    rounded = spinor.astype(jnp.bfloat16)
    own_part = intersection_part(rounded, vectors)
    partner_part = intersection_part(rounded, partner_vectors)
    lower_half = jnp.where(section_index == 0, own_part, partner_part)
    upper_half = jnp.where(section_index == 0, partner_part, own_part)
    partial_value = jnp.concatenate([lower_half, upper_half], axis=4)
    return lax.psum_scatter(partial_value, "sa", scatter_dimension=4, tiled=True)


def solution(mesh):
    in_specs = (
        P(None, None, None, None, "ta", "sa", None),
        P("sec", None, None, "ta", "sa", None),
        P(),
        P("ta", "sec", None, None, "sa", None),
    )
    out_specs = P("sec", None, None, "ta", "sa")
    return jax.shard_map(local, mesh=mesh, in_specs=in_specs, out_specs=out_specs, check_vma=False)
```

profile of v0, /device:TPU:0, one launch (start us, length us, event | category | flops | bytes accessed | tf_op | source)
XLA Modules:
  0.0 103.5 jit_solution(8466890881726755689)
XLA Ops:
  0.0 0.1 fusion.11
  0.1 0.8 dynamic_slice.3
  0.9 0.1 compare_convert_fusion
  1.0 1.0 broadcast_multiply_fusion.5
  2.0 0.5 broadcast_multiply_fusion.src_ref
  2.5 1.2 %fusion.18 = (f32[4,4,3,2,1,4,256]{6,5,4,3,2,1,0:T(4,128)}, f32[4,4,3,2,1,4,256]{6,5,4,3,2,1,0:T(4,128)}) fusion(f32[4,4,3,2,4,4,256]{6,5,4,3,2,1,0:T(4,128)S(1)} %broadcast_multiply_fusion.src_ref), kind=kLoop, calls=%fused_computation.67 | loop fusion | bytes 1572864 | tf_op jit(solution)/shard_map/slice | solution.py:158
  3.7 5.1 %collective-permute-start.3 = (f32[4,4,3,2,1,4,256]{6,5,4,3,2,1,0:T(4,128)}, f32[4,4,3,2,1,4,256]{6,5,4,3,2,1,0:T(4,128)}, u32[]{:S(2)}, u32[]{:S(2)}) collective-permute-start(f32[4,4,3,2,1,4,256]{6,5,4,3,2,1,0:T(4,128)} %get-tuple-element.12), channel_id=1, source_target_pairs={{0,12},{4,0},{8,4},{12,8},{1,13},{5,1},{9,5},{13,9},{2,14},{6,2},{... | collective-permute-start | bytes 1179656 | tf_op jit(solution)/shard_map/ppermute | solution.py:25
  8.8 1.6 %fusion.17 = (f32[4,4,3,2,4,1,256]{6,5,4,3,2,1,0:T(1,128)}, f32[4,4,3,2,4,1,256]{6,5,4,3,2,1,0:T(1,128)}) fusion(f32[4,4,3,2,4,4,256]{6,5,4,3,2,1,0:T(4,128)S(1)} %broadcast_multiply_fusion.src_ref), kind=kLoop, calls=%fused_computation.66 | loop fusion | bytes 1572864 | tf_op jit(solution)/shard_map/slice | solution.py:161
  10.4 0.7 collective-permute-start.1
  11.0 0.1 slice_bitcast_fusion.9
  11.1 1.0 collective-permute-start.4
  12.2 0.2 slice_bitcast_fusion.1
  12.4 0.1 slice_bitcast_fusion.6
  12.7 0.1 slice.126
  12.9 0.3 maximum_select_fusion
  13.2 0.2 maximum_bitcast_fusion
  13.4 0.1 pad.46.clone
  13.5 9.3 %collective-permute-done.4 = f32[3,3,2,4,1,256]{5,4,3,2,1,0:T(1,128)S(1)} collective-permute-done((f32[3,3,2,4,1,256]{5,4,3,2,1,0:T(1,128)S(1)}, f32[3,3,2,4,1,256]{5,4,3,2,1,0:T(1,128)S(1)}, u32[]{:S(2)}, u32[]{:S(2)}) %collective-permute-start.4) | collective-permute-done | bytes 73760 | tf_op jit(solution)/shard_map/ppermute | solution.py:25
  22.8 0.1 maximum_bitcast_fusion.1
  23.0 6.0 %collective-permute-done.5 = f32[3,3,2,1,4,256]{5,4,3,2,1,0:T(4,128)S(1)} collective-permute-done((f32[3,3,2,1,4,256]{5,4,3,2,1,0:T(4,128)S(1)}, f32[3,3,2,1,4,256]{5,4,3,2,1,0:T(4,128)S(1)}, u32[]{:S(2)}, u32[]{:S(2)}) %collective-permute-start.5) | collective-permute-done | bytes 73760 | tf_op jit(solution)/shard_map/ppermute | solution.py:25
  29.0 0.1 maximum_bitcast_fusion.2
  29.1 1.4 %pad_maximum_fusion.b_ref = f32[4,3,3,2,4,4,256]{6,5,4,3,2,1,0:T(4,128)} fusion(f32[1,3,3,2,4,4,256]{6,5,4,3,2,1,0:T(4,128)S(1)} %maximum_bitcast_fusion.2, f32[1,3,3,2,4,4,256]{6,5,4,3,2,1,0:T(4,128)S(1)} %maximum_bitcast_fusion.1, f32[1,3,3,2,4,4,256]{6,5,4,3,2,1,0:T(4,128)S(1)} %maximum_bitcast_fusion, f32[1,3,3,2,4,4,256]{6,5,4,3,2,1,0:T(4,128)S(1)} %maximum_select_fusion), kind=kLoop, calls=%fused_computation.6 | loop fusion | flops 884736 | bytes 2359296 | tf_op jit(solution)/shard_map/stack | solution.py:198
  30.5 1.1 %broadcast_multiply_fusion.2 = f32[4,4,3,2,1,4,256]{6,5,4,3,2,1,0:T(4,128)S(1)} fusion(f32[4,4,3,2,1,4,256]{6,5,4,3,2,1,0:T(4,128)} %collective-permute-done.3, f32[]{:T(128)S(6)} %select_n.67), kind=kLoop, calls=%fused_computation.26 | loop fusion | flops 98304 | bytes 786436 | tf_op jit(solution)/shard_map/mul | solution.py:159
  31.6 1.1 %broadcast_multiply_fusion.4 = f32[4,4,3,2,1,4,256]{6,5,4,3,2,1,0:T(4,128)S(1)} fusion(f32[4,4,3,2,1,4,256]{6,5,4,3,2,1,0:T(4,128)} %collective-permute-done, f32[]{:T(128)S(6)} %select_n.66), kind=kLoop, calls=%fused_computation.28 | loop fusion | flops 98304 | bytes 786436 | tf_op jit(solution)/shard_map/mul | solution.py:158
  32.7 3.8 %select_maximum_fusion.2.p_ref = f32[4,4,3,2,6,8,256]{6,5,4,3,2,1,0:T(8,128)} fusion(f32[4,4,3,2,1,4,256]{6,5,4,3,2,1,0:T(4,128)S(1)} %broadcast_multiply_fusion.2, f32[4,4,3,2,1,4,256]{6,5,4,3,2,1,0:T(4,128)S(1)} %broadcast_multiply_fusion.4, f32[4,4,3,2,4,1,256]{6,5,4,3,2,1,0:T(1,128)} %collective-permute-done.2, ...), kind=kLoop, calls=%fused_computation.2 | loop fusion | flops 10616832 | bytes 7864512 | tf_op jit(solution)/shard_map/concatenate | solution.py:165
  36.5 11.7 %shard_map.49 = f32[4,4,3,2,4,4,256]{6,5,4,3,2,1,0:T(4,128)} custom-call(f32[4,4,3,2,6,8,256]{6,5,4,3,2,1,0:T(8,128)} %select_maximum_fusion.2.p_ref, f32[4,3,3,2,4,4,256]{6,5,4,3,2,1,0:T(4,128)} %u_ref.3, f32[4,3,3,2,4,4,256]{6,5,4,3,2,1,0:T(4,128)} %pad_maximum_fusion.b_ref, f32[4,4,3,2,4,4,256]{6,5,4,3,2,1,0:T(4,128)} %copy-done), custom_call_target="tpu_custom_call" | custom-call | tf_op jit(solution)/shard_map/pallas_call | solution.py:144
  48.2 2.1 %fusion.16 = (f32[4,4,3,2,1,4,256]{6,5,4,3,2,1,0:T(4,128)}, f32[4,4,3,2,1,4,256]{6,5,4,3,2,1,0:T(4,128)S(1)}) fusion(f32[4,4,3,2,4,4,256]{6,5,4,3,2,1,0:T(4,128)} %shard_map.49), kind=kLoop, calls=%fused_computation.65 | loop fusion | bytes 1572864 | tf_op jit(solution)/shard_map/slice | solution.py:158
  50.3 0.9 collective-permute-start.6
  51.3 0.2 copy.31
  51.4 1.6 %collective-permute-start.10 = (bf16[4,16,3,2,4,256]{5,1,4,2,3,0:T(8,128)(2,1)S(1)}, bf16[4,16,3,2,4,256]{5,1,4,2,3,0:T(8,128)(2,1)}, u32[]{:S(2)}, u32[]{:S(2)}) collective-permute-start(bf16[4,16,3,2,4,256]{5,1,4,2,3,0:T(8,128)(2,1)S(1)} %copy.31), channel_id=1, source_target_pairs={{0,16},{16,0},{1,17},{17,1},{2,18},{18,2},{3,19},{19,3},{4,20},{20... | collective-permute-start | bytes 2359304 | tf_op jit(solution)/shard_map/ppermute | solution.py:29
  53.0 0.6 dynamic-slice
  54.2 3.0 %collective-permute-start.9 = (f32[4,4,3,2,1,4,256]{6,5,4,3,2,1,0:T(4,128)S(1)}, f32[4,4,3,2,1,4,256]{6,5,4,3,2,1,0:T(4,128)S(1)}, u32[]{:S(2)}, u32[]{:S(2)}) collective-permute-start(f32[4,4,3,2,1,4,256]{6,5,4,3,2,1,0:T(4,128)S(1)} %get-tuple-element.8), channel_id=1, source_target_pairs={{0,12},{4,0},{8,4},{12,8},{1,13},{5,1},{9,5},{13,9},{2,14},{6,2},{... | collective-permute-start | bytes 1179656 | tf_op jit(solution)/shard_map/ppermute | solution.py:25
  57.2 2.8 %fusion.15 = (f32[4,4,3,2,4,1,256]{6,5,4,3,2,1,0:T(1,128)S(1)}, f32[4,4,3,2,4,1,256]{6,5,4,3,2,1,0:T(1,128)S(1)}) fusion(f32[4,4,3,2,4,4,256]{6,5,4,3,2,1,0:T(4,128)} %shard_map.49), kind=kLoop, calls=%fused_computation.64 | loop fusion | bytes 1572864 | tf_op jit(solution)/shard_map/slice | solution.py:161
  60.1 0.5 collective-permute-start.8
  60.6 3.9 %collective-permute-done.6 = f32[4,4,3,2,1,4,256]{6,5,4,3,2,1,0:T(4,128)} collective-permute-done((f32[4,4,3,2,1,4,256]{6,5,4,3,2,1,0:T(4,128)}, f32[4,4,3,2,1,4,256]{6,5,4,3,2,1,0:T(4,128)}, u32[]{:S(2)}, u32[]{:S(2)}) %collective-permute-start.6) | collective-permute-done | bytes 393248 | tf_op jit(solution)/shard_map/ppermute | solution.py:25
  64.5 1.1 %broadcast_multiply_fusion.3 = f32[4,4,3,2,1,4,256]{6,5,4,3,2,1,0:T(4,128)S(1)} fusion(f32[4,4,3,2,1,4,256]{6,5,4,3,2,1,0:T(4,128)} %collective-permute-done.6, f32[]{:T(128)S(6)} %select_n.66), kind=kLoop, calls=%fused_computation.27 | loop fusion | flops 98304 | bytes 786436 | tf_op jit(solution)/shard_map/mul | solution.py:158
  65.6 4.8 %collective-permute-done.9 = f32[4,4,3,2,1,4,256]{6,5,4,3,2,1,0:T(4,128)S(1)} collective-permute-done((f32[4,4,3,2,1,4,256]{6,5,4,3,2,1,0:T(4,128)S(1)}, f32[4,4,3,2,1,4,256]{6,5,4,3,2,1,0:T(4,128)S(1)}, u32[]{:S(2)}, u32[]{:S(2)}) %collective-permute-start.9) | collective-permute-done | bytes 393248 | tf_op jit(solution)/shard_map/ppermute | solution.py:25
  70.4 0.1 broadcast_multiply_fusion.1
  70.5 0.7 collective-permute-done.8
  71.2 2.8 %select_maximum_fusion.p_ref = f32[4,4,3,2,6,8,256]{6,5,4,3,2,1,0:T(8,128)} fusion(f32[4,4,3,2,1,4,256]{6,5,4,3,2,1,0:T(4,128)S(1)} %broadcast_multiply_fusion.1, f32[4,4,3,2,1,4,256]{6,5,4,3,2,1,0:T(4,128)S(1)} %broadcast_multiply_fusion.3, f32[4,4,3,2,4,1,256]{6,5,4,3,2,1,0:T(1,128)S(1)} %collective-permute-done.8, ...), kind=kLoop, calls=%fused_computation | loop fusion | flops 10616832 | bytes 7864512 | tf_op jit(solution)/shard_map/concatenate | solution.py:165
  74.0 11.6 %shard_map.50 = f32[4,4,3,2,4,4,256]{6,5,4,3,2,1,0:T(4,128)} custom-call(f32[4,4,3,2,6,8,256]{6,5,4,3,2,1,0:T(8,128)} %select_maximum_fusion.p_ref, f32[4,3,3,2,4,4,256]{6,5,4,3,2,1,0:T(4,128)} %u_ref.3, f32[4,3,3,2,4,4,256]{6,5,4,3,2,1,0:T(4,128)} %pad_maximum_fusion.b_ref, f32[4,4,3,2,4,4,256]{6,5,4,3,2,1,0:T(4,128)} %copy-done), custom_call_target="tpu_custom_call" | custom-call | tf_op jit(solution)/shard_map/pallas_call | solution.py:144
  85.6 1.8 %convert_bitcast_fusion = bf16[4,4,3,2,4,4,256,1]{6,5,4,3,2,1,0,7:T(4,128)(2,1)S(1)} fusion(f32[4,4,3,2,4,4,256]{6,5,4,3,2,1,0:T(4,128)} %shard_map.50), kind=kLoop, calls=%fused_computation.11 | loop fusion | flops 393216 | bytes 2359296 | tf_op jit(solution)/shard_map/convert_element_type | solution.py:210
  87.4 2.5 %convolution_bitcast_fusion = f32[4,4,4,2,16,2]{4,2,5,3,1,0:T(4,128)S(1)} fusion(bf16[4,16,3,2,4,256]{5,1,4,2,3,0:T(8,128)(2,1)} %collective-permute-done.10, bf16[4,4,3,2,4,4,256,1]{6,5,4,3,2,1,0,7:T(4,128)(2,1)S(1)} %convert_bitcast_fusion), kind=kOutput, calls=%fused_computation.7 | convolution fusion | flops 25165824 | bytes 1589248 | tf_op jit(solution)/shard_map/tvcazs,rqcbtzs->rqabtv/dot_general | solution.py:169
  89.9 1.3 %convolution_bitcast_fusion.1 = f32[4,4,2,2,4,16]{5,1,2,3,0,4:T(4,128)S(1)} fusion(bf16[4,16,3,2,4,256,1,1]{5,4,3,2,1,0,7,6:T(4,128)(2,1)S(1)} %bitcast.76, bf16[4,4,3,2,4,4,256,1]{6,5,4,3,2,1,0,7:T(4,128)(2,1)S(1)} %convert_bitcast_fusion), kind=kOutput, calls=%fused_computation.8 | convolution fusion | flops 25165824 | bytes 1589248 | tf_op jit(solution)/shard_map/tvcazs,rqcbtzs->rqabtv/dot_general | solution.py:169
  91.3 0.1 pad_maximum_fusion.3
  91.5 11.3 %all-reduce.4 = f32[4,4,2,4,32]{4,1,0,3,2:T(4,128)S(1)} all-reduce(f32[4,4,2,4,32]{4,1,0,3,2:T(4,128)S(1)} %pad_maximum_fusion.3), channel_id=2, replica_groups=mesh['sec'=2,'ta'=4,'sa'=4] {'sa'}, use_global_device_ids=true, to_apply=%region_0.1.clone | all-reduce | flops 4096 | bytes 32768
  102.7 0.1 constant_dynamic-slice_fusion
  102.8 0.7 copy.34
  (34 shorter events, 0.4 us)
Async XLA Ops:
  0.0 11.0 %copy-start.2 = (f32[4,3,3,2,4,4,256]{6,5,4,3,2,1,0:T(4,128)S(1)}, f32[4,3,3,2,4,4,256]{6,5,4,3,2,1,0:T(4,128)}, u32[]{:S(2)}) copy-start(f32[4,3,3,2,4,4,256]{6,5,4,3,2,1,0:T(4,128)} %u_ref.3) | copy-start | bytes 3538948
  2.5 30.2 %copy-start = (f32[4,4,3,2,4,4,256]{6,5,4,3,2,1,0:T(4,128)}, f32[4,4,3,2,4,4,256]{6,5,4,3,2,1,0:T(4,128)S(1)}, u32[]{:S(2)}) copy-start(f32[4,4,3,2,4,4,256]{6,5,4,3,2,1,0:T(4,128)S(1)} %broadcast_multiply_fusion.src_ref) | copy-start | bytes 4718596
  3.7 26.8 %collective-permute-start.3 = (f32[4,4,3,2,1,4,256]{6,5,4,3,2,1,0:T(4,128)}, f32[4,4,3,2,1,4,256]{6,5,4,3,2,1,0:T(4,128)}, u32[]{:S(2)}, u32[]{:S(2)}) collective-permute-start(f32[4,4,3,2,1,4,256]{6,5,4,3,2,1,0:T(4,128)} %get-tuple-element.12), channel_id=1, source_target_pairs={{0,12},{4,0},{8,4},{12,8},{1,13},{5,1},{9,5},{13,9},{2,14},{6,2},{... | collective-permute-start | bytes 1179656 | tf_op jit(solution)/shard_map/ppermute | solution.py:25
  8.8 22.8 %collective-permute-start = (f32[4,4,3,2,1,4,256]{6,5,4,3,2,1,0:T(4,128)}, f32[4,4,3,2,1,4,256]{6,5,4,3,2,1,0:T(4,128)}, u32[]{:S(2)}, u32[]{:S(2)}) collective-permute-start(f32[4,4,3,2,1,4,256]{6,5,4,3,2,1,0:T(4,128)} %get-tuple-element.11), channel_id=1, source_target_pairs={{0,4},{4,8},{8,12},{12,0},{1,5},{5,9},{9,13},{13,1},{2,6},{6,10},{... | collective-permute-start | bytes 1179656 | tf_op jit(solution)/shard_map/ppermute | solution.py:25
  10.4 22.3 %collective-permute-start.1 = (f32[4,4,3,2,4,1,256]{6,5,4,3,2,1,0:T(1,128)}, f32[4,4,3,2,4,1,256]{6,5,4,3,2,1,0:T(1,128)}, u32[]{:S(2)}, u32[]{:S(2)}) collective-permute-start(f32[4,4,3,2,4,1,256]{6,5,4,3,2,1,0:T(1,128)} %get-tuple-element.9), channel_id=1, source_target_pairs={{0,3},{1,0},{2,1},{3,2},{4,7},{5,4},{6,5},{7,6},{8,11},{9,8},{10,9... | collective-permute-start | bytes 1179656 | tf_op jit(solution)/shard_map/ppermute | solution.py:25
  11.0 21.6 %collective-permute-start.2 = (f32[4,4,3,2,4,1,256]{6,5,4,3,2,1,0:T(1,128)}, f32[4,4,3,2,4,1,256]{6,5,4,3,2,1,0:T(1,128)}, u32[]{:S(2)}, u32[]{:S(2)}) collective-permute-start(f32[4,4,3,2,4,1,256]{6,5,4,3,2,1,0:T(1,128)} %get-tuple-element.10), channel_id=1, source_target_pairs={{0,1},{1,2},{2,3},{3,0},{4,5},{5,6},{6,7},{7,4},{8,9},{9,10},{10,1... | collective-permute-start | bytes 1179656 | tf_op jit(solution)/shard_map/ppermute | solution.py:25
  11.1 11.7 %collective-permute-start.4 = (f32[3,3,2,4,1,256]{5,4,3,2,1,0:T(1,128)S(1)}, f32[3,3,2,4,1,256]{5,4,3,2,1,0:T(1,128)S(1)}, u32[]{:S(2)}, u32[]{:S(2)}) collective-permute-start(f32[3,3,2,4,1,256]{5,4,3,2,1,0:T(1,128)S(1)} %slice_bitcast_fusion.9), channel_id=1, source_target_pairs={{0,1},{1,2},{2,3},{3,0},{4,5},{5,6},{6,7},{7,4},{8,9},{9,10},{10,1... | collective-permute-start | bytes 221192 | tf_op jit(solution)/shard_map/ppermute | solution.py:25
  22.8 6.2 %collective-permute-start.5 = (f32[3,3,2,1,4,256]{5,4,3,2,1,0:T(4,128)S(1)}, f32[3,3,2,1,4,256]{5,4,3,2,1,0:T(4,128)S(1)}, u32[]{:S(2)}, u32[]{:S(2)}) collective-permute-start(f32[3,3,2,1,4,256]{5,4,3,2,1,0:T(4,128)S(1)} %slice_bitcast_fusion.8), channel_id=1, source_target_pairs={{0,4},{4,8},{8,12},{12,0},{1,5},{5,9},{9,13},{13,1},{2,6},{6,10},{... | collective-permute-start | bytes 221192 | tf_op jit(solution)/shard_map/ppermute | solution.py:25
  36.5 14.8 %copy-start.3 = (bf16[4,16,3,2,4,256]{5,4,3,2,1,0:T(4,128)(2,1)S(1)}, bf16[4,16,3,2,4,256]{5,4,3,2,1,0:T(4,128)(2,1)}, u32[]{:S(2)}) copy-start(bf16[4,16,3,2,4,256]{5,4,3,2,1,0:T(4,128)(2,1)} %param.7) | copy-start | bytes 2359300
  36.5 16.5 %copy-start.4 = (u32[32]{0:T(128)S(1)}, u32[32]{0:T(128)}, u32[]{:S(2)}) copy-start(u32[32]{0:T(128)} %constant.72) | copy-start | bytes 388
  48.2 23.0 %copy-start.1 = (f32[4,4,3,2,4,4,256]{6,5,4,3,2,1,0:T(4,128)S(1)}, f32[4,4,3,2,4,4,256]{6,5,4,3,2,1,0:T(4,128)}, u32[]{:S(2)}) copy-start(f32[4,4,3,2,4,4,256]{6,5,4,3,2,1,0:T(4,128)} %shard_map.49) | copy-start | bytes 4718596
  50.3 14.1 %collective-permute-start.6 = (f32[4,4,3,2,1,4,256]{6,5,4,3,2,1,0:T(4,128)}, f32[4,4,3,2,1,4,256]{6,5,4,3,2,1,0:T(4,128)}, u32[]{:S(2)}, u32[]{:S(2)}) collective-permute-start(f32[4,4,3,2,1,4,256]{6,5,4,3,2,1,0:T(4,128)} %get-tuple-element.7), channel_id=1, source_target_pairs={{0,4},{4,8},{8,12},{12,0},{1,5},{5,9},{9,13},{13,1},{2,6},{6,10},{... | collective-permute-start | bytes 1179656 | tf_op jit(solution)/shard_map/ppermute | solution.py:25
  51.4 36.0 %collective-permute-start.10 = (bf16[4,16,3,2,4,256]{5,1,4,2,3,0:T(8,128)(2,1)S(1)}, bf16[4,16,3,2,4,256]{5,1,4,2,3,0:T(8,128)(2,1)}, u32[]{:S(2)}, u32[]{:S(2)}) collective-permute-start(bf16[4,16,3,2,4,256]{5,1,4,2,3,0:T(8,128)(2,1)S(1)} %copy.31), channel_id=1, source_target_pairs={{0,16},{16,0},{1,17},{17,1},{2,18},{18,2},{3,19},{19,3},{4,20},{20... | collective-permute-start | bytes 2359304 | tf_op jit(solution)/shard_map/ppermute | solution.py:29
  54.2 16.2 %collective-permute-start.9 = (f32[4,4,3,2,1,4,256]{6,5,4,3,2,1,0:T(4,128)S(1)}, f32[4,4,3,2,1,4,256]{6,5,4,3,2,1,0:T(4,128)S(1)}, u32[]{:S(2)}, u32[]{:S(2)}) collective-permute-start(f32[4,4,3,2,1,4,256]{6,5,4,3,2,1,0:T(4,128)S(1)} %get-tuple-element.8), channel_id=1, source_target_pairs={{0,12},{4,0},{8,4},{12,8},{1,13},{5,1},{9,5},{13,9},{2,14},{6,2},{... | collective-permute-start | bytes 1179656 | tf_op jit(solution)/shard_map/ppermute | solution.py:25
  60.0 10.5 %collective-permute-start.7 = (f32[4,4,3,2,4,1,256]{6,5,4,3,2,1,0:T(1,128)S(1)}, f32[4,4,3,2,4,1,256]{6,5,4,3,2,1,0:T(1,128)S(1)}, u32[]{:S(2)}, u32[]{:S(2)}) collective-permute-start(f32[4,4,3,2,4,1,256]{6,5,4,3,2,1,0:T(1,128)S(1)} %get-tuple-element.5), channel_id=1, source_target_pairs={{0,3},{1,0},{2,1},{3,2},{4,7},{5,4},{6,5},{7,6},{8,11},{9,8},{10,9... | collective-permute-start | bytes 1179656 | tf_op jit(solution)/shard_map/ppermute | solution.py:25
  60.1 11.1 %collective-permute-start.8 = (f32[4,4,3,2,4,1,256]{6,5,4,3,2,1,0:T(1,128)S(1)}, f32[4,4,3,2,4,1,256]{6,5,4,3,2,1,0:T(1,128)S(1)}, u32[]{:S(2)}, u32[]{:S(2)}) collective-permute-start(f32[4,4,3,2,4,1,256]{6,5,4,3,2,1,0:T(1,128)S(1)} %get-tuple-element.6), channel_id=1, source_target_pairs={{0,1},{1,2},{2,3},{3,0},{4,5},{5,6},{6,7},{7,4},{8,9},{9,10},{10,1... | collective-permute-start | bytes 1179656 | tf_op jit(solution)/shard_map/ppermute | solution.py:25
where the time goes:
time: 104 us
  waiting for transfers between devices  24.9 us (24%)
  Pallas kernels  23.4 us (22%)
  other arithmetic  15.6 us (15%)
  starting transfers between devices  12.8 us (12%)
  blocking collectives  11.3 us (11%)
  local copies, waits for them, and re-layouts  10.9 us (10%)
  matrix products  3.76 us (4%)
    ppermute x10, waiting for transfers between devices, passed_along(): return lax.ppermute(value, axis, pairs)  24.9 us
    pallas_call x2, Pallas kernels, hopping_step(): pl.pallas_call(hop_kernel, grid=(R,), in_specs=[spinor_block, link_block,...  23.4 us
    unnamed x1, blocking collectives  11.3 us
    ppermute x10, starting transfers between devices, passed_along(): return lax.ppermute(value, axis, pairs)  11.2 us
    concatenate x2, other arithmetic, padded_spinor(): jnp.concatenate([jnp.pad(t_lo, t_pad), middle, jnp.pad(t_hi, t_pad)], axi...  6.6 us
    slice x2, local copies, waits for them, and re-layouts, padded_spinor(): z_hi = passed_along(spinor[:, :, :, :, :, :1, :], 'sa', -1)  4.39 us
    dot_general x2, matrix products, intersection_part(): jnp.einsum('tvcazs,rqcbtzs->rqabtv', vector_piece, rounded, preferred_ele...  3.76 us
    slice x2, local copies, waits for them, and re-layouts, padded_spinor(): t_lo = passed_along(spinor[:, :, :, :, T - 1:, :, :], 'ta', 1) * lower_sign  3.34 us
  transfers between devices with their start and end apart: 11, of which 5 were waited for; matrix products, arithmetic and copies ran while one was open for 15% of the time, Pallas kernels for 11%

commit v1 on v0

--- a/solution.py
+++ b/solution.py
@@ -54,26 +54,37 @@
     return jnp.roll(operand, -stride * NX, axis=-1)
 
 
-def hop_kernel(p_ref, u_ref, b_ref, src_ref, out_ref):
-    T = out_ref.shape[3]
-    Z = out_ref.shape[4]
-    L = out_ref.shape[5]
-    rows = p_ref.shape[4]
+def hop_kernel(sign_ref, psi_ref, tlo_ref, thi_ref, zlo_ref, zhi_ref, u_ref, b_ref, src_ref, *rest):
+    out_ref = rest[0]
+    halo_refs = rest[1:-1]
+    pad_ref = rest[-1]
+    S, C, RI, T, Z, L = out_ref.shape
+    for s in range(S):
+        for c in range(C):
+            for ri in range(RI):
+                pad_ref[s, c, ri, pl.ds(1, T)] = psi_ref[s, c, ri]
+                pad_ref[s, c, ri, pl.ds(0, 1)] = tlo_ref[s, c, ri] * sign_ref[0]
+                pad_ref[s, c, ri, pl.ds(T + 1, 1)] = thi_ref[s, c, ri] * sign_ref[1]
     xpos = lax.broadcasted_iota(jnp.int32, (Z, L), 1) % NX
+    zpos = lax.broadcasted_iota(jnp.int32, (Z, L), 0)
     x_last = xpos == NX - 1
     x_first = xpos == 0
+    z_last = zpos == Z - 1
+    z_first = zpos == 0
 
     def body(t, carry):
         acc = [[[None, None] for _ in range(3)] for _ in range(4)]
 
         def shifted(s, c, ri, mu, stride):
             if mu == 3:
-                return p_ref[s, c, ri, t + 1 + stride, pl.ds(0, Z), :]
+                return pad_ref[s, c, ri, t + 1 + stride]
+            v = pad_ref[s, c, ri, t + 1]
             if mu == 2:
-                full = p_ref[s, c, ri, t + 1, :, :]
-                full = pltpu.roll(full, rows - 1 if stride == 1 else 1, axis=0)
-                return full[:Z]
-            v = p_ref[s, c, ri, t + 1, pl.ds(0, Z), :]
+                if stride == 1:
+                    halo = jnp.broadcast_to(zhi_ref[s, c, ri, t], (Z, L))
+                    return jnp.where(z_last, halo, pltpu.roll(v, Z - 1, axis=0))
+                halo = jnp.broadcast_to(zlo_ref[s, c, ri, t], (Z, L))
+                return jnp.where(z_first, halo, pltpu.roll(v, 1, axis=0))
             if mu == 1:
                 return pltpu.roll(v, (L - NX) if stride == 1 else NX, axis=1)
             if stride == 1:
@@ -104,16 +115,15 @@
                         sum_re = None
                         sum_im = None
                         for b in range(3):
+                            hre, him = half[k][b]
                             if stride == 1:
                                 lre = links[mu, a, b, 0, t]
                                 lim = links[mu, a, b, 1, t]
-                                hre, him = half[k][b]
                                 tre = lre * hre - lim * him
                                 tim = lre * him + lim * hre
                             else:
                                 lre = links[mu, b, a, 0, t]
                                 lim = links[mu, b, a, 1, t]
-                                hre, him = half[k][b]
                                 tre = lre * hre + lim * him
                                 tim = lre * him - lim * hre
                             sum_re = tre if sum_re is None else sum_re + tre
@@ -126,43 +136,67 @@
         for s in range(4):
             for c in range(3):
                 for ri in range(2):
-                    psi = p_ref[s, c, ri, t + 1, pl.ds(0, Z), :]
+                    psi = pad_ref[s, c, ri, t + 1]
                     src = src_ref[s, c, ri, t]
                     residual = src - (psi - kappa_hop * acc[s][c][ri])
                     out_ref[s, c, ri, t] = psi + residual
         return carry
 
     lax.fori_loop(0, T, body, 0)
-
-
-def hopping_step(padded, links, back_links, source):
+    if halo_refs:
+        tfirst_ref, tlast_ref, zfirst_ref, zlast_ref = halo_refs
+        for s in range(S):
+            for c in range(C):
+                for ri in range(RI):
+                    tfirst_ref[s, c, ri] = out_ref[s, c, ri, pl.ds(0, 1)]
+                    tlast_ref[s, c, ri] = out_ref[s, c, ri, pl.ds(T - 1, 1)]
+                    zfirst_ref[s, c, ri] = out_ref[s, c, ri, :, pl.ds(0, 1), :]
+                    zlast_ref[s, c, ri] = out_ref[s, c, ri, :, pl.ds(Z - 1, 1), :]
+
+
+def hopping_step(signs, spinor, halos, links, back_links, source, emit_halos):
     R, S, C, RI, T, Z, L = source.shape
-    rows = padded.shape[5]
-    spinor_block = pl.BlockSpec((None, S, C, RI, T + 2, rows, L), lambda r: (r, 0, 0, 0, 0, 0, 0))
+    index = lambda r: (r, 0, 0, 0, 0, 0, 0)
+    site_block = pl.BlockSpec((None, S, C, RI, T, Z, L), index)
+    t_block = pl.BlockSpec((None, S, C, RI, 1, Z, L), index)
+    z_block = pl.BlockSpec((None, S, C, RI, T, 1, L), index)
     link_block = pl.BlockSpec(links.shape, lambda r: (0,) * 7)
-    site_block = pl.BlockSpec((None, S, C, RI, T, Z, L), lambda r: (r, 0, 0, 0, 0, 0, 0))
+    out_shape = [jax.ShapeDtypeStruct(source.shape, jnp.float32)]
+    out_specs = [site_block]
+    if emit_halos:
+        t_shape = jax.ShapeDtypeStruct((R, S, C, RI, 1, Z, L), jnp.float32)
+        z_shape = jax.ShapeDtypeStruct((R, S, C, RI, T, 1, L), jnp.float32)
+        out_shape += [t_shape, t_shape, z_shape, z_shape]
+        out_specs += [t_block, t_block, z_block, z_block]
     return pl.pallas_call(
         hop_kernel,
         grid=(R,),
-        in_specs=[spinor_block, link_block, link_block, site_block],
-        out_specs=site_block,
-        out_shape=jax.ShapeDtypeStruct(source.shape, jnp.float32),
+        in_specs=[pl.BlockSpec(memory_space=pltpu.SMEM), site_block, t_block, t_block, z_block, z_block,
+                  link_block, link_block, site_block],
+        out_specs=out_specs,
+        out_shape=out_shape,
+        scratch_shapes=[pltpu.VMEM((S, C, RI, T + 2, Z, L), jnp.float32)],
         compiler_params=pltpu.CompilerParams(dimension_semantics=("arbitrary",)),
         interpret=INTERPRET,
-    )(padded, links, back_links, source)
-
-
-def padded_spinor(spinor, lower_sign, upper_sign):
-    R, S, C, RI, T, Z, L = spinor.shape
-    rows = -(-(Z + 2) // 8) * 8
-    t_lo = passed_along(spinor[:, :, :, :, T - 1:, :, :], "ta", 1) * lower_sign
-    t_hi = passed_along(spinor[:, :, :, :, :1, :, :], "ta", -1) * upper_sign
-    z_lo = passed_along(spinor[:, :, :, :, :, Z - 1:, :], "sa", 1)
-    z_hi = passed_along(spinor[:, :, :, :, :, :1, :], "sa", -1)
-    gap = jnp.zeros((R, S, C, RI, T, rows - Z - 2, L), jnp.float32)
-    middle = jnp.concatenate([spinor, z_hi, gap, z_lo], axis=5)
-    t_pad = ((0, 0),) * 5 + ((0, rows - Z), (0, 0))
-    return jnp.concatenate([jnp.pad(t_lo, t_pad), middle, jnp.pad(t_hi, t_pad)], axis=4)
+    )(signs, spinor, *halos, links, back_links, source)
+
+
+def reduce_scatter_sa(partial_value):
+    n = lax.axis_size("sa")
+    if n & (n - 1):
+        return lax.psum_scatter(partial_value, "sa", scatter_dimension=4, tiled=True)
+    lead = partial_value.shape[:-1]
+    width = partial_value.shape[-1] // n
+    x = jnp.moveaxis(partial_value.reshape(lead + (n, width)), -2, 0)
+    me = lax.axis_index("sa")
+    d = n // 2
+    while d >= 1:
+        upper_mine = (me // d) % 2 == 1
+        keep = jnp.where(upper_mine, x[d:], x[:d])
+        send = jnp.where(upper_mine, x[:d], x[d:])
+        x = keep + lax.ppermute(send, "sa", [(j, j ^ d) for j in range(n)])
+        d //= 2
+    return x[0]
 
 
 def intersection_part(rounded, vector_piece):
@@ -178,20 +212,37 @@
     partner_vectors = from_partner(vectors, "sec", 0)
     batch_rows = noise_slabs.shape[0]
     slab_length = gauge_links.shape[4]
+    Z = gauge_links.shape[5]
+    K = noise_slabs.shape[3]
     section_index = lax.axis_index("sec")
     slab_index = lax.axis_index("ta")
     slab_count = lax.axis_size("ta")
     lower_sign = jnp.where(slab_index == 0, -1.0, 1.0).astype(jnp.float32)
     upper_sign = jnp.where(slab_index == slab_count - 1, -1.0, 1.0).astype(jnp.float32)
-    filled = jnp.repeat(noise_slabs, TDIL, axis=3)
-    global_time = slab_index * slab_length + jnp.arange(slab_length)
+    signs = jnp.stack([lower_sign, upper_sign])
+    t_start = slab_index * slab_length
+    global_time = t_start + jnp.arange(slab_length)
     own_offsets = lax.dynamic_slice_in_dim(offsets, section_index * batch_rows, batch_rows)
-    time_mask = (global_time[None, :] % TDIL == own_offsets[:, None]).astype(jnp.float32)
     rhs_index = section_index * batch_rows + jnp.arange(batch_rows)
     spin_mask = (jnp.arange(4)[None, :] == rhs_index[:, None] % 4).astype(jnp.float32)
-    source = (
-        spin_mask[:, :, None, None, None, None, None]
-        * (filled * time_mask[:, None, None, :, None, None])[:, None]
+
+    def make_source(noise_t, times):
+        time_mask = (times[None, :] % TDIL == own_offsets[:, None]).astype(jnp.float32)
+        return (
+            spin_mask[:, :, None, None, None, None, None]
+            * (noise_t * time_mask[:, None, None, :, None, None])[:, None]
+        )
+
+    source = make_source(jnp.repeat(noise_slabs, TDIL, axis=3), global_time)
+    noise_t_lo = passed_along(noise_slabs[:, :, :, K - 1:], "ta", 1)
+    noise_t_hi = passed_along(noise_slabs[:, :, :, :1], "ta", -1)
+    noise_z_lo = passed_along(noise_slabs[:, :, :, :, Z - 1:], "sa", 1)
+    noise_z_hi = passed_along(noise_slabs[:, :, :, :, :1], "sa", -1)
+    halos = (
+        make_source(noise_t_lo, t_start - 1 + jnp.arange(1)),
+        make_source(noise_t_hi, t_start + slab_length + jnp.arange(1)),
+        make_source(jnp.repeat(noise_z_lo, TDIL, axis=3), global_time),
+        make_source(jnp.repeat(noise_z_hi, TDIL, axis=3), global_time),
     )
     time_edge = passed_along(gauge_links[3, :, :, :, -1:, :, :], "ta", 1)
     space_edge = passed_along(gauge_links[2, :, :, :, :, -1:, :], "sa", 1)
@@ -204,16 +255,25 @@
         ]
     )
     spinor = source
-    for _ in range(ITERS):
-        padded = padded_spinor(spinor, lower_sign, upper_sign)
-        spinor = hopping_step(padded, gauge_links, back_links, source)
+    for step in range(ITERS):
+        last = step == ITERS - 1
+        result = hopping_step(signs, spinor, halos, gauge_links, back_links, source, not last)
+        spinor = result[0]
+        if not last:
+            t_first, t_last, z_first, z_last = result[1:]
+            halos = (
+                passed_along(t_last, "ta", 1),
+                passed_along(t_first, "ta", -1),
+                passed_along(z_last, "sa", 1),
+                passed_along(z_first, "sa", -1),
+            )
     rounded = spinor.astype(jnp.bfloat16)
     own_part = intersection_part(rounded, vectors)
     partner_part = intersection_part(rounded, partner_vectors)
     lower_half = jnp.where(section_index == 0, own_part, partner_part)
     upper_half = jnp.where(section_index == 0, partner_part, own_part)
     partial_value = jnp.concatenate([lower_half, upper_half], axis=4)
-    return lax.psum_scatter(partial_value, "sa", scatter_dimension=4, tiled=True)
+    return reduce_scatter_sa(partial_value)
 
 
 def solution(mesh):

time: 104 us -> 82.4 us (0.79)
  blocking collectives: 11.3 us -> 0 us
  other arithmetic: 15.6 us -> 10.3 us
  local copies, waits for them, and re-layouts: 10.9 us -> 6.45 us
  waiting for transfers between devices: 24.9 us -> 22.8 us
  starting transfers between devices: 12.8 us -> 14.4 us
    unnamed x1 -> x0, blocking collectives: 11.3 us -> none
    ppermute x10, waiting for transfers between devices: 24.9 us -> 16.6 us  [passed_along(): return lax.ppermute(value, axis, pairs)]
    slice x4 -> x1, local copies, waits for them, and re-layouts: 7.73 us -> 1.01 us  [local(): noise_z_hi = passed_along(noise_slabs[:, :, :, :, :1], 'sa', -1)]
    concatenate x3 -> x0, other arithmetic: 6.7 us -> none  [the longest x2 6.6 us: padded_spinor(): jnp.concatenate([jnp.pad(t_lo, t_pad), middle, jnp.pad(t_hi, t_pad)], axi...]
    ppermute x0 -> x2, waiting for transfers between devices: none -> 6.18 us  [reduce_scatter_sa(): x = keep + lax.ppermute(send, 'sa', [(j, j ^ d) for j in range(n)])]
    ppermute x10, starting transfers between devices: 11.2 us -> 12.7 us  [passed_along(): return lax.ppermute(value, axis, pairs)]
    unnamed x13 -> x21, local copies, waits for them, and re-layouts: 0.86 us -> 2.18 us
    squeeze x1, local copies, waits for them, and re-layouts: 0.07 us -> 1.11 us  [local(): gauge_links[0]]
  transfers between devices with their start and end apart: 11 -> 13, of which waited for: 5 -> 5; matrix products, arithmetic and copies ran while one was open for 15% -> 17% of each run, Pallas kernels for 11% -> 14%
where the time goes in v1:
time: 82.4 us; the launch traced here: 82.1 us
  Pallas kernels  24.1 us (29%)
  waiting for transfers between devices  22.8 us (28%)
  starting transfers between devices  14.4 us (17%)
  other arithmetic  10.3 us (12%)
  local copies, waits for them, and re-layouts  6.45 us (8%)
  matrix products  3.65 us (4%)
    pallas_call x2, Pallas kernels, hopping_step(): pl.pallas_call(hop_kernel, grid=(R,), in_specs=[pl.BlockSpec(memory_space...  24.1 us
    ppermute x10, waiting for transfers between devices, passed_along(): return lax.ppermute(value, axis, pairs)  16.6 us
    ppermute x10, starting transfers between devices, passed_along(): return lax.ppermute(value, axis, pairs)  12.7 us
    ppermute x2, waiting for transfers between devices, reduce_scatter_sa(): x = keep + lax.ppermute(send, 'sa', [(j, j ^ d) for j in range(n)])  6.18 us
    mul x5, other arithmetic, make_source(): spin_mask[:, :, None, None, None, None, None]  4.46 us
    dot_general x2, matrix products, intersection_part(): jnp.einsum('tvcazs,rqcbtzs->rqabtv', vector_piece, rounded, preferred_ele...  3.65 us
    unnamed x21, local copies, waits for them, and re-layouts  2.18 us
    another operation x4, other arithmetic, local(): jnp.stack([move_first(gauge_links[0], -1), move_second(gauge_links[1], -1...  1.79 us
  transfers between devices with their start and end apart: 13, of which 5 were waited for; matrix products, arithmetic and copies ran while one was open for 17% of the time, Pallas kernels for 14%

profile of v1, /device:TPU:0, one launch (start us, length us, event | category | flops | bytes accessed | tf_op | source)
XLA Modules:
  0.0 82.1 jit_solution(14683263814652941207)
XLA Ops:
  0.0 3.1 %collective-permute-start = (f32[4,3,2,1,4,256]{5,4,3,2,1,0:T(4,128)}, f32[4,3,2,1,4,256]{5,4,3,2,1,0:T(4,128)S(1)}, u32[]{:S(2)}, u32[]{:S(2)}) collective-permute-start(f32[4,3,2,1,4,256]{5,4,3,2,1,0:T(4,128)} %param.5), channel_id=1, source_target_pairs={{0,4},{4,8},{8,12},{12,0},{1,5},{5,9},{9,13},{13,1},{2,6},{6,10},{... | collective-permute-start | bytes 294920 | tf_op jit(solution)/shard_map/ppermute | solution.py:25
  3.1 2.0 %collective-permute-start.1 = (f32[4,3,2,1,4,256]{5,4,3,2,1,0:T(4,128)}, f32[4,3,2,1,4,256]{5,4,3,2,1,0:T(4,128)S(1)}, u32[]{:S(2)}, u32[]{:S(2)}) collective-permute-start(f32[4,3,2,1,4,256]{5,4,3,2,1,0:T(4,128)} %param.5), channel_id=1, source_target_pairs={{0,12},{4,0},{8,4},{12,8},{1,13},{5,1},{9,5},{13,9},{2,14},{6,2},{... | collective-permute-start | bytes 294920 | tf_op jit(solution)/shard_map/ppermute | solution.py:25
  5.1 1.0 %fusion.8 = (f32[4,3,2,1,1,256]{5,4,3,2,1,0:T(1,128)S(1)}, f32[4,3,2,1,1,256]{5,4,3,2,1,0:T(1,128)S(1)}) fusion(f32[4,3,2,1,4,256]{5,4,3,2,1,0:T(4,128)} %param.5), kind=kLoop, calls=%fused_computation.65 | loop fusion | bytes 98304 | tf_op jit(solution)/shard_map/slice | solution.py:240
  6.1 0.7 collective-permute-start.3
  6.8 1.0 %slice_bitcast_fusion.9 = f32[3,3,2,4,1,256]{5,4,3,2,1,0:T(1,128)S(1)} fusion(f32[4,3,3,2,4,4,256]{6,5,4,3,2,1,0:T(4,128)} %u_ref.3), kind=kLoop, calls=%fused_computation.32 | loop fusion | bytes 147456 | tf_op jit(solution)/shard_map/squeeze | solution.py:248
  7.9 1.3 %collective-permute-start.4 = (f32[3,3,2,4,1,256]{5,4,3,2,1,0:T(1,128)S(1)}, f32[3,3,2,4,1,256]{5,4,3,2,1,0:T(1,128)S(1)}, u32[]{:S(2)}, u32[]{:S(2)}) collective-permute-start(f32[3,3,2,4,1,256]{5,4,3,2,1,0:T(1,128)S(1)} %slice_bitcast_fusion.9), channel_id=1, source_target_pairs={{0,1},{1,2},{2,3},{3,0},{4,5},{5,6},{6,7},{7,4},{8,9},{9,10},{10,1... | collective-permute-start | bytes 221192 | tf_op jit(solution)/shard_map/ppermute | solution.py:25
  9.2 1.1 %slice_bitcast_fusion.4 = (f32[3,3,2,4,4,256]{5,4,3,2,1,0:T(4,128)S(1)}, f32[3,3,2,4,4,256]{5,4,3,2,1,0:T(4,128)S(1)}) fusion(f32[4,3,3,2,4,4,256]{6,5,4,3,2,1,0:T(4,128)} %u_ref.3), kind=kLoop, calls=%fused_computation.17 | loop fusion | bytes 1179648 | tf_op jit(solution)/shard_map/squeeze | solution.py:251
  10.3 0.2 slice_bitcast_fusion.1
  10.6 0.1 slice_bitcast_fusion.6
  10.8 0.8 copy-done
  11.7 0.1 compare_convert_fusion
  11.9 0.1 slice.118
  12.0 0.1 broadcast_multiply_fusion.5
  12.2 1.7 %broadcast_multiply_fusion.psi_ref.src_ref = f32[4,4,3,2,4,4,256]{6,5,4,3,2,1,0:T(4,128)} fusion(f32[4,3,2,4,4,256]{5,4,3,2,1,0:T(4,128)S(1)} %broadcast_multiply_fusion.5, f32[4,4]{1,0:T(4,128)S(1)} %fusion.4), kind=kLoop, calls=%fused_computation.6 | loop fusion | flops 393216 | bytes 1966144 | tf_op jit(solution)/shard_map/mul | solution.py:232
  13.8 0.2 maximum_bitcast_fusion
  14.1 0.3 maximum_select_fusion
  14.4 0.6 pad_maximum_fusion.1.sign_ref
  15.0 0.1 broadcast_multiply_fusion.6
  15.2 1.5 %broadcast_multiply_fusion.1 = (f32[4,4,3,2,4,1,256]{6,5,4,3,2,1,0:T(1,128)}, f32[4,4,3,2,4,1,256]{6,5,4,3,2,1,0:T(1,128)}) fusion(f32[4,3,2,4,256]{4,3,2,1,0:T(4,128)S(1)} %get-tuple-element.29, f32[4,4]{1,0:T(4,128)S(1)} %fusion.4, f32[4,3,2,4,256]{4,3,2,1,0:T(4,128)S(1)} %get-tuple-element.30), kind=kLoop, calls=%fused_computation.20 | loop fusion | flops 196608 | bytes 983104 | tf_op jit(solution)/shard_map/mul | solution.py:232
  16.7 0.1 maximum_bitcast_fusion.1
  16.8 4.6 %collective-permute-done.5 = f32[3,3,2,1,4,256]{5,4,3,2,1,0:T(4,128)S(1)} collective-permute-done((f32[3,3,2,1,4,256]{5,4,3,2,1,0:T(4,128)S(1)}, f32[3,3,2,1,4,256]{5,4,3,2,1,0:T(4,128)S(1)}, u32[]{:S(2)}, u32[]{:S(2)}) %collective-permute-start.5) | collective-permute-done | bytes 73760 | tf_op jit(solution)/shard_map/ppermute | solution.py:25
  21.4 0.1 maximum_bitcast_fusion.2
  21.5 1.4 %pad_maximum_fusion.b_ref = f32[4,3,3,2,4,4,256]{6,5,4,3,2,1,0:T(4,128)} fusion(f32[1,3,3,2,4,4,256]{6,5,4,3,2,1,0:T(4,128)S(1)} %maximum_bitcast_fusion.2, f32[1,3,3,2,4,4,256]{6,5,4,3,2,1,0:T(4,128)S(1)} %maximum_bitcast_fusion.1, f32[1,3,3,2,4,4,256]{6,5,4,3,2,1,0:T(4,128)S(1)} %maximum_bitcast_fusion, f32[1,3,3,2,4,4,256]{6,5,4,3,2,1,0:T(4,128)S(1)} %maximum_select_fusion), kind=kLoop, calls=%fused_computation | loop fusion | flops 884736 | bytes 2359296 | tf_op jit(solution)/shard_map/stack | solution.py:249
  22.9 0.1 multiply_bitcast_fusion.1
  23.0 0.1 multiply_bitcast_fusion
  23.0 1.1 %broadcast_multiply_fusion.3 = (f32[4,4,3,2,1,4,256]{6,5,4,3,2,1,0:T(4,128)}, f32[4,4,3,2,1,4,256]{6,5,4,3,2,1,0:T(4,128)}) fusion(f32[4,3,2,4,256]{4,3,2,1,0:T(4,128)S(1)} %multiply_bitcast_fusion, f32[4,4]{1,0:T(4,128)S(1)} %fusion.4, f32[4,3,2,4,256]{4,3,2,1,0:T(4,128)S(1)} %multiply_bitcast_fusion.1), kind=kLoop, calls=%fused_computation.22 | loop fusion | flops 196608 | bytes 983104 | tf_op jit(solution)/shard_map/mul | solution.py:232
  24.1 12.3 %shard_map.49 = (f32[4,4,3,2,4,4,256]{6,5,4,3,2,1,0:T(4,128)}, f32[4,4,3,2,1,4,256]{6,5,4,3,2,1,0:T(4,128)}, f32[4,4,3,2,1,4,256]{6,5,4,3,2,1,0:T(4,128)}, f32[4...) custom-call(f32[2]{0:T(128)} %pad_maximum_fusion.1.sign_ref, ...), custom_call_target="tpu_custom_call" | custom-call | tf_op jit(solution)/shard_map/pallas_call | solution.py:171
  36.5 3.8 %collective-permute-start.7 = (f32[4,4,3,2,1,4,256]{6,5,4,3,2,1,0:T(4,128)}, f32[4,4,3,2,1,4,256]{6,5,4,3,2,1,0:T(4,128)S(1)}, u32[]{:S(2)}, u32[]{:S(2)}) collective-permute-start(f32[4,4,3,2,1,4,256]{6,5,4,3,2,1,0:T(4,128)} %get-tuple-element.12), channel_id=1, source_target_pairs={{0,12},{4,0},{8,4},{12,8},{1,13},{5,1},{9,5},{13,9},{2,14},{6,2},{... | collective-permute-start | bytes 1179656 | tf_op jit(solution)/shard_map/ppermute | solution.py:25
  40.3 1.7 %collective-permute-start.9 = (f32[4,4,3,2,4,1,256]{6,5,4,3,2,1,0:T(1,128)}, f32[4,4,3,2,4,1,256]{6,5,4,3,2,1,0:T(1,128)S(1)}, u32[]{:S(2)}, u32[]{:S(2)}) collective-permute-start(f32[4,4,3,2,4,1,256]{6,5,4,3,2,1,0:T(1,128)} %get-tuple-element.14), channel_id=1, source_target_pairs={{0,3},{1,0},{2,1},{3,2},{4,7},{5,4},{6,5},{7,6},{8,11},{9,8},{10,9... | collective-permute-start | bytes 1179656 | tf_op jit(solution)/shard_map/ppermute | solution.py:25
  42.1 0.2 copy.21
  42.3 1.6 %collective-permute-start.10 = (bf16[4,16,3,2,4,256]{5,1,4,2,3,0:T(8,128)(2,1)S(1)}, bf16[4,16,3,2,4,256]{5,1,4,2,3,0:T(8,128)(2,1)}, u32[]{:S(2)}, u32[]{:S(2)}) collective-permute-start(bf16[4,16,3,2,4,256]{5,1,4,2,3,0:T(8,128)(2,1)S(1)} %copy.21), channel_id=1, source_target_pairs={{0,16},{16,0},{1,17},{17,1},{2,18},{18,2},{3,19},{19,3},{4,20},{20... | collective-permute-start | bytes 2359304 | tf_op jit(solution)/shard_map/ppermute | solution.py:29
  43.8 6.7 %collective-permute-done.6.tlo_ref = f32[4,4,3,2,1,4,256]{6,5,4,3,2,1,0:T(4,128)S(1)} collective-permute-done((f32[4,4,3,2,1,4,256]{6,5,4,3,2,1,0:T(4,128)}, f32[4,4,3,2,1,4,256]{6,5,4,3,2,1,0:T(4,128)S(1)}, u32[]{:S(2)}, u32[]{:S(2)}) %collective-permute-start.6) | collective-permute-done | bytes 393248 | tf_op jit(solution)/shard_map/ppermute | solution.py:25
  50.5 5.3 %collective-permute-done.7.thi_ref = f32[4,4,3,2,1,4,256]{6,5,4,3,2,1,0:T(4,128)S(1)} collective-permute-done((f32[4,4,3,2,1,4,256]{6,5,4,3,2,1,0:T(4,128)}, f32[4,4,3,2,1,4,256]{6,5,4,3,2,1,0:T(4,128)S(1)}, u32[]{:S(2)}, u32[]{:S(2)}) %collective-permute-start.7) | collective-permute-done | bytes 393248 | tf_op jit(solution)/shard_map/ppermute | solution.py:25
  55.9 0.7 copy-done.3
  56.6 0.2 copy-done.4
  56.7 0.2 copy-done.5
  56.9 11.7 %shard_map.50 = f32[4,4,3,2,4,4,256]{6,5,4,3,2,1,0:T(4,128)} custom-call(f32[2]{0:T(128)} %pad_maximum_fusion.1.sign_ref, f32[4,4,3,2,4,4,256]{6,5,4,3,2,1,0:T(4,128)} %get-tuple-element.10.psi_ref, f32[4,4,3,2,1,4,256]{6,5,4,3,2,1,0:T(4,128)} %copy-done.2, f32[4,4,3,2,1,4,256]{6,5,4,3,2,1,0:T(4,128)} %copy-done.3, f32[4,4,3,2,4,1,256]{6,5,4,3,2,1,0:T(1,128)} %copy-done.4, ...), custom_call_target="tpu_custom_call" | custom-call | tf_op jit(solution)/shard_map/pallas_call | solution.py:171
  68.7 1.8 %convert_bitcast_fusion = bf16[4,4,3,2,4,4,256,1]{6,5,4,3,2,1,0,7:T(4,128)(2,1)S(1)} fusion(f32[4,4,3,2,4,4,256]{6,5,4,3,2,1,0:T(4,128)} %shard_map.50), kind=kLoop, calls=%fused_computation.5 | loop fusion | flops 393216 | bytes 2359296 | tf_op jit(solution)/shard_map/convert_element_type | solution.py:270
  70.4 1.3 %convolution_bitcast_fusion.1 = f32[4,4,2,2,4,16]{5,1,2,3,0,4:T(4,128)S(1)} fusion(bf16[4,16,3,2,4,256,1,1]{5,4,3,2,1,0,7,6:T(4,128)(2,1)S(1)} %bitcast.84, bf16[4,4,3,2,4,4,256,1]{6,5,4,3,2,1,0,7:T(4,128)(2,1)S(1)} %convert_bitcast_fusion), kind=kOutput, calls=%fused_computation.2 | convolution fusion | flops 25165824 | bytes 1589248 | tf_op jit(solution)/shard_map/tvcazs,rqcbtzs->rqabtv/dot_general | solution.py:203
  71.7 0.1 add.126
  71.9 0.1 sub.39
  72.0 2.4 %convolution_bitcast_fusion = f32[4,4,2,2,4,16]{5,1,2,3,0,4:T(4,128)S(1)} fusion(bf16[4,16,3,2,4,256]{5,1,4,2,3,0:T(8,128)(2,1)} %collective-permute-done.10, bf16[4,4,3,2,4,4,256,1]{6,5,4,3,2,1,0,7:T(4,128)(2,1)S(1)} %convert_bitcast_fusion), kind=kOutput, calls=%fused_computation.1 | convolution fusion | flops 25165824 | bytes 1589248 | tf_op jit(solution)/shard_map/tvcazs,rqcbtzs->rqabtv/dot_general | solution.py:203
  74.4 0.1 add.128
  74.6 0.1 sub.41
  74.7 0.1 copy_dynamic-update-slice_fusion
  75.1 4.9 %collective-permute-done.11 = f32[2,4,4,2,4,8]{5,4,3,2,1,0:T(4,128)S(1)} collective-permute-done((f32[2,4,4,2,4,8]{5,4,3,2,1,0:T(4,128)S(1)}, f32[2,4,4,2,4,8]{5,4,3,2,1,0:T(4,128)S(1)}, u32[]{:S(2)}, u32[]{:S(2)}) %collective-permute-start.11) | collective-permute-done | bytes 8224 | tf_op jit(solution)/shard_map/ppermute | solution.py:197
  80.2 1.2 %collective-permute-done.12 = f32[1,4,4,2,4,8]{5,4,3,2,1,0:T(4,128)S(1)} collective-permute-done((f32[1,4,4,2,4,8]{5,4,3,2,1,0:T(4,128)S(1)}, f32[1,4,4,2,4,8]{5,4,3,2,1,0:T(4,128)S(1)}, u32[]{:S(2)}, u32[]{:S(2)}) %collective-permute-start.12) | collective-permute-done | bytes 4128 | tf_op jit(solution)/shard_map/ppermute | solution.py:197
  81.4 0.7 add_bitcast_fusion
  (48 shorter events, 0.9 us)
Async XLA Ops:
  0.0 22.9 %collective-permute-start = (f32[4,3,2,1,4,256]{5,4,3,2,1,0:T(4,128)}, f32[4,3,2,1,4,256]{5,4,3,2,1,0:T(4,128)S(1)}, u32[]{:S(2)}, u32[]{:S(2)}) collective-permute-start(f32[4,3,2,1,4,256]{5,4,3,2,1,0:T(4,128)} %param.5), channel_id=1, source_target_pairs={{0,4},{4,8},{8,12},{12,0},{1,5},{5,9},{9,13},{13,1},{2,6},{6,10},{... | collective-permute-start | bytes 294920 | tf_op jit(solution)/shard_map/ppermute | solution.py:25
  3.1 19.9 %collective-permute-start.1 = (f32[4,3,2,1,4,256]{5,4,3,2,1,0:T(4,128)}, f32[4,3,2,1,4,256]{5,4,3,2,1,0:T(4,128)S(1)}, u32[]{:S(2)}, u32[]{:S(2)}) collective-permute-start(f32[4,3,2,1,4,256]{5,4,3,2,1,0:T(4,128)} %param.5), channel_id=1, source_target_pairs={{0,12},{4,0},{8,4},{12,8},{1,13},{5,1},{9,5},{13,9},{2,14},{6,2},{... | collective-permute-start | bytes 294920 | tf_op jit(solution)/shard_map/ppermute | solution.py:25
  6.1 8.9 %collective-permute-start.3 = (f32[4,3,2,1,1,256]{5,4,3,2,1,0:T(1,128)S(1)}, f32[4,3,2,1,1,256]{5,4,3,2,1,0:T(1,128)S(1)}, u32[]{:S(2)}, u32[]{:S(2)}) collective-permute-start(f32[4,3,2,1,1,256]{5,4,3,2,1,0:T(1,128)S(1)} %get-tuple-element.25), channel_id=1, source_target_pairs={{0,3},{1,0},{2,1},{3,2},{4,7},{5,4},{6,5},{7,6},{8,11},{9,8},{10,9... | collective-permute-start | bytes 73736 | tf_op jit(solution)/shard_map/ppermute | solution.py:25
  6.8 8.2 %collective-permute-start.2 = (f32[4,3,2,1,1,256]{5,4,3,2,1,0:T(1,128)S(1)}, f32[4,3,2,1,1,256]{5,4,3,2,1,0:T(1,128)S(1)}, u32[]{:S(2)}, u32[]{:S(2)}) collective-permute-start(f32[4,3,2,1,1,256]{5,4,3,2,1,0:T(1,128)S(1)} %get-tuple-element.26), channel_id=1, source_target_pairs={{0,1},{1,2},{2,3},{3,0},{4,5},{5,6},{6,7},{7,4},{8,9},{9,10},{10,1... | collective-permute-start | bytes 73736 | tf_op jit(solution)/shard_map/ppermute | solution.py:25
  7.9 8.8 %collective-permute-start.4 = (f32[3,3,2,4,1,256]{5,4,3,2,1,0:T(1,128)S(1)}, f32[3,3,2,4,1,256]{5,4,3,2,1,0:T(1,128)S(1)}, u32[]{:S(2)}, u32[]{:S(2)}) collective-permute-start(f32[3,3,2,4,1,256]{5,4,3,2,1,0:T(1,128)S(1)} %slice_bitcast_fusion.9), channel_id=1, source_target_pairs={{0,1},{1,2},{2,3},{3,0},{4,5},{5,6},{6,7},{7,4},{8,9},{9,10},{10,1... | collective-permute-start | bytes 221192 | tf_op jit(solution)/shard_map/ppermute | solution.py:25
  10.3 1.3 %copy-start = (f32[4,3,3,2,4,4,256]{6,5,4,3,2,1,0:T(4,128)S(1)}, f32[4,3,3,2,4,4,256]{6,5,4,3,2,1,0:T(4,128)}, u32[]{:S(2)}) copy-start(f32[4,3,3,2,4,4,256]{6,5,4,3,2,1,0:T(4,128)} %u_ref.3) | copy-start | bytes 3538948
  10.3 1.4 %copy-start.7 = (s32[8]{0:T(128)S(1)}, s32[8]{0:T(128)}, u32[]{:S(2)}) copy-start(s32[8]{0:T(128)} %param.6) | copy-start | bytes 100
  10.6 1.5 %copy-start.6 = (f32[4,3,2,1,4,256]{5,4,3,2,1,0:T(4,128)S(1)}, f32[4,3,2,1,4,256]{5,4,3,2,1,0:T(4,128)}, u32[]{:S(2)}) copy-start(f32[4,3,2,1,4,256]{5,4,3,2,1,0:T(4,128)} %param.5) | copy-start | bytes 294916
  15.0 6.4 %collective-permute-start.5 = (f32[3,3,2,1,4,256]{5,4,3,2,1,0:T(4,128)S(1)}, f32[3,3,2,1,4,256]{5,4,3,2,1,0:T(4,128)S(1)}, u32[]{:S(2)}, u32[]{:S(2)}) collective-permute-start(f32[3,3,2,1,4,256]{5,4,3,2,1,0:T(4,128)S(1)} %slice_bitcast_fusion.8), channel_id=1, source_target_pairs={{0,4},{4,8},{8,12},{12,0},{1,5},{5,9},{9,13},{13,1},{2,6},{6,10},{... | collective-permute-start | bytes 221192 | tf_op jit(solution)/shard_map/ppermute | solution.py:25
  24.1 18.0 %copy-start.1 = (bf16[4,16,3,2,4,256]{5,4,3,2,1,0:T(4,128)(2,1)S(1)}, bf16[4,16,3,2,4,256]{5,4,3,2,1,0:T(4,128)(2,1)}, u32[]{:S(2)}) copy-start(bf16[4,16,3,2,4,256]{5,4,3,2,1,0:T(4,128)(2,1)} %param.7) | copy-start | bytes 2359300
  36.5 14.0 %collective-permute-start.6 = (f32[4,4,3,2,1,4,256]{6,5,4,3,2,1,0:T(4,128)}, f32[4,4,3,2,1,4,256]{6,5,4,3,2,1,0:T(4,128)S(1)}, u32[]{:S(2)}, u32[]{:S(2)}) collective-permute-start(f32[4,4,3,2,1,4,256]{6,5,4,3,2,1,0:T(4,128)} %get-tuple-element.11), channel_id=1, source_target_pairs={{0,4},{4,8},{8,12},{12,0},{1,5},{5,9},{9,13},{13,1},{2,6},{6,10},{... | collective-permute-start | bytes 1179656 | tf_op jit(solution)/shard_map/ppermute | solution.py:25
  36.5 19.3 %collective-permute-start.7 = (f32[4,4,3,2,1,4,256]{6,5,4,3,2,1,0:T(4,128)}, f32[4,4,3,2,1,4,256]{6,5,4,3,2,1,0:T(4,128)S(1)}, u32[]{:S(2)}, u32[]{:S(2)}) collective-permute-start(f32[4,4,3,2,1,4,256]{6,5,4,3,2,1,0:T(4,128)} %get-tuple-element.12), channel_id=1, source_target_pairs={{0,12},{4,0},{8,4},{12,8},{1,13},{5,1},{9,5},{13,9},{2,14},{6,2},{... | collective-permute-start | bytes 1179656 | tf_op jit(solution)/shard_map/ppermute | solution.py:25
  40.3 15.5 %collective-permute-start.8 = (f32[4,4,3,2,4,1,256]{6,5,4,3,2,1,0:T(1,128)}, f32[4,4,3,2,4,1,256]{6,5,4,3,2,1,0:T(1,128)S(1)}, u32[]{:S(2)}, u32[]{:S(2)}) collective-permute-start(f32[4,4,3,2,4,1,256]{6,5,4,3,2,1,0:T(1,128)} %get-tuple-element.13), channel_id=1, source_target_pairs={{0,1},{1,2},{2,3},{3,0},{4,5},{5,6},{6,7},{7,4},{8,9},{9,10},{10,1... | collective-permute-start | bytes 1179656 | tf_op jit(solution)/shard_map/ppermute | solution.py:25
  40.3 15.5 %collective-permute-start.9 = (f32[4,4,3,2,4,1,256]{6,5,4,3,2,1,0:T(1,128)}, f32[4,4,3,2,4,1,256]{6,5,4,3,2,1,0:T(1,128)S(1)}, u32[]{:S(2)}, u32[]{:S(2)}) collective-permute-start(f32[4,4,3,2,4,1,256]{6,5,4,3,2,1,0:T(1,128)} %get-tuple-element.14), channel_id=1, source_target_pairs={{0,3},{1,0},{2,1},{3,2},{4,7},{5,4},{6,5},{7,6},{8,11},{9,8},{10,9... | collective-permute-start | bytes 1179656 | tf_op jit(solution)/shard_map/ppermute | solution.py:25
  42.3 29.8 %collective-permute-start.10 = (bf16[4,16,3,2,4,256]{5,1,4,2,3,0:T(8,128)(2,1)S(1)}, bf16[4,16,3,2,4,256]{5,1,4,2,3,0:T(8,128)(2,1)}, u32[]{:S(2)}, u32[]{:S(2)}) collective-permute-start(bf16[4,16,3,2,4,256]{5,1,4,2,3,0:T(8,128)(2,1)S(1)} %copy.21), channel_id=1, source_target_pairs={{0,16},{16,0},{1,17},{17,1},{2,18},{18,2},{3,19},{19,3},{4,20},{20... | collective-permute-start | bytes 2359304 | tf_op jit(solution)/shard_map/ppermute | solution.py:29
  50.5 5.3 %copy-start.2 = (f32[4,4,3,2,1,4,256]{6,5,4,3,2,1,0:T(4,128)}, f32[4,4,3,2,1,4,256]{6,5,4,3,2,1,0:T(4,128)S(1)}, u32[]{:S(2)}) copy-start(f32[4,4,3,2,1,4,256]{6,5,4,3,2,1,0:T(4,128)S(1)} %collective-permute-done.6.tlo_ref) | copy-start | bytes 1179652
  55.8 0.7 copy-start.3
  55.8 0.9 %copy-start.4 = (f32[4,4,3,2,4,1,256]{6,5,4,3,2,1,0:T(1,128)}, f32[4,4,3,2,4,1,256]{6,5,4,3,2,1,0:T(1,128)S(1)}, u32[]{:S(2)}) copy-start(f32[4,4,3,2,4,1,256]{6,5,4,3,2,1,0:T(1,128)S(1)} %collective-permute-done.8.zlo_ref) | copy-start | bytes 1179652
  55.8 1.1 %copy-start.5 = (f32[4,4,3,2,4,1,256]{6,5,4,3,2,1,0:T(1,128)}, f32[4,4,3,2,4,1,256]{6,5,4,3,2,1,0:T(1,128)S(1)}, u32[]{:S(2)}) copy-start(f32[4,4,3,2,4,1,256]{6,5,4,3,2,1,0:T(1,128)S(1)} %collective-permute-done.9.zhi_ref) | copy-start | bytes 1179652
  75.0 5.0 %collective-permute-start.11 = (f32[2,4,4,2,4,8]{5,4,3,2,1,0:T(4,128)S(1)}, f32[2,4,4,2,4,8]{5,4,3,2,1,0:T(4,128)S(1)}, u32[]{:S(2)}, u32[]{:S(2)}) collective-permute-start(f32[2,4,4,2,4,8]{5,4,3,2,1,0:T(4,128)S(1)} %slice_select_fusion), channel_id=1, source_target_pairs={{0,2},{1,3},{2,0},{3,1},{4,6},{5,7},{6,4},{7,5},{8,10},{9,11},{10,... | collective-permute-start | bytes 24584 | tf_op jit(solution)/shard_map/ppermute | solution.py:197
  80.1 1.3 %collective-permute-start.12 = (f32[1,4,4,2,4,8]{5,4,3,2,1,0:T(4,128)S(1)}, f32[1,4,4,2,4,8]{5,4,3,2,1,0:T(4,128)S(1)}, u32[]{:S(2)}, u32[]{:S(2)}) collective-permute-start(f32[1,4,4,2,4,8]{5,4,3,2,1,0:T(4,128)S(1)} %slice_select_fusion.1), channel_id=1, source_target_pairs={{0,1},{1,0},{2,3},{3,2},{4,5},{5,4},{6,7},{7,6},{8,9},{9,8},{10,11... | collective-permute-start | bytes 12296 | tf_op jit(solution)/shard_map/ppermute | solution.py:197

commit v2 on v1

--- a/solution.py
+++ b/solution.py
@@ -1,11 +1,10 @@
-import functools
-
 import jax
 import jax.numpy as jnp
 from jax import lax
 from jax.experimental import pallas as pl
 from jax.experimental.pallas import tpu as pltpu
 from jax.sharding import PartitionSpec as P
+
 
 NX = 32
 TDIL = 4
@@ -208,7 +207,7 @@
     return jnp.stack([real_part, imag_part], axis=2)
 
 
-def local(gauge_links, noise_slabs, offsets, vectors):
+def local_body(gauge_links, noise_slabs, offsets, vectors):
     partner_vectors = from_partner(vectors, "sec", 0)
     batch_rows = noise_slabs.shape[0]
     slab_length = gauge_links.shape[4]
@@ -261,11 +260,14 @@
         spinor = result[0]
         if not last:
             t_first, t_last, z_first, z_last = result[1:]
-            halos = (
-                passed_along(t_last, "ta", 1),
-                passed_along(t_first, "ta", -1),
-                passed_along(z_last, "sa", 1),
-                passed_along(z_first, "sa", -1),
+            halos = tuple(
+                passed_along(plane.astype(jnp.bfloat16), axis, steps).astype(jnp.float32)
+                for plane, axis, steps in (
+                    (t_last, "ta", 1),
+                    (t_first, "ta", -1),
+                    (z_last, "sa", 1),
+                    (z_first, "sa", -1),
+                )
             )
     rounded = spinor.astype(jnp.bfloat16)
     own_part = intersection_part(rounded, vectors)
@@ -284,4 +286,4 @@
         P("ta", "sec", None, None, "sa", None),
     )
     out_specs = P("sec", None, None, "ta", "sa")
-    return jax.shard_map(local, mesh=mesh, in_specs=in_specs, out_specs=out_specs, check_vma=False)
+    return jax.shard_map(local_body, mesh=mesh, in_specs=in_specs, out_specs=out_specs, check_vma=False)

time: 82.4 us -> 79.6 us (0.966)
  waiting for transfers between devices: 22.8 us -> 11.1 us
  other arithmetic: 10.3 us -> 18.8 us
  starting transfers between devices: 14.4 us -> 15.8 us
  local copies, waits for them, and re-layouts: 6.45 us -> 5.39 us
    ppermute x10, waiting for transfers between devices: 16.6 us -> 6.32 us  [passed_along(): return lax.ppermute(value, axis, pairs)]
    convert_element_type x2 -> x10, other arithmetic: 1.85 us -> 10.3 us  [the longest x4 4.87 us: local_body(): passed_along(plane.astype(jnp.bfloat16), axis, steps).astype(jnp.float32)]
    ppermute x2, starting transfers between devices: 0.14 us -> 1.53 us  [reduce_scatter_sa(): x = keep + lax.ppermute(send, 'sa', [(j, j ^ d) for j in range(n)])]
    ppermute x2, waiting for transfers between devices: 6.18 us -> 4.82 us  [reduce_scatter_sa(): x = keep + lax.ppermute(send, 'sa', [(j, j ^ d) for j in range(n)])]
    unnamed x21 -> x17, local copies, waits for them, and re-layouts: 2.18 us -> 1.11 us
  transfers between devices with their start and end apart: 13 -> 13, of which waited for: 5 -> 5; matrix products, arithmetic and copies ran while one was open for 17% -> 26% of each run, Pallas kernels for 14% -> 15%
where the time goes in v2:
time: 79.6 us; the launch traced here: 79.2 us
  Pallas kernels  24 us (30%)
  other arithmetic  18.8 us (24%)
  starting transfers between devices  15.8 us (20%)
  waiting for transfers between devices  11.1 us (14%)
  local copies, waits for them, and re-layouts  5.39 us (7%)
  matrix products  3.65 us (5%)
    pallas_call x2, Pallas kernels, hopping_step(): pl.pallas_call(hop_kernel, grid=(R,), in_specs=[pl.BlockSpec(memory_space...  24 us
    ppermute x10, starting transfers between devices, passed_along(): return lax.ppermute(value, axis, pairs)  12.7 us
    ppermute x10, waiting for transfers between devices, passed_along(): return lax.ppermute(value, axis, pairs)  6.32 us
    convert_element_type x4, other arithmetic, local_body(): passed_along(plane.astype(jnp.bfloat16), axis, steps).astype(jnp.float32)  4.87 us
    ppermute x2, waiting for transfers between devices, reduce_scatter_sa(): x = keep + lax.ppermute(send, 'sa', [(j, j ^ d) for j in range(n)])  4.82 us
    mul x5, other arithmetic, make_source(): spin_mask[:, :, None, None, None, None, None]  4.43 us
    dot_general x2, matrix products, intersection_part(): jnp.einsum('tvcazs,rqcbtzs->rqabtv', vector_piece, rounded, preferred_ele...  3.65 us
    convert_element_type x4, other arithmetic, local_body(): plane.astype(jnp.bfloat16)  3.56 us
  transfers between devices with their start and end apart: 13, of which 5 were waited for; matrix products, arithmetic and copies ran while one was open for 26% of the time, Pallas kernels for 15%

profile of v2, /device:TPU:0, one launch (start us, length us, event | category | flops | bytes accessed | tf_op | source)
XLA Modules:
  0.0 79.2 jit_solution(5471504749087860777)
XLA Ops:
  0.0 3.1 %collective-permute-start = (f32[4,3,2,1,4,256]{5,4,3,2,1,0:T(4,128)}, f32[4,3,2,1,4,256]{5,4,3,2,1,0:T(4,128)S(1)}, u32[]{:S(2)}, u32[]{:S(2)}) collective-permute-start(f32[4,3,2,1,4,256]{5,4,3,2,1,0:T(4,128)} %param.5), channel_id=1, source_target_pairs={{0,4},{4,8},{8,12},{12,0},{1,5},{5,9},{9,13},{13,1},{2,6},{6,10},{... | collective-permute-start | bytes 294920 | tf_op jit(solution)/shard_map/ppermute | solution.py:24
  3.1 2.0 %collective-permute-start.1 = (f32[4,3,2,1,4,256]{5,4,3,2,1,0:T(4,128)}, f32[4,3,2,1,4,256]{5,4,3,2,1,0:T(4,128)S(1)}, u32[]{:S(2)}, u32[]{:S(2)}) collective-permute-start(f32[4,3,2,1,4,256]{5,4,3,2,1,0:T(4,128)} %param.5), channel_id=1, source_target_pairs={{0,12},{4,0},{8,4},{12,8},{1,13},{5,1},{9,5},{13,9},{2,14},{6,2},{... | collective-permute-start | bytes 294920 | tf_op jit(solution)/shard_map/ppermute | solution.py:24
  5.1 1.0 %fusion.8 = (f32[4,3,2,1,1,256]{5,4,3,2,1,0:T(1,128)S(1)}, f32[4,3,2,1,1,256]{5,4,3,2,1,0:T(1,128)S(1)}) fusion(f32[4,3,2,1,4,256]{5,4,3,2,1,0:T(4,128)} %param.5), kind=kLoop, calls=%fused_computation.65 | loop fusion | bytes 98304 | tf_op jit(solution)/shard_map/slice | solution.py:239
  6.1 0.7 collective-permute-start.3
  6.8 1.0 %slice_bitcast_fusion.9 = f32[3,3,2,4,1,256]{5,4,3,2,1,0:T(1,128)S(1)} fusion(f32[4,3,3,2,4,4,256]{6,5,4,3,2,1,0:T(4,128)} %u_ref.3), kind=kLoop, calls=%fused_computation.32 | loop fusion | bytes 147456 | tf_op jit(solution)/shard_map/squeeze | solution.py:247
  7.9 1.3 %collective-permute-start.4 = (f32[3,3,2,4,1,256]{5,4,3,2,1,0:T(1,128)S(1)}, f32[3,3,2,4,1,256]{5,4,3,2,1,0:T(1,128)S(1)}, u32[]{:S(2)}, u32[]{:S(2)}) collective-permute-start(f32[3,3,2,4,1,256]{5,4,3,2,1,0:T(1,128)S(1)} %slice_bitcast_fusion.9), channel_id=1, source_target_pairs={{0,1},{1,2},{2,3},{3,0},{4,5},{5,6},{6,7},{7,4},{8,9},{9,10},{10,1... | collective-permute-start | bytes 221192 | tf_op jit(solution)/shard_map/ppermute | solution.py:24
  9.2 1.1 %slice_bitcast_fusion.4 = (f32[3,3,2,4,4,256]{5,4,3,2,1,0:T(4,128)S(1)}, f32[3,3,2,4,4,256]{5,4,3,2,1,0:T(4,128)S(1)}) fusion(f32[4,3,3,2,4,4,256]{6,5,4,3,2,1,0:T(4,128)} %u_ref.3), kind=kLoop, calls=%fused_computation.17 | loop fusion | bytes 1179648 | tf_op jit(solution)/shard_map/squeeze | solution.py:250
  10.3 0.2 slice_bitcast_fusion.1
  10.6 0.1 slice_bitcast_fusion.6
  10.8 0.8 %copy-done = f32[4,3,3,2,4,4,256]{6,5,4,3,2,1,0:T(4,128)S(1)} copy-done((f32[4,3,3,2,4,4,256]{6,5,4,3,2,1,0:T(4,128)S(1)}, f32[4,3,3,2,4,4,256]{6,5,4,3,2,1,0:T(4,128)}, u32[]{:S(2)}) %copy-start) | copy-done | bytes 1179672
  11.9 0.1 slice.118
  12.0 0.1 broadcast_multiply_fusion.5
  12.2 1.7 %broadcast_multiply_fusion.psi_ref.src_ref = f32[4,4,3,2,4,4,256]{6,5,4,3,2,1,0:T(4,128)} fusion(f32[4,3,2,4,4,256]{5,4,3,2,1,0:T(4,128)S(1)} %broadcast_multiply_fusion.5, f32[4,4]{1,0:T(4,128)S(1)} %fusion.4), kind=kLoop, calls=%fused_computation.6 | loop fusion | flops 393216 | bytes 1966144 | tf_op jit(solution)/shard_map/mul | solution.py:231
  13.8 0.2 maximum_bitcast_fusion
  14.1 0.3 maximum_select_fusion
  14.4 0.7 pad_maximum_fusion.1.sign_ref
  15.2 1.5 %broadcast_multiply_fusion.1 = (f32[4,4,3,2,4,1,256]{6,5,4,3,2,1,0:T(1,128)}, f32[4,4,3,2,4,1,256]{6,5,4,3,2,1,0:T(1,128)}) fusion(f32[4,3,2,4,256]{4,3,2,1,0:T(4,128)S(1)} %get-tuple-element.29, f32[4,4]{1,0:T(4,128)S(1)} %fusion.4, f32[4,3,2,4,256]{4,3,2,1,0:T(4,128)S(1)} %get-tuple-element.30), kind=kLoop, calls=%fused_computation.20 | loop fusion | flops 196608 | bytes 983104 | tf_op jit(solution)/shard_map/mul | solution.py:231
  16.7 0.1 maximum_bitcast_fusion.1
  16.9 4.6 %collective-permute-done.5 = f32[3,3,2,1,4,256]{5,4,3,2,1,0:T(4,128)S(1)} collective-permute-done((f32[3,3,2,1,4,256]{5,4,3,2,1,0:T(4,128)S(1)}, f32[3,3,2,1,4,256]{5,4,3,2,1,0:T(4,128)S(1)}, u32[]{:S(2)}, u32[]{:S(2)}) %collective-permute-start.5) | collective-permute-done | bytes 73760 | tf_op jit(solution)/shard_map/ppermute | solution.py:24
  21.5 1.4 %pad_maximum_fusion.b_ref = f32[4,3,3,2,4,4,256]{6,5,4,3,2,1,0:T(4,128)} fusion(f32[1,3,3,2,4,4,256]{6,5,4,3,2,1,0:T(4,128)S(1)} %maximum_bitcast_fusion.2, f32[1,3,3,2,4,4,256]{6,5,4,3,2,1,0:T(4,128)S(1)} %maximum_bitcast_fusion.1, f32[1,3,3,2,4,4,256]{6,5,4,3,2,1,0:T(4,128)S(1)} %maximum_bitcast_fusion, f32[1,3,3,2,4,4,256]{6,5,4,3,2,1,0:T(4,128)S(1)} %maximum_select_fusion), kind=kLoop, calls=%fused_computation | loop fusion | flops 884736 | bytes 2359296 | tf_op jit(solution)/shard_map/stack | solution.py:248
  23.1 1.1 %broadcast_multiply_fusion.3 = (f32[4,4,3,2,1,4,256]{6,5,4,3,2,1,0:T(4,128)}, f32[4,4,3,2,1,4,256]{6,5,4,3,2,1,0:T(4,128)}) fusion(f32[4,3,2,4,256]{4,3,2,1,0:T(4,128)S(1)} %multiply_bitcast_fusion, f32[4,4]{1,0:T(4,128)S(1)} %fusion.4, f32[4,3,2,4,256]{4,3,2,1,0:T(4,128)S(1)} %multiply_bitcast_fusion.1), kind=kLoop, calls=%fused_computation.22 | loop fusion | flops 196608 | bytes 983104 | tf_op jit(solution)/shard_map/mul | solution.py:231
  24.2 12.3 %shard_map.49 = (f32[4,4,3,2,4,4,256]{6,5,4,3,2,1,0:T(4,128)}, f32[4,4,3,2,1,4,256]{6,5,4,3,2,1,0:T(4,128)}, f32[4,4,3,2,1,4,256]{6,5,4,3,2,1,0:T(4,128)}, f32[4...) custom-call(f32[2]{0:T(128)} %pad_maximum_fusion.1.sign_ref, ...), custom_call_target="tpu_custom_call" | custom-call | tf_op jit(solution)/shard_map/pallas_call | solution.py:170
  36.5 1.4 %convert_element_type.55 = bf16[4,4,3,2,4,1,256]{6,5,4,3,2,1,0:T(2,128)(2,1)S(1)} convert(f32[4,4,3,2,4,1,256]{6,5,4,3,2,1,0:T(1,128)} %get-tuple-element.13) | non-fusion elementwise | flops 98304 | bytes 589824 | tf_op jit(solution)/shard_map/convert_element_type | solution.py:264
  37.9 1.4 %convert_element_type.57 = bf16[4,4,3,2,4,1,256]{6,5,4,3,2,1,0:T(2,128)(2,1)S(1)} convert(f32[4,4,3,2,4,1,256]{6,5,4,3,2,1,0:T(1,128)} %get-tuple-element.14) | non-fusion elementwise | flops 98304 | bytes 589824 | tf_op jit(solution)/shard_map/convert_element_type | solution.py:264
  39.3 1.7 %collective-permute-start.9 = (bf16[4,4,3,2,4,1,256]{6,5,4,3,2,1,0:T(2,128)(2,1)S(1)}, bf16[4,4,3,2,4,1,256]{6,5,4,3,2,1,0:T(2,128)(2,1)S(1)}, u32[]{:S(2)}, u32[]{:S(2)}) collective-permute-start(bf16[4,4,3,2,4,1,256]{6,5,4,3,2,1,0:T(2,128)(2,1)S(1)} %convert_element_type.57), channel_id=1, source_target_pairs={{0,3},{1,0},{2,1},{3,2},{4,7},{5,4},{6,5},{7,6},{8,11},{9,8},{10,9... | collective-permute-start | bytes 589832 | tf_op jit(solution)/shard_map/ppermute | solution.py:24
  41.2 0.7 convert_element_type.53
  41.9 3.8 %collective-permute-start.7 = (bf16[4,4,3,2,1,4,256]{6,5,4,3,2,1,0:T(4,128)(2,1)}, bf16[4,4,3,2,1,4,256]{6,5,4,3,2,1,0:T(4,128)(2,1)}, u32[]{:S(2)}, u32[]{:S(2)}) collective-permute-start(bf16[4,4,3,2,1,4,256]{6,5,4,3,2,1,0:T(4,128)(2,1)} %convert_element_type.53), channel_id=1, source_target_pairs={{0,12},{4,0},{8,4},{12,8},{1,13},{5,1},{9,5},{13,9},{2,14},{6,2},{... | collective-permute-start | bytes 589832 | tf_op jit(solution)/shard_map/ppermute | solution.py:24
  45.7 0.2 copy.21
  45.9 1.6 %collective-permute-start.10 = (bf16[4,16,3,2,4,256]{5,1,4,2,3,0:T(8,128)(2,1)S(1)}, bf16[4,16,3,2,4,256]{5,1,4,2,3,0:T(8,128)(2,1)}, u32[]{:S(2)}, u32[]{:S(2)}) collective-permute-start(bf16[4,16,3,2,4,256]{5,1,4,2,3,0:T(8,128)(2,1)S(1)} %copy.21), channel_id=1, source_target_pairs={{0,16},{16,0},{1,17},{17,1},{2,18},{18,2},{3,19},{19,3},{4,20},{20... | collective-permute-start | bytes 2359304 | tf_op jit(solution)/shard_map/ppermute | solution.py:28
  47.5 1.2 %convert_element_type.56.zlo_ref = f32[4,4,3,2,4,1,256]{6,5,4,3,2,1,0:T(1,128)} convert(bf16[4,4,3,2,4,1,256]{6,5,4,3,2,1,0:T(2,128)(2,1)S(1)} %collective-permute-done.8) | non-fusion elementwise | flops 98304 | bytes 589824 | tf_op jit(solution)/shard_map/convert_element_type | solution.py:264
  48.6 1.2 %convert_element_type.58.zhi_ref = f32[4,4,3,2,4,1,256]{6,5,4,3,2,1,0:T(1,128)} convert(bf16[4,4,3,2,4,1,256]{6,5,4,3,2,1,0:T(2,128)(2,1)S(1)} %collective-permute-done.9) | non-fusion elementwise | flops 98304 | bytes 589824 | tf_op jit(solution)/shard_map/convert_element_type | solution.py:264
  49.8 0.9 %collective-permute-done.6 = bf16[4,4,3,2,1,4,256]{6,5,4,3,2,1,0:T(4,128)(2,1)S(1)} collective-permute-done((bf16[4,4,3,2,1,4,256]{6,5,4,3,2,1,0:T(4,128)(2,1)S(1)}, bf16[4,4,3,2,1,4,256]{6,5,4,3,2,1,0:T(4,128)(2,1)S(1)}, u32[]{:S(2)}, u32[]{:S(2)}) %collective-permute-start.6) | collective-permute-done | bytes 196640 | tf_op jit(solution)/shard_map/ppermute | solution.py:24
  50.8 0.8 convert_element_type.52.tlo_ref
  51.5 0.8 collective-permute-done.7
  52.3 1.8 %convert_element_type.54.thi_ref = f32[4,4,3,2,1,4,256]{6,5,4,3,2,1,0:T(4,128)} convert(bf16[4,4,3,2,1,4,256]{6,5,4,3,2,1,0:T(4,128)(2,1)} %collective-permute-done.7) | non-fusion elementwise | flops 98304 | bytes 589824 | tf_op jit(solution)/shard_map/convert_element_type | solution.py:264
  54.1 11.7 %shard_map.50 = f32[4,4,3,2,4,4,256]{6,5,4,3,2,1,0:T(4,128)} custom-call(f32[2]{0:T(128)} %pad_maximum_fusion.1.sign_ref, f32[4,4,3,2,4,4,256]{6,5,4,3,2,1,0:T(4,128)} %get-tuple-element.10.psi_ref, f32[4,4,3,2,1,4,256]{6,5,4,3,2,1,0:T(4,128)} %convert_element_type.52.tlo_ref, f32[4,4,3,2,1,4,256]{6,5,4,3,2,1,0:T(4,128)} %convert_element_type.54.thi_ref, ...), custom_call_target="tpu_custom_call" | custom-call | tf_op jit(solution)/shard_map/pallas_call | solution.py:170
  65.8 1.8 %convert_bitcast_fusion = bf16[4,4,3,2,4,4,256,1]{6,5,4,3,2,1,0,7:T(4,128)(2,1)S(1)} fusion(f32[4,4,3,2,4,4,256]{6,5,4,3,2,1,0:T(4,128)} %shard_map.50), kind=kLoop, calls=%fused_computation.5 | loop fusion | flops 393216 | bytes 2359296 | tf_op jit(solution)/shard_map/convert_element_type | solution.py:272
  67.6 1.3 %convolution_bitcast_fusion.1 = f32[4,4,2,2,4,16]{5,1,2,3,0,4:T(4,128)S(1)} fusion(bf16[4,16,3,2,4,256,1,1]{5,4,3,2,1,0,7,6:T(4,128)(2,1)S(1)} %bitcast.84, bf16[4,4,3,2,4,4,256,1]{6,5,4,3,2,1,0,7:T(4,128)(2,1)S(1)} %convert_bitcast_fusion), kind=kOutput, calls=%fused_computation.2 | convolution fusion | flops 25165824 | bytes 1589248 | tf_op jit(solution)/shard_map/tvcazs,rqcbtzs->rqabtv/dot_general | solution.py:202
  68.8 0.1 add.126
  69.0 0.1 sub.39
  69.1 2.4 %convolution_bitcast_fusion = f32[4,4,2,2,4,16]{5,1,2,3,0,4:T(4,128)S(1)} fusion(bf16[4,16,3,2,4,256]{5,1,4,2,3,0:T(8,128)(2,1)} %collective-permute-done.10, bf16[4,4,3,2,4,4,256,1]{6,5,4,3,2,1,0,7:T(4,128)(2,1)S(1)} %convert_bitcast_fusion), kind=kOutput, calls=%fused_computation.1 | convolution fusion | flops 25165824 | bytes 1589248 | tf_op jit(solution)/shard_map/tvcazs,rqcbtzs->rqabtv/dot_general | solution.py:202
  71.6 0.1 add.128
  71.7 0.1 sub.41
  71.8 0.1 copy_dynamic-update-slice_fusion
  72.1 1.5 %collective-permute-start.11 = (f32[2,4,4,2,4,8]{5,4,3,2,1,0:T(4,128)S(1)}, f32[2,4,4,2,4,8]{5,4,3,2,1,0:T(4,128)S(1)}, u32[]{:S(2)}, u32[]{:S(2)}) collective-permute-start(f32[2,4,4,2,4,8]{5,4,3,2,1,0:T(4,128)S(1)} %slice_select_fusion), channel_id=1, source_target_pairs={{0,2},{1,3},{2,0},{3,1},{4,6},{5,7},{6,4},{7,5},{8,10},{9,11},{10,... | collective-permute-start | bytes 24584 | tf_op jit(solution)/shard_map/ppermute | solution.py:196
  73.6 3.6 %collective-permute-done.11 = f32[2,4,4,2,4,8]{5,4,3,2,1,0:T(4,128)S(1)} collective-permute-done((f32[2,4,4,2,4,8]{5,4,3,2,1,0:T(4,128)S(1)}, f32[2,4,4,2,4,8]{5,4,3,2,1,0:T(4,128)S(1)}, u32[]{:S(2)}, u32[]{:S(2)}) %collective-permute-start.11) | collective-permute-done | bytes 8224 | tf_op jit(solution)/shard_map/ppermute | solution.py:196
  77.3 1.2 %collective-permute-done.12 = f32[1,4,4,2,4,8]{5,4,3,2,1,0:T(4,128)S(1)} collective-permute-done((f32[1,4,4,2,4,8]{5,4,3,2,1,0:T(4,128)S(1)}, f32[1,4,4,2,4,8]{5,4,3,2,1,0:T(4,128)S(1)}, u32[]{:S(2)}, u32[]{:S(2)}) %collective-permute-start.12) | collective-permute-done | bytes 4128 | tf_op jit(solution)/shard_map/ppermute | solution.py:196
  78.5 0.7 add_bitcast_fusion
  (52 shorter events, 1.4 us)
Async XLA Ops:
  0.0 22.9 %collective-permute-start = (f32[4,3,2,1,4,256]{5,4,3,2,1,0:T(4,128)}, f32[4,3,2,1,4,256]{5,4,3,2,1,0:T(4,128)S(1)}, u32[]{:S(2)}, u32[]{:S(2)}) collective-permute-start(f32[4,3,2,1,4,256]{5,4,3,2,1,0:T(4,128)} %param.5), channel_id=1, source_target_pairs={{0,4},{4,8},{8,12},{12,0},{1,5},{5,9},{9,13},{13,1},{2,6},{6,10},{... | collective-permute-start | bytes 294920 | tf_op jit(solution)/shard_map/ppermute | solution.py:24
  3.1 19.9 %collective-permute-start.1 = (f32[4,3,2,1,4,256]{5,4,3,2,1,0:T(4,128)}, f32[4,3,2,1,4,256]{5,4,3,2,1,0:T(4,128)S(1)}, u32[]{:S(2)}, u32[]{:S(2)}) collective-permute-start(f32[4,3,2,1,4,256]{5,4,3,2,1,0:T(4,128)} %param.5), channel_id=1, source_target_pairs={{0,12},{4,0},{8,4},{12,8},{1,13},{5,1},{9,5},{13,9},{2,14},{6,2},{... | collective-permute-start | bytes 294920 | tf_op jit(solution)/shard_map/ppermute | solution.py:24
  6.1 8.9 %collective-permute-start.3 = (f32[4,3,2,1,1,256]{5,4,3,2,1,0:T(1,128)S(1)}, f32[4,3,2,1,1,256]{5,4,3,2,1,0:T(1,128)S(1)}, u32[]{:S(2)}, u32[]{:S(2)}) collective-permute-start(f32[4,3,2,1,1,256]{5,4,3,2,1,0:T(1,128)S(1)} %get-tuple-element.25), channel_id=1, source_target_pairs={{0,3},{1,0},{2,1},{3,2},{4,7},{5,4},{6,5},{7,6},{8,11},{9,8},{10,9... | collective-permute-start | bytes 73736 | tf_op jit(solution)/shard_map/ppermute | solution.py:24
  6.8 8.2 %collective-permute-start.2 = (f32[4,3,2,1,1,256]{5,4,3,2,1,0:T(1,128)S(1)}, f32[4,3,2,1,1,256]{5,4,3,2,1,0:T(1,128)S(1)}, u32[]{:S(2)}, u32[]{:S(2)}) collective-permute-start(f32[4,3,2,1,1,256]{5,4,3,2,1,0:T(1,128)S(1)} %get-tuple-element.26), channel_id=1, source_target_pairs={{0,1},{1,2},{2,3},{3,0},{4,5},{5,6},{6,7},{7,4},{8,9},{9,10},{10,1... | collective-permute-start | bytes 73736 | tf_op jit(solution)/shard_map/ppermute | solution.py:24
  7.9 8.8 %collective-permute-start.4 = (f32[3,3,2,4,1,256]{5,4,3,2,1,0:T(1,128)S(1)}, f32[3,3,2,4,1,256]{5,4,3,2,1,0:T(1,128)S(1)}, u32[]{:S(2)}, u32[]{:S(2)}) collective-permute-start(f32[3,3,2,4,1,256]{5,4,3,2,1,0:T(1,128)S(1)} %slice_bitcast_fusion.9), channel_id=1, source_target_pairs={{0,1},{1,2},{2,3},{3,0},{4,5},{5,6},{6,7},{7,4},{8,9},{9,10},{10,1... | collective-permute-start | bytes 221192 | tf_op jit(solution)/shard_map/ppermute | solution.py:24
  10.3 1.3 %copy-start = (f32[4,3,3,2,4,4,256]{6,5,4,3,2,1,0:T(4,128)S(1)}, f32[4,3,3,2,4,4,256]{6,5,4,3,2,1,0:T(4,128)}, u32[]{:S(2)}) copy-start(f32[4,3,3,2,4,4,256]{6,5,4,3,2,1,0:T(4,128)} %u_ref.3) | copy-start | bytes 3538948
  10.3 1.4 %copy-start.5 = (s32[8]{0:T(128)S(1)}, s32[8]{0:T(128)}, u32[]{:S(2)}) copy-start(s32[8]{0:T(128)} %param.6) | copy-start | bytes 100
  10.6 1.5 %copy-start.4 = (f32[4,3,2,1,4,256]{5,4,3,2,1,0:T(4,128)S(1)}, f32[4,3,2,1,4,256]{5,4,3,2,1,0:T(4,128)}, u32[]{:S(2)}) copy-start(f32[4,3,2,1,4,256]{5,4,3,2,1,0:T(4,128)} %param.5) | copy-start | bytes 294916
  15.0 6.4 %collective-permute-start.5 = (f32[3,3,2,1,4,256]{5,4,3,2,1,0:T(4,128)S(1)}, f32[3,3,2,1,4,256]{5,4,3,2,1,0:T(4,128)S(1)}, u32[]{:S(2)}, u32[]{:S(2)}) collective-permute-start(f32[3,3,2,1,4,256]{5,4,3,2,1,0:T(4,128)S(1)} %slice_bitcast_fusion.8), channel_id=1, source_target_pairs={{0,4},{4,8},{8,12},{12,0},{1,5},{5,9},{9,13},{13,1},{2,6},{6,10},{... | collective-permute-start | bytes 221192 | tf_op jit(solution)/shard_map/ppermute | solution.py:24
  36.5 4.6 %copy-start.3 = (f32[4,4,3,2,1,4,256]{6,5,4,3,2,1,0:T(4,128)S(1)}, f32[4,4,3,2,1,4,256]{6,5,4,3,2,1,0:T(4,128)}, u32[]{:S(2)}) copy-start(f32[4,4,3,2,1,4,256]{6,5,4,3,2,1,0:T(4,128)} %get-tuple-element.11) | copy-start | bytes 1179652
  36.5 4.7 %copy-start.2 = (f32[4,4,3,2,1,4,256]{6,5,4,3,2,1,0:T(4,128)S(1)}, f32[4,4,3,2,1,4,256]{6,5,4,3,2,1,0:T(4,128)}, u32[]{:S(2)}) copy-start(f32[4,4,3,2,1,4,256]{6,5,4,3,2,1,0:T(4,128)} %get-tuple-element.12) | copy-start | bytes 1179652
  37.9 7.9 %copy-start.1 = (bf16[4,16,3,2,4,256]{5,4,3,2,1,0:T(4,128)(2,1)S(1)}, bf16[4,16,3,2,4,256]{5,4,3,2,1,0:T(4,128)(2,1)}, u32[]{:S(2)}) copy-start(bf16[4,16,3,2,4,256]{5,4,3,2,1,0:T(4,128)(2,1)} %param.7) | copy-start | bytes 2359300
  37.9 9.6 %collective-permute-start.8 = (bf16[4,4,3,2,4,1,256]{6,5,4,3,2,1,0:T(2,128)(2,1)S(1)}, bf16[4,4,3,2,4,1,256]{6,5,4,3,2,1,0:T(2,128)(2,1)S(1)}, u32[]{:S(2)}, u32[]{:S(2)}) collective-permute-start(bf16[4,4,3,2,4,1,256]{6,5,4,3,2,1,0:T(2,128)(2,1)S(1)} %convert_element_type.55), channel_id=1, source_target_pairs={{0,1},{1,2},{2,3},{3,0},{4,5},{5,6},{6,7},{7,4},{8,9},{9,10},{10,1... | collective-permute-start | bytes 589832 | tf_op jit(solution)/shard_map/ppermute | solution.py:24
  39.3 9.3 %collective-permute-start.9 = (bf16[4,4,3,2,4,1,256]{6,5,4,3,2,1,0:T(2,128)(2,1)S(1)}, bf16[4,4,3,2,4,1,256]{6,5,4,3,2,1,0:T(2,128)(2,1)S(1)}, u32[]{:S(2)}, u32[]{:S(2)}) collective-permute-start(bf16[4,4,3,2,4,1,256]{6,5,4,3,2,1,0:T(2,128)(2,1)S(1)} %convert_element_type.57), channel_id=1, source_target_pairs={{0,3},{1,0},{2,1},{3,2},{4,7},{5,4},{6,5},{7,6},{8,11},{9,8},{10,9... | collective-permute-start | bytes 589832 | tf_op jit(solution)/shard_map/ppermute | solution.py:24
  41.1 9.6 %collective-permute-start.6 = (bf16[4,4,3,2,1,4,256]{6,5,4,3,2,1,0:T(4,128)(2,1)S(1)}, bf16[4,4,3,2,1,4,256]{6,5,4,3,2,1,0:T(4,128)(2,1)S(1)}, u32[]{:S(2)}, u32[]{:S(2)}) collective-permute-start(bf16[4,4,3,2,1,4,256]{6,5,4,3,2,1,0:T(4,128)(2,1)S(1)} %convert_element_type.51), channel_id=1, source_target_pairs={{0,4},{4,8},{8,12},{12,0},{1,5},{5,9},{9,13},{13,1},{2,6},{6,10},{... | collective-permute-start | bytes 589832 | tf_op jit(solution)/shard_map/ppermute | solution.py:24
  41.9 10.4 %collective-permute-start.7 = (bf16[4,4,3,2,1,4,256]{6,5,4,3,2,1,0:T(4,128)(2,1)}, bf16[4,4,3,2,1,4,256]{6,5,4,3,2,1,0:T(4,128)(2,1)}, u32[]{:S(2)}, u32[]{:S(2)}) collective-permute-start(bf16[4,4,3,2,1,4,256]{6,5,4,3,2,1,0:T(4,128)(2,1)} %convert_element_type.53), channel_id=1, source_target_pairs={{0,12},{4,0},{8,4},{12,8},{1,13},{5,1},{9,5},{13,9},{2,14},{6,2},{... | collective-permute-start | bytes 589832 | tf_op jit(solution)/shard_map/ppermute | solution.py:24
  45.9 23.2 %collective-permute-start.10 = (bf16[4,16,3,2,4,256]{5,1,4,2,3,0:T(8,128)(2,1)S(1)}, bf16[4,16,3,2,4,256]{5,1,4,2,3,0:T(8,128)(2,1)}, u32[]{:S(2)}, u32[]{:S(2)}) collective-permute-start(bf16[4,16,3,2,4,256]{5,1,4,2,3,0:T(8,128)(2,1)S(1)} %copy.21), channel_id=1, source_target_pairs={{0,16},{16,0},{1,17},{17,1},{2,18},{18,2},{3,19},{19,3},{4,20},{20... | collective-permute-start | bytes 2359304 | tf_op jit(solution)/shard_map/ppermute | solution.py:28
  72.1 5.0 %collective-permute-start.11 = (f32[2,4,4,2,4,8]{5,4,3,2,1,0:T(4,128)S(1)}, f32[2,4,4,2,4,8]{5,4,3,2,1,0:T(4,128)S(1)}, u32[]{:S(2)}, u32[]{:S(2)}) collective-permute-start(f32[2,4,4,2,4,8]{5,4,3,2,1,0:T(4,128)S(1)} %slice_select_fusion), channel_id=1, source_target_pairs={{0,2},{1,3},{2,0},{3,1},{4,6},{5,7},{6,4},{7,5},{8,10},{9,11},{10,... | collective-permute-start | bytes 24584 | tf_op jit(solution)/shard_map/ppermute | solution.py:196
  77.2 1.3 %collective-permute-start.12 = (f32[1,4,4,2,4,8]{5,4,3,2,1,0:T(4,128)S(1)}, f32[1,4,4,2,4,8]{5,4,3,2,1,0:T(4,128)S(1)}, u32[]{:S(2)}, u32[]{:S(2)}) collective-permute-start(f32[1,4,4,2,4,8]{5,4,3,2,1,0:T(4,128)S(1)} %slice_select_fusion.1), channel_id=1, source_target_pairs={{0,1},{1,0},{2,3},{3,2},{4,5},{5,4},{6,7},{7,6},{8,9},{9,8},{10,11... | collective-permute-start | bytes 12296 | tf_op jit(solution)/shard_map/ppermute | solution.py:196

commit v3 on v2

v3 whole, which is shorter than its diff:
```python
import functools

import jax
import jax.numpy as jnp
from jax import lax
from jax.experimental import pallas as pl
from jax.experimental.pallas import tpu as pltpu
from jax.sharding import PartitionSpec as P


NX = 32
TDIL = 4
INTERPRET = False


kappa_hop = 0.12
GAMMA_PERM = ((3, 2, 1, 0), (3, 2, 1, 0), (2, 3, 0, 1), (2, 3, 0, 1))
GAMMA_REAL = ((0, 0, 0, 0), (-1, 1, 1, -1), (0, 0, 0, 0), (1, 1, 1, 1))
GAMMA_IMAG = ((1, 1, -1, -1), (0, 0, 0, 0), (1, -1, -1, 1), (0, 0, 0, 0))


def passed_along(value, axis, steps):
    count = lax.axis_size(axis)
    pairs = [(source, (source + steps) % count) for source in range(count)]
    return lax.ppermute(value, axis, pairs)


def from_partner(x, axis, stride):
    return lax.ppermute(x, axis, [(i, i ^ 1 << stride) for i in range(lax.axis_size(axis))])


def times_phase(re, im, cr, ci):
    if ci == 0:
        if cr == 1:
            return re, im
        return -re, -im
    if ci == 1:
        return -im, re
    return im, -re


def hop_kernel(first, *refs):
    (smask_ref, tmask_ref, sign_ref, noise_ref, ntlo_ref, nthi_ref, nzlo_ref, nzhi_ref,
     u_ref, utedge_ref, uzedge_ref) = refs[:11]
    rest = refs[11:]
    if first:
        out_ref, tfirst_ref, tlast_ref, zfirst_ref, zlast_ref = rest[:5]
        pad_ref, src_ref, zlo_s, zhi_s, ut_s = rest[5:]
        zlo_src, zhi_src = zlo_s, zhi_s
    else:
        psi_ref, tlo_ref, thi_ref, zlo_src, zhi_src = rest[:5]
        out_ref = rest[5]
        pad_ref, src_ref, ut_s = rest[6:]
    S, C, RI, T, Z, L = src_ref.shape
    K = noise_ref.shape[2]
    span = T // K
    r = pl.program_id(0)

    @pl.when(r == 0)
    def _():
        for a in range(3):
            for b in range(3):
                for ri in range(RI):
                    ut_s[a, b, ri, pl.ds(0, 1)] = utedge_ref[a, b, ri]
                    ut_s[a, b, ri, pl.ds(1, T)] = u_ref[3, a, b, ri]

    for s in range(S):
        fs = smask_ref[r * S + s]
        for c in range(C):
            for ri in range(RI):
                for t in range(T):
                    src_ref[s, c, ri, t] = noise_ref[c, ri, t // span] * (fs * tmask_ref[r * (T + 2) + t + 1])
                if first:
                    pad_ref[s, c, ri, pl.ds(1, T)] = src_ref[s, c, ri]
                    pad_ref[s, c, ri, 0] = ntlo_ref[c, ri, 0] * (fs * tmask_ref[r * (T + 2)] * sign_ref[0])
                    pad_ref[s, c, ri, T + 1] = nthi_ref[c, ri, 0] * (
                        fs * tmask_ref[r * (T + 2) + T + 1] * sign_ref[1])
                    for t in range(T):
                        f = fs * tmask_ref[r * (T + 2) + t + 1]
                        zlo_s[s, c, ri, t] = nzlo_ref[c, ri, t // span] * f
                        zhi_s[s, c, ri, t] = nzhi_ref[c, ri, t // span] * f
                else:
                    pad_ref[s, c, ri, pl.ds(1, T)] = psi_ref[s, c, ri]
                    pad_ref[s, c, ri, pl.ds(0, 1)] = tlo_ref[s, c, ri].astype(jnp.float32) * sign_ref[0]
                    pad_ref[s, c, ri, pl.ds(T + 1, 1)] = thi_ref[s, c, ri].astype(jnp.float32) * sign_ref[1]
    xpos = lax.broadcasted_iota(jnp.int32, (Z, L), 1) % NX
    zpos = lax.broadcasted_iota(jnp.int32, (Z, L), 0)
    x_last = xpos == NX - 1
    x_first = xpos == 0
    z_last = zpos == Z - 1
    z_first = zpos == 0

    def x_back(v):
        return jnp.where(x_first, pltpu.roll(v, L - NX + 1, axis=1), pltpu.roll(v, 1, axis=1))

    def body(t, carry):
        acc = [[[None, None] for _ in range(3)] for _ in range(4)]

        def shifted(s, c, ri, mu, stride):
            if mu == 3:
                return pad_ref[s, c, ri, t + 1 + stride]
            v = pad_ref[s, c, ri, t + 1]
            if mu == 2:
                if stride == 1:
                    halo = jnp.broadcast_to(zhi_src[s, c, ri, t], (Z, L))
                    return jnp.where(z_last, halo, pltpu.roll(v, Z - 1, axis=0))
                halo = jnp.broadcast_to(zlo_src[s, c, ri, t], (Z, L))
                return jnp.where(z_first, halo, pltpu.roll(v, 1, axis=0))
            if mu == 1:
                return pltpu.roll(v, (L - NX) if stride == 1 else NX, axis=1)
            if stride == 1:
                return jnp.where(x_last, pltpu.roll(v, NX - 1, axis=1), pltpu.roll(v, L - 1, axis=1))
            return x_back(v)

        def back_link(mu, a, b, ri):
            if mu == 3:
                return ut_s[a, b, ri, t]
            v = u_ref[mu, a, b, ri, t]
            if mu == 2:
                edge = jnp.broadcast_to(uzedge_ref[a, b, ri, t], (Z, L))
                return jnp.where(z_first, edge, pltpu.roll(v, 1, axis=0))
            if mu == 1:
                return pltpu.roll(v, NX, axis=1)
            return x_back(v)

        for mu in range(4):
            perm = GAMMA_PERM[mu]
            heads = [0, 1]
            for stride in (1, -1):
                orient = -1 if stride == 1 else 1
                half = []
                for s in heads:
                    p = perm[s]
                    cr, ci = orient * GAMMA_REAL[mu][s], orient * GAMMA_IMAG[mu][s]
                    colours = []
                    for c in range(3):
                        sre = shifted(s, c, 0, mu, stride)
                        sim = shifted(s, c, 1, mu, stride)
                        pre, pim = times_phase(shifted(p, c, 0, mu, stride), shifted(p, c, 1, mu, stride), cr, ci)
                        colours.append((sre + pre, sim + pim))
                    half.append(colours)
                if stride == 1:
                    links = [[(u_ref[mu, a, b, 0, t], u_ref[mu, a, b, 1, t]) for b in range(3)] for a in range(3)]
                else:
                    links = [[(back_link(mu, b, a, 0), back_link(mu, b, a, 1)) for b in range(3)] for a in range(3)]
                for k, s in enumerate(heads):
                    p = perm[s]
                    cpr, cpi = orient * GAMMA_REAL[mu][p], orient * GAMMA_IMAG[mu][p]
                    for a in range(3):
                        sum_re = None
                        sum_im = None
                        for b in range(3):
                            hre, him = half[k][b]
                            lre, lim = links[a][b]
                            if stride == 1:
                                tre = lre * hre - lim * him
                                tim = lre * him + lim * hre
                            else:
                                tre = lre * hre + lim * him
                                tim = lre * him - lim * hre
                            sum_re = tre if sum_re is None else sum_re + tre
                            sum_im = tim if sum_im is None else sum_im + tim
                        for row, (vre, vim) in ((s, (sum_re, sum_im)), (p, times_phase(sum_re, sum_im, cpr, cpi))):
                            if acc[row][a][0] is None:
                                acc[row][a] = [vre, vim]
                            else:
                                acc[row][a] = [acc[row][a][0] + vre, acc[row][a][1] + vim]
        for s in range(4):
            for c in range(3):
                for ri in range(2):
                    psi = pad_ref[s, c, ri, t + 1]
                    src = src_ref[s, c, ri, t]
                    residual = src - (psi - kappa_hop * acc[s][c][ri])
                    out_ref[s, c, ri, t] = (psi + residual).astype(out_ref.dtype)
        return carry

    lax.fori_loop(0, T, body, 0)
    if first:
        for s in range(S):
            for c in range(C):
                for ri in range(RI):
                    tfirst_ref[s, c, ri] = out_ref[s, c, ri, pl.ds(0, 1)].astype(tfirst_ref.dtype)
                    tlast_ref[s, c, ri] = out_ref[s, c, ri, pl.ds(T - 1, 1)].astype(tlast_ref.dtype)
                    zfirst_ref[s, c, ri] = out_ref[s, c, ri, :, pl.ds(0, 1), :]
                    zlast_ref[s, c, ri] = out_ref[s, c, ri, :, pl.ds(Z - 1, 1), :]


def hopping_step(first, scalars, noise_parts, link_parts, spinor_parts):
    R, C, RI, K, Z, L = noise_parts[0].shape
    T = link_parts[0].shape[4]
    S = 4
    index = lambda r: (r,) + (0,) * 6
    index6 = lambda r: (r,) + (0,) * 5
    whole = lambda x: pl.BlockSpec(x.shape, lambda r: (0,) * x.ndim)
    smem = pl.BlockSpec(memory_space=pltpu.SMEM)
    site_block = pl.BlockSpec((None, S, C, RI, T, Z, L), index)
    t_block = pl.BlockSpec((None, S, C, RI, 1, Z, L), index)
    z_block = pl.BlockSpec((None, S, C, RI, T, 1, L), index)
    noise_specs = [
        pl.BlockSpec((None, C, RI, K, Z, L), index6),
        pl.BlockSpec((None, C, RI, 1, Z, L), index6),
        pl.BlockSpec((None, C, RI, 1, Z, L), index6),
        pl.BlockSpec((None, C, RI, K, 1, L), index6),
        pl.BlockSpec((None, C, RI, K, 1, L), index6),
    ]
    in_specs = [smem, smem, smem] + noise_specs + [whole(x) for x in link_parts]
    scratch = [pltpu.VMEM((S, C, RI, T + 2, Z, L), jnp.float32), pltpu.VMEM((S, C, RI, T, Z, L), jnp.float32)]
    if first:
        t_shape = jax.ShapeDtypeStruct((R, S, C, RI, 1, Z, L), jnp.bfloat16)
        z_shape = jax.ShapeDtypeStruct((R, S, C, RI, T, 1, L), jnp.float32)
        out_shape = [jax.ShapeDtypeStruct((R, S, C, RI, T, Z, L), jnp.float32), t_shape, t_shape, z_shape, z_shape]
        out_specs = [site_block, t_block, t_block, z_block, z_block]
        scratch += [pltpu.VMEM((S, C, RI, T, 1, L), jnp.float32)] * 2
    else:
        in_specs += [site_block, t_block, t_block, z_block, z_block]
        out_shape = jax.ShapeDtypeStruct((R, S, C, RI, T, Z, L), jnp.bfloat16)
        out_specs = site_block
    scratch += [pltpu.VMEM((3, 3, RI, T + 1, Z, L), jnp.float32)]
    return pl.pallas_call(
        functools.partial(hop_kernel, first),
        grid=(R,),
        in_specs=in_specs,
        out_specs=out_specs,
        out_shape=out_shape,
        scratch_shapes=scratch,
        compiler_params=pltpu.CompilerParams(dimension_semantics=("arbitrary",)),
        interpret=INTERPRET,
    )(*scalars, *noise_parts, *link_parts, *spinor_parts)


def reduce_scatter_sa(partial_value):
    n = lax.axis_size("sa")
    if n & (n - 1):
        return lax.psum_scatter(partial_value, "sa", scatter_dimension=4, tiled=True)
    lead = partial_value.shape[:-1]
    width = partial_value.shape[-1] // n
    x = jnp.moveaxis(partial_value.reshape(lead + (n, width)), -2, 0)
    me = lax.axis_index("sa")
    d = n // 2
    while d >= 1:
        upper_mine = (me // d) % 2 == 1
        keep = jnp.where(upper_mine, x[d:], x[:d])
        send = jnp.where(upper_mine, x[:d], x[d:])
        x = keep + lax.ppermute(send, "sa", [(j, j ^ d) for j in range(n)])
        d //= 2
    return x[0]


def intersection_part(rounded, vector_piece):
    products = jnp.einsum(
        "tvcazs,rqcbtzs->rqabtv", vector_piece, rounded, preferred_element_type=jnp.float32
    )
    real_part = products[:, :, 0, 0] + products[:, :, 1, 1]
    imag_part = products[:, :, 0, 1] - products[:, :, 1, 0]
    return jnp.stack([real_part, imag_part], axis=2)


def local_body(gauge_links, noise_slabs, offsets, vectors):
    partner_vectors = from_partner(vectors, "sec", 0)
    batch_rows = noise_slabs.shape[0]
    slab_length = gauge_links.shape[4]
    Z = gauge_links.shape[5]
    K = noise_slabs.shape[3]
    section_index = lax.axis_index("sec")
    slab_index = lax.axis_index("ta")
    slab_count = lax.axis_size("ta")
    lower_sign = jnp.where(slab_index == 0, -1.0, 1.0).astype(jnp.float32)
    upper_sign = jnp.where(slab_index == slab_count - 1, -1.0, 1.0).astype(jnp.float32)
    signs = jnp.stack([lower_sign, upper_sign])
    t_start = slab_index * slab_length
    own_offsets = lax.dynamic_slice_in_dim(offsets, section_index * batch_rows, batch_rows)
    rhs_index = section_index * batch_rows + jnp.arange(batch_rows)
    spin_mask = (jnp.arange(4)[None, :] == rhs_index[:, None] % 4).astype(jnp.float32)
    times = t_start - 1 + jnp.arange(slab_length + 2)
    time_mask = (times[None, :] % TDIL == own_offsets[:, None]).astype(jnp.float32)
    scalars = (spin_mask.reshape(-1), time_mask.reshape(-1), signs)
    noise_parts = (
        noise_slabs,
        passed_along(noise_slabs[:, :, :, K - 1:], "ta", 1),
        passed_along(noise_slabs[:, :, :, :1], "ta", -1),
        passed_along(noise_slabs[:, :, :, :, Z - 1:], "sa", 1),
        passed_along(noise_slabs[:, :, :, :, :1], "sa", -1),
    )
    link_parts = (
        gauge_links,
        passed_along(gauge_links[3, :, :, :, -1:, :, :], "ta", 1),
        passed_along(gauge_links[2, :, :, :, :, -1:, :], "sa", 1),
    )
    spinor, t_first, t_last, z_first, z_last = hopping_step(True, scalars, noise_parts, link_parts, ())
    halos = (
        passed_along(t_last, "ta", 1),
        passed_along(t_first, "ta", -1),
        passed_along(z_last, "sa", 1),
        passed_along(z_first, "sa", -1),
    )
    rounded = hopping_step(False, scalars, noise_parts, link_parts, (spinor,) + halos)
    own_part = intersection_part(rounded, vectors)
    partner_part = intersection_part(rounded, partner_vectors)
    lower_half = jnp.where(section_index == 0, own_part, partner_part)
    upper_half = jnp.where(section_index == 0, partner_part, own_part)
    partial_value = jnp.concatenate([lower_half, upper_half], axis=4)
    return reduce_scatter_sa(partial_value)


def solution(mesh):
    in_specs = (
        P(None, None, None, None, "ta", "sa", None),
        P("sec", None, None, "ta", "sa", None),
        P(),
        P("ta", "sec", None, None, "sa", None),
    )
    out_specs = P("sec", None, None, "ta", "sa")
    return jax.shard_map(local_body, mesh=mesh, in_specs=in_specs, out_specs=out_specs, check_vma=False)
```

time: 79.6 us -> 72.2 us (0.907)
  other arithmetic: 18.8 us -> 1.62 us
  Pallas kernels: 24 us -> 29.1 us
  waiting for transfers between devices: 11.1 us -> 14.2 us
  local copies, waits for them, and re-layouts: 5.39 us -> 7.96 us
  starting transfers between devices: 15.8 us -> 15 us
    convert_element_type x12 -> x1, other arithmetic: 10.4 us -> 0.07 us  [local_body(): (times[None, :] % TDIL == own_offsets[:, None]).astype(jnp.float32)]
    pallas_call x2, Pallas kernels: 24 us -> 29.1 us  [hopping_step(): pl.pallas_call(functools.partial(hop_kernel, first), grid=(R,), in_specs=...]
    mul x7 -> x0, other arithmetic: 4.66 us -> none  [the longest x5 4.43 us: make_source(): spin_mask[:, :, None, None, None, None, None]]
    ppermute x10, waiting for transfers between devices: 6.32 us -> 8.51 us  [passed_along(): return lax.ppermute(value, axis, pairs)]
    another operation x4 -> x0, other arithmetic: 1.78 us -> none  [local_body(): jnp.stack([move_first(gauge_links[0], -1), move_second(gauge_links[1], -1...]
    unnamed x17 -> x27, local copies, waits for them, and re-layouts: 1.11 us -> 2.48 us
    convert_element_type x0 -> x2, local copies, waits for them, and re-layouts: none -> 1.27 us  [the longest x1 0.67 us: local_body(): (times[None, :] % TDIL == own_offsets[:, None]).astype(jnp.float32)]
    ppermute x2, starting transfers between devices: 1.53 us -> 0.64 us  [reduce_scatter_sa(): x = keep + lax.ppermute(send, 'sa', [(j, j ^ d) for j in range(n)])]
  transfers between devices with their start and end apart: 13 -> 13, of which waited for: 5 -> 5; matrix products, arithmetic and copies ran while one was open for 26% -> 12% of each run, Pallas kernels for 15% -> 20%
where the time goes in v3:
time: 72.2 us; the launch traced here: 71.9 us
  Pallas kernels  29.1 us (40%)
  starting transfers between devices  15 us (21%)
  waiting for transfers between devices  14.2 us (20%)
  local copies, waits for them, and re-layouts  7.96 us (11%)
  matrix products  3.71 us (5%)
  other arithmetic  1.62 us (2%)
    pallas_call x2, Pallas kernels, hopping_step(): pl.pallas_call(functools.partial(hop_kernel, first), grid=(R,), in_specs=...  29.1 us
    ppermute x10, starting transfers between devices, passed_along(): return lax.ppermute(value, axis, pairs)  12.6 us
    ppermute x10, waiting for transfers between devices, passed_along(): return lax.ppermute(value, axis, pairs)  8.51 us
    ppermute x2, waiting for transfers between devices, reduce_scatter_sa(): x = keep + lax.ppermute(send, 'sa', [(j, j ^ d) for j in range(n)])  5.7 us
    dot_general x2, matrix products, intersection_part(): jnp.einsum('tvcazs,rqcbtzs->rqabtv', vector_piece, rounded, preferred_ele...  3.71 us
    unnamed x27, local copies, waits for them, and re-layouts  2.48 us
    ppermute x1, starting transfers between devices, from_partner(): lax.ppermute(x, axis, [(i, i ^ 1 << stride) for i in range(lax.axis_size(...  1.73 us
  transfers between devices with their start and end apart: 13, of which 5 were waited for; matrix products, arithmetic and copies ran while one was open for 12% of the time, Pallas kernels for 20%

profile of v3, /device:TPU:0, one launch (start us, length us, event | category | flops | bytes accessed | tf_op | source)
XLA Modules:
  0.0 71.9 jit_solution(5909332351946017653)
XLA Ops:
  0.0 3.1 %collective-permute-start = (f32[4,3,2,1,4,256]{5,4,3,2,1,0:T(4,128)}, f32[4,3,2,1,4,256]{5,4,3,2,1,0:T(4,128)S(1)}, u32[]{:S(2)}, u32[]{:S(2)}) collective-permute-start(f32[4,3,2,1,4,256]{5,4,3,2,1,0:T(4,128)} %refs_3_.3), channel_id=1, source_target_pairs={{0,4},{4,8},{8,12},{12,0},{1,5},{5,9},{9,13},{13,1},{2,6},{6,10},{... | collective-permute-start | bytes 294920 | tf_op jit(solution)/shard_map/ppermute | solution.py:25
  3.1 2.1 %collective-permute-start.1 = (f32[4,3,2,1,4,256]{5,4,3,2,1,0:T(4,128)}, f32[4,3,2,1,4,256]{5,4,3,2,1,0:T(4,128)S(1)}, u32[]{:S(2)}, u32[]{:S(2)}) collective-permute-start(f32[4,3,2,1,4,256]{5,4,3,2,1,0:T(4,128)} %refs_3_.3), channel_id=1, source_target_pairs={{0,12},{4,0},{8,4},{12,8},{1,13},{5,1},{9,5},{13,9},{2,14},{6,2},{... | collective-permute-start | bytes 294920 | tf_op jit(solution)/shard_map/ppermute | solution.py:25
  5.1 1.0 %fusion.7 = (f32[4,3,2,1,1,256]{5,4,3,2,1,0:T(1,128)S(1)}, f32[4,3,2,1,1,256]{5,4,3,2,1,0:T(1,128)S(1)}) fusion(f32[4,3,2,1,4,256]{5,4,3,2,1,0:T(4,128)} %refs_3_.3), kind=kLoop, calls=%fused_computation.35 | loop fusion | bytes 98304 | tf_op jit(solution)/shard_map/slice | solution.py:282
  6.1 0.1 collective-permute-start.2
  6.2 1.7 %collective-permute-start.3 = (f32[4,3,2,1,1,256]{5,4,3,2,1,0:T(1,128)S(1)}, f32[4,3,2,1,1,256]{5,4,3,2,1,0:T(1,128)S(1)}, u32[]{:S(2)}, u32[]{:S(2)}) collective-permute-start(f32[4,3,2,1,1,256]{5,4,3,2,1,0:T(1,128)S(1)} %get-tuple-element.21), channel_id=1, source_target_pairs={{0,3},{1,0},{2,1},{3,2},{4,7},{5,4},{6,5},{7,6},{8,11},{9,8},{10,9... | collective-permute-start | bytes 73736 | tf_op jit(solution)/shard_map/ppermute | solution.py:25
  7.9 0.9 %slice_bitcast_fusion.1 = f32[3,3,2,1,4,256]{5,4,3,2,1,0:T(4,128)S(1)} fusion(f32[4,3,3,2,4,4,256]{6,5,4,3,2,1,0:T(4,128)} %refs_8_.3), kind=kLoop, calls=%fused_computation.10 | loop fusion | bytes 147456 | tf_op jit(solution)/shard_map/squeeze | solution.py:286
  8.8 0.0 collective-permute-start.4
  8.8 1.0 %slice_bitcast_fusion = f32[3,3,2,4,1,256]{5,4,3,2,1,0:T(1,128)S(1)} fusion(f32[4,3,3,2,4,4,256]{6,5,4,3,2,1,0:T(4,128)} %refs_8_.3), kind=kLoop, calls=%fused_computation.9 | loop fusion | bytes 147456 | tf_op jit(solution)/shard_map/squeeze | solution.py:287
  9.9 0.7 %dynamic_slice.3 = s32[4]{0:T(128)S(1)} dynamic-slice(s32[8]{0:T(128)} %param.6, s32[]{:T(128)S(6)} %select_n.94), dynamic_slice_sizes={4} | dynamic-slice | bytes 36 | tf_op jit(solution)/shard_map/dynamic_slice | solution.py:271
  10.7 0.1 compare_convert_fusion
  10.7 0.1 fusion.4
  10.8 0.0 collective-permute-done.2.refs_6_
  10.8 0.1 collective-permute-start.5
  10.9 0.6 pad_maximum_fusion.refs_2_
  11.4 0.7 reshape.147.refs_1_
  12.1 0.6 reshape.146.refs_0_
  12.7 2.3 %collective-permute-done.4.refs_9_ = f32[3,3,2,1,4,256]{5,4,3,2,1,0:T(4,128)S(1)} collective-permute-done((f32[3,3,2,1,4,256]{5,4,3,2,1,0:T(4,128)S(1)}, f32[3,3,2,1,4,256]{5,4,3,2,1,0:T(4,128)S(1)}, u32[]{:S(2)}, u32[]{:S(2)}) %collective-permute-start.4) | collective-permute-done | bytes 73760 | tf_op jit(solution)/shard_map/ppermute | solution.py:25
  15.0 0.6 copy-done.6
  15.6 0.0 copy-done.7
  15.6 0.0 copy-done.4
  15.7 0.6 copy-done.5
  16.3 14.8 %shard_map.46 = (f32[4,4,3,2,4,4,256]{6,5,4,3,2,1,0:T(4,128)}, bf16[4,4,3,2,1,4,256]{6,5,4,3,2,1,0:T(4,128)(2,1)}, bf16[4,4,3,2,1,4,256]{6,5,4,3,2,1,0:T(4,128)(...) custom-call(f32[16]{0:T(128)} %reshape.146.refs_0_, f32[24]{0:T(128)} %reshape.147.refs_1_, ...), custom_call_target="tpu_custom_call" | custom-call | tf_op jit(solution)/shard_map/pallas_call | solution.py:219
  31.2 0.1 collective-permute-start.8
  31.2 1.7 %collective-permute-start.9 = (f32[4,4,3,2,4,1,256]{6,5,4,3,2,1,0:T(1,128)}, f32[4,4,3,2,4,1,256]{6,5,4,3,2,1,0:T(1,128)S(1)}, u32[]{:S(2)}, u32[]{:S(2)}) collective-permute-start(f32[4,4,3,2,4,1,256]{6,5,4,3,2,1,0:T(1,128)} %get-tuple-element.14), channel_id=1, source_target_pairs={{0,3},{1,0},{2,1},{3,2},{4,7},{5,4},{6,5},{7,6},{8,11},{9,8},{10,9... | collective-permute-start | bytes 1179656 | tf_op jit(solution)/shard_map/ppermute | solution.py:25
  33.0 1.1 %collective-permute-start.6 = (bf16[4,4,3,2,1,4,256]{6,5,4,3,2,1,0:T(4,128)(2,1)}, bf16[4,4,3,2,1,4,256]{6,5,4,3,2,1,0:T(4,128)(2,1)S(1)}, u32[]{:S(2)}, u32[]{:S(2)}) collective-permute-start(bf16[4,4,3,2,1,4,256]{6,5,4,3,2,1,0:T(4,128)(2,1)} %get-tuple-element.11), channel_id=1, source_target_pairs={{0,4},{4,8},{8,12},{12,0},{1,5},{5,9},{9,13},{13,1},{2,6},{6,10},{... | collective-permute-start | bytes 589832 | tf_op jit(solution)/shard_map/ppermute | solution.py:25
  34.1 2.7 %collective-permute-start.7 = (bf16[4,4,3,2,1,4,256]{6,5,4,3,2,1,0:T(4,128)(2,1)}, bf16[4,4,3,2,1,4,256]{6,5,4,3,2,1,0:T(4,128)(2,1)S(1)}, u32[]{:S(2)}, u32[]{:S(2)}) collective-permute-start(bf16[4,4,3,2,1,4,256]{6,5,4,3,2,1,0:T(4,128)(2,1)} %get-tuple-element.12), channel_id=1, source_target_pairs={{0,12},{4,0},{8,4},{12,8},{1,13},{5,1},{9,5},{13,9},{2,14},{6,2},{... | collective-permute-start | bytes 589832 | tf_op jit(solution)/shard_map/ppermute | solution.py:25
  36.8 0.2 copy.10
  36.9 1.7 %collective-permute-start.10 = (bf16[4,16,3,2,4,256]{5,1,4,2,3,0:T(8,128)(2,1)S(1)}, bf16[4,16,3,2,4,256]{5,1,4,2,3,0:T(8,128)(2,1)S(1)}, u32[]{:S(2)}, u32[]{:S(2)}) collective-permute-start(bf16[4,16,3,2,4,256]{5,1,4,2,3,0:T(8,128)(2,1)S(1)} %copy.10), channel_id=1, source_target_pairs={{0,16},{16,0},{1,17},{17,1},{2,18},{18,2},{3,19},{19,3},{4,20},{20... | collective-permute-start | bytes 2359304 | tf_op jit(solution)/shard_map/ppermute | solution.py:29
  38.7 4.1 %collective-permute-done.6.refs_12_ = bf16[4,4,3,2,1,4,256]{6,5,4,3,2,1,0:T(4,128)(2,1)S(1)} collective-permute-done((bf16[4,4,3,2,1,4,256]{6,5,4,3,2,1,0:T(4,128)(2,1)}, bf16[4,4,3,2,1,4,256]{6,5,4,3,2,1,0:T(4,128)(2,1)S(1)}, u32[]{:S(2)}, u32[]{:S(2)}) %collective-permute-start.6) | collective-permute-done | bytes 196640 | tf_op jit(solution)/shard_map/ppermute | solution.py:25
  42.8 2.1 %collective-permute-done.7.refs_13_ = bf16[4,4,3,2,1,4,256]{6,5,4,3,2,1,0:T(4,128)(2,1)S(1)} collective-permute-done((bf16[4,4,3,2,1,4,256]{6,5,4,3,2,1,0:T(4,128)(2,1)}, bf16[4,4,3,2,1,4,256]{6,5,4,3,2,1,0:T(4,128)(2,1)S(1)}, u32[]{:S(2)}, u32[]{:S(2)}) %collective-permute-start.7) | collective-permute-done | bytes 196640 | tf_op jit(solution)/shard_map/ppermute | solution.py:25
  44.9 0.6 copy-done.9
  45.6 0.2 copy-done.2
  45.7 0.1 copy-done.3
  45.8 14.3 %shard_map.47 = bf16[4,4,3,2,4,4,256]{6,5,4,3,2,1,0:T(4,128)(2,1)} custom-call(f32[16]{0:T(128)} %reshape.146.refs_0_, f32[24]{0:T(128)} %reshape.147.refs_1_, f32[2]{0:T(128)} %pad_maximum_fusion.refs_2_, f32[4,3,2,1,4,256]{5,4,3,2,1,0:T(4,128)} %refs_3_.3, f32[4,3,2,1,4,256]{5,4,3,2,1,0:T(4,128)} %copy-done.4, f32[4,3,2,1,4,256]{5,4,3,2,1,0:T(4,128)} %copy-done.5, ...), custom_call_target="tpu_custom_call" | custom-call | tf_op jit(solution)/shard_map/pallas_call | solution.py:219
  60.2 2.5 %convolution_bitcast_fusion.1 = f32[4,4,2,2,4,16]{5,1,2,3,0,4:T(4,128)S(1)} fusion(bf16[4,16,3,2,4,256,1,1]{5,4,3,2,1,0,7,6:T(4,128)(2,1)S(1)} %bitcast.44, bf16[4,4,3,2,4,4,256,1]{6,5,4,3,2,1,0,7:T(4,128)(2,1)} %bitcast.45), kind=kOutput, calls=%fused_computation.1 | convolution fusion | flops 25165824 | bytes 1589248 | tf_op jit(solution)/shard_map/tvcazs,rqcbtzs->rqabtv/dot_general | solution.py:250
  62.7 0.1 add.99
  62.8 0.1 sub.39
  62.9 1.3 %convolution_bitcast_fusion = f32[4,4,2,2,4,16]{5,1,2,3,0,4:T(4,128)S(1)} fusion(bf16[4,16,3,2,4,256]{5,1,4,2,3,0:T(8,128)(2,1)S(1)} %collective-permute-done.10, bf16[4,4,3,2,4,4,256,1]{6,5,4,3,2,1,0,7:T(4,128)(2,1)S(1)} %bitcast.46), kind=kOutput, calls=%fused_computation | convolution fusion | flops 25165824 | bytes 1589248 | tf_op jit(solution)/shard_map/tvcazs,rqcbtzs->rqabtv/dot_general | solution.py:250
  64.2 0.1 add.101
  64.4 0.1 sub.41
  64.5 0.1 copy_dynamic-update-slice_fusion
  64.7 0.1 maximum_bitcast_fusion
  64.8 0.6 collective-permute-start.11
  65.4 4.5 %collective-permute-done.11 = f32[2,4,4,2,4,8]{5,4,3,2,1,0:T(4,128)S(1)} collective-permute-done((f32[2,4,4,2,4,8]{5,4,3,2,1,0:T(4,128)S(1)}, f32[2,4,4,2,4,8]{5,4,3,2,1,0:T(4,128)S(1)}, u32[]{:S(2)}, u32[]{:S(2)}) %collective-permute-start.11) | collective-permute-done | bytes 8224 | tf_op jit(solution)/shard_map/ppermute | solution.py:244
  69.8 0.1 select_add_fusion
  69.9 0.1 collective-permute-start.12
  70.0 1.2 %collective-permute-done.12 = f32[1,4,4,2,4,8]{5,4,3,2,1,0:T(4,128)S(1)} collective-permute-done((f32[1,4,4,2,4,8]{5,4,3,2,1,0:T(4,128)S(1)}, f32[1,4,4,2,4,8]{5,4,3,2,1,0:T(4,128)S(1)}, u32[]{:S(2)}, u32[]{:S(2)}) %collective-permute-start.12) | collective-permute-done | bytes 4128 | tf_op jit(solution)/shard_map/ppermute | solution.py:244
  71.2 0.7 add_bitcast_fusion
  (33 shorter events, 0.3 us)
Async XLA Ops:
  0.0 36.8 %copy-start = (bf16[4,16,3,2,4,256]{5,4,3,2,1,0:T(4,128)(2,1)S(1)}, bf16[4,16,3,2,4,256]{5,4,3,2,1,0:T(4,128)(2,1)}, u32[]{:S(2)}) copy-start(bf16[4,16,3,2,4,256]{5,4,3,2,1,0:T(4,128)(2,1)} %param.7) | copy-start | bytes 2359300
  0.0 15.0 %collective-permute-start = (f32[4,3,2,1,4,256]{5,4,3,2,1,0:T(4,128)}, f32[4,3,2,1,4,256]{5,4,3,2,1,0:T(4,128)S(1)}, u32[]{:S(2)}, u32[]{:S(2)}) collective-permute-start(f32[4,3,2,1,4,256]{5,4,3,2,1,0:T(4,128)} %refs_3_.3), channel_id=1, source_target_pairs={{0,4},{4,8},{8,12},{12,0},{1,5},{5,9},{9,13},{13,1},{2,6},{6,10},{... | collective-permute-start | bytes 294920 | tf_op jit(solution)/shard_map/ppermute | solution.py:25
  3.1 12.0 %collective-permute-start.1 = (f32[4,3,2,1,4,256]{5,4,3,2,1,0:T(4,128)}, f32[4,3,2,1,4,256]{5,4,3,2,1,0:T(4,128)S(1)}, u32[]{:S(2)}, u32[]{:S(2)}) collective-permute-start(f32[4,3,2,1,4,256]{5,4,3,2,1,0:T(4,128)} %refs_3_.3), channel_id=1, source_target_pairs={{0,12},{4,0},{8,4},{12,8},{1,13},{5,1},{9,5},{13,9},{2,14},{6,2},{... | collective-permute-start | bytes 294920 | tf_op jit(solution)/shard_map/ppermute | solution.py:25
  6.1 4.7 %collective-permute-start.2 = (f32[4,3,2,1,1,256]{5,4,3,2,1,0:T(1,128)S(1)}, f32[4,3,2,1,1,256]{5,4,3,2,1,0:T(1,128)S(1)}, u32[]{:S(2)}, u32[]{:S(2)}) collective-permute-start(f32[4,3,2,1,1,256]{5,4,3,2,1,0:T(1,128)S(1)} %get-tuple-element.22), channel_id=1, source_target_pairs={{0,1},{1,2},{2,3},{3,0},{4,5},{5,6},{6,7},{7,4},{8,9},{9,10},{10,1... | collective-permute-start | bytes 73736 | tf_op jit(solution)/shard_map/ppermute | solution.py:25
  6.2 6.5 %collective-permute-start.3 = (f32[4,3,2,1,1,256]{5,4,3,2,1,0:T(1,128)S(1)}, f32[4,3,2,1,1,256]{5,4,3,2,1,0:T(1,128)S(1)}, u32[]{:S(2)}, u32[]{:S(2)}) collective-permute-start(f32[4,3,2,1,1,256]{5,4,3,2,1,0:T(1,128)S(1)} %get-tuple-element.21), channel_id=1, source_target_pairs={{0,3},{1,0},{2,1},{3,2},{4,7},{5,4},{6,5},{7,6},{8,11},{9,8},{10,9... | collective-permute-start | bytes 73736 | tf_op jit(solution)/shard_map/ppermute | solution.py:25
  8.8 6.2 %collective-permute-start.4 = (f32[3,3,2,1,4,256]{5,4,3,2,1,0:T(4,128)S(1)}, f32[3,3,2,1,4,256]{5,4,3,2,1,0:T(4,128)S(1)}, u32[]{:S(2)}, u32[]{:S(2)}) collective-permute-start(f32[3,3,2,1,4,256]{5,4,3,2,1,0:T(4,128)S(1)} %slice_bitcast_fusion.1), channel_id=1, source_target_pairs={{0,4},{4,8},{8,12},{12,0},{1,5},{5,9},{9,13},{13,1},{2,6},{6,10},{... | collective-permute-start | bytes 221192 | tf_op jit(solution)/shard_map/ppermute | solution.py:25
  10.8 4.2 %copy-start.10 = (f32[4,3,2,1,1,256]{5,4,3,2,1,0:T(1,128)}, f32[4,3,2,1,1,256]{5,4,3,2,1,0:T(1,128)S(1)}, u32[]{:S(2)}) copy-start(f32[4,3,2,1,1,256]{5,4,3,2,1,0:T(1,128)S(1)} %collective-permute-done.2.refs_6_) | copy-start | bytes 73732
  10.8 4.2 %collective-permute-start.5 = (f32[3,3,2,4,1,256]{5,4,3,2,1,0:T(1,128)S(1)}, f32[3,3,2,4,1,256]{5,4,3,2,1,0:T(1,128)S(1)}, u32[]{:S(2)}, u32[]{:S(2)}) collective-permute-start(f32[3,3,2,4,1,256]{5,4,3,2,1,0:T(1,128)S(1)} %slice_bitcast_fusion), channel_id=1, source_target_pairs={{0,1},{1,2},{2,3},{3,0},{4,5},{5,6},{6,7},{7,4},{8,9},{9,10},{10,1... | collective-permute-start | bytes 221192 | tf_op jit(solution)/shard_map/ppermute | solution.py:25
  12.7 2.3 %copy-start.11 = (f32[4,3,2,1,1,256]{5,4,3,2,1,0:T(1,128)}, f32[4,3,2,1,1,256]{5,4,3,2,1,0:T(1,128)S(1)}, u32[]{:S(2)}) copy-start(f32[4,3,2,1,1,256]{5,4,3,2,1,0:T(1,128)S(1)} %collective-permute-done.3.refs_7_) | copy-start | bytes 73732
  15.0 0.6 copy-start.6
  15.0 0.6 copy-start.7
  15.0 0.7 copy-start.4
  15.7 0.6 copy-start.5
  31.2 13.7 %collective-permute-start.8 = (f32[4,4,3,2,4,1,256]{6,5,4,3,2,1,0:T(1,128)}, f32[4,4,3,2,4,1,256]{6,5,4,3,2,1,0:T(1,128)S(1)}, u32[]{:S(2)}, u32[]{:S(2)}) collective-permute-start(f32[4,4,3,2,4,1,256]{6,5,4,3,2,1,0:T(1,128)} %get-tuple-element.13), channel_id=1, source_target_pairs={{0,1},{1,2},{2,3},{3,0},{4,5},{5,6},{6,7},{7,4},{8,9},{9,10},{10,1... | collective-permute-start | bytes 1179656 | tf_op jit(solution)/shard_map/ppermute | solution.py:25
  31.2 13.7 %collective-permute-start.9 = (f32[4,4,3,2,4,1,256]{6,5,4,3,2,1,0:T(1,128)}, f32[4,4,3,2,4,1,256]{6,5,4,3,2,1,0:T(1,128)S(1)}, u32[]{:S(2)}, u32[]{:S(2)}) collective-permute-start(f32[4,4,3,2,4,1,256]{6,5,4,3,2,1,0:T(1,128)} %get-tuple-element.14), channel_id=1, source_target_pairs={{0,3},{1,0},{2,1},{3,2},{4,7},{5,4},{6,5},{7,6},{8,11},{9,8},{10,9... | collective-permute-start | bytes 1179656 | tf_op jit(solution)/shard_map/ppermute | solution.py:25
  33.0 9.8 %collective-permute-start.6 = (bf16[4,4,3,2,1,4,256]{6,5,4,3,2,1,0:T(4,128)(2,1)}, bf16[4,4,3,2,1,4,256]{6,5,4,3,2,1,0:T(4,128)(2,1)S(1)}, u32[]{:S(2)}, u32[]{:S(2)}) collective-permute-start(bf16[4,4,3,2,1,4,256]{6,5,4,3,2,1,0:T(4,128)(2,1)} %get-tuple-element.11), channel_id=1, source_target_pairs={{0,4},{4,8},{8,12},{12,0},{1,5},{5,9},{9,13},{13,1},{2,6},{6,10},{... | collective-permute-start | bytes 589832 | tf_op jit(solution)/shard_map/ppermute | solution.py:25
  34.1 10.8 %collective-permute-start.7 = (bf16[4,4,3,2,1,4,256]{6,5,4,3,2,1,0:T(4,128)(2,1)}, bf16[4,4,3,2,1,4,256]{6,5,4,3,2,1,0:T(4,128)(2,1)S(1)}, u32[]{:S(2)}, u32[]{:S(2)}) collective-permute-start(bf16[4,4,3,2,1,4,256]{6,5,4,3,2,1,0:T(4,128)(2,1)} %get-tuple-element.12), channel_id=1, source_target_pairs={{0,12},{4,0},{8,4},{12,8},{1,13},{5,1},{9,5},{13,9},{2,14},{6,2},{... | collective-permute-start | bytes 589832 | tf_op jit(solution)/shard_map/ppermute | solution.py:25
  36.9 26.0 %collective-permute-start.10 = (bf16[4,16,3,2,4,256]{5,1,4,2,3,0:T(8,128)(2,1)S(1)}, bf16[4,16,3,2,4,256]{5,1,4,2,3,0:T(8,128)(2,1)S(1)}, u32[]{:S(2)}, u32[]{:S(2)}) collective-permute-start(bf16[4,16,3,2,4,256]{5,1,4,2,3,0:T(8,128)(2,1)S(1)} %copy.10), channel_id=1, source_target_pairs={{0,16},{16,0},{1,17},{17,1},{2,18},{18,2},{3,19},{19,3},{4,20},{20... | collective-permute-start | bytes 2359304 | tf_op jit(solution)/shard_map/ppermute | solution.py:29
  42.8 2.1 %copy-start.8 = (bf16[4,4,3,2,1,4,256]{6,5,4,3,2,1,0:T(4,128)(2,1)}, bf16[4,4,3,2,1,4,256]{6,5,4,3,2,1,0:T(4,128)(2,1)S(1)}, u32[]{:S(2)}) copy-start(bf16[4,4,3,2,1,4,256]{6,5,4,3,2,1,0:T(4,128)(2,1)S(1)} %collective-permute-done.6.refs_12_) | copy-start | bytes 589828
  44.9 0.7 copy-start.9
  44.9 0.8 %copy-start.2 = (f32[4,4,3,2,4,1,256]{6,5,4,3,2,1,0:T(1,128)}, f32[4,4,3,2,4,1,256]{6,5,4,3,2,1,0:T(1,128)S(1)}, u32[]{:S(2)}) copy-start(f32[4,4,3,2,4,1,256]{6,5,4,3,2,1,0:T(1,128)S(1)} %collective-permute-done.8.refs_14_) | copy-start | bytes 1179652
  44.9 0.9 %copy-start.3 = (f32[4,4,3,2,4,1,256]{6,5,4,3,2,1,0:T(1,128)}, f32[4,4,3,2,4,1,256]{6,5,4,3,2,1,0:T(1,128)S(1)}, u32[]{:S(2)}) copy-start(f32[4,4,3,2,4,1,256]{6,5,4,3,2,1,0:T(1,128)S(1)} %collective-permute-done.9.refs_15_) | copy-start | bytes 1179652
  60.2 2.8 %copy-start.1 = (bf16[4,4,3,2,4,4,256]{6,5,4,3,2,1,0:T(4,128)(2,1)S(1)}, bf16[4,4,3,2,4,4,256]{6,5,4,3,2,1,0:T(4,128)(2,1)}, u32[]{:S(2)}) copy-start(bf16[4,4,3,2,4,4,256]{6,5,4,3,2,1,0:T(4,128)(2,1)} %shard_map.47) | copy-start | bytes 2359300
  64.8 5.0 %collective-permute-start.11 = (f32[2,4,4,2,4,8]{5,4,3,2,1,0:T(4,128)S(1)}, f32[2,4,4,2,4,8]{5,4,3,2,1,0:T(4,128)S(1)}, u32[]{:S(2)}, u32[]{:S(2)}) collective-permute-start(f32[2,4,4,2,4,8]{5,4,3,2,1,0:T(4,128)S(1)} %slice_select_fusion), channel_id=1, source_target_pairs={{0,2},{1,3},{2,0},{3,1},{4,6},{5,7},{6,4},{7,5},{8,10},{9,11},{10,... | collective-permute-start | bytes 24584 | tf_op jit(solution)/shard_map/ppermute | solution.py:244
  69.9 1.3 %collective-permute-start.12 = (f32[1,4,4,2,4,8]{5,4,3,2,1,0:T(4,128)S(1)}, f32[1,4,4,2,4,8]{5,4,3,2,1,0:T(4,128)S(1)}, u32[]{:S(2)}, u32[]{:S(2)}) collective-permute-start(f32[1,4,4,2,4,8]{5,4,3,2,1,0:T(4,128)S(1)} %slice_select_fusion.1), channel_id=1, source_target_pairs={{0,1},{1,0},{2,3},{3,2},{4,5},{5,4},{6,7},{7,6},{8,9},{9,8},{10,11... | collective-permute-start | bytes 12296 | tf_op jit(solution)/shard_map/ppermute | solution.py:244

commit v4 on v3

--- a/solution.py
+++ b/solution.py
@@ -45,46 +45,63 @@
     rest = refs[11:]
     if first:
         out_ref, tfirst_ref, tlast_ref, zfirst_ref, zlast_ref = rest[:5]
-        pad_ref, src_ref, zlo_s, zhi_s, ut_s = rest[5:]
-        zlo_src, zhi_src = zlo_s, zhi_s
+        scratch = rest[5:]
     else:
-        psi_ref, tlo_ref, thi_ref, zlo_src, zhi_src = rest[:5]
+        psi_ref, tlo_ref, thi_ref, zlo_ref, zhi_ref = rest[:5]
         out_ref = rest[5]
-        pad_ref, src_ref, ut_s = rest[6:]
-    S, C, RI, T, Z, L = src_ref.shape
-    K = noise_ref.shape[2]
+        scratch = rest[6:]
+    pad_ref, src_ref, zlo_s, zhi_s, u8, ut8, uz8 = scratch
+    S, C, RI, T, ROWS, L = src_ref.shape
+    Z = ROWS // 2
+    K = noise_ref.shape[3]
     span = T // K
-    r = pl.program_id(0)
-
-    @pl.when(r == 0)
+    h = pl.program_id(0)
+    lower = pl.ds(0, Z)
+    upper = pl.ds(Z, Z)
+
+    @pl.when(h == 0)
     def _():
         for a in range(3):
             for b in range(3):
                 for ri in range(RI):
-                    ut_s[a, b, ri, pl.ds(0, 1)] = utedge_ref[a, b, ri]
-                    ut_s[a, b, ri, pl.ds(1, T)] = u_ref[3, a, b, ri]
+                    for half in (lower, upper):
+                        ut8[a, b, ri, pl.ds(0, 1), half] = utedge_ref[a, b, ri]
+                        ut8[a, b, ri, pl.ds(1, T), half] = u_ref[3, a, b, ri]
+                        for t in range(T):
+                            uz8[a, b, ri, t, half] = jnp.broadcast_to(uzedge_ref[a, b, ri, t], (Z, L))
+                        for mu in range(4):
+                            u8[mu, a, b, ri, :, half] = u_ref[mu, a, b, ri]
 
     for s in range(S):
-        fs = smask_ref[r * S + s]
         for c in range(C):
             for ri in range(RI):
-                for t in range(T):
-                    src_ref[s, c, ri, t] = noise_ref[c, ri, t // span] * (fs * tmask_ref[r * (T + 2) + t + 1])
+                for g, half in ((0, lower), (1, upper)):
+                    r = 2 * h + g
+                    fs = smask_ref[r * S + s]
+                    for t in range(T):
+                        src_ref[s, c, ri, t, half] = noise_ref[g, c, ri, t // span] * (
+                            fs * tmask_ref[r * (T + 2) + t + 1])
+                    if first:
+                        pad_ref[s, c, ri, 0, half] = ntlo_ref[g, c, ri, 0] * (
+                            fs * tmask_ref[r * (T + 2)] * sign_ref[0])
+                        pad_ref[s, c, ri, T + 1, half] = nthi_ref[g, c, ri, 0] * (
+                            fs * tmask_ref[r * (T + 2) + T + 1] * sign_ref[1])
+                        for t in range(T):
+                            f = fs * tmask_ref[r * (T + 2) + t + 1]
+                            zlo_s[s, c, ri, t, half] = jnp.broadcast_to(nzlo_ref[g, c, ri, t // span] * f, (Z, L))
+                            zhi_s[s, c, ri, t, half] = jnp.broadcast_to(nzhi_ref[g, c, ri, t // span] * f, (Z, L))
+                    else:
+                        for t in range(T):
+                            zlo_s[s, c, ri, t, half] = jnp.broadcast_to(zlo_ref[s, c, ri, t, pl.ds(g, 1)], (Z, L))
+                            zhi_s[s, c, ri, t, half] = jnp.broadcast_to(zhi_ref[s, c, ri, t, pl.ds(g, 1)], (Z, L))
                 if first:
                     pad_ref[s, c, ri, pl.ds(1, T)] = src_ref[s, c, ri]
-                    pad_ref[s, c, ri, 0] = ntlo_ref[c, ri, 0] * (fs * tmask_ref[r * (T + 2)] * sign_ref[0])
-                    pad_ref[s, c, ri, T + 1] = nthi_ref[c, ri, 0] * (
-                        fs * tmask_ref[r * (T + 2) + T + 1] * sign_ref[1])
-                    for t in range(T):
-                        f = fs * tmask_ref[r * (T + 2) + t + 1]
-                        zlo_s[s, c, ri, t] = nzlo_ref[c, ri, t // span] * f
-                        zhi_s[s, c, ri, t] = nzhi_ref[c, ri, t // span] * f
                 else:
                     pad_ref[s, c, ri, pl.ds(1, T)] = psi_ref[s, c, ri]
                     pad_ref[s, c, ri, pl.ds(0, 1)] = tlo_ref[s, c, ri].astype(jnp.float32) * sign_ref[0]
                     pad_ref[s, c, ri, pl.ds(T + 1, 1)] = thi_ref[s, c, ri].astype(jnp.float32) * sign_ref[1]
-    xpos = lax.broadcasted_iota(jnp.int32, (Z, L), 1) % NX
-    zpos = lax.broadcasted_iota(jnp.int32, (Z, L), 0)
+    xpos = lax.broadcasted_iota(jnp.int32, (ROWS, L), 1) % NX
+    zpos = lax.broadcasted_iota(jnp.int32, (ROWS, L), 0) % Z
     x_last = xpos == NX - 1
     x_first = xpos == 0
     z_last = zpos == Z - 1
@@ -102,10 +119,8 @@
             v = pad_ref[s, c, ri, t + 1]
             if mu == 2:
                 if stride == 1:
-                    halo = jnp.broadcast_to(zhi_src[s, c, ri, t], (Z, L))
-                    return jnp.where(z_last, halo, pltpu.roll(v, Z - 1, axis=0))
-                halo = jnp.broadcast_to(zlo_src[s, c, ri, t], (Z, L))
-                return jnp.where(z_first, halo, pltpu.roll(v, 1, axis=0))
+                    return jnp.where(z_last, zhi_s[s, c, ri, t], pltpu.roll(v, ROWS - 1, axis=0))
+                return jnp.where(z_first, zlo_s[s, c, ri, t], pltpu.roll(v, 1, axis=0))
             if mu == 1:
                 return pltpu.roll(v, (L - NX) if stride == 1 else NX, axis=1)
             if stride == 1:
@@ -114,11 +129,10 @@
 
         def back_link(mu, a, b, ri):
             if mu == 3:
-                return ut_s[a, b, ri, t]
-            v = u_ref[mu, a, b, ri, t]
+                return ut8[a, b, ri, t]
+            v = u8[mu, a, b, ri, t]
             if mu == 2:
-                edge = jnp.broadcast_to(uzedge_ref[a, b, ri, t], (Z, L))
-                return jnp.where(z_first, edge, pltpu.roll(v, 1, axis=0))
+                return jnp.where(z_first, uz8[a, b, ri, t], pltpu.roll(v, 1, axis=0))
             if mu == 1:
                 return pltpu.roll(v, NX, axis=1)
             return x_back(v)
@@ -140,7 +154,7 @@
                         colours.append((sre + pre, sim + pim))
                     half.append(colours)
                 if stride == 1:
-                    links = [[(u_ref[mu, a, b, 0, t], u_ref[mu, a, b, 1, t]) for b in range(3)] for a in range(3)]
+                    links = [[(u8[mu, a, b, 0, t], u8[mu, a, b, 1, t]) for b in range(3)] for a in range(3)]
                 else:
                     links = [[(back_link(mu, b, a, 0), back_link(mu, b, a, 1)) for b in range(3)] for a in range(3)]
                 for k, s in enumerate(heads):
@@ -181,44 +195,54 @@
                 for ri in range(RI):
                     tfirst_ref[s, c, ri] = out_ref[s, c, ri, pl.ds(0, 1)].astype(tfirst_ref.dtype)
                     tlast_ref[s, c, ri] = out_ref[s, c, ri, pl.ds(T - 1, 1)].astype(tlast_ref.dtype)
-                    zfirst_ref[s, c, ri] = out_ref[s, c, ri, :, pl.ds(0, 1), :]
-                    zlast_ref[s, c, ri] = out_ref[s, c, ri, :, pl.ds(Z - 1, 1), :]
+                    for g in range(2):
+                        zfirst_ref[s, c, ri, :, pl.ds(g, 1), :] = out_ref[s, c, ri, :, pl.ds(g * Z, 1), :]
+                        zlast_ref[s, c, ri, :, pl.ds(g, 1), :] = out_ref[s, c, ri, :, pl.ds(g * Z + Z - 1, 1), :]
 
 
 def hopping_step(first, scalars, noise_parts, link_parts, spinor_parts):
     R, C, RI, K, Z, L = noise_parts[0].shape
     T = link_parts[0].shape[4]
     S = 4
-    index = lambda r: (r,) + (0,) * 6
-    index6 = lambda r: (r,) + (0,) * 5
-    whole = lambda x: pl.BlockSpec(x.shape, lambda r: (0,) * x.ndim)
+    H = R // 2
+    ROWS = 2 * Z
+    index = lambda h: (h,) + (0,) * 6
+    index6 = lambda h: (h,) + (0,) * 5
+    whole = lambda x: pl.BlockSpec(x.shape, lambda h: (0,) * x.ndim)
     smem = pl.BlockSpec(memory_space=pltpu.SMEM)
-    site_block = pl.BlockSpec((None, S, C, RI, T, Z, L), index)
-    t_block = pl.BlockSpec((None, S, C, RI, 1, Z, L), index)
-    z_block = pl.BlockSpec((None, S, C, RI, T, 1, L), index)
+    site_block = pl.BlockSpec((None, S, C, RI, T, ROWS, L), index)
+    t_block = pl.BlockSpec((None, S, C, RI, 1, ROWS, L), index)
+    z_block = pl.BlockSpec((None, S, C, RI, T, 2, L), index)
     noise_specs = [
-        pl.BlockSpec((None, C, RI, K, Z, L), index6),
-        pl.BlockSpec((None, C, RI, 1, Z, L), index6),
-        pl.BlockSpec((None, C, RI, 1, Z, L), index6),
-        pl.BlockSpec((None, C, RI, K, 1, L), index6),
-        pl.BlockSpec((None, C, RI, K, 1, L), index6),
+        pl.BlockSpec((2, C, RI, K, Z, L), index6),
+        pl.BlockSpec((2, C, RI, 1, Z, L), index6),
+        pl.BlockSpec((2, C, RI, 1, Z, L), index6),
+        pl.BlockSpec((2, C, RI, K, 1, L), index6),
+        pl.BlockSpec((2, C, RI, K, 1, L), index6),
     ]
     in_specs = [smem, smem, smem] + noise_specs + [whole(x) for x in link_parts]
-    scratch = [pltpu.VMEM((S, C, RI, T + 2, Z, L), jnp.float32), pltpu.VMEM((S, C, RI, T, Z, L), jnp.float32)]
+    site_shape = (H, S, C, RI, T, ROWS, L)
     if first:
-        t_shape = jax.ShapeDtypeStruct((R, S, C, RI, 1, Z, L), jnp.bfloat16)
-        z_shape = jax.ShapeDtypeStruct((R, S, C, RI, T, 1, L), jnp.float32)
-        out_shape = [jax.ShapeDtypeStruct((R, S, C, RI, T, Z, L), jnp.float32), t_shape, t_shape, z_shape, z_shape]
+        t_shape = jax.ShapeDtypeStruct((H, S, C, RI, 1, ROWS, L), jnp.bfloat16)
+        z_shape = jax.ShapeDtypeStruct((H, S, C, RI, T, 2, L), jnp.float32)
+        out_shape = [jax.ShapeDtypeStruct(site_shape, jnp.float32), t_shape, t_shape, z_shape, z_shape]
         out_specs = [site_block, t_block, t_block, z_block, z_block]
-        scratch += [pltpu.VMEM((S, C, RI, T, 1, L), jnp.float32)] * 2
     else:
         in_specs += [site_block, t_block, t_block, z_block, z_block]
-        out_shape = jax.ShapeDtypeStruct((R, S, C, RI, T, Z, L), jnp.bfloat16)
+        out_shape = jax.ShapeDtypeStruct(site_shape, jnp.bfloat16)
         out_specs = site_block
-    scratch += [pltpu.VMEM((3, 3, RI, T + 1, Z, L), jnp.float32)]
+    scratch = [
+        pltpu.VMEM((S, C, RI, T + 2, ROWS, L), jnp.float32),
+        pltpu.VMEM((S, C, RI, T, ROWS, L), jnp.float32),
+        pltpu.VMEM((S, C, RI, T, ROWS, L), jnp.float32),
+        pltpu.VMEM((S, C, RI, T, ROWS, L), jnp.float32),
+        pltpu.VMEM((4, 3, 3, RI, T, ROWS, L), jnp.float32),
+        pltpu.VMEM((3, 3, RI, T + 1, ROWS, L), jnp.float32),
+        pltpu.VMEM((3, 3, RI, T, ROWS, L), jnp.float32),
+    ]
     return pl.pallas_call(
         functools.partial(hop_kernel, first),
-        grid=(R,),
+        grid=(H,),
         in_specs=in_specs,
         out_specs=out_specs,
         out_shape=out_shape,
@@ -294,6 +318,9 @@
         passed_along(z_first, "sa", -1),
     )
     rounded = hopping_step(False, scalars, noise_parts, link_parts, (spinor,) + halos)
+    H, S, C, RI, T, ROWS, L = rounded.shape
+    rounded = jnp.moveaxis(rounded.reshape(H, S, C, RI, T, 2, ROWS // 2, L), 5, 1).reshape(
+        2 * H, S, C, RI, T, ROWS // 2, L)
     own_part = intersection_part(rounded, vectors)
     partner_part = intersection_part(rounded, partner_vectors)
     lower_half = jnp.where(section_index == 0, own_part, partner_part)

time: 72.2 us -> 64.5 us (0.89)
  Pallas kernels: 29.1 us -> 20.4 us
  local copies, waits for them, and re-layouts: 7.96 us -> 9.75 us
  matrix products: 3.71 us -> 2.52 us
    pallas_call x2, Pallas kernels: 29.1 us -> 20.4 us  [hopping_step(): pl.pallas_call(functools.partial(hop_kernel, first), grid=(H,), in_specs=...]
    slice x0 -> x1, local copies, waits for them, and re-layouts: none -> 1.8 us
    dot_general x2, matrix products: 3.71 us -> 2.52 us  [intersection_part(): jnp.einsum('tvcazs,rqcbtzs->rqabtv', vector_piece, rounded, preferred_ele...]
    unnamed x27 -> x25, local copies, waits for them, and re-layouts: 2.48 us -> 2.48 us
  transfers between devices with their start and end apart: 13 -> 13, of which waited for: 5 -> 5; matrix products, arithmetic and copies ran while one was open for 12% -> 15% of each run, Pallas kernels for 20% -> 16%
where the time goes in v4:
time: 64.5 us; the launch traced here: 64.2 us
  Pallas kernels  20.4 us (32%)
  starting transfers between devices  15 us (23%)
  waiting for transfers between devices  14.2 us (22%)
  local copies, waits for them, and re-layouts  9.75 us (15%)
  matrix products  2.52 us (4%)
  other arithmetic  2.13 us (3%)
    pallas_call x2, Pallas kernels, hopping_step(): pl.pallas_call(functools.partial(hop_kernel, first), grid=(H,), in_specs=...  20.4 us
    ppermute x10, starting transfers between devices, passed_along(): return lax.ppermute(value, axis, pairs)  12.6 us
    ppermute x10, waiting for transfers between devices, passed_along(): return lax.ppermute(value, axis, pairs)  8.51 us
    ppermute x2, waiting for transfers between devices, reduce_scatter_sa(): x = keep + lax.ppermute(send, 'sa', [(j, j ^ d) for j in range(n)])  5.7 us
    dot_general x2, matrix products, intersection_part(): jnp.einsum('tvcazs,rqcbtzs->rqabtv', vector_piece, rounded, preferred_ele...  2.52 us
    unnamed x25, local copies, waits for them, and re-layouts  2.48 us
    slice x1, local copies, waits for them, and re-layouts  1.8 us
    ppermute x1, starting transfers between devices, from_partner(): lax.ppermute(x, axis, [(i, i ^ 1 << stride) for i in range(lax.axis_size(...  1.73 us
  transfers between devices with their start and end apart: 13, of which 5 were waited for; matrix products, arithmetic and copies ran while one was open for 15% of the time, Pallas kernels for 16%

profile of v4, /device:TPU:0, one launch (start us, length us, event | category | flops | bytes accessed | tf_op | source)
XLA Modules:
  0.0 64.2 jit_solution(15914156180499208216)
XLA Ops:
  0.0 3.1 %collective-permute-start = (f32[4,3,2,1,4,256]{5,4,3,2,1,0:T(4,128)}, f32[4,3,2,1,4,256]{5,4,3,2,1,0:T(4,128)S(1)}, u32[]{:S(2)}, u32[]{:S(2)}) collective-permute-start(f32[4,3,2,1,4,256]{5,4,3,2,1,0:T(4,128)} %refs_3_.3), channel_id=1, source_target_pairs={{0,4},{4,8},{8,12},{12,0},{1,5},{5,9},{9,13},{13,1},{2,6},{6,10},{... | collective-permute-start | bytes 294920 | tf_op jit(solution)/shard_map/ppermute | solution.py:25
  3.1 2.1 %collective-permute-start.1 = (f32[4,3,2,1,4,256]{5,4,3,2,1,0:T(4,128)}, f32[4,3,2,1,4,256]{5,4,3,2,1,0:T(4,128)S(1)}, u32[]{:S(2)}, u32[]{:S(2)}) collective-permute-start(f32[4,3,2,1,4,256]{5,4,3,2,1,0:T(4,128)} %refs_3_.3), channel_id=1, source_target_pairs={{0,12},{4,0},{8,4},{12,8},{1,13},{5,1},{9,5},{13,9},{2,14},{6,2},{... | collective-permute-start | bytes 294920 | tf_op jit(solution)/shard_map/ppermute | solution.py:25
  5.1 1.0 %fusion.8 = (f32[4,3,2,1,1,256]{5,4,3,2,1,0:T(1,128)S(1)}, f32[4,3,2,1,1,256]{5,4,3,2,1,0:T(1,128)S(1)}) fusion(f32[4,3,2,1,4,256]{5,4,3,2,1,0:T(4,128)} %refs_3_.3), kind=kLoop, calls=%fused_computation.37 | loop fusion | bytes 98304 | tf_op jit(solution)/shard_map/slice | solution.py:306
  6.1 0.1 collective-permute-start.2
  6.2 1.7 %collective-permute-start.3 = (f32[4,3,2,1,1,256]{5,4,3,2,1,0:T(1,128)S(1)}, f32[4,3,2,1,1,256]{5,4,3,2,1,0:T(1,128)S(1)}, u32[]{:S(2)}, u32[]{:S(2)}) collective-permute-start(f32[4,3,2,1,1,256]{5,4,3,2,1,0:T(1,128)S(1)} %get-tuple-element.23), channel_id=1, source_target_pairs={{0,3},{1,0},{2,1},{3,2},{4,7},{5,4},{6,5},{7,6},{8,11},{9,8},{10,9... | collective-permute-start | bytes 73736 | tf_op jit(solution)/shard_map/ppermute | solution.py:25
  7.9 0.9 %slice_bitcast_fusion.1 = f32[3,3,2,1,4,256]{5,4,3,2,1,0:T(4,128)S(1)} fusion(f32[4,3,3,2,4,4,256]{6,5,4,3,2,1,0:T(4,128)} %refs_8_.3), kind=kLoop, calls=%fused_computation.11 | loop fusion | bytes 147456 | tf_op jit(solution)/shard_map/squeeze | solution.py:310
  8.8 1.0 %slice_bitcast_fusion = f32[3,3,2,4,1,256]{5,4,3,2,1,0:T(1,128)S(1)} fusion(f32[4,3,3,2,4,4,256]{6,5,4,3,2,1,0:T(4,128)} %refs_8_.3), kind=kLoop, calls=%fused_computation.10 | loop fusion | bytes 147456 | tf_op jit(solution)/shard_map/squeeze | solution.py:311
  9.9 0.7 %dynamic_slice.3 = s32[4]{0:T(128)S(1)} dynamic-slice(s32[8]{0:T(128)} %param.6, s32[]{:T(128)S(6)} %select_n.94), dynamic_slice_sizes={4} | dynamic-slice | bytes 36 | tf_op jit(solution)/shard_map/dynamic_slice | solution.py:295
  10.7 0.1 compare_convert_fusion
  10.7 0.1 fusion.4
  10.8 0.1 collective-permute-start.5
  10.9 0.6 pad_maximum_fusion.1.refs_2_
  11.4 0.7 %reshape.152.refs_1_ = f32[24]{0:T(128)} reshape(f32[4,6]{1,0:T(4,128)S(1)} %compare_convert_fusion) | data formatting | bytes 192 | tf_op jit(solution)/shard_map/convert_element_type | solution.py:299
  12.1 0.6 reshape.151.refs_0_
  12.7 2.3 %collective-permute-done.4.refs_9_ = f32[3,3,2,1,4,256]{5,4,3,2,1,0:T(4,128)S(1)} collective-permute-done((f32[3,3,2,1,4,256]{5,4,3,2,1,0:T(4,128)S(1)}, f32[3,3,2,1,4,256]{5,4,3,2,1,0:T(4,128)S(1)}, u32[]{:S(2)}, u32[]{:S(2)}) %collective-permute-start.4) | collective-permute-done | bytes 73760 | tf_op jit(solution)/shard_map/ppermute | solution.py:25
  15.0 0.6 copy-done.5
  15.6 0.0 copy-done.6
  15.6 0.0 copy-done.3
  15.7 0.6 %copy-done.4 = f32[4,3,2,1,4,256]{5,4,3,2,1,0:T(4,128)} copy-done((f32[4,3,2,1,4,256]{5,4,3,2,1,0:T(4,128)}, f32[4,3,2,1,4,256]{5,4,3,2,1,0:T(4,128)S(1)}, u32[]{:S(2)}) %copy-start.4) | copy-done | bytes 98328
  16.3 10.3 %shard_map.46 = (f32[2,4,3,2,4,8,256]{6,5,4,3,2,1,0:T(8,128)}, bf16[2,4,3,2,1,8,256]{6,5,4,3,2,1,0:T(8,128)(2,1)}, bf16[2,4,3,2,1,8,256]{6,5,4,3,2,1,0:T(8,128)(...) custom-call(f32[16]{0:T(128)} %reshape.151.refs_0_, f32[24]{0:T(128)} %reshape.152.refs_1_, ...), custom_call_target="tpu_custom_call" | custom-call | tf_op jit(solution)/shard_map/pallas_call | solution.py:243
  26.6 0.1 collective-permute-start.8
  26.7 1.7 %collective-permute-start.9 = (f32[2,4,3,2,4,2,256]{6,5,4,3,2,1,0:T(2,128)}, f32[2,4,3,2,4,2,256]{6,5,4,3,2,1,0:T(2,128)S(1)}, u32[]{:S(2)}, u32[]{:S(2)}) collective-permute-start(f32[2,4,3,2,4,2,256]{6,5,4,3,2,1,0:T(2,128)} %get-tuple-element.14), channel_id=1, source_target_pairs={{0,3},{1,0},{2,1},{3,2},{4,7},{5,4},{6,5},{7,6},{8,11},{9,8},{10,9... | collective-permute-start | bytes 1179656 | tf_op jit(solution)/shard_map/ppermute | solution.py:25
  28.4 1.1 %collective-permute-start.6 = (bf16[2,4,3,2,1,8,256]{6,5,4,3,2,1,0:T(8,128)(2,1)}, bf16[2,4,3,2,1,8,256]{6,5,4,3,2,1,0:T(8,128)(2,1)S(1)}, u32[]{:S(2)}, u32[]{:S(2)}) collective-permute-start(bf16[2,4,3,2,1,8,256]{6,5,4,3,2,1,0:T(8,128)(2,1)} %get-tuple-element.11), channel_id=1, source_target_pairs={{0,4},{4,8},{8,12},{12,0},{1,5},{5,9},{9,13},{13,1},{2,6},{6,10},{... | collective-permute-start | bytes 589832 | tf_op jit(solution)/shard_map/ppermute | solution.py:25
  29.5 2.7 %collective-permute-start.7 = (bf16[2,4,3,2,1,8,256]{6,5,4,3,2,1,0:T(8,128)(2,1)}, bf16[2,4,3,2,1,8,256]{6,5,4,3,2,1,0:T(8,128)(2,1)S(1)}, u32[]{:S(2)}, u32[]{:S(2)}) collective-permute-start(bf16[2,4,3,2,1,8,256]{6,5,4,3,2,1,0:T(8,128)(2,1)} %get-tuple-element.12), channel_id=1, source_target_pairs={{0,12},{4,0},{8,4},{12,8},{1,13},{5,1},{9,5},{13,9},{2,14},{6,2},{... | collective-permute-start | bytes 589832 | tf_op jit(solution)/shard_map/ppermute | solution.py:25
  32.3 0.2 copy.10
  32.4 1.7 %collective-permute-start.10 = (bf16[4,16,3,2,4,256]{5,1,4,2,3,0:T(8,128)(2,1)S(1)}, bf16[4,16,3,2,4,256]{5,1,4,2,3,0:T(8,128)(2,1)S(1)}, u32[]{:S(2)}, u32[]{:S(2)}) collective-permute-start(bf16[4,16,3,2,4,256]{5,1,4,2,3,0:T(8,128)(2,1)S(1)} %copy.10), channel_id=1, source_target_pairs={{0,16},{16,0},{1,17},{17,1},{2,18},{18,2},{3,19},{19,3},{4,20},{20... | collective-permute-start | bytes 2359304 | tf_op jit(solution)/shard_map/ppermute | solution.py:29
  34.2 4.1 %collective-permute-done.6.refs_12_ = bf16[2,4,3,2,1,8,256]{6,5,4,3,2,1,0:T(8,128)(2,1)S(1)} collective-permute-done((bf16[2,4,3,2,1,8,256]{6,5,4,3,2,1,0:T(8,128)(2,1)}, bf16[2,4,3,2,1,8,256]{6,5,4,3,2,1,0:T(8,128)(2,1)S(1)}, u32[]{:S(2)}, u32[]{:S(2)}) %collective-permute-start.6) | collective-permute-done | bytes 196640 | tf_op jit(solution)/shard_map/ppermute | solution.py:25
  38.3 2.1 %collective-permute-done.7.refs_13_ = bf16[2,4,3,2,1,8,256]{6,5,4,3,2,1,0:T(8,128)(2,1)S(1)} collective-permute-done((bf16[2,4,3,2,1,8,256]{6,5,4,3,2,1,0:T(8,128)(2,1)}, bf16[2,4,3,2,1,8,256]{6,5,4,3,2,1,0:T(8,128)(2,1)S(1)}, u32[]{:S(2)}, u32[]{:S(2)}) %collective-permute-start.7) | collective-permute-done | bytes 196640 | tf_op jit(solution)/shard_map/ppermute | solution.py:25
  40.4 0.6 copy-done.8
  41.1 0.2 copy-done.1
  41.2 0.1 copy-done.2
  41.3 10.1 %shard_map.47 = bf16[2,4,3,2,4,8,256]{6,5,4,3,2,1,0:T(8,128)(2,1)} custom-call(f32[16]{0:T(128)} %reshape.151.refs_0_, f32[24]{0:T(128)} %reshape.152.refs_1_, f32[2]{0:T(128)} %pad_maximum_fusion.1.refs_2_, f32[4,3,2,1,4,256]{5,4,3,2,1,0:T(4,128)} %refs_3_.3, f32[4,3,2,1,4,256]{5,4,3,2,1,0:T(4,128)} %copy-done.3, f32[4,3,2,1,4,256]{5,4,3,2,1,0:T(4,128)} %copy-done.4, ...), custom_call_target="tpu_custom_call" | custom-call | tf_op jit(solution)/shard_map/pallas_call | solution.py:243
  51.4 1.8 %fusion.7 = (bf16[2,4,3,2,4,4,256]{6,5,4,3,2,1,0:T(4,128)(2,1)S(1)}, bf16[2,4,3,2,4,4,256]{6,5,4,3,2,1,0:T(4,128)(2,1)S(1)}) fusion(bf16[2,4,3,2,4,8,256]{6,5,4,3,2,1,0:T(8,128)(2,1)} %shard_map.47), kind=kLoop, calls=%fused_computation.36 | loop fusion | bytes 1572864 | tf_op jit(solution)/shard_map/slice
  53.2 0.5 pad_maximum_fusion
  53.7 1.3 %convolution_bitcast_fusion.1 = f32[4,4,2,2,4,16]{5,1,2,3,0,4:T(4,128)S(1)} fusion(bf16[4,16,3,2,4,256,1,1]{5,4,3,2,1,0,7,6:T(4,128)(2,1)S(1)} %bitcast.46, bf16[4,4,3,2,4,4,256,1]{6,5,4,3,2,1,0,7:T(4,128)(2,1)S(1)} %bitcast.47), kind=kOutput, calls=%fused_computation.1 | convolution fusion | flops 25165824 | bytes 1589248 | tf_op jit(solution)/shard_map/tvcazs,rqcbtzs->rqabtv/dot_general | solution.py:274
  55.0 0.1 add.99
  55.1 0.1 sub.39
  55.3 1.3 %convolution_bitcast_fusion = f32[4,4,2,2,4,16]{5,1,2,3,0,4:T(4,128)S(1)} fusion(bf16[4,16,3,2,4,256]{5,1,4,2,3,0:T(8,128)(2,1)S(1)} %collective-permute-done.10, bf16[4,4,3,2,4,4,256,1]{6,5,4,3,2,1,0,7:T(4,128)(2,1)S(1)} %bitcast.48), kind=kOutput, calls=%fused_computation | convolution fusion | flops 25165824 | bytes 1589248 | tf_op jit(solution)/shard_map/tvcazs,rqcbtzs->rqabtv/dot_general | solution.py:274
  56.6 0.1 add.101
  56.8 0.1 sub.41
  56.9 0.1 copy_dynamic-update-slice_fusion
  57.0 0.1 maximum_bitcast_fusion
  57.1 0.6 collective-permute-start.11
  57.7 4.5 %collective-permute-done.11 = f32[2,4,4,2,4,8]{5,4,3,2,1,0:T(4,128)S(1)} collective-permute-done((f32[2,4,4,2,4,8]{5,4,3,2,1,0:T(4,128)S(1)}, f32[2,4,4,2,4,8]{5,4,3,2,1,0:T(4,128)S(1)}, u32[]{:S(2)}, u32[]{:S(2)}) %collective-permute-start.11) | collective-permute-done | bytes 8224 | tf_op jit(solution)/shard_map/ppermute | solution.py:268
  62.2 0.1 select_add_fusion
  62.3 0.1 collective-permute-start.12
  62.3 1.2 %collective-permute-done.12 = f32[1,4,4,2,4,8]{5,4,3,2,1,0:T(4,128)S(1)} collective-permute-done((f32[1,4,4,2,4,8]{5,4,3,2,1,0:T(4,128)S(1)}, f32[1,4,4,2,4,8]{5,4,3,2,1,0:T(4,128)S(1)}, u32[]{:S(2)}, u32[]{:S(2)}) %collective-permute-start.12) | collective-permute-done | bytes 4128 | tf_op jit(solution)/shard_map/ppermute | solution.py:268
  63.6 0.7 %add_bitcast_fusion = f32[4,4,2,4,8]{4,3,2,1,0:T(4,128)} fusion(f32[1,4,4,2,4,8]{5,4,3,2,1,0:T(4,128)S(1)} %collective-permute-done.12, f32[2,4,4,2,4,8]{5,4,3,2,1,0:T(4,128)S(1)} %select_add_fusion, pred[]{:T(512)S(6)} %eq.53), kind=kLoop, calls=%fused_computation.16 | loop fusion | flops 2048 | bytes 16385 | tf_op jit(solution)/shard_map/squeeze | solution.py:270
  (33 shorter events, 0.3 us)
Async XLA Ops:
  0.0 32.3 %copy-start = (bf16[4,16,3,2,4,256]{5,4,3,2,1,0:T(4,128)(2,1)S(1)}, bf16[4,16,3,2,4,256]{5,4,3,2,1,0:T(4,128)(2,1)}, u32[]{:S(2)}) copy-start(bf16[4,16,3,2,4,256]{5,4,3,2,1,0:T(4,128)(2,1)} %param.7) | copy-start | bytes 2359300
  0.0 15.0 %collective-permute-start = (f32[4,3,2,1,4,256]{5,4,3,2,1,0:T(4,128)}, f32[4,3,2,1,4,256]{5,4,3,2,1,0:T(4,128)S(1)}, u32[]{:S(2)}, u32[]{:S(2)}) collective-permute-start(f32[4,3,2,1,4,256]{5,4,3,2,1,0:T(4,128)} %refs_3_.3), channel_id=1, source_target_pairs={{0,4},{4,8},{8,12},{12,0},{1,5},{5,9},{9,13},{13,1},{2,6},{6,10},{... | collective-permute-start | bytes 294920 | tf_op jit(solution)/shard_map/ppermute | solution.py:25
  3.1 12.0 %collective-permute-start.1 = (f32[4,3,2,1,4,256]{5,4,3,2,1,0:T(4,128)}, f32[4,3,2,1,4,256]{5,4,3,2,1,0:T(4,128)S(1)}, u32[]{:S(2)}, u32[]{:S(2)}) collective-permute-start(f32[4,3,2,1,4,256]{5,4,3,2,1,0:T(4,128)} %refs_3_.3), channel_id=1, source_target_pairs={{0,12},{4,0},{8,4},{12,8},{1,13},{5,1},{9,5},{13,9},{2,14},{6,2},{... | collective-permute-start | bytes 294920 | tf_op jit(solution)/shard_map/ppermute | solution.py:25
  6.1 4.7 %collective-permute-start.2 = (f32[4,3,2,1,1,256]{5,4,3,2,1,0:T(1,128)S(1)}, f32[4,3,2,1,1,256]{5,4,3,2,1,0:T(1,128)S(1)}, u32[]{:S(2)}, u32[]{:S(2)}) collective-permute-start(f32[4,3,2,1,1,256]{5,4,3,2,1,0:T(1,128)S(1)} %get-tuple-element.24), channel_id=1, source_target_pairs={{0,1},{1,2},{2,3},{3,0},{4,5},{5,6},{6,7},{7,4},{8,9},{9,10},{10,1... | collective-permute-start | bytes 73736 | tf_op jit(solution)/shard_map/ppermute | solution.py:25
  6.2 6.5 %collective-permute-start.3 = (f32[4,3,2,1,1,256]{5,4,3,2,1,0:T(1,128)S(1)}, f32[4,3,2,1,1,256]{5,4,3,2,1,0:T(1,128)S(1)}, u32[]{:S(2)}, u32[]{:S(2)}) collective-permute-start(f32[4,3,2,1,1,256]{5,4,3,2,1,0:T(1,128)S(1)} %get-tuple-element.23), channel_id=1, source_target_pairs={{0,3},{1,0},{2,1},{3,2},{4,7},{5,4},{6,5},{7,6},{8,11},{9,8},{10,9... | collective-permute-start | bytes 73736 | tf_op jit(solution)/shard_map/ppermute | solution.py:25
  8.8 6.2 %collective-permute-start.4 = (f32[3,3,2,1,4,256]{5,4,3,2,1,0:T(4,128)S(1)}, f32[3,3,2,1,4,256]{5,4,3,2,1,0:T(4,128)S(1)}, u32[]{:S(2)}, u32[]{:S(2)}) collective-permute-start(f32[3,3,2,1,4,256]{5,4,3,2,1,0:T(4,128)S(1)} %slice_bitcast_fusion.1), channel_id=1, source_target_pairs={{0,4},{4,8},{8,12},{12,0},{1,5},{5,9},{9,13},{13,1},{2,6},{6,10},{... | collective-permute-start | bytes 221192 | tf_op jit(solution)/shard_map/ppermute | solution.py:25
  10.8 4.2 %copy-start.9 = (f32[4,3,2,1,1,256]{5,4,3,2,1,0:T(1,128)}, f32[4,3,2,1,1,256]{5,4,3,2,1,0:T(1,128)S(1)}, u32[]{:S(2)}) copy-start(f32[4,3,2,1,1,256]{5,4,3,2,1,0:T(1,128)S(1)} %collective-permute-done.2.refs_6_) | copy-start | bytes 73732
  10.8 4.2 %collective-permute-start.5 = (f32[3,3,2,4,1,256]{5,4,3,2,1,0:T(1,128)S(1)}, f32[3,3,2,4,1,256]{5,4,3,2,1,0:T(1,128)S(1)}, u32[]{:S(2)}, u32[]{:S(2)}) collective-permute-start(f32[3,3,2,4,1,256]{5,4,3,2,1,0:T(1,128)S(1)} %slice_bitcast_fusion), channel_id=1, source_target_pairs={{0,1},{1,2},{2,3},{3,0},{4,5},{5,6},{6,7},{7,4},{8,9},{9,10},{10,1... | collective-permute-start | bytes 221192 | tf_op jit(solution)/shard_map/ppermute | solution.py:25
  12.7 2.3 %copy-start.10 = (f32[4,3,2,1,1,256]{5,4,3,2,1,0:T(1,128)}, f32[4,3,2,1,1,256]{5,4,3,2,1,0:T(1,128)S(1)}, u32[]{:S(2)}) copy-start(f32[4,3,2,1,1,256]{5,4,3,2,1,0:T(1,128)S(1)} %collective-permute-done.3.refs_7_) | copy-start | bytes 73732
  15.0 0.6 copy-start.5
  15.0 0.6 %copy-start.6 = (f32[3,3,2,4,1,256]{5,4,3,2,1,0:T(1,128)}, f32[3,3,2,4,1,256]{5,4,3,2,1,0:T(1,128)S(1)}, u32[]{:S(2)}) copy-start(f32[3,3,2,4,1,256]{5,4,3,2,1,0:T(1,128)S(1)} %collective-permute-done.5.refs_10_) | copy-start | bytes 221188
  15.0 0.7 %copy-start.3 = (f32[4,3,2,1,4,256]{5,4,3,2,1,0:T(4,128)}, f32[4,3,2,1,4,256]{5,4,3,2,1,0:T(4,128)S(1)}, u32[]{:S(2)}) copy-start(f32[4,3,2,1,4,256]{5,4,3,2,1,0:T(4,128)S(1)} %collective-permute-done.refs_4_) | copy-start | bytes 294916
  15.7 0.6 %copy-start.4 = (f32[4,3,2,1,4,256]{5,4,3,2,1,0:T(4,128)}, f32[4,3,2,1,4,256]{5,4,3,2,1,0:T(4,128)S(1)}, u32[]{:S(2)}) copy-start(f32[4,3,2,1,4,256]{5,4,3,2,1,0:T(4,128)S(1)} %collective-permute-done.1.refs_5_) | copy-start | bytes 294916
  26.6 13.7 %collective-permute-start.8 = (f32[2,4,3,2,4,2,256]{6,5,4,3,2,1,0:T(2,128)}, f32[2,4,3,2,4,2,256]{6,5,4,3,2,1,0:T(2,128)S(1)}, u32[]{:S(2)}, u32[]{:S(2)}) collective-permute-start(f32[2,4,3,2,4,2,256]{6,5,4,3,2,1,0:T(2,128)} %get-tuple-element.13), channel_id=1, source_target_pairs={{0,1},{1,2},{2,3},{3,0},{4,5},{5,6},{6,7},{7,4},{8,9},{9,10},{10,1... | collective-permute-start | bytes 1179656 | tf_op jit(solution)/shard_map/ppermute | solution.py:25
  26.7 13.7 %collective-permute-start.9 = (f32[2,4,3,2,4,2,256]{6,5,4,3,2,1,0:T(2,128)}, f32[2,4,3,2,4,2,256]{6,5,4,3,2,1,0:T(2,128)S(1)}, u32[]{:S(2)}, u32[]{:S(2)}) collective-permute-start(f32[2,4,3,2,4,2,256]{6,5,4,3,2,1,0:T(2,128)} %get-tuple-element.14), channel_id=1, source_target_pairs={{0,3},{1,0},{2,1},{3,2},{4,7},{5,4},{6,5},{7,6},{8,11},{9,8},{10,9... | collective-permute-start | bytes 1179656 | tf_op jit(solution)/shard_map/ppermute | solution.py:25
  28.4 9.8 %collective-permute-start.6 = (bf16[2,4,3,2,1,8,256]{6,5,4,3,2,1,0:T(8,128)(2,1)}, bf16[2,4,3,2,1,8,256]{6,5,4,3,2,1,0:T(8,128)(2,1)S(1)}, u32[]{:S(2)}, u32[]{:S(2)}) collective-permute-start(bf16[2,4,3,2,1,8,256]{6,5,4,3,2,1,0:T(8,128)(2,1)} %get-tuple-element.11), channel_id=1, source_target_pairs={{0,4},{4,8},{8,12},{12,0},{1,5},{5,9},{9,13},{13,1},{2,6},{6,10},{... | collective-permute-start | bytes 589832 | tf_op jit(solution)/shard_map/ppermute | solution.py:25
  29.5 10.8 %collective-permute-start.7 = (bf16[2,4,3,2,1,8,256]{6,5,4,3,2,1,0:T(8,128)(2,1)}, bf16[2,4,3,2,1,8,256]{6,5,4,3,2,1,0:T(8,128)(2,1)S(1)}, u32[]{:S(2)}, u32[]{:S(2)}) collective-permute-start(bf16[2,4,3,2,1,8,256]{6,5,4,3,2,1,0:T(8,128)(2,1)} %get-tuple-element.12), channel_id=1, source_target_pairs={{0,12},{4,0},{8,4},{12,8},{1,13},{5,1},{9,5},{13,9},{2,14},{6,2},{... | collective-permute-start | bytes 589832 | tf_op jit(solution)/shard_map/ppermute | solution.py:25
  32.4 22.9 %collective-permute-start.10 = (bf16[4,16,3,2,4,256]{5,1,4,2,3,0:T(8,128)(2,1)S(1)}, bf16[4,16,3,2,4,256]{5,1,4,2,3,0:T(8,128)(2,1)S(1)}, u32[]{:S(2)}, u32[]{:S(2)}) collective-permute-start(bf16[4,16,3,2,4,256]{5,1,4,2,3,0:T(8,128)(2,1)S(1)} %copy.10), channel_id=1, source_target_pairs={{0,16},{16,0},{1,17},{17,1},{2,18},{18,2},{3,19},{19,3},{4,20},{20... | collective-permute-start | bytes 2359304 | tf_op jit(solution)/shard_map/ppermute | solution.py:29
  38.3 2.1 %copy-start.7 = (bf16[2,4,3,2,1,8,256]{6,5,4,3,2,1,0:T(8,128)(2,1)}, bf16[2,4,3,2,1,8,256]{6,5,4,3,2,1,0:T(8,128)(2,1)S(1)}, u32[]{:S(2)}) copy-start(bf16[2,4,3,2,1,8,256]{6,5,4,3,2,1,0:T(8,128)(2,1)S(1)} %collective-permute-done.6.refs_12_) | copy-start | bytes 589828
  40.4 0.7 %copy-start.8 = (bf16[2,4,3,2,1,8,256]{6,5,4,3,2,1,0:T(8,128)(2,1)}, bf16[2,4,3,2,1,8,256]{6,5,4,3,2,1,0:T(8,128)(2,1)S(1)}, u32[]{:S(2)}) copy-start(bf16[2,4,3,2,1,8,256]{6,5,4,3,2,1,0:T(8,128)(2,1)S(1)} %collective-permute-done.7.refs_13_) | copy-start | bytes 589828
  40.4 0.8 %copy-start.1 = (f32[2,4,3,2,4,2,256]{6,5,4,3,2,1,0:T(2,128)}, f32[2,4,3,2,4,2,256]{6,5,4,3,2,1,0:T(2,128)S(1)}, u32[]{:S(2)}) copy-start(f32[2,4,3,2,4,2,256]{6,5,4,3,2,1,0:T(2,128)S(1)} %collective-permute-done.8.refs_14_) | copy-start | bytes 1179652
  40.4 0.9 %copy-start.2 = (f32[2,4,3,2,4,2,256]{6,5,4,3,2,1,0:T(2,128)}, f32[2,4,3,2,4,2,256]{6,5,4,3,2,1,0:T(2,128)S(1)}, u32[]{:S(2)}) copy-start(f32[2,4,3,2,4,2,256]{6,5,4,3,2,1,0:T(2,128)S(1)} %collective-permute-done.9.refs_15_) | copy-start | bytes 1179652
  57.1 5.0 %collective-permute-start.11 = (f32[2,4,4,2,4,8]{5,4,3,2,1,0:T(4,128)S(1)}, f32[2,4,4,2,4,8]{5,4,3,2,1,0:T(4,128)S(1)}, u32[]{:S(2)}, u32[]{:S(2)}) collective-permute-start(f32[2,4,4,2,4,8]{5,4,3,2,1,0:T(4,128)S(1)} %slice_select_fusion), channel_id=1, source_target_pairs={{0,2},{1,3},{2,0},{3,1},{4,6},{5,7},{6,4},{7,5},{8,10},{9,11},{10,... | collective-permute-start | bytes 24584 | tf_op jit(solution)/shard_map/ppermute | solution.py:268
  62.3 1.3 %collective-permute-start.12 = (f32[1,4,4,2,4,8]{5,4,3,2,1,0:T(4,128)S(1)}, f32[1,4,4,2,4,8]{5,4,3,2,1,0:T(4,128)S(1)}, u32[]{:S(2)}, u32[]{:S(2)}) collective-permute-start(f32[1,4,4,2,4,8]{5,4,3,2,1,0:T(4,128)S(1)} %slice_select_fusion.1), channel_id=1, source_target_pairs={{0,1},{1,0},{2,3},{3,2},{4,5},{5,4},{6,7},{7,6},{8,9},{9,8},{10,11... | collective-permute-start | bytes 12296 | tf_op jit(solution)/shard_map/ppermute | solution.py:268

commit v5 on v4

--- a/solution.py
+++ b/solution.py
@@ -92,14 +92,22 @@
                             zhi_s[s, c, ri, t, half] = jnp.broadcast_to(nzhi_ref[g, c, ri, t // span] * f, (Z, L))
                     else:
                         for t in range(T):
-                            zlo_s[s, c, ri, t, half] = jnp.broadcast_to(zlo_ref[s, c, ri, t, pl.ds(g, 1)], (Z, L))
-                            zhi_s[s, c, ri, t, half] = jnp.broadcast_to(zhi_ref[s, c, ri, t, pl.ds(g, 1)], (Z, L))
+                            if s < 2:
+                                zlo_s[s, c, ri, t, half] = jnp.broadcast_to(zlo_ref[s, c, ri, t, pl.ds(g, 1)], (Z, L))
+                                zhi_s[s, c, ri, t, half] = jnp.broadcast_to(zhi_ref[s, c, ri, t, pl.ds(g, 1)], (Z, L))
+                            else:
+                                zlo_s[s, c, ri, t, half] = jnp.zeros((Z, L), jnp.float32)
+                                zhi_s[s, c, ri, t, half] = jnp.zeros((Z, L), jnp.float32)
                 if first:
                     pad_ref[s, c, ri, pl.ds(1, T)] = src_ref[s, c, ri]
                 else:
                     pad_ref[s, c, ri, pl.ds(1, T)] = psi_ref[s, c, ri]
-                    pad_ref[s, c, ri, pl.ds(0, 1)] = tlo_ref[s, c, ri].astype(jnp.float32) * sign_ref[0]
-                    pad_ref[s, c, ri, pl.ds(T + 1, 1)] = thi_ref[s, c, ri].astype(jnp.float32) * sign_ref[1]
+                    if s < 2:
+                        pad_ref[s, c, ri, pl.ds(0, 1)] = tlo_ref[s, c, ri].astype(jnp.float32) * sign_ref[0]
+                        pad_ref[s, c, ri, pl.ds(T + 1, 1)] = thi_ref[s, c, ri].astype(jnp.float32) * sign_ref[1]
+                    else:
+                        pad_ref[s, c, ri, pl.ds(0, 1)] = jnp.zeros((1, ROWS, L), jnp.float32)
+                        pad_ref[s, c, ri, pl.ds(T + 1, 1)] = jnp.zeros((1, ROWS, L), jnp.float32)
     xpos = lax.broadcasted_iota(jnp.int32, (ROWS, L), 1) % NX
     zpos = lax.broadcasted_iota(jnp.int32, (ROWS, L), 0) % Z
     x_last = xpos == NX - 1
@@ -190,14 +198,36 @@
 
     lax.fori_loop(0, T, body, 0)
     if first:
-        for s in range(S):
-            for c in range(C):
-                for ri in range(RI):
-                    tfirst_ref[s, c, ri] = out_ref[s, c, ri, pl.ds(0, 1)].astype(tfirst_ref.dtype)
-                    tlast_ref[s, c, ri] = out_ref[s, c, ri, pl.ds(T - 1, 1)].astype(tlast_ref.dtype)
-                    for g in range(2):
-                        zfirst_ref[s, c, ri, :, pl.ds(g, 1), :] = out_ref[s, c, ri, :, pl.ds(g * Z, 1), :]
-                        zlast_ref[s, c, ri, :, pl.ds(g, 1), :] = out_ref[s, c, ri, :, pl.ds(g * Z + Z - 1, 1), :]
+        for mu, stride, target, pick in (
+            (3, 1, tfirst_ref, lambda s, c, ri: out_ref[s, c, ri, pl.ds(0, 1)]),
+            (3, -1, tlast_ref, lambda s, c, ri: out_ref[s, c, ri, pl.ds(T - 1, 1)]),
+        ):
+            for k, (re, im) in enumerate(half_spinor(pick, mu, stride)):
+                for c in range(C):
+                    target[k, c, 0] = re[c].astype(target.dtype)
+                    target[k, c, 1] = im[c].astype(target.dtype)
+        for g in range(2):
+            for mu, stride, target, row in ((2, 1, zfirst_ref, g * Z), (2, -1, zlast_ref, g * Z + Z - 1)):
+                pick = lambda s, c, ri: out_ref[s, c, ri, :, pl.ds(row, 1), :]
+                for k, (re, im) in enumerate(half_spinor(pick, mu, stride)):
+                    for c in range(C):
+                        target[k, c, 0, :, pl.ds(g, 1), :] = re[c]
+                        target[k, c, 1, :, pl.ds(g, 1), :] = im[c]
+
+
+def half_spinor(pick, mu, stride):
+    orient = -1 if stride == 1 else 1
+    rows = []
+    for s in (0, 1):
+        p = GAMMA_PERM[mu][s]
+        cr, ci = orient * GAMMA_REAL[mu][s], orient * GAMMA_IMAG[mu][s]
+        res, ims = [], []
+        for c in range(3):
+            pre, pim = times_phase(pick(p, c, 0), pick(p, c, 1), cr, ci)
+            res.append(pick(s, c, 0) + pre)
+            ims.append(pick(s, c, 1) + pim)
+        rows.append((res, ims))
+    return rows
 
 
 def hopping_step(first, scalars, noise_parts, link_parts, spinor_parts):
@@ -211,8 +241,8 @@
     whole = lambda x: pl.BlockSpec(x.shape, lambda h: (0,) * x.ndim)
     smem = pl.BlockSpec(memory_space=pltpu.SMEM)
     site_block = pl.BlockSpec((None, S, C, RI, T, ROWS, L), index)
-    t_block = pl.BlockSpec((None, S, C, RI, 1, ROWS, L), index)
-    z_block = pl.BlockSpec((None, S, C, RI, T, 2, L), index)
+    t_block = pl.BlockSpec((None, 2, C, RI, 1, ROWS, L), index)
+    z_block = pl.BlockSpec((None, 2, C, RI, T, 2, L), index)
     noise_specs = [
         pl.BlockSpec((2, C, RI, K, Z, L), index6),
         pl.BlockSpec((2, C, RI, 1, Z, L), index6),
@@ -223,8 +253,8 @@
     in_specs = [smem, smem, smem] + noise_specs + [whole(x) for x in link_parts]
     site_shape = (H, S, C, RI, T, ROWS, L)
     if first:
-        t_shape = jax.ShapeDtypeStruct((H, S, C, RI, 1, ROWS, L), jnp.bfloat16)
-        z_shape = jax.ShapeDtypeStruct((H, S, C, RI, T, 2, L), jnp.float32)
+        t_shape = jax.ShapeDtypeStruct((H, 2, C, RI, 1, ROWS, L), jnp.bfloat16)
+        z_shape = jax.ShapeDtypeStruct((H, 2, C, RI, T, 2, L), jnp.float32)
         out_shape = [jax.ShapeDtypeStruct(site_shape, jnp.float32), t_shape, t_shape, z_shape, z_shape]
         out_specs = [site_block, t_block, t_block, z_block, z_block]
     else:
@@ -272,8 +302,9 @@
 
 def intersection_part(rounded, vector_piece):
     products = jnp.einsum(
-        "tvcazs,rqcbtzs->rqabtv", vector_piece, rounded, preferred_element_type=jnp.float32
-    )
+        "tvcazs,hqcbtgzs->hgqabtv", vector_piece, rounded, preferred_element_type=jnp.float32
+    )
+    products = products.reshape((-1,) + products.shape[2:])
     real_part = products[:, :, 0, 0] + products[:, :, 1, 1]
     imag_part = products[:, :, 0, 1] - products[:, :, 1, 0]
     return jnp.stack([real_part, imag_part], axis=2)
@@ -319,8 +350,7 @@
     )
     rounded = hopping_step(False, scalars, noise_parts, link_parts, (spinor,) + halos)
     H, S, C, RI, T, ROWS, L = rounded.shape
-    rounded = jnp.moveaxis(rounded.reshape(H, S, C, RI, T, 2, ROWS // 2, L), 5, 1).reshape(
-        2 * H, S, C, RI, T, ROWS // 2, L)
+    rounded = rounded.reshape(H, S, C, RI, T, 2, ROWS // 2, L)
     own_part = intersection_part(rounded, vectors)
     partner_part = intersection_part(rounded, partner_vectors)
     lower_half = jnp.where(section_index == 0, own_part, partner_part)

time: 64.5 us -> 61.2 us (0.949)
  waiting for transfers between devices: 14.2 us -> 11.5 us
  other arithmetic: 2.13 us -> 1.33 us
    ppermute x10, waiting for transfers between devices: 8.51 us -> 5.91 us  [passed_along(): return lax.ppermute(value, axis, pairs)]
    slice x1 -> x0, local copies, waits for them, and re-layouts: 1.8 us -> none
    reshape x0 -> x1, local copies, waits for them, and re-layouts: none -> 1.68 us  [local_body(): rounded = rounded.reshape(H, S, C, RI, T, 2, ROWS // 2, L)]
    squeeze x1 -> x0, other arithmetic: 0.66 us -> none  [reduce_scatter_sa(): return x[0]]
    unnamed x25 -> x29, local copies, waits for them, and re-layouts: 2.48 us -> 2.26 us
  transfers between devices with their start and end apart: 13 -> 13, of which waited for: 5 -> 4; matrix products, arithmetic and copies ran while one was open for 15% -> 15% of each run, Pallas kernels for 16% -> 16%
where the time goes in v5:
time: 61.2 us; the launch traced here: 60.9 us
  Pallas kernels  20.1 us (33%)
  starting transfers between devices  15.1 us (25%)
  waiting for transfers between devices  11.5 us (19%)
  local copies, waits for them, and re-layouts  10.1 us (17%)
  matrix products  2.51 us (4%)
  other arithmetic  1.33 us (2%)
    pallas_call x2, Pallas kernels, hopping_step(): pl.pallas_call(functools.partial(hop_kernel, first), grid=(H,), in_specs=...  20.1 us
    ppermute x10, starting transfers between devices, passed_along(): return lax.ppermute(value, axis, pairs)  12.6 us
    ppermute x10, waiting for transfers between devices, passed_along(): return lax.ppermute(value, axis, pairs)  5.91 us
    ppermute x2, waiting for transfers between devices, reduce_scatter_sa(): x = keep + lax.ppermute(send, 'sa', [(j, j ^ d) for j in range(n)])  5.57 us
    dot_general x2, matrix products, intersection_part(): jnp.einsum('tvcazs,hqcbtgzs->hgqabtv', vector_piece, rounded, preferred_e...  2.51 us
    unnamed x29, local copies, waits for them, and re-layouts  2.26 us
    ppermute x1, starting transfers between devices, from_partner(): lax.ppermute(x, axis, [(i, i ^ 1 << stride) for i in range(lax.axis_size(...  1.73 us
    reshape x1, local copies, waits for them, and re-layouts, local_body(): rounded = rounded.reshape(H, S, C, RI, T, 2, ROWS // 2, L)  1.68 us
  transfers between devices with their start and end apart: 13, of which 4 were waited for; matrix products, arithmetic and copies ran while one was open for 15% of the time, Pallas kernels for 16%

profile of v5, /device:TPU:0, one launch (start us, length us, event | category | flops | bytes accessed | tf_op | source)
XLA Modules:
  0.0 60.9 jit_solution(8089660683744376363)
XLA Ops:
  0.0 3.1 %collective-permute-start = (f32[4,3,2,1,4,256]{5,4,3,2,1,0:T(4,128)}, f32[4,3,2,1,4,256]{5,4,3,2,1,0:T(4,128)S(1)}, u32[]{:S(2)}, u32[]{:S(2)}) collective-permute-start(f32[4,3,2,1,4,256]{5,4,3,2,1,0:T(4,128)} %refs_3_.3), channel_id=1, source_target_pairs={{0,4},{4,8},{8,12},{12,0},{1,5},{5,9},{9,13},{13,1},{2,6},{6,10},{... | collective-permute-start | bytes 294920 | tf_op jit(solution)/shard_map/ppermute | solution.py:25
  3.1 2.1 %collective-permute-start.1 = (f32[4,3,2,1,4,256]{5,4,3,2,1,0:T(4,128)}, f32[4,3,2,1,4,256]{5,4,3,2,1,0:T(4,128)S(1)}, u32[]{:S(2)}, u32[]{:S(2)}) collective-permute-start(f32[4,3,2,1,4,256]{5,4,3,2,1,0:T(4,128)} %refs_3_.3), channel_id=1, source_target_pairs={{0,12},{4,0},{8,4},{12,8},{1,13},{5,1},{9,5},{13,9},{2,14},{6,2},{... | collective-permute-start | bytes 294920 | tf_op jit(solution)/shard_map/ppermute | solution.py:25
  5.1 1.0 %fusion.8 = (f32[4,3,2,1,1,256]{5,4,3,2,1,0:T(1,128)S(1)}, f32[4,3,2,1,1,256]{5,4,3,2,1,0:T(1,128)S(1)}) fusion(f32[4,3,2,1,4,256]{5,4,3,2,1,0:T(4,128)} %refs_3_.3), kind=kLoop, calls=%fused_computation.36 | loop fusion | bytes 98304 | tf_op jit(solution)/shard_map/slice | solution.py:337
  6.1 0.1 collective-permute-start.2
  6.2 1.7 %collective-permute-start.3 = (f32[4,3,2,1,1,256]{5,4,3,2,1,0:T(1,128)S(1)}, f32[4,3,2,1,1,256]{5,4,3,2,1,0:T(1,128)S(1)}, u32[]{:S(2)}, u32[]{:S(2)}) collective-permute-start(f32[4,3,2,1,1,256]{5,4,3,2,1,0:T(1,128)S(1)} %get-tuple-element.21), channel_id=1, source_target_pairs={{0,3},{1,0},{2,1},{3,2},{4,7},{5,4},{6,5},{7,6},{8,11},{9,8},{10,9... | collective-permute-start | bytes 73736 | tf_op jit(solution)/shard_map/ppermute | solution.py:25
  7.9 0.9 %slice_bitcast_fusion.1 = f32[3,3,2,1,4,256]{5,4,3,2,1,0:T(4,128)S(1)} fusion(f32[4,3,3,2,4,4,256]{6,5,4,3,2,1,0:T(4,128)} %refs_8_.3), kind=kLoop, calls=%fused_computation.14 | loop fusion | bytes 147456 | tf_op jit(solution)/shard_map/squeeze | solution.py:341
  8.8 1.0 %slice_bitcast_fusion = f32[3,3,2,4,1,256]{5,4,3,2,1,0:T(1,128)S(1)} fusion(f32[4,3,3,2,4,4,256]{6,5,4,3,2,1,0:T(4,128)} %refs_8_.3), kind=kLoop, calls=%fused_computation.13 | loop fusion | bytes 147456 | tf_op jit(solution)/shard_map/squeeze | solution.py:342
  9.9 0.7 %dynamic_slice.3 = s32[4]{0:T(128)S(1)} dynamic-slice(s32[8]{0:T(128)} %param.6, s32[]{:T(128)S(6)} %select_n.94), dynamic_slice_sizes={4} | dynamic-slice | bytes 36 | tf_op jit(solution)/shard_map/dynamic_slice | solution.py:326
  10.7 0.1 compare_convert_fusion
  10.7 0.1 fusion.5
  10.8 0.1 collective-permute-start.5
  10.9 0.6 pad_maximum_fusion.refs_2_
  11.5 0.7 %reshape.159.refs_1_ = f32[24]{0:T(128)} reshape(f32[4,6]{1,0:T(4,128)S(1)} %compare_convert_fusion) | data formatting | bytes 192 | tf_op jit(solution)/shard_map/convert_element_type | solution.py:330
  12.1 0.6 reshape.158.refs_0_
  12.7 2.3 %collective-permute-done.4.refs_9_ = f32[3,3,2,1,4,256]{5,4,3,2,1,0:T(4,128)S(1)} collective-permute-done((f32[3,3,2,1,4,256]{5,4,3,2,1,0:T(4,128)S(1)}, f32[3,3,2,1,4,256]{5,4,3,2,1,0:T(4,128)S(1)}, u32[]{:S(2)}, u32[]{:S(2)}) %collective-permute-start.4) | collective-permute-done | bytes 73760 | tf_op jit(solution)/shard_map/ppermute | solution.py:25
  15.0 0.6 copy-done.3
  15.7 0.6 %copy-done.2 = f32[4,3,2,1,4,256]{5,4,3,2,1,0:T(4,128)} copy-done((f32[4,3,2,1,4,256]{5,4,3,2,1,0:T(4,128)}, f32[4,3,2,1,4,256]{5,4,3,2,1,0:T(4,128)S(1)}, u32[]{:S(2)}) %copy-start.2) | copy-done | bytes 98328
  16.3 10.2 %shard_map.46 = (f32[2,4,3,2,4,8,256]{6,5,4,3,2,1,0:T(8,128)}, bf16[2,2,3,2,1,8,256]{6,5,4,3,2,1,0:T(8,128)(2,1)}, bf16[2,2,3,2,1,8,256]{6,5,4,3,2,1,0:T(8,128)(...) custom-call(f32[16]{0:T(128)} %reshape.158.refs_0_, f32[24]{0:T(128)} %reshape.159.refs_1_, ...), custom_call_target="tpu_custom_call" | custom-call | tf_op jit(solution)/shard_map/pallas_call | solution.py:273
  26.5 0.1 collective-permute-start.8
  26.6 1.7 %collective-permute-start.9 = (f32[2,2,3,2,4,2,256]{6,5,4,3,2,1,0:T(2,128)}, f32[2,2,3,2,4,2,256]{6,5,4,3,2,1,0:T(2,128)S(1)}, u32[]{:S(2)}, u32[]{:S(2)}) collective-permute-start(f32[2,2,3,2,4,2,256]{6,5,4,3,2,1,0:T(2,128)} %get-tuple-element.14), channel_id=1, source_target_pairs={{0,3},{1,0},{2,1},{3,2},{4,7},{5,4},{6,5},{7,6},{8,11},{9,8},{10,9... | collective-permute-start | bytes 589832 | tf_op jit(solution)/shard_map/ppermute | solution.py:25
  28.3 0.2 copy.14
  28.5 1.7 %collective-permute-start.10 = (bf16[4,16,3,2,4,256]{5,1,4,2,3,0:T(8,128)(2,1)S(1)}, bf16[4,16,3,2,4,256]{5,1,4,2,3,0:T(8,128)(2,1)S(1)}, u32[]{:S(2)}, u32[]{:S(2)}) collective-permute-start(bf16[4,16,3,2,4,256]{5,1,4,2,3,0:T(8,128)(2,1)S(1)} %copy.14), channel_id=1, source_target_pairs={{0,16},{16,0},{1,17},{17,1},{2,18},{18,2},{3,19},{19,3},{4,20},{20... | collective-permute-start | bytes 2359304 | tf_op jit(solution)/shard_map/ppermute | solution.py:29
  30.2 0.9 %collective-permute-start.6 = (bf16[2,2,3,2,1,8,256]{6,5,4,3,2,1,0:T(8,128)(2,1)S(1)}, bf16[2,2,3,2,1,8,256]{6,5,4,3,2,1,0:T(8,128)(2,1)S(1)}, u32[]{:S(2)}, u32[]{:S(2)}) collective-permute-start(bf16[2,2,3,2,1,8,256]{6,5,4,3,2,1,0:T(8,128)(2,1)S(1)} %copy-done.12), channel_id=1, source_target_pairs={{0,4},{4,8},{8,12},{12,0},{1,5},{5,9},{9,13},{13,1},{2,6},{6,10},{... | collective-permute-start | bytes 294920 | tf_op jit(solution)/shard_map/ppermute | solution.py:25
  31.1 2.9 %collective-permute-start.7 = (bf16[2,2,3,2,1,8,256]{6,5,4,3,2,1,0:T(8,128)(2,1)S(1)}, bf16[2,2,3,2,1,8,256]{6,5,4,3,2,1,0:T(8,128)(2,1)S(1)}, u32[]{:S(2)}, u32[]{:S(2)}) collective-permute-start(bf16[2,2,3,2,1,8,256]{6,5,4,3,2,1,0:T(8,128)(2,1)S(1)} %copy-done.11), channel_id=1, source_target_pairs={{0,12},{4,0},{8,4},{12,8},{1,13},{5,1},{9,5},{13,9},{2,14},{6,2},{... | collective-permute-start | bytes 294920 | tf_op jit(solution)/shard_map/ppermute | solution.py:25
  34.0 3.6 %collective-permute-done.6.refs_12_ = bf16[2,2,3,2,1,8,256]{6,5,4,3,2,1,0:T(8,128)(2,1)S(1)} collective-permute-done((bf16[2,2,3,2,1,8,256]{6,5,4,3,2,1,0:T(8,128)(2,1)S(1)}, bf16[2,2,3,2,1,8,256]{6,5,4,3,2,1,0:T(8,128)(2,1)S(1)}, u32[]{:S(2)}, u32[]{:S(2)}) %collective-permute-start.6) | collective-permute-done | bytes 98336 | tf_op jit(solution)/shard_map/ppermute | solution.py:25
  37.7 0.6 copy-done.9
  38.3 0.1 copy-done.5
  38.4 0.1 copy-done.6
  38.5 9.9 %shard_map.47 = bf16[2,4,3,2,4,8,256]{6,5,4,3,2,1,0:T(8,128)(2,1)} custom-call(f32[16]{0:T(128)} %reshape.158.refs_0_, f32[24]{0:T(128)} %reshape.159.refs_1_, f32[2]{0:T(128)} %pad_maximum_fusion.refs_2_, f32[4,3,2,1,4,256]{5,4,3,2,1,0:T(4,128)} %refs_3_.3, f32[4,3,2,1,4,256]{5,4,3,2,1,0:T(4,128)} %copy-done.1, f32[4,3,2,1,4,256]{5,4,3,2,1,0:T(4,128)} %copy-done.2, ...), custom_call_target="tpu_custom_call" | custom-call | tf_op jit(solution)/shard_map/pallas_call | solution.py:273
  48.4 1.7 %reshape.155 = bf16[2,4,3,2,4,2,4,256]{7,6,5,4,3,2,1,0:T(4,128)(2,1)S(1)} reshape(bf16[2,4,3,2,4,8,256]{6,5,4,3,2,1,0:T(8,128)(2,1)} %shard_map.47) | data formatting | bytes 1572864 | tf_op jit(solution)/shard_map/reshape | solution.py:353
  50.1 1.2 %convolution_bitcast_fusion.1 = f32[2,2,4,2,2,4,16]{6,2,3,1,4,0,5:T(4,128)S(1)} fusion(bf16[4,16,3,2,4,256,1,1,1]{5,4,3,2,1,0,8,7,6:T(4,128)(2,1)S(1)} %bitcast.39, bf16[2,4,3,2,4,2,4,256,1]{7,6,5,4,3,2,1,0,8:T(4,128)(2,1)S(1)} %bitcast.40), kind=kOutput, calls=%fused_computation.1 | convolution fusion | flops 25165824 | bytes 1589248 | tf_op jit(solution)/shard_map/tvcazs,hqcbtgzs->hgqabtv/dot_general | solution.py:304
  51.3 0.1 copy.13
  51.5 0.1 add.99
  51.6 0.1 sub.39
  51.7 1.3 %convolution_bitcast_fusion = f32[2,2,4,2,2,4,16]{6,2,3,1,4,0,5:T(4,128)S(1)} fusion(bf16[4,16,3,2,4,256]{5,1,4,2,3,0:T(8,128)(2,1)S(1)} %collective-permute-done.10, bf16[2,4,3,2,4,2,4,256,1]{7,6,5,4,3,2,1,0,8:T(4,128)(2,1)S(1)} %bitcast.41), kind=kOutput, calls=%fused_computation | convolution fusion | flops 25165824 | bytes 1589248 | tf_op jit(solution)/shard_map/tvcazs,hqcbtgzs->hgqabtv/dot_general | solution.py:304
  53.0 0.1 copy.16
  53.1 0.1 add.101
  53.2 0.1 sub.41
  53.4 0.1 maximum_bitcast_fusion
  53.6 0.1 broadcast_select_fusion.2
  53.6 0.7 %collective-permute-start.11 = (f32[2,4,4,2,4,8]{5,0,4,2,1,3:T(2,128)S(1)}, f32[2,4,4,2,4,8]{5,0,4,2,1,3:T(2,128)S(1)}, u32[]{:S(2)}, u32[]{:S(2)}) collective-permute-start(f32[2,4,4,2,4,8]{5,0,4,2,1,3:T(2,128)S(1)} %broadcast_select_fusion.2), channel_id=1, source_target_pairs={{0,2},{1,3},{2,0},{3,1},{4,6},{5,7},{6,4},{7,5},{8,10},{9,11},{10,... | collective-permute-start | bytes 24584 | tf_op jit(solution)/shard_map/ppermute | solution.py:298
  54.3 4.3 %collective-permute-done.11 = f32[2,4,4,2,4,8]{5,0,4,2,1,3:T(2,128)S(1)} collective-permute-done((f32[2,4,4,2,4,8]{5,0,4,2,1,3:T(2,128)S(1)}, f32[2,4,4,2,4,8]{5,0,4,2,1,3:T(2,128)S(1)}, u32[]{:S(2)}, u32[]{:S(2)}) %collective-permute-start.11) | collective-permute-done | bytes 8224 | tf_op jit(solution)/shard_map/ppermute | solution.py:298
  58.7 0.1 select_add_fusion
  58.8 0.1 broadcast_select_fusion.3
  58.9 0.1 collective-permute-start.12
  58.9 1.2 %collective-permute-done.12 = f32[1,4,4,2,4,8]{5,0,4,2,1,3:T(1,128)S(1)} collective-permute-done((f32[1,4,4,2,4,8]{5,0,4,2,1,3:T(1,128)S(1)}, f32[1,4,4,2,4,8]{5,0,4,2,1,3:T(1,128)S(1)}, u32[]{:S(2)}, u32[]{:S(2)}) %collective-permute-start.12) | collective-permute-done | bytes 4128 | tf_op jit(solution)/shard_map/ppermute | solution.py:298
  60.2 0.1 fusion.4
  60.3 0.6 %copy.17 = f32[4,4,2,4,8]{4,3,2,1,0:T(4,128)} copy(f32[4,4,2,4,8]{4,3,1,0,2:T(4,128)S(1)} %bitcast.48) | data formatting | bytes 8192 | tf_op jit(solution)/shard_map/squeeze | solution.py:300
  (39 shorter events, 0.3 us)
Async XLA Ops:
  0.0 28.3 %copy-start = (bf16[4,16,3,2,4,256]{5,4,3,2,1,0:T(4,128)(2,1)S(1)}, bf16[4,16,3,2,4,256]{5,4,3,2,1,0:T(4,128)(2,1)}, u32[]{:S(2)}) copy-start(bf16[4,16,3,2,4,256]{5,4,3,2,1,0:T(4,128)(2,1)} %param.7) | copy-start | bytes 2359300
  0.0 15.0 %collective-permute-start = (f32[4,3,2,1,4,256]{5,4,3,2,1,0:T(4,128)}, f32[4,3,2,1,4,256]{5,4,3,2,1,0:T(4,128)S(1)}, u32[]{:S(2)}, u32[]{:S(2)}) collective-permute-start(f32[4,3,2,1,4,256]{5,4,3,2,1,0:T(4,128)} %refs_3_.3), channel_id=1, source_target_pairs={{0,4},{4,8},{8,12},{12,0},{1,5},{5,9},{9,13},{13,1},{2,6},{6,10},{... | collective-permute-start | bytes 294920 | tf_op jit(solution)/shard_map/ppermute | solution.py:25
  3.1 12.0 %collective-permute-start.1 = (f32[4,3,2,1,4,256]{5,4,3,2,1,0:T(4,128)}, f32[4,3,2,1,4,256]{5,4,3,2,1,0:T(4,128)S(1)}, u32[]{:S(2)}, u32[]{:S(2)}) collective-permute-start(f32[4,3,2,1,4,256]{5,4,3,2,1,0:T(4,128)} %refs_3_.3), channel_id=1, source_target_pairs={{0,12},{4,0},{8,4},{12,8},{1,13},{5,1},{9,5},{13,9},{2,14},{6,2},{... | collective-permute-start | bytes 294920 | tf_op jit(solution)/shard_map/ppermute | solution.py:25
  6.1 4.7 %collective-permute-start.2 = (f32[4,3,2,1,1,256]{5,4,3,2,1,0:T(1,128)S(1)}, f32[4,3,2,1,1,256]{5,4,3,2,1,0:T(1,128)S(1)}, u32[]{:S(2)}, u32[]{:S(2)}) collective-permute-start(f32[4,3,2,1,1,256]{5,4,3,2,1,0:T(1,128)S(1)} %get-tuple-element.22), channel_id=1, source_target_pairs={{0,1},{1,2},{2,3},{3,0},{4,5},{5,6},{6,7},{7,4},{8,9},{9,10},{10,1... | collective-permute-start | bytes 73736 | tf_op jit(solution)/shard_map/ppermute | solution.py:25
  6.2 6.5 %collective-permute-start.3 = (f32[4,3,2,1,1,256]{5,4,3,2,1,0:T(1,128)S(1)}, f32[4,3,2,1,1,256]{5,4,3,2,1,0:T(1,128)S(1)}, u32[]{:S(2)}, u32[]{:S(2)}) collective-permute-start(f32[4,3,2,1,1,256]{5,4,3,2,1,0:T(1,128)S(1)} %get-tuple-element.21), channel_id=1, source_target_pairs={{0,3},{1,0},{2,1},{3,2},{4,7},{5,4},{6,5},{7,6},{8,11},{9,8},{10,9... | collective-permute-start | bytes 73736 | tf_op jit(solution)/shard_map/ppermute | solution.py:25
  8.8 6.2 %collective-permute-start.4 = (f32[3,3,2,1,4,256]{5,4,3,2,1,0:T(4,128)S(1)}, f32[3,3,2,1,4,256]{5,4,3,2,1,0:T(4,128)S(1)}, u32[]{:S(2)}, u32[]{:S(2)}) collective-permute-start(f32[3,3,2,1,4,256]{5,4,3,2,1,0:T(4,128)S(1)} %slice_bitcast_fusion.1), channel_id=1, source_target_pairs={{0,4},{4,8},{8,12},{12,0},{1,5},{5,9},{9,13},{13,1},{2,6},{6,10},{... | collective-permute-start | bytes 221192 | tf_op jit(solution)/shard_map/ppermute | solution.py:25
  10.8 4.2 %copy-start.7 = (f32[4,3,2,1,1,256]{5,4,3,2,1,0:T(1,128)}, f32[4,3,2,1,1,256]{5,4,3,2,1,0:T(1,128)S(1)}, u32[]{:S(2)}) copy-start(f32[4,3,2,1,1,256]{5,4,3,2,1,0:T(1,128)S(1)} %collective-permute-done.2.refs_6_) | copy-start | bytes 73732
  10.8 4.2 %collective-permute-start.5 = (f32[3,3,2,4,1,256]{5,4,3,2,1,0:T(1,128)S(1)}, f32[3,3,2,4,1,256]{5,4,3,2,1,0:T(1,128)S(1)}, u32[]{:S(2)}, u32[]{:S(2)}) collective-permute-start(f32[3,3,2,4,1,256]{5,4,3,2,1,0:T(1,128)S(1)} %slice_bitcast_fusion), channel_id=1, source_target_pairs={{0,1},{1,2},{2,3},{3,0},{4,5},{5,6},{6,7},{7,4},{8,9},{9,10},{10,1... | collective-permute-start | bytes 221192 | tf_op jit(solution)/shard_map/ppermute | solution.py:25
  12.7 2.3 %copy-start.8 = (f32[4,3,2,1,1,256]{5,4,3,2,1,0:T(1,128)}, f32[4,3,2,1,1,256]{5,4,3,2,1,0:T(1,128)S(1)}, u32[]{:S(2)}) copy-start(f32[4,3,2,1,1,256]{5,4,3,2,1,0:T(1,128)S(1)} %collective-permute-done.3.refs_7_) | copy-start | bytes 73732
  15.0 0.6 %copy-start.3 = (f32[3,3,2,1,4,256]{5,4,3,2,1,0:T(4,128)}, f32[3,3,2,1,4,256]{5,4,3,2,1,0:T(4,128)S(1)}, u32[]{:S(2)}) copy-start(f32[3,3,2,1,4,256]{5,4,3,2,1,0:T(4,128)S(1)} %collective-permute-done.4.refs_9_) | copy-start | bytes 221188
  15.0 0.6 %copy-start.4 = (f32[3,3,2,4,1,256]{5,4,3,2,1,0:T(1,128)}, f32[3,3,2,4,1,256]{5,4,3,2,1,0:T(1,128)S(1)}, u32[]{:S(2)}) copy-start(f32[3,3,2,4,1,256]{5,4,3,2,1,0:T(1,128)S(1)} %collective-permute-done.5.refs_10_) | copy-start | bytes 221188
  15.0 0.7 %copy-start.1 = (f32[4,3,2,1,4,256]{5,4,3,2,1,0:T(4,128)}, f32[4,3,2,1,4,256]{5,4,3,2,1,0:T(4,128)S(1)}, u32[]{:S(2)}) copy-start(f32[4,3,2,1,4,256]{5,4,3,2,1,0:T(4,128)S(1)} %collective-permute-done.refs_4_) | copy-start | bytes 294916
  15.7 0.6 %copy-start.2 = (f32[4,3,2,1,4,256]{5,4,3,2,1,0:T(4,128)}, f32[4,3,2,1,4,256]{5,4,3,2,1,0:T(4,128)S(1)}, u32[]{:S(2)}) copy-start(f32[4,3,2,1,4,256]{5,4,3,2,1,0:T(4,128)S(1)} %collective-permute-done.1.refs_5_) | copy-start | bytes 294916
  26.5 3.7 %copy-start.12 = (bf16[2,2,3,2,1,8,256]{6,5,4,3,2,1,0:T(8,128)(2,1)S(1)}, bf16[2,2,3,2,1,8,256]{6,5,4,3,2,1,0:T(8,128)(2,1)}, u32[]{:S(2)}) copy-start(bf16[2,2,3,2,1,8,256]{6,5,4,3,2,1,0:T(8,128)(2,1)} %get-tuple-element.11) | copy-start | bytes 294916
  26.5 4.6 %copy-start.11 = (bf16[2,2,3,2,1,8,256]{6,5,4,3,2,1,0:T(8,128)(2,1)S(1)}, bf16[2,2,3,2,1,8,256]{6,5,4,3,2,1,0:T(8,128)(2,1)}, u32[]{:S(2)}) copy-start(bf16[2,2,3,2,1,8,256]{6,5,4,3,2,1,0:T(8,128)(2,1)} %get-tuple-element.12) | copy-start | bytes 294916
  26.5 11.1 %collective-permute-start.8 = (f32[2,2,3,2,4,2,256]{6,5,4,3,2,1,0:T(2,128)}, f32[2,2,3,2,4,2,256]{6,5,4,3,2,1,0:T(2,128)S(1)}, u32[]{:S(2)}, u32[]{:S(2)}) collective-permute-start(f32[2,2,3,2,4,2,256]{6,5,4,3,2,1,0:T(2,128)} %get-tuple-element.13), channel_id=1, source_target_pairs={{0,1},{1,2},{2,3},{3,0},{4,5},{5,6},{6,7},{7,4},{8,9},{9,10},{10,1... | collective-permute-start | bytes 589832 | tf_op jit(solution)/shard_map/ppermute | solution.py:25
  26.6 11.1 %collective-permute-start.9 = (f32[2,2,3,2,4,2,256]{6,5,4,3,2,1,0:T(2,128)}, f32[2,2,3,2,4,2,256]{6,5,4,3,2,1,0:T(2,128)S(1)}, u32[]{:S(2)}, u32[]{:S(2)}) collective-permute-start(f32[2,2,3,2,4,2,256]{6,5,4,3,2,1,0:T(2,128)} %get-tuple-element.14), channel_id=1, source_target_pairs={{0,3},{1,0},{2,1},{3,2},{4,7},{5,4},{6,5},{7,6},{8,11},{9,8},{10,9... | collective-permute-start | bytes 589832 | tf_op jit(solution)/shard_map/ppermute | solution.py:25
  28.5 23.2 %collective-permute-start.10 = (bf16[4,16,3,2,4,256]{5,1,4,2,3,0:T(8,128)(2,1)S(1)}, bf16[4,16,3,2,4,256]{5,1,4,2,3,0:T(8,128)(2,1)S(1)}, u32[]{:S(2)}, u32[]{:S(2)}) collective-permute-start(bf16[4,16,3,2,4,256]{5,1,4,2,3,0:T(8,128)(2,1)S(1)} %copy.14), channel_id=1, source_target_pairs={{0,16},{16,0},{1,17},{17,1},{2,18},{18,2},{3,19},{19,3},{4,20},{20... | collective-permute-start | bytes 2359304 | tf_op jit(solution)/shard_map/ppermute | solution.py:29
  30.2 7.4 %collective-permute-start.6 = (bf16[2,2,3,2,1,8,256]{6,5,4,3,2,1,0:T(8,128)(2,1)S(1)}, bf16[2,2,3,2,1,8,256]{6,5,4,3,2,1,0:T(8,128)(2,1)S(1)}, u32[]{:S(2)}, u32[]{:S(2)}) collective-permute-start(bf16[2,2,3,2,1,8,256]{6,5,4,3,2,1,0:T(8,128)(2,1)S(1)} %copy-done.12), channel_id=1, source_target_pairs={{0,4},{4,8},{8,12},{12,0},{1,5},{5,9},{9,13},{13,1},{2,6},{6,10},{... | collective-permute-start | bytes 294920 | tf_op jit(solution)/shard_map/ppermute | solution.py:25
  31.1 6.5 %collective-permute-start.7 = (bf16[2,2,3,2,1,8,256]{6,5,4,3,2,1,0:T(8,128)(2,1)S(1)}, bf16[2,2,3,2,1,8,256]{6,5,4,3,2,1,0:T(8,128)(2,1)S(1)}, u32[]{:S(2)}, u32[]{:S(2)}) collective-permute-start(bf16[2,2,3,2,1,8,256]{6,5,4,3,2,1,0:T(8,128)(2,1)S(1)} %copy-done.11), channel_id=1, source_target_pairs={{0,12},{4,0},{8,4},{12,8},{1,13},{5,1},{9,5},{13,9},{2,14},{6,2},{... | collective-permute-start | bytes 294920 | tf_op jit(solution)/shard_map/ppermute | solution.py:25
  37.6 0.6 %copy-start.9 = (bf16[2,2,3,2,1,8,256]{6,5,4,3,2,1,0:T(8,128)(2,1)}, bf16[2,2,3,2,1,8,256]{6,5,4,3,2,1,0:T(8,128)(2,1)S(1)}, u32[]{:S(2)}) copy-start(bf16[2,2,3,2,1,8,256]{6,5,4,3,2,1,0:T(8,128)(2,1)S(1)} %collective-permute-done.6.refs_12_) | copy-start | bytes 294916
  37.6 0.7 %copy-start.10 = (bf16[2,2,3,2,1,8,256]{6,5,4,3,2,1,0:T(8,128)(2,1)}, bf16[2,2,3,2,1,8,256]{6,5,4,3,2,1,0:T(8,128)(2,1)S(1)}, u32[]{:S(2)}) copy-start(bf16[2,2,3,2,1,8,256]{6,5,4,3,2,1,0:T(8,128)(2,1)S(1)} %collective-permute-done.7.refs_13_) | copy-start | bytes 294916
  37.6 0.7 %copy-start.5 = (f32[2,2,3,2,4,2,256]{6,5,4,3,2,1,0:T(2,128)}, f32[2,2,3,2,4,2,256]{6,5,4,3,2,1,0:T(2,128)S(1)}, u32[]{:S(2)}) copy-start(f32[2,2,3,2,4,2,256]{6,5,4,3,2,1,0:T(2,128)S(1)} %collective-permute-done.8.refs_14_) | copy-start | bytes 589828
  37.7 0.8 %copy-start.6 = (f32[2,2,3,2,4,2,256]{6,5,4,3,2,1,0:T(2,128)}, f32[2,2,3,2,4,2,256]{6,5,4,3,2,1,0:T(2,128)S(1)}, u32[]{:S(2)}) copy-start(f32[2,2,3,2,4,2,256]{6,5,4,3,2,1,0:T(2,128)S(1)} %collective-permute-done.9.refs_15_) | copy-start | bytes 589828
  53.6 5.0 %collective-permute-start.11 = (f32[2,4,4,2,4,8]{5,0,4,2,1,3:T(2,128)S(1)}, f32[2,4,4,2,4,8]{5,0,4,2,1,3:T(2,128)S(1)}, u32[]{:S(2)}, u32[]{:S(2)}) collective-permute-start(f32[2,4,4,2,4,8]{5,0,4,2,1,3:T(2,128)S(1)} %broadcast_select_fusion.2), channel_id=1, source_target_pairs={{0,2},{1,3},{2,0},{3,1},{4,6},{5,7},{6,4},{7,5},{8,10},{9,11},{10,... | collective-permute-start | bytes 24584 | tf_op jit(solution)/shard_map/ppermute | solution.py:298
  58.9 1.3 %collective-permute-start.12 = (f32[1,4,4,2,4,8]{5,0,4,2,1,3:T(1,128)S(1)}, f32[1,4,4,2,4,8]{5,0,4,2,1,3:T(1,128)S(1)}, u32[]{:S(2)}, u32[]{:S(2)}) collective-permute-start(f32[1,4,4,2,4,8]{5,0,4,2,1,3:T(1,128)S(1)} %broadcast_select_fusion.3), channel_id=1, source_target_pairs={{0,1},{1,0},{2,3},{3,2},{4,5},{5,4},{6,7},{7,6},{8,9},{9,8},{10,11... | collective-permute-start | bytes 12296 | tf_op jit(solution)/shard_map/ppermute | solution.py:298

commit v6 on v5

--- a/solution.py
+++ b/solution.py
@@ -39,10 +39,9 @@
     return im, -re
 
 
-def hop_kernel(first, *refs):
-    (smask_ref, tmask_ref, sign_ref, noise_ref, ntlo_ref, nthi_ref, nzlo_ref, nzhi_ref,
-     u_ref, utedge_ref, uzedge_ref) = refs[:11]
-    rest = refs[11:]
+def hop_kernel(first, R, *refs):
+    (smask_ref, tmask_ref, sign_ref, noise_ref, tup_ref, nthi_ref, zup_ref, nzhi_ref, u_ref) = refs[:9]
+    rest = refs[9:]
     if first:
         out_ref, tfirst_ref, tlast_ref, zfirst_ref, zlast_ref = rest[:5]
         scratch = rest[5:]
@@ -64,11 +63,12 @@
         for a in range(3):
             for b in range(3):
                 for ri in range(RI):
+                    edge = (a * 3 + b) * RI + ri
                     for half in (lower, upper):
-                        ut8[a, b, ri, pl.ds(0, 1), half] = utedge_ref[a, b, ri]
+                        ut8[a, b, ri, 0, half] = tup_ref[R * 6 + edge]
                         ut8[a, b, ri, pl.ds(1, T), half] = u_ref[3, a, b, ri]
                         for t in range(T):
-                            uz8[a, b, ri, t, half] = jnp.broadcast_to(uzedge_ref[a, b, ri, t], (Z, L))
+                            uz8[a, b, ri, t, half] = jnp.broadcast_to(zup_ref[R * 6 * K + edge * T + t], (Z, L))
                         for mu in range(4):
                             u8[mu, a, b, ri, :, half] = u_ref[mu, a, b, ri]
 
@@ -82,13 +82,14 @@
                         src_ref[s, c, ri, t, half] = noise_ref[g, c, ri, t // span] * (
                             fs * tmask_ref[r * (T + 2) + t + 1])
                     if first:
-                        pad_ref[s, c, ri, 0, half] = ntlo_ref[g, c, ri, 0] * (
+                        pad_ref[s, c, ri, 0, half] = tup_ref[(r * 3 + c) * RI + ri] * (
                             fs * tmask_ref[r * (T + 2)] * sign_ref[0])
                         pad_ref[s, c, ri, T + 1, half] = nthi_ref[g, c, ri, 0] * (
                             fs * tmask_ref[r * (T + 2) + T + 1] * sign_ref[1])
                         for t in range(T):
                             f = fs * tmask_ref[r * (T + 2) + t + 1]
-                            zlo_s[s, c, ri, t, half] = jnp.broadcast_to(nzlo_ref[g, c, ri, t // span] * f, (Z, L))
+                            zlo_s[s, c, ri, t, half] = jnp.broadcast_to(
+                                zup_ref[((r * 3 + c) * RI + ri) * K + t // span] * f, (Z, L))
                             zhi_s[s, c, ri, t, half] = jnp.broadcast_to(nzhi_ref[g, c, ri, t // span] * f, (Z, L))
                     else:
                         for t in range(T):
@@ -193,7 +194,12 @@
                     psi = pad_ref[s, c, ri, t + 1]
                     src = src_ref[s, c, ri, t]
                     residual = src - (psi - kappa_hop * acc[s][c][ri])
-                    out_ref[s, c, ri, t] = (psi + residual).astype(out_ref.dtype)
+                    value = psi + residual
+                    if first:
+                        out_ref[s, c, ri, t] = value
+                    else:
+                        for g in range(2):
+                            out_ref[s, c, ri, t, g] = value[g * Z:(g + 1) * Z].astype(out_ref.dtype)
         return carry
 
     lax.fori_loop(0, T, body, 0)
@@ -233,6 +239,7 @@
 def hopping_step(first, scalars, noise_parts, link_parts, spinor_parts):
     R, C, RI, K, Z, L = noise_parts[0].shape
     T = link_parts[0].shape[4]
+    tup, zup = noise_parts[1], noise_parts[3]
     S = 4
     H = R // 2
     ROWS = 2 * Z
@@ -245,9 +252,9 @@
     z_block = pl.BlockSpec((None, 2, C, RI, T, 2, L), index)
     noise_specs = [
         pl.BlockSpec((2, C, RI, K, Z, L), index6),
+        whole(tup),
         pl.BlockSpec((2, C, RI, 1, Z, L), index6),
-        pl.BlockSpec((2, C, RI, 1, Z, L), index6),
-        pl.BlockSpec((2, C, RI, K, 1, L), index6),
+        whole(zup),
         pl.BlockSpec((2, C, RI, K, 1, L), index6),
     ]
     in_specs = [smem, smem, smem] + noise_specs + [whole(x) for x in link_parts]
@@ -259,8 +266,8 @@
         out_specs = [site_block, t_block, t_block, z_block, z_block]
     else:
         in_specs += [site_block, t_block, t_block, z_block, z_block]
-        out_shape = jax.ShapeDtypeStruct(site_shape, jnp.bfloat16)
-        out_specs = site_block
+        out_shape = jax.ShapeDtypeStruct((H, S, C, RI, T, 2, Z, L), jnp.bfloat16)
+        out_specs = pl.BlockSpec((None, S, C, RI, T, 2, Z, L), lambda h: (h,) + (0,) * 7)
     scratch = [
         pltpu.VMEM((S, C, RI, T + 2, ROWS, L), jnp.float32),
         pltpu.VMEM((S, C, RI, T, ROWS, L), jnp.float32),
@@ -271,7 +278,7 @@
         pltpu.VMEM((3, 3, RI, T, ROWS, L), jnp.float32),
     ]
     return pl.pallas_call(
-        functools.partial(hop_kernel, first),
+        functools.partial(hop_kernel, first, R),
         grid=(H,),
         in_specs=in_specs,
         out_specs=out_specs,
@@ -329,18 +336,23 @@
     times = t_start - 1 + jnp.arange(slab_length + 2)
     time_mask = (times[None, :] % TDIL == own_offsets[:, None]).astype(jnp.float32)
     scalars = (spin_mask.reshape(-1), time_mask.reshape(-1), signs)
+    L = noise_slabs.shape[-1]
+    t_up = jnp.concatenate([
+        noise_slabs[:, :, :, K - 1].reshape(-1, Z, L),
+        gauge_links[3, :, :, :, slab_length - 1].reshape(-1, Z, L),
+    ])
+    z_up = jnp.concatenate([
+        noise_slabs[:, :, :, :, Z - 1].reshape(-1, 1, L),
+        gauge_links[2, :, :, :, :, Z - 1].reshape(-1, 1, L),
+    ])
     noise_parts = (
         noise_slabs,
-        passed_along(noise_slabs[:, :, :, K - 1:], "ta", 1),
+        passed_along(t_up, "ta", 1),
         passed_along(noise_slabs[:, :, :, :1], "ta", -1),
-        passed_along(noise_slabs[:, :, :, :, Z - 1:], "sa", 1),
+        passed_along(z_up, "sa", 1),
         passed_along(noise_slabs[:, :, :, :, :1], "sa", -1),
     )
-    link_parts = (
-        gauge_links,
-        passed_along(gauge_links[3, :, :, :, -1:, :, :], "ta", 1),
-        passed_along(gauge_links[2, :, :, :, :, -1:, :], "sa", 1),
-    )
+    link_parts = (gauge_links,)
     spinor, t_first, t_last, z_first, z_last = hopping_step(True, scalars, noise_parts, link_parts, ())
     halos = (
         passed_along(t_last, "ta", 1),
@@ -349,8 +361,6 @@
         passed_along(z_first, "sa", -1),
     )
     rounded = hopping_step(False, scalars, noise_parts, link_parts, (spinor,) + halos)
-    H, S, C, RI, T, ROWS, L = rounded.shape
-    rounded = rounded.reshape(H, S, C, RI, T, 2, ROWS // 2, L)
     own_part = intersection_part(rounded, vectors)
     partner_part = intersection_part(rounded, partner_vectors)
     lower_half = jnp.where(section_index == 0, own_part, partner_part)

time: 61.2 us -> 63 us (1.029)
  local copies, waits for them, and re-layouts: 10.1 us -> 7.88 us
  matrix products: 2.51 us -> 3.73 us
  waiting for transfers between devices: 11.5 us -> 12.6 us
  other arithmetic: 1.33 us -> 2.38 us
    slice x0 -> x2, local copies, waits for them, and re-layouts: none -> 1.93 us  [the longest x1 1.04 us: local_body(): gauge_links[2, :, :, :, :, Z - 1].reshape(-1, 1, L)]
    squeeze x2 -> x0, local copies, waits for them, and re-layouts: 1.93 us -> none  [the longest x1 1.04 us: local_body(): gauge_links[2, :, :, :, :, -1:, :]]
    ppermute x10 -> x8, waiting for transfers between devices: 5.91 us -> 7.68 us  [passed_along(): return lax.ppermute(value, axis, pairs)]
    reshape x1 -> x0, local copies, waits for them, and re-layouts: 1.68 us -> none  [local_body(): rounded = rounded.reshape(H, S, C, RI, T, 2, ROWS // 2, L)]
    dot_general x2, matrix products: 2.51 us -> 3.73 us  [intersection_part(): jnp.einsum('tvcazs,hqcbtgzs->hgqabtv', vector_piece, rounded, preferred_e...]
    concatenate x0 -> x2, other arithmetic: none -> 1.02 us  [the longest x1 0.93 us: local_body(): jnp.concatenate([noise_slabs[:, :, :, K - 1].reshape(-1, Z, L), gauge_lin...]
    unnamed x29 -> x27, local copies, waits for them, and re-layouts: 2.26 us -> 1.67 us
    ppermute x10 -> x8, starting transfers between devices: 12.6 us -> 12.5 us  [passed_along(): return lax.ppermute(value, axis, pairs)]
  transfers between devices with their start and end apart: 13 -> 11, of which waited for: 4 -> 4; matrix products, arithmetic and copies ran while one was open for 15% -> 15% of each run, Pallas kernels for 16% -> 16%
where the time goes in v6:
time: 63 us; the launch traced here: 62.7 us
  Pallas kernels  20.3 us (32%)
  starting transfers between devices  15.5 us (25%)
  waiting for transfers between devices  12.6 us (20%)
  local copies, waits for them, and re-layouts  7.88 us (13%)
  matrix products  3.73 us (6%)
  other arithmetic  2.38 us (4%)
    pallas_call x2, Pallas kernels, hopping_step(): pl.pallas_call(functools.partial(hop_kernel, first, R), grid=(H,), in_spe...  20.3 us
    ppermute x8, starting transfers between devices, passed_along(): return lax.ppermute(value, axis, pairs)  12.5 us
    ppermute x8, waiting for transfers between devices, passed_along(): return lax.ppermute(value, axis, pairs)  7.68 us
    ppermute x2, waiting for transfers between devices, reduce_scatter_sa(): x = keep + lax.ppermute(send, 'sa', [(j, j ^ d) for j in range(n)])  4.95 us
    dot_general x2, matrix products, intersection_part(): jnp.einsum('tvcazs,hqcbtgzs->hgqabtv', vector_piece, rounded, preferred_e...  3.73 us
    unnamed x27, local copies, waits for them, and re-layouts  1.67 us
    ppermute x1, starting transfers between devices, from_partner(): lax.ppermute(x, axis, [(i, i ^ 1 << stride) for i in range(lax.axis_size(...  1.56 us
    ppermute x2, starting transfers between devices, reduce_scatter_sa(): x = keep + lax.ppermute(send, 'sa', [(j, j ^ d) for j in range(n)])  1.39 us
  transfers between devices with their start and end apart: 11, of which 4 were waited for; matrix products, arithmetic and copies ran while one was open for 15% of the time, Pallas kernels for 16%

profile of v6, /device:TPU:0, one launch (start us, length us, event | category | flops | bytes accessed | tf_op | source)
XLA Modules:
  0.0 62.7 jit_solution(10247881743639303698)
XLA Ops:
  0.0 5.1 %collective-permute-start.1 = (f32[4,3,2,1,4,256]{5,4,3,2,1,0:T(4,128)}, f32[4,3,2,1,4,256]{5,4,3,2,1,0:T(4,128)S(1)}, u32[]{:S(2)}, u32[]{:S(2)}) collective-permute-start(f32[4,3,2,1,4,256]{5,4,3,2,1,0:T(4,128)} %refs_3_.3), channel_id=1, source_target_pairs={{0,12},{4,0},{8,4},{12,8},{1,13},{5,1},{9,5},{13,9},{2,14},{6,2},{... | collective-permute-start | bytes 294920 | tf_op jit(solution)/shard_map/ppermute | solution.py:25
  5.1 1.0 %fusion.8 = (f32[4,3,2,1,1,256]{5,4,3,2,1,0:T(1,128)S(1)}, f32[4,3,2,1,1,256]{5,4,3,2,1,0:T(1,128)S(1)}) fusion(f32[4,3,2,1,4,256]{5,4,3,2,1,0:T(4,128)} %refs_3_.3), kind=kLoop, calls=%fused_computation.36 | loop fusion | bytes 98304 | tf_op jit(solution)/shard_map/slice | solution.py:353
  6.1 1.0 %slice.54 = f32[1,3,3,2,4,1,256]{6,5,4,3,2,1,0:T(1,128)S(1)} slice(f32[4,3,3,2,4,4,256]{6,5,4,3,2,1,0:T(4,128)} %refs_8_.3), slice={[2:3], [0:3], [0:3], [0:2], [0:4], [3:4], [0:256]} | slice | bytes 147456 | tf_op jit(solution)/shard_map/slice | solution.py:346
  7.1 0.1 pad_maximum_fusion.1
  7.2 0.1 collective-permute-start.2
  7.3 1.7 %collective-permute-start.3 = (f32[4,3,2,1,1,256]{5,4,3,2,1,0:T(1,128)S(1)}, f32[4,3,2,1,1,256]{5,4,3,2,1,0:T(1,128)S(1)}, u32[]{:S(2)}, u32[]{:S(2)}) collective-permute-start(f32[4,3,2,1,1,256]{5,4,3,2,1,0:T(1,128)S(1)} %get-tuple-element.21), channel_id=1, source_target_pairs={{0,3},{1,0},{2,1},{3,2},{4,7},{5,4},{6,5},{7,6},{8,11},{9,8},{10,9... | collective-permute-start | bytes 73736 | tf_op jit(solution)/shard_map/ppermute | solution.py:25
  9.0 0.9 %slice.52 = f32[1,3,3,2,1,4,256]{6,5,4,3,2,1,0:T(4,128)S(1)} slice(f32[4,3,3,2,4,4,256]{6,5,4,3,2,1,0:T(4,128)} %refs_8_.3), slice={[3:4], [0:3], [0:3], [0:2], [3:4], [0:4], [0:256]} | slice | bytes 147456 | tf_op jit(solution)/shard_map/slice | solution.py:342
  9.9 0.9 %pad_maximum_fusion = f32[42,4,256]{2,1,0:T(4,128)S(1)} fusion(f32[18,4,256]{2,1,0:T(4,128)S(1)} %bitcast.46, f32[24,4,256]{2,1,0:T(4,128)} %bitcast.35), kind=kLoop, calls=%fused_computation.7 | loop fusion | flops 43008 | bytes 344064 | tf_op jit(solution)/shard_map/concatenate | solution.py:340
  10.9 0.1 collective-permute-start
  11.0 0.7 %dynamic_slice.3 = s32[4]{0:T(128)S(1)} dynamic-slice(s32[8]{0:T(128)} %param.6, s32[]{:T(128)S(6)} %select_n.94), dynamic_slice_sizes={4} | dynamic-slice | bytes 36 | tf_op jit(solution)/shard_map/dynamic_slice | solution.py:333
  11.7 0.1 compare_convert_fusion
  11.8 0.1 fusion.5
  11.8 0.6 %pad_maximum_fusion.2.refs_2_ = f32[2]{0:T(128)} fusion(f32[1]{0:T(128)} %bitcast.1, f32[1]{0:T(128)} %bitcast), kind=kLoop, calls=%fused_computation.35 | loop fusion | flops 2 | bytes 16 | tf_op jit(solution)/shard_map/stack | solution.py:331
  12.5 0.7 %reshape.155.refs_1_ = f32[24]{0:T(128)} reshape(f32[4,6]{1,0:T(4,128)S(1)} %compare_convert_fusion) | data formatting | bytes 192 | tf_op jit(solution)/shard_map/convert_element_type | solution.py:337
  13.2 0.6 reshape.154.refs_0_
  13.8 0.0 collective-permute-done.1.refs_5_
  13.8 5.1 %collective-permute-done.refs_4_ = f32[42,4,256]{2,1,0:T(4,128)S(1)} collective-permute-done((f32[42,4,256]{2,1,0:T(4,128)S(1)}, f32[42,4,256]{2,1,0:T(4,128)S(1)}, u32[]{:S(2)}, u32[]{:S(2)}) %collective-permute-start) | collective-permute-done | bytes 172064 | tf_op jit(solution)/shard_map/ppermute | solution.py:25
  18.9 0.7 %copy-done.2 = f32[42,4,256]{2,1,0:T(4,128)} copy-done((f32[42,4,256]{2,1,0:T(4,128)}, f32[42,4,256]{2,1,0:T(4,128)S(1)}, u32[]{:S(2)}) %copy-start.2) | copy-done | bytes 172056
  19.6 10.2 %shard_map.46 = (f32[2,4,3,2,4,8,256]{6,5,4,3,2,1,0:T(8,128)}, bf16[2,2,3,2,1,8,256]{6,5,4,3,2,1,0:T(8,128)(2,1)}, bf16[2,2,3,2,1,8,256]{6,5,4,3,2,1,0:T(8,128)(...) custom-call(f32[16]{0:T(128)} %reshape.154.refs_0_, f32[24]{0:T(128)} %reshape.155.refs_1_, ...), custom_call_target="tpu_custom_call" | custom-call | tf_op jit(solution)/shard_map/pallas_call | solution.py:280
  29.8 0.1 collective-permute-start.6
  29.9 1.7 %collective-permute-start.7 = (f32[2,2,3,2,4,2,256]{6,5,4,3,2,1,0:T(2,128)}, f32[2,2,3,2,4,2,256]{6,5,4,3,2,1,0:T(2,128)S(1)}, u32[]{:S(2)}, u32[]{:S(2)}) collective-permute-start(f32[2,2,3,2,4,2,256]{6,5,4,3,2,1,0:T(2,128)} %get-tuple-element.14), channel_id=1, source_target_pairs={{0,3},{1,0},{2,1},{3,2},{4,7},{5,4},{6,5},{7,6},{8,11},{9,8},{10,9... | collective-permute-start | bytes 589832 | tf_op jit(solution)/shard_map/ppermute | solution.py:25
  31.6 0.2 copy.12
  31.8 1.6 %collective-permute-start.8 = (bf16[4,16,3,2,4,256]{5,1,4,2,3,0:T(8,128)(2,1)S(1)}, bf16[4,16,3,2,4,256]{5,1,4,2,3,0:T(8,128)(2,1)S(1)}, u32[]{:S(2)}, u32[]{:S(2)}) collective-permute-start(bf16[4,16,3,2,4,256]{5,1,4,2,3,0:T(8,128)(2,1)S(1)} %copy.12), channel_id=1, source_target_pairs={{0,16},{16,0},{1,17},{17,1},{2,18},{18,2},{3,19},{19,3},{4,20},{20... | collective-permute-start | bytes 2359304 | tf_op jit(solution)/shard_map/ppermute | solution.py:29
  33.3 3.8 %collective-permute-start.5 = (bf16[2,2,3,2,1,8,256]{6,5,4,3,2,1,0:T(8,128)(2,1)S(1)}, bf16[2,2,3,2,1,8,256]{6,5,4,3,2,1,0:T(8,128)(2,1)S(1)}, u32[]{:S(2)}, u32[]{:S(2)}) collective-permute-start(bf16[2,2,3,2,1,8,256]{6,5,4,3,2,1,0:T(8,128)(2,1)S(1)} %copy-done.10), channel_id=1, source_target_pairs={{0,12},{4,0},{8,4},{12,8},{1,13},{5,1},{9,5},{13,9},{2,14},{6,2},{... | collective-permute-start | bytes 294920 | tf_op jit(solution)/shard_map/ppermute | solution.py:25
  37.1 2.6 %collective-permute-done.4.refs_10_ = bf16[2,2,3,2,1,8,256]{6,5,4,3,2,1,0:T(8,128)(2,1)S(1)} collective-permute-done((bf16[2,2,3,2,1,8,256]{6,5,4,3,2,1,0:T(8,128)(2,1)S(1)}, bf16[2,2,3,2,1,8,256]{6,5,4,3,2,1,0:T(8,128)(2,1)S(1)}, u32[]{:S(2)}, u32[]{:S(2)}) %collective-permute-start.4) | collective-permute-done | bytes 98336 | tf_op jit(solution)/shard_map/ppermute | solution.py:25
  39.8 0.6 copy-done.8
  40.4 0.0 copy-done.9
  40.4 0.1 copy-done.5
  40.5 0.1 copy-done.6
  40.6 10.0 %shard_map.47 = bf16[2,4,3,2,4,2,4,256]{7,6,5,4,3,2,1,0:T(4,128)(2,1)} custom-call(f32[16]{0:T(128)} %reshape.154.refs_0_, f32[24]{0:T(128)} %reshape.155.refs_1_, f32[2]{0:T(128)} %pad_maximum_fusion.2.refs_2_, f32[4,3,2,1,4,256]{5,4,3,2,1,0:T(4,128)} %refs_3_.3, f32[42,4,256]{2,1,0:T(4,128)} %copy-done.2, f32[4,3,2,1,4,256]{5,4,3,2,1,0:T(4,128)} %copy-done.3, ...), custom_call_target="tpu_custom_call" | custom-call | tf_op jit(solution)/shard_map/pallas_call | solution.py:280
  50.6 2.5 %convolution_bitcast_fusion.1 = f32[2,2,4,2,2,4,16]{6,2,3,1,4,0,5:T(4,128)S(1)} fusion(bf16[4,16,3,2,4,256,1,1,1]{5,4,3,2,1,0,8,7,6:T(4,128)(2,1)S(1)} %bitcast.36, bf16[2,4,3,2,4,2,4,256,1]{7,6,5,4,3,2,1,0,8:T(4,128)(2,1)} %bitcast.37), kind=kOutput, calls=%fused_computation.1 | convolution fusion | flops 25165824 | bytes 1589248 | tf_op jit(solution)/shard_map/tvcazs,hqcbtgzs->hgqabtv/dot_general | solution.py:311
  53.1 0.1 copy.11
  53.2 0.1 add.99
  53.3 0.1 sub.39
  53.5 1.3 %convolution_bitcast_fusion = f32[2,2,4,2,2,4,16]{6,2,3,1,4,0,5:T(4,128)S(1)} fusion(bf16[4,16,3,2,4,256]{5,1,4,2,3,0:T(8,128)(2,1)S(1)} %collective-permute-done.8, bf16[2,4,3,2,4,2,4,256,1]{7,6,5,4,3,2,1,0,8:T(4,128)(2,1)S(1)} %bitcast.38), kind=kOutput, calls=%fused_computation | convolution fusion | flops 25165824 | bytes 1589248 | tf_op jit(solution)/shard_map/tvcazs,hqcbtgzs->hgqabtv/dot_general | solution.py:311
  54.7 0.1 copy.14
  54.9 0.1 add.101
  55.0 0.1 sub.41
  55.2 0.1 maximum_bitcast_fusion
  55.3 0.1 broadcast_select_fusion.2
  55.4 1.3 %collective-permute-start.9 = (f32[2,4,4,2,4,8]{5,0,4,2,1,3:T(2,128)S(1)}, f32[2,4,4,2,4,8]{5,0,4,2,1,3:T(2,128)S(1)}, u32[]{:S(2)}, u32[]{:S(2)}) collective-permute-start(f32[2,4,4,2,4,8]{5,0,4,2,1,3:T(2,128)S(1)} %broadcast_select_fusion.2), channel_id=1, source_target_pairs={{0,2},{1,3},{2,0},{3,1},{4,6},{5,7},{6,4},{7,5},{8,10},{9,11},{10,... | collective-permute-start | bytes 24584 | tf_op jit(solution)/shard_map/ppermute | solution.py:305
  56.7 3.7 %collective-permute-done.9 = f32[2,4,4,2,4,8]{5,0,4,2,1,3:T(2,128)S(1)} collective-permute-done((f32[2,4,4,2,4,8]{5,0,4,2,1,3:T(2,128)S(1)}, f32[2,4,4,2,4,8]{5,0,4,2,1,3:T(2,128)S(1)}, u32[]{:S(2)}, u32[]{:S(2)}) %collective-permute-start.9) | collective-permute-done | bytes 8224 | tf_op jit(solution)/shard_map/ppermute | solution.py:305
  60.4 0.1 select_add_fusion
  60.5 0.1 broadcast_select_fusion.3
  60.6 0.1 collective-permute-start.10
  60.7 1.2 %collective-permute-done.10 = f32[1,4,4,2,4,8]{5,0,4,2,1,3:T(1,128)S(1)} collective-permute-done((f32[1,4,4,2,4,8]{5,0,4,2,1,3:T(1,128)S(1)}, f32[1,4,4,2,4,8]{5,0,4,2,1,3:T(1,128)S(1)}, u32[]{:S(2)}, u32[]{:S(2)}) %collective-permute-start.10) | collective-permute-done | bytes 4128 | tf_op jit(solution)/shard_map/ppermute | solution.py:305
  61.9 0.1 fusion.4
  62.0 0.6 %copy.15 = f32[4,4,2,4,8]{4,3,2,1,0:T(4,128)} copy(f32[4,4,2,4,8]{4,3,1,0,2:T(4,128)S(1)} %bitcast.47) | data formatting | bytes 8192 | tf_op jit(solution)/shard_map/squeeze | solution.py:307
  (34 shorter events, 0.2 us)
Async XLA Ops:
  0.0 31.6 %copy-start = (bf16[4,16,3,2,4,256]{5,4,3,2,1,0:T(4,128)(2,1)S(1)}, bf16[4,16,3,2,4,256]{5,4,3,2,1,0:T(4,128)(2,1)}, u32[]{:S(2)}) copy-start(bf16[4,16,3,2,4,256]{5,4,3,2,1,0:T(4,128)(2,1)} %param.7) | copy-start | bytes 2359300
  0.0 13.8 %collective-permute-start.1 = (f32[4,3,2,1,4,256]{5,4,3,2,1,0:T(4,128)}, f32[4,3,2,1,4,256]{5,4,3,2,1,0:T(4,128)S(1)}, u32[]{:S(2)}, u32[]{:S(2)}) collective-permute-start(f32[4,3,2,1,4,256]{5,4,3,2,1,0:T(4,128)} %refs_3_.3), channel_id=1, source_target_pairs={{0,12},{4,0},{8,4},{12,8},{1,13},{5,1},{9,5},{13,9},{2,14},{6,2},{... | collective-permute-start | bytes 294920 | tf_op jit(solution)/shard_map/ppermute | solution.py:25
  7.2 6.5 %collective-permute-start.2 = (f32[96,1,256]{2,1,0:T(1,128)S(1)}, f32[96,1,256]{2,1,0:T(1,128)S(1)}, u32[]{:S(2)}, u32[]{:S(2)}) collective-permute-start(f32[96,1,256]{2,1,0:T(1,128)S(1)} %pad_maximum_fusion.1), channel_id=1, source_target_pairs={{0,1},{1,2},{2,3},{3,0},{4,5},{5,6},{6,7},{7,4},{8,9},{9,10},{10,1... | collective-permute-start | bytes 294920 | tf_op jit(solution)/shard_map/ppermute | solution.py:25
  7.3 6.5 %collective-permute-start.3 = (f32[4,3,2,1,1,256]{5,4,3,2,1,0:T(1,128)S(1)}, f32[4,3,2,1,1,256]{5,4,3,2,1,0:T(1,128)S(1)}, u32[]{:S(2)}, u32[]{:S(2)}) collective-permute-start(f32[4,3,2,1,1,256]{5,4,3,2,1,0:T(1,128)S(1)} %get-tuple-element.21), channel_id=1, source_target_pairs={{0,3},{1,0},{2,1},{3,2},{4,7},{5,4},{6,5},{7,6},{8,11},{9,8},{10,9... | collective-permute-start | bytes 73736 | tf_op jit(solution)/shard_map/ppermute | solution.py:25
  10.9 8.0 %collective-permute-start = (f32[42,4,256]{2,1,0:T(4,128)S(1)}, f32[42,4,256]{2,1,0:T(4,128)S(1)}, u32[]{:S(2)}, u32[]{:S(2)}) collective-permute-start(f32[42,4,256]{2,1,0:T(4,128)S(1)} %pad_maximum_fusion), channel_id=1, source_target_pairs={{0,4},{4,8},{8,12},{12,0},{1,5},{5,9},{9,13},{13,1},{2,6},{6,10},{... | collective-permute-start | bytes 516104 | tf_op jit(solution)/shard_map/ppermute | solution.py:25
  13.8 5.1 %copy-start.7 = (f32[4,3,2,1,1,256]{5,4,3,2,1,0:T(1,128)}, f32[4,3,2,1,1,256]{5,4,3,2,1,0:T(1,128)S(1)}, u32[]{:S(2)}) copy-start(f32[4,3,2,1,1,256]{5,4,3,2,1,0:T(1,128)S(1)} %collective-permute-done.3.refs_7_) | copy-start | bytes 73732
  13.8 5.1 %copy-start.4 = (f32[96,1,256]{2,1,0:T(1,128)}, f32[96,1,256]{2,1,0:T(1,128)S(1)}, u32[]{:S(2)}) copy-start(f32[96,1,256]{2,1,0:T(1,128)S(1)} %collective-permute-done.2.refs_6_) | copy-start | bytes 294916
  13.8 5.1 %copy-start.3 = (f32[4,3,2,1,4,256]{5,4,3,2,1,0:T(4,128)}, f32[4,3,2,1,4,256]{5,4,3,2,1,0:T(4,128)S(1)}, u32[]{:S(2)}) copy-start(f32[4,3,2,1,4,256]{5,4,3,2,1,0:T(4,128)S(1)} %collective-permute-done.1.refs_5_) | copy-start | bytes 294916
  18.9 0.7 %copy-start.2 = (f32[42,4,256]{2,1,0:T(4,128)}, f32[42,4,256]{2,1,0:T(4,128)S(1)}, u32[]{:S(2)}) copy-start(f32[42,4,256]{2,1,0:T(4,128)S(1)} %collective-permute-done.refs_4_) | copy-start | bytes 516100
  29.8 3.5 %copy-start.11 = (bf16[2,2,3,2,1,8,256]{6,5,4,3,2,1,0:T(8,128)(2,1)S(1)}, bf16[2,2,3,2,1,8,256]{6,5,4,3,2,1,0:T(8,128)(2,1)}, u32[]{:S(2)}) copy-start(bf16[2,2,3,2,1,8,256]{6,5,4,3,2,1,0:T(8,128)(2,1)} %get-tuple-element.11) | copy-start | bytes 294916
  29.8 3.5 %copy-start.10 = (bf16[2,2,3,2,1,8,256]{6,5,4,3,2,1,0:T(8,128)(2,1)S(1)}, bf16[2,2,3,2,1,8,256]{6,5,4,3,2,1,0:T(8,128)(2,1)}, u32[]{:S(2)}) copy-start(bf16[2,2,3,2,1,8,256]{6,5,4,3,2,1,0:T(8,128)(2,1)} %get-tuple-element.12) | copy-start | bytes 294916
  29.8 10.0 %collective-permute-start.6 = (f32[2,2,3,2,4,2,256]{6,5,4,3,2,1,0:T(2,128)}, f32[2,2,3,2,4,2,256]{6,5,4,3,2,1,0:T(2,128)S(1)}, u32[]{:S(2)}, u32[]{:S(2)}) collective-permute-start(f32[2,2,3,2,4,2,256]{6,5,4,3,2,1,0:T(2,128)} %get-tuple-element.13), channel_id=1, source_target_pairs={{0,1},{1,2},{2,3},{3,0},{4,5},{5,6},{6,7},{7,4},{8,9},{9,10},{10,1... | collective-permute-start | bytes 589832 | tf_op jit(solution)/shard_map/ppermute | solution.py:25
  29.9 9.9 %collective-permute-start.7 = (f32[2,2,3,2,4,2,256]{6,5,4,3,2,1,0:T(2,128)}, f32[2,2,3,2,4,2,256]{6,5,4,3,2,1,0:T(2,128)S(1)}, u32[]{:S(2)}, u32[]{:S(2)}) collective-permute-start(f32[2,2,3,2,4,2,256]{6,5,4,3,2,1,0:T(2,128)} %get-tuple-element.14), channel_id=1, source_target_pairs={{0,3},{1,0},{2,1},{3,2},{4,7},{5,4},{6,5},{7,6},{8,11},{9,8},{10,9... | collective-permute-start | bytes 589832 | tf_op jit(solution)/shard_map/ppermute | solution.py:25
  31.8 21.7 %collective-permute-start.8 = (bf16[4,16,3,2,4,256]{5,1,4,2,3,0:T(8,128)(2,1)S(1)}, bf16[4,16,3,2,4,256]{5,1,4,2,3,0:T(8,128)(2,1)S(1)}, u32[]{:S(2)}, u32[]{:S(2)}) collective-permute-start(bf16[4,16,3,2,4,256]{5,1,4,2,3,0:T(8,128)(2,1)S(1)} %copy.12), channel_id=1, source_target_pairs={{0,16},{16,0},{1,17},{17,1},{2,18},{18,2},{3,19},{19,3},{4,20},{20... | collective-permute-start | bytes 2359304 | tf_op jit(solution)/shard_map/ppermute | solution.py:29
  33.3 6.4 %collective-permute-start.4 = (bf16[2,2,3,2,1,8,256]{6,5,4,3,2,1,0:T(8,128)(2,1)S(1)}, bf16[2,2,3,2,1,8,256]{6,5,4,3,2,1,0:T(8,128)(2,1)S(1)}, u32[]{:S(2)}, u32[]{:S(2)}) collective-permute-start(bf16[2,2,3,2,1,8,256]{6,5,4,3,2,1,0:T(8,128)(2,1)S(1)} %copy-done.11), channel_id=1, source_target_pairs={{0,4},{4,8},{8,12},{12,0},{1,5},{5,9},{9,13},{13,1},{2,6},{6,10},{... | collective-permute-start | bytes 294920 | tf_op jit(solution)/shard_map/ppermute | solution.py:25
  33.3 6.4 %collective-permute-start.5 = (bf16[2,2,3,2,1,8,256]{6,5,4,3,2,1,0:T(8,128)(2,1)S(1)}, bf16[2,2,3,2,1,8,256]{6,5,4,3,2,1,0:T(8,128)(2,1)S(1)}, u32[]{:S(2)}, u32[]{:S(2)}) collective-permute-start(bf16[2,2,3,2,1,8,256]{6,5,4,3,2,1,0:T(8,128)(2,1)S(1)} %copy-done.10), channel_id=1, source_target_pairs={{0,12},{4,0},{8,4},{12,8},{1,13},{5,1},{9,5},{13,9},{2,14},{6,2},{... | collective-permute-start | bytes 294920 | tf_op jit(solution)/shard_map/ppermute | solution.py:25
  39.7 0.6 %copy-start.8 = (bf16[2,2,3,2,1,8,256]{6,5,4,3,2,1,0:T(8,128)(2,1)}, bf16[2,2,3,2,1,8,256]{6,5,4,3,2,1,0:T(8,128)(2,1)S(1)}, u32[]{:S(2)}) copy-start(bf16[2,2,3,2,1,8,256]{6,5,4,3,2,1,0:T(8,128)(2,1)S(1)} %collective-permute-done.4.refs_10_) | copy-start | bytes 294916
  39.7 0.7 %copy-start.9 = (bf16[2,2,3,2,1,8,256]{6,5,4,3,2,1,0:T(8,128)(2,1)}, bf16[2,2,3,2,1,8,256]{6,5,4,3,2,1,0:T(8,128)(2,1)S(1)}, u32[]{:S(2)}) copy-start(bf16[2,2,3,2,1,8,256]{6,5,4,3,2,1,0:T(8,128)(2,1)S(1)} %collective-permute-done.5.refs_11_) | copy-start | bytes 294916
  39.7 0.7 %copy-start.5 = (f32[2,2,3,2,4,2,256]{6,5,4,3,2,1,0:T(2,128)}, f32[2,2,3,2,4,2,256]{6,5,4,3,2,1,0:T(2,128)S(1)}, u32[]{:S(2)}) copy-start(f32[2,2,3,2,4,2,256]{6,5,4,3,2,1,0:T(2,128)S(1)} %collective-permute-done.6.refs_12_) | copy-start | bytes 589828
  39.8 0.8 %copy-start.6 = (f32[2,2,3,2,4,2,256]{6,5,4,3,2,1,0:T(2,128)}, f32[2,2,3,2,4,2,256]{6,5,4,3,2,1,0:T(2,128)S(1)}, u32[]{:S(2)}) copy-start(f32[2,2,3,2,4,2,256]{6,5,4,3,2,1,0:T(2,128)S(1)} %collective-permute-done.7.refs_13_) | copy-start | bytes 589828
  50.6 2.8 %copy-start.1 = (bf16[2,4,3,2,4,2,4,256]{7,6,5,4,3,2,1,0:T(4,128)(2,1)S(1)}, bf16[2,4,3,2,4,2,4,256]{7,6,5,4,3,2,1,0:T(4,128)(2,1)}, u32[]{:S(2)}) copy-start(bf16[2,4,3,2,4,2,4,256]{7,6,5,4,3,2,1,0:T(4,128)(2,1)} %shard_map.47) | copy-start | bytes 2359300
  55.4 5.0 %collective-permute-start.9 = (f32[2,4,4,2,4,8]{5,0,4,2,1,3:T(2,128)S(1)}, f32[2,4,4,2,4,8]{5,0,4,2,1,3:T(2,128)S(1)}, u32[]{:S(2)}, u32[]{:S(2)}) collective-permute-start(f32[2,4,4,2,4,8]{5,0,4,2,1,3:T(2,128)S(1)} %broadcast_select_fusion.2), channel_id=1, source_target_pairs={{0,2},{1,3},{2,0},{3,1},{4,6},{5,7},{6,4},{7,5},{8,10},{9,11},{10,... | collective-permute-start | bytes 24584 | tf_op jit(solution)/shard_map/ppermute | solution.py:305
  60.6 1.3 %collective-permute-start.10 = (f32[1,4,4,2,4,8]{5,0,4,2,1,3:T(1,128)S(1)}, f32[1,4,4,2,4,8]{5,0,4,2,1,3:T(1,128)S(1)}, u32[]{:S(2)}, u32[]{:S(2)}) collective-permute-start(f32[1,4,4,2,4,8]{5,0,4,2,1,3:T(1,128)S(1)} %broadcast_select_fusion.3), channel_id=1, source_target_pairs={{0,1},{1,0},{2,3},{3,2},{4,5},{5,4},{6,7},{7,6},{8,9},{9,8},{10,11... | collective-permute-start | bytes 12296 | tf_op jit(solution)/shard_map/ppermute | solution.py:305

commit v7 on v5

--- a/solution.py
+++ b/solution.py
@@ -193,7 +193,12 @@
                     psi = pad_ref[s, c, ri, t + 1]
                     src = src_ref[s, c, ri, t]
                     residual = src - (psi - kappa_hop * acc[s][c][ri])
-                    out_ref[s, c, ri, t] = (psi + residual).astype(out_ref.dtype)
+                    value = psi + residual
+                    if first:
+                        out_ref[s, c, ri, t] = value
+                    else:
+                        for g in range(2):
+                            out_ref[s, c, ri, t, g] = value[g * Z:(g + 1) * Z].astype(out_ref.dtype)
         return carry
 
     lax.fori_loop(0, T, body, 0)
@@ -259,8 +264,8 @@
         out_specs = [site_block, t_block, t_block, z_block, z_block]
     else:
         in_specs += [site_block, t_block, t_block, z_block, z_block]
-        out_shape = jax.ShapeDtypeStruct(site_shape, jnp.bfloat16)
-        out_specs = site_block
+        out_shape = jax.ShapeDtypeStruct((H, S, C, RI, T, 2, Z, L), jnp.bfloat16)
+        out_specs = pl.BlockSpec((None, S, C, RI, T, 2, Z, L), lambda h: (h,) + (0,) * 7)
     scratch = [
         pltpu.VMEM((S, C, RI, T + 2, ROWS, L), jnp.float32),
         pltpu.VMEM((S, C, RI, T, ROWS, L), jnp.float32),
@@ -349,8 +354,6 @@
         passed_along(z_first, "sa", -1),
     )
     rounded = hopping_step(False, scalars, noise_parts, link_parts, (spinor,) + halos)
-    H, S, C, RI, T, ROWS, L = rounded.shape
-    rounded = rounded.reshape(H, S, C, RI, T, 2, ROWS // 2, L)
     own_part = intersection_part(rounded, vectors)
     partner_part = intersection_part(rounded, partner_vectors)
     lower_half = jnp.where(section_index == 0, own_part, partner_part)

time: 61.2 us -> 60.9 us (level)
  local copies, waits for them, and re-layouts: 10.1 us -> 8.53 us
  matrix products: 2.51 us -> 3.73 us
    reshape x1 -> x0, local copies, waits for them, and re-layouts: 1.68 us -> none  [local_body(): rounded = rounded.reshape(H, S, C, RI, T, 2, ROWS // 2, L)]
    dot_general x2, matrix products: 2.51 us -> 3.73 us  [intersection_part(): jnp.einsum('tvcazs,hqcbtgzs->hgqabtv', vector_piece, rounded, preferred_e...]
    unnamed x29 -> x31, local copies, waits for them, and re-layouts: 2.26 us -> 2.28 us
  transfers between devices with their start and end apart: 13 -> 13, of which waited for: 4 -> 4; matrix products, arithmetic and copies ran while one was open for 15% -> 14% of each run, Pallas kernels for 16% -> 17%
where the time goes in v7:
time: 60.9 us; the launch traced here: 60.6 us
  Pallas kernels  20.2 us (33%)
  starting transfers between devices  15.1 us (25%)
  waiting for transfers between devices  11.4 us (19%)
  local copies, waits for them, and re-layouts  8.53 us (14%)
  matrix products  3.73 us (6%)
  other arithmetic  1.28 us (2%)
    pallas_call x2, Pallas kernels, hopping_step(): pl.pallas_call(functools.partial(hop_kernel, first), grid=(H,), in_specs=...  20.2 us
    ppermute x10, starting transfers between devices, passed_along(): return lax.ppermute(value, axis, pairs)  12.6 us
    ppermute x10, waiting for transfers between devices, passed_along(): return lax.ppermute(value, axis, pairs)  5.87 us
    ppermute x2, waiting for transfers between devices, reduce_scatter_sa(): x = keep + lax.ppermute(send, 'sa', [(j, j ^ d) for j in range(n)])  5.57 us
    dot_general x2, matrix products, intersection_part(): jnp.einsum('tvcazs,hqcbtgzs->hgqabtv', vector_piece, rounded, preferred_e...  3.73 us
    unnamed x31, local copies, waits for them, and re-layouts  2.28 us
    ppermute x1, starting transfers between devices, from_partner(): lax.ppermute(x, axis, [(i, i ^ 1 << stride) for i in range(lax.axis_size(...  1.73 us
  transfers between devices with their start and end apart: 13, of which 4 were waited for; matrix products, arithmetic and copies ran while one was open for 14% of the time, Pallas kernels for 17%

profile of v7, /device:TPU:0, one launch (start us, length us, event | category | flops | bytes accessed | tf_op | source)
XLA Modules:
  0.0 60.6 jit_solution(14035831260070818293)
XLA Ops:
  0.0 3.1 %collective-permute-start = (f32[4,3,2,1,4,256]{5,4,3,2,1,0:T(4,128)}, f32[4,3,2,1,4,256]{5,4,3,2,1,0:T(4,128)S(1)}, u32[]{:S(2)}, u32[]{:S(2)}) collective-permute-start(f32[4,3,2,1,4,256]{5,4,3,2,1,0:T(4,128)} %refs_3_.3), channel_id=1, source_target_pairs={{0,4},{4,8},{8,12},{12,0},{1,5},{5,9},{9,13},{13,1},{2,6},{6,10},{... | collective-permute-start | bytes 294920 | tf_op jit(solution)/shard_map/ppermute | solution.py:25
  3.1 2.1 %collective-permute-start.1 = (f32[4,3,2,1,4,256]{5,4,3,2,1,0:T(4,128)}, f32[4,3,2,1,4,256]{5,4,3,2,1,0:T(4,128)S(1)}, u32[]{:S(2)}, u32[]{:S(2)}) collective-permute-start(f32[4,3,2,1,4,256]{5,4,3,2,1,0:T(4,128)} %refs_3_.3), channel_id=1, source_target_pairs={{0,12},{4,0},{8,4},{12,8},{1,13},{5,1},{9,5},{13,9},{2,14},{6,2},{... | collective-permute-start | bytes 294920 | tf_op jit(solution)/shard_map/ppermute | solution.py:25
  5.1 1.0 %fusion.8 = (f32[4,3,2,1,1,256]{5,4,3,2,1,0:T(1,128)S(1)}, f32[4,3,2,1,1,256]{5,4,3,2,1,0:T(1,128)S(1)}) fusion(f32[4,3,2,1,4,256]{5,4,3,2,1,0:T(4,128)} %refs_3_.3), kind=kLoop, calls=%fused_computation.36 | loop fusion | bytes 98304 | tf_op jit(solution)/shard_map/slice | solution.py:342
  6.1 0.1 collective-permute-start.2
  6.2 1.7 %collective-permute-start.3 = (f32[4,3,2,1,1,256]{5,4,3,2,1,0:T(1,128)S(1)}, f32[4,3,2,1,1,256]{5,4,3,2,1,0:T(1,128)S(1)}, u32[]{:S(2)}, u32[]{:S(2)}) collective-permute-start(f32[4,3,2,1,1,256]{5,4,3,2,1,0:T(1,128)S(1)} %get-tuple-element.21), channel_id=1, source_target_pairs={{0,3},{1,0},{2,1},{3,2},{4,7},{5,4},{6,5},{7,6},{8,11},{9,8},{10,9... | collective-permute-start | bytes 73736 | tf_op jit(solution)/shard_map/ppermute | solution.py:25
  7.9 0.9 %slice_bitcast_fusion.1 = f32[3,3,2,1,4,256]{5,4,3,2,1,0:T(4,128)S(1)} fusion(f32[4,3,3,2,4,4,256]{6,5,4,3,2,1,0:T(4,128)} %refs_8_.3), kind=kLoop, calls=%fused_computation.14 | loop fusion | bytes 147456 | tf_op jit(solution)/shard_map/squeeze | solution.py:346
  8.8 1.0 %slice_bitcast_fusion = f32[3,3,2,4,1,256]{5,4,3,2,1,0:T(1,128)S(1)} fusion(f32[4,3,3,2,4,4,256]{6,5,4,3,2,1,0:T(4,128)} %refs_8_.3), kind=kLoop, calls=%fused_computation.13 | loop fusion | bytes 147456 | tf_op jit(solution)/shard_map/squeeze | solution.py:347
  9.9 0.7 %dynamic_slice.3 = s32[4]{0:T(128)S(1)} dynamic-slice(s32[8]{0:T(128)} %param.6, s32[]{:T(128)S(6)} %select_n.94), dynamic_slice_sizes={4} | dynamic-slice | bytes 36 | tf_op jit(solution)/shard_map/dynamic_slice | solution.py:331
  10.7 0.1 compare_convert_fusion
  10.7 0.1 fusion.5
  10.8 0.1 collective-permute-start.5
  10.9 0.6 pad_maximum_fusion.refs_2_
  11.4 0.7 %reshape.155.refs_1_ = f32[24]{0:T(128)} reshape(f32[4,6]{1,0:T(4,128)S(1)} %compare_convert_fusion) | data formatting | bytes 192 | tf_op jit(solution)/shard_map/convert_element_type | solution.py:335
  12.1 0.7 %reshape.154.refs_0_ = f32[16]{0:T(128)} reshape(f32[4,4]{1,0:T(4,128)S(1)} %fusion.5) | data formatting | bytes 128 | tf_op jit(solution)/shard_map/convert_element_type | solution.py:333
  12.7 2.2 %collective-permute-done.4.refs_9_ = f32[3,3,2,1,4,256]{5,4,3,2,1,0:T(4,128)S(1)} collective-permute-done((f32[3,3,2,1,4,256]{5,4,3,2,1,0:T(4,128)S(1)}, f32[3,3,2,1,4,256]{5,4,3,2,1,0:T(4,128)S(1)}, u32[]{:S(2)}, u32[]{:S(2)}) %collective-permute-start.4) | collective-permute-done | bytes 73760 | tf_op jit(solution)/shard_map/ppermute | solution.py:25
  15.0 0.6 copy-done.4
  15.7 0.6 %copy-done.3 = f32[4,3,2,1,4,256]{5,4,3,2,1,0:T(4,128)} copy-done((f32[4,3,2,1,4,256]{5,4,3,2,1,0:T(4,128)}, f32[4,3,2,1,4,256]{5,4,3,2,1,0:T(4,128)S(1)}, u32[]{:S(2)}) %copy-start.3) | copy-done | bytes 98328
  16.3 10.2 %shard_map.46 = (f32[2,4,3,2,4,8,256]{6,5,4,3,2,1,0:T(8,128)}, bf16[2,2,3,2,1,8,256]{6,5,4,3,2,1,0:T(8,128)(2,1)}, bf16[2,2,3,2,1,8,256]{6,5,4,3,2,1,0:T(8,128)(...) custom-call(f32[16]{0:T(128)} %reshape.154.refs_0_, f32[24]{0:T(128)} %reshape.155.refs_1_, ...), custom_call_target="tpu_custom_call" | custom-call | tf_op jit(solution)/shard_map/pallas_call | solution.py:278
  26.5 0.1 collective-permute-start.8
  26.6 1.7 %collective-permute-start.9 = (f32[2,2,3,2,4,2,256]{6,5,4,3,2,1,0:T(2,128)}, f32[2,2,3,2,4,2,256]{6,5,4,3,2,1,0:T(2,128)S(1)}, u32[]{:S(2)}, u32[]{:S(2)}) collective-permute-start(f32[2,2,3,2,4,2,256]{6,5,4,3,2,1,0:T(2,128)} %get-tuple-element.14), channel_id=1, source_target_pairs={{0,3},{1,0},{2,1},{3,2},{4,7},{5,4},{6,5},{7,6},{8,11},{9,8},{10,9... | collective-permute-start | bytes 589832 | tf_op jit(solution)/shard_map/ppermute | solution.py:25
  28.3 0.2 copy.14
  28.5 1.7 %collective-permute-start.10 = (bf16[4,16,3,2,4,256]{5,1,4,2,3,0:T(8,128)(2,1)S(1)}, bf16[4,16,3,2,4,256]{5,1,4,2,3,0:T(8,128)(2,1)S(1)}, u32[]{:S(2)}, u32[]{:S(2)}) collective-permute-start(bf16[4,16,3,2,4,256]{5,1,4,2,3,0:T(8,128)(2,1)S(1)} %copy.14), channel_id=1, source_target_pairs={{0,16},{16,0},{1,17},{17,1},{2,18},{18,2},{3,19},{19,3},{4,20},{20... | collective-permute-start | bytes 2359304 | tf_op jit(solution)/shard_map/ppermute | solution.py:29
  30.2 0.9 %collective-permute-start.6 = (bf16[2,2,3,2,1,8,256]{6,5,4,3,2,1,0:T(8,128)(2,1)S(1)}, bf16[2,2,3,2,1,8,256]{6,5,4,3,2,1,0:T(8,128)(2,1)S(1)}, u32[]{:S(2)}, u32[]{:S(2)}) collective-permute-start(bf16[2,2,3,2,1,8,256]{6,5,4,3,2,1,0:T(8,128)(2,1)S(1)} %copy-done.13), channel_id=1, source_target_pairs={{0,4},{4,8},{8,12},{12,0},{1,5},{5,9},{9,13},{13,1},{2,6},{6,10},{... | collective-permute-start | bytes 294920 | tf_op jit(solution)/shard_map/ppermute | solution.py:25
  31.2 2.9 %collective-permute-start.7 = (bf16[2,2,3,2,1,8,256]{6,5,4,3,2,1,0:T(8,128)(2,1)S(1)}, bf16[2,2,3,2,1,8,256]{6,5,4,3,2,1,0:T(8,128)(2,1)S(1)}, u32[]{:S(2)}, u32[]{:S(2)}) collective-permute-start(bf16[2,2,3,2,1,8,256]{6,5,4,3,2,1,0:T(8,128)(2,1)S(1)} %copy-done.12), channel_id=1, source_target_pairs={{0,12},{4,0},{8,4},{12,8},{1,13},{5,1},{9,5},{13,9},{2,14},{6,2},{... | collective-permute-start | bytes 294920 | tf_op jit(solution)/shard_map/ppermute | solution.py:25
  34.1 3.6 %collective-permute-done.6.refs_12_ = bf16[2,2,3,2,1,8,256]{6,5,4,3,2,1,0:T(8,128)(2,1)S(1)} collective-permute-done((bf16[2,2,3,2,1,8,256]{6,5,4,3,2,1,0:T(8,128)(2,1)S(1)}, bf16[2,2,3,2,1,8,256]{6,5,4,3,2,1,0:T(8,128)(2,1)S(1)}, u32[]{:S(2)}, u32[]{:S(2)}) %collective-permute-start.6) | collective-permute-done | bytes 98336 | tf_op jit(solution)/shard_map/ppermute | solution.py:25
  37.7 0.6 copy-done.10
  38.3 0.1 copy-done.11
  38.3 0.1 copy-done.6
  38.4 0.1 copy-done.7
  38.5 10.0 %shard_map.47 = bf16[2,4,3,2,4,2,4,256]{7,6,5,4,3,2,1,0:T(4,128)(2,1)} custom-call(f32[16]{0:T(128)} %reshape.154.refs_0_, f32[24]{0:T(128)} %reshape.155.refs_1_, f32[2]{0:T(128)} %pad_maximum_fusion.refs_2_, f32[4,3,2,1,4,256]{5,4,3,2,1,0:T(4,128)} %refs_3_.3, f32[4,3,2,1,4,256]{5,4,3,2,1,0:T(4,128)} %copy-done.2, f32[4,3,2,1,4,256]{5,4,3,2,1,0:T(4,128)} %copy-done.3, ...), custom_call_target="tpu_custom_call" | custom-call | tf_op jit(solution)/shard_map/pallas_call | solution.py:278
  48.5 2.5 %convolution_bitcast_fusion.1 = f32[2,2,4,2,2,4,16]{6,2,3,1,4,0,5:T(4,128)S(1)} fusion(bf16[4,16,3,2,4,256,1,1,1]{5,4,3,2,1,0,8,7,6:T(4,128)(2,1)S(1)} %bitcast.37, bf16[2,4,3,2,4,2,4,256,1]{7,6,5,4,3,2,1,0,8:T(4,128)(2,1)} %bitcast.38), kind=kOutput, calls=%fused_computation.1 | convolution fusion | flops 25165824 | bytes 1589248 | tf_op jit(solution)/shard_map/tvcazs,hqcbtgzs->hgqabtv/dot_general | solution.py:309
  51.0 0.1 copy.13
  51.1 0.1 add.99
  51.2 0.1 sub.39
  51.4 1.3 %convolution_bitcast_fusion = f32[2,2,4,2,2,4,16]{6,2,3,1,4,0,5:T(4,128)S(1)} fusion(bf16[4,16,3,2,4,256]{5,1,4,2,3,0:T(8,128)(2,1)S(1)} %collective-permute-done.10, bf16[2,4,3,2,4,2,4,256,1]{7,6,5,4,3,2,1,0,8:T(4,128)(2,1)S(1)} %bitcast.39), kind=kOutput, calls=%fused_computation | convolution fusion | flops 25165824 | bytes 1589248 | tf_op jit(solution)/shard_map/tvcazs,hqcbtgzs->hgqabtv/dot_general | solution.py:309
  52.6 0.1 copy.16
  52.8 0.1 add.101
  52.9 0.1 sub.41
  53.1 0.1 maximum_bitcast_fusion
  53.2 0.1 broadcast_select_fusion.2
  53.3 0.7 %collective-permute-start.11 = (f32[2,4,4,2,4,8]{5,0,4,2,1,3:T(2,128)S(1)}, f32[2,4,4,2,4,8]{5,0,4,2,1,3:T(2,128)S(1)}, u32[]{:S(2)}, u32[]{:S(2)}) collective-permute-start(f32[2,4,4,2,4,8]{5,0,4,2,1,3:T(2,128)S(1)} %broadcast_select_fusion.2), channel_id=1, source_target_pairs={{0,2},{1,3},{2,0},{3,1},{4,6},{5,7},{6,4},{7,5},{8,10},{9,11},{10,... | collective-permute-start | bytes 24584 | tf_op jit(solution)/shard_map/ppermute | solution.py:303
  54.0 4.3 %collective-permute-done.11 = f32[2,4,4,2,4,8]{5,0,4,2,1,3:T(2,128)S(1)} collective-permute-done((f32[2,4,4,2,4,8]{5,0,4,2,1,3:T(2,128)S(1)}, f32[2,4,4,2,4,8]{5,0,4,2,1,3:T(2,128)S(1)}, u32[]{:S(2)}, u32[]{:S(2)}) %collective-permute-start.11) | collective-permute-done | bytes 8224 | tf_op jit(solution)/shard_map/ppermute | solution.py:303
  58.3 0.1 select_add_fusion
  58.4 0.1 broadcast_select_fusion.3
  58.5 0.1 collective-permute-start.12
  58.6 1.2 %collective-permute-done.12 = f32[1,4,4,2,4,8]{5,0,4,2,1,3:T(1,128)S(1)} collective-permute-done((f32[1,4,4,2,4,8]{5,0,4,2,1,3:T(1,128)S(1)}, f32[1,4,4,2,4,8]{5,0,4,2,1,3:T(1,128)S(1)}, u32[]{:S(2)}, u32[]{:S(2)}) %collective-permute-start.12) | collective-permute-done | bytes 4128 | tf_op jit(solution)/shard_map/ppermute | solution.py:303
  59.8 0.1 fusion.4
  60.0 0.6 %copy.17 = f32[4,4,2,4,8]{4,3,2,1,0:T(4,128)} copy(f32[4,4,2,4,8]{4,3,1,0,2:T(4,128)S(1)} %bitcast.46) | data formatting | bytes 8192 | tf_op jit(solution)/shard_map/squeeze | solution.py:305
  (40 shorter events, 0.3 us)
Async XLA Ops:
  0.0 28.3 %copy-start = (bf16[4,16,3,2,4,256]{5,4,3,2,1,0:T(4,128)(2,1)S(1)}, bf16[4,16,3,2,4,256]{5,4,3,2,1,0:T(4,128)(2,1)}, u32[]{:S(2)}) copy-start(bf16[4,16,3,2,4,256]{5,4,3,2,1,0:T(4,128)(2,1)} %param.7) | copy-start | bytes 2359300
  0.0 15.0 %collective-permute-start = (f32[4,3,2,1,4,256]{5,4,3,2,1,0:T(4,128)}, f32[4,3,2,1,4,256]{5,4,3,2,1,0:T(4,128)S(1)}, u32[]{:S(2)}, u32[]{:S(2)}) collective-permute-start(f32[4,3,2,1,4,256]{5,4,3,2,1,0:T(4,128)} %refs_3_.3), channel_id=1, source_target_pairs={{0,4},{4,8},{8,12},{12,0},{1,5},{5,9},{9,13},{13,1},{2,6},{6,10},{... | collective-permute-start | bytes 294920 | tf_op jit(solution)/shard_map/ppermute | solution.py:25
  3.1 12.0 %collective-permute-start.1 = (f32[4,3,2,1,4,256]{5,4,3,2,1,0:T(4,128)}, f32[4,3,2,1,4,256]{5,4,3,2,1,0:T(4,128)S(1)}, u32[]{:S(2)}, u32[]{:S(2)}) collective-permute-start(f32[4,3,2,1,4,256]{5,4,3,2,1,0:T(4,128)} %refs_3_.3), channel_id=1, source_target_pairs={{0,12},{4,0},{8,4},{12,8},{1,13},{5,1},{9,5},{13,9},{2,14},{6,2},{... | collective-permute-start | bytes 294920 | tf_op jit(solution)/shard_map/ppermute | solution.py:25
  6.1 4.7 %collective-permute-start.2 = (f32[4,3,2,1,1,256]{5,4,3,2,1,0:T(1,128)S(1)}, f32[4,3,2,1,1,256]{5,4,3,2,1,0:T(1,128)S(1)}, u32[]{:S(2)}, u32[]{:S(2)}) collective-permute-start(f32[4,3,2,1,1,256]{5,4,3,2,1,0:T(1,128)S(1)} %get-tuple-element.22), channel_id=1, source_target_pairs={{0,1},{1,2},{2,3},{3,0},{4,5},{5,6},{6,7},{7,4},{8,9},{9,10},{10,1... | collective-permute-start | bytes 73736 | tf_op jit(solution)/shard_map/ppermute | solution.py:25
  6.2 6.5 %collective-permute-start.3 = (f32[4,3,2,1,1,256]{5,4,3,2,1,0:T(1,128)S(1)}, f32[4,3,2,1,1,256]{5,4,3,2,1,0:T(1,128)S(1)}, u32[]{:S(2)}, u32[]{:S(2)}) collective-permute-start(f32[4,3,2,1,1,256]{5,4,3,2,1,0:T(1,128)S(1)} %get-tuple-element.21), channel_id=1, source_target_pairs={{0,3},{1,0},{2,1},{3,2},{4,7},{5,4},{6,5},{7,6},{8,11},{9,8},{10,9... | collective-permute-start | bytes 73736 | tf_op jit(solution)/shard_map/ppermute | solution.py:25
  8.8 6.2 %collective-permute-start.4 = (f32[3,3,2,1,4,256]{5,4,3,2,1,0:T(4,128)S(1)}, f32[3,3,2,1,4,256]{5,4,3,2,1,0:T(4,128)S(1)}, u32[]{:S(2)}, u32[]{:S(2)}) collective-permute-start(f32[3,3,2,1,4,256]{5,4,3,2,1,0:T(4,128)S(1)} %slice_bitcast_fusion.1), channel_id=1, source_target_pairs={{0,4},{4,8},{8,12},{12,0},{1,5},{5,9},{9,13},{13,1},{2,6},{6,10},{... | collective-permute-start | bytes 221192 | tf_op jit(solution)/shard_map/ppermute | solution.py:25
  10.8 4.2 %copy-start.8 = (f32[4,3,2,1,1,256]{5,4,3,2,1,0:T(1,128)}, f32[4,3,2,1,1,256]{5,4,3,2,1,0:T(1,128)S(1)}, u32[]{:S(2)}) copy-start(f32[4,3,2,1,1,256]{5,4,3,2,1,0:T(1,128)S(1)} %collective-permute-done.2.refs_6_) | copy-start | bytes 73732
  10.8 4.2 %collective-permute-start.5 = (f32[3,3,2,4,1,256]{5,4,3,2,1,0:T(1,128)S(1)}, f32[3,3,2,4,1,256]{5,4,3,2,1,0:T(1,128)S(1)}, u32[]{:S(2)}, u32[]{:S(2)}) collective-permute-start(f32[3,3,2,4,1,256]{5,4,3,2,1,0:T(1,128)S(1)} %slice_bitcast_fusion), channel_id=1, source_target_pairs={{0,1},{1,2},{2,3},{3,0},{4,5},{5,6},{6,7},{7,4},{8,9},{9,10},{10,1... | collective-permute-start | bytes 221192 | tf_op jit(solution)/shard_map/ppermute | solution.py:25
  12.7 2.3 %copy-start.9 = (f32[4,3,2,1,1,256]{5,4,3,2,1,0:T(1,128)}, f32[4,3,2,1,1,256]{5,4,3,2,1,0:T(1,128)S(1)}, u32[]{:S(2)}) copy-start(f32[4,3,2,1,1,256]{5,4,3,2,1,0:T(1,128)S(1)} %collective-permute-done.3.refs_7_) | copy-start | bytes 73732
  15.0 0.6 %copy-start.4 = (f32[3,3,2,1,4,256]{5,4,3,2,1,0:T(4,128)}, f32[3,3,2,1,4,256]{5,4,3,2,1,0:T(4,128)S(1)}, u32[]{:S(2)}) copy-start(f32[3,3,2,1,4,256]{5,4,3,2,1,0:T(4,128)S(1)} %collective-permute-done.4.refs_9_) | copy-start | bytes 221188
  15.0 0.7 %copy-start.5 = (f32[3,3,2,4,1,256]{5,4,3,2,1,0:T(1,128)}, f32[3,3,2,4,1,256]{5,4,3,2,1,0:T(1,128)S(1)}, u32[]{:S(2)}) copy-start(f32[3,3,2,4,1,256]{5,4,3,2,1,0:T(1,128)S(1)} %collective-permute-done.5.refs_10_) | copy-start | bytes 221188
  15.0 0.7 %copy-start.2 = (f32[4,3,2,1,4,256]{5,4,3,2,1,0:T(4,128)}, f32[4,3,2,1,4,256]{5,4,3,2,1,0:T(4,128)S(1)}, u32[]{:S(2)}) copy-start(f32[4,3,2,1,4,256]{5,4,3,2,1,0:T(4,128)S(1)} %collective-permute-done.refs_4_) | copy-start | bytes 294916
  15.7 0.6 %copy-start.3 = (f32[4,3,2,1,4,256]{5,4,3,2,1,0:T(4,128)}, f32[4,3,2,1,4,256]{5,4,3,2,1,0:T(4,128)S(1)}, u32[]{:S(2)}) copy-start(f32[4,3,2,1,4,256]{5,4,3,2,1,0:T(4,128)S(1)} %collective-permute-done.1.refs_5_) | copy-start | bytes 294916
  26.5 3.7 %copy-start.13 = (bf16[2,2,3,2,1,8,256]{6,5,4,3,2,1,0:T(8,128)(2,1)S(1)}, bf16[2,2,3,2,1,8,256]{6,5,4,3,2,1,0:T(8,128)(2,1)}, u32[]{:S(2)}) copy-start(bf16[2,2,3,2,1,8,256]{6,5,4,3,2,1,0:T(8,128)(2,1)} %get-tuple-element.11) | copy-start | bytes 294916
  26.5 4.6 %copy-start.12 = (bf16[2,2,3,2,1,8,256]{6,5,4,3,2,1,0:T(8,128)(2,1)S(1)}, bf16[2,2,3,2,1,8,256]{6,5,4,3,2,1,0:T(8,128)(2,1)}, u32[]{:S(2)}) copy-start(bf16[2,2,3,2,1,8,256]{6,5,4,3,2,1,0:T(8,128)(2,1)} %get-tuple-element.12) | copy-start | bytes 294916
  26.5 11.2 %collective-permute-start.8 = (f32[2,2,3,2,4,2,256]{6,5,4,3,2,1,0:T(2,128)}, f32[2,2,3,2,4,2,256]{6,5,4,3,2,1,0:T(2,128)S(1)}, u32[]{:S(2)}, u32[]{:S(2)}) collective-permute-start(f32[2,2,3,2,4,2,256]{6,5,4,3,2,1,0:T(2,128)} %get-tuple-element.13), channel_id=1, source_target_pairs={{0,1},{1,2},{2,3},{3,0},{4,5},{5,6},{6,7},{7,4},{8,9},{9,10},{10,1... | collective-permute-start | bytes 589832 | tf_op jit(solution)/shard_map/ppermute | solution.py:25
  26.6 11.1 %collective-permute-start.9 = (f32[2,2,3,2,4,2,256]{6,5,4,3,2,1,0:T(2,128)}, f32[2,2,3,2,4,2,256]{6,5,4,3,2,1,0:T(2,128)S(1)}, u32[]{:S(2)}, u32[]{:S(2)}) collective-permute-start(f32[2,2,3,2,4,2,256]{6,5,4,3,2,1,0:T(2,128)} %get-tuple-element.14), channel_id=1, source_target_pairs={{0,3},{1,0},{2,1},{3,2},{4,7},{5,4},{6,5},{7,6},{8,11},{9,8},{10,9... | collective-permute-start | bytes 589832 | tf_op jit(solution)/shard_map/ppermute | solution.py:25
  28.5 22.9 %collective-permute-start.10 = (bf16[4,16,3,2,4,256]{5,1,4,2,3,0:T(8,128)(2,1)S(1)}, bf16[4,16,3,2,4,256]{5,1,4,2,3,0:T(8,128)(2,1)S(1)}, u32[]{:S(2)}, u32[]{:S(2)}) collective-permute-start(bf16[4,16,3,2,4,256]{5,1,4,2,3,0:T(8,128)(2,1)S(1)} %copy.14), channel_id=1, source_target_pairs={{0,16},{16,0},{1,17},{17,1},{2,18},{18,2},{3,19},{19,3},{4,20},{20... | collective-permute-start | bytes 2359304 | tf_op jit(solution)/shard_map/ppermute | solution.py:29
  30.2 7.4 %collective-permute-start.6 = (bf16[2,2,3,2,1,8,256]{6,5,4,3,2,1,0:T(8,128)(2,1)S(1)}, bf16[2,2,3,2,1,8,256]{6,5,4,3,2,1,0:T(8,128)(2,1)S(1)}, u32[]{:S(2)}, u32[]{:S(2)}) collective-permute-start(bf16[2,2,3,2,1,8,256]{6,5,4,3,2,1,0:T(8,128)(2,1)S(1)} %copy-done.13), channel_id=1, source_target_pairs={{0,4},{4,8},{8,12},{12,0},{1,5},{5,9},{9,13},{13,1},{2,6},{6,10},{... | collective-permute-start | bytes 294920 | tf_op jit(solution)/shard_map/ppermute | solution.py:25
  31.2 6.5 %collective-permute-start.7 = (bf16[2,2,3,2,1,8,256]{6,5,4,3,2,1,0:T(8,128)(2,1)S(1)}, bf16[2,2,3,2,1,8,256]{6,5,4,3,2,1,0:T(8,128)(2,1)S(1)}, u32[]{:S(2)}, u32[]{:S(2)}) collective-permute-start(bf16[2,2,3,2,1,8,256]{6,5,4,3,2,1,0:T(8,128)(2,1)S(1)} %copy-done.12), channel_id=1, source_target_pairs={{0,12},{4,0},{8,4},{12,8},{1,13},{5,1},{9,5},{13,9},{2,14},{6,2},{... | collective-permute-start | bytes 294920 | tf_op jit(solution)/shard_map/ppermute | solution.py:25
  37.7 0.6 %copy-start.10 = (bf16[2,2,3,2,1,8,256]{6,5,4,3,2,1,0:T(8,128)(2,1)}, bf16[2,2,3,2,1,8,256]{6,5,4,3,2,1,0:T(8,128)(2,1)S(1)}, u32[]{:S(2)}) copy-start(bf16[2,2,3,2,1,8,256]{6,5,4,3,2,1,0:T(8,128)(2,1)S(1)} %collective-permute-done.6.refs_12_) | copy-start | bytes 294916
  37.7 0.7 %copy-start.11 = (bf16[2,2,3,2,1,8,256]{6,5,4,3,2,1,0:T(8,128)(2,1)}, bf16[2,2,3,2,1,8,256]{6,5,4,3,2,1,0:T(8,128)(2,1)S(1)}, u32[]{:S(2)}) copy-start(bf16[2,2,3,2,1,8,256]{6,5,4,3,2,1,0:T(8,128)(2,1)S(1)} %collective-permute-done.7.refs_13_) | copy-start | bytes 294916
  37.7 0.7 %copy-start.6 = (f32[2,2,3,2,4,2,256]{6,5,4,3,2,1,0:T(2,128)}, f32[2,2,3,2,4,2,256]{6,5,4,3,2,1,0:T(2,128)S(1)}, u32[]{:S(2)}) copy-start(f32[2,2,3,2,4,2,256]{6,5,4,3,2,1,0:T(2,128)S(1)} %collective-permute-done.8.refs_14_) | copy-start | bytes 589828
  37.7 0.8 %copy-start.7 = (f32[2,2,3,2,4,2,256]{6,5,4,3,2,1,0:T(2,128)}, f32[2,2,3,2,4,2,256]{6,5,4,3,2,1,0:T(2,128)S(1)}, u32[]{:S(2)}) copy-start(f32[2,2,3,2,4,2,256]{6,5,4,3,2,1,0:T(2,128)S(1)} %collective-permute-done.9.refs_15_) | copy-start | bytes 589828
  48.5 2.9 %copy-start.1 = (bf16[2,4,3,2,4,2,4,256]{7,6,5,4,3,2,1,0:T(4,128)(2,1)S(1)}, bf16[2,4,3,2,4,2,4,256]{7,6,5,4,3,2,1,0:T(4,128)(2,1)}, u32[]{:S(2)}) copy-start(bf16[2,4,3,2,4,2,4,256]{7,6,5,4,3,2,1,0:T(4,128)(2,1)} %shard_map.47) | copy-start | bytes 2359300
  53.3 5.0 %collective-permute-start.11 = (f32[2,4,4,2,4,8]{5,0,4,2,1,3:T(2,128)S(1)}, f32[2,4,4,2,4,8]{5,0,4,2,1,3:T(2,128)S(1)}, u32[]{:S(2)}, u32[]{:S(2)}) collective-permute-start(f32[2,4,4,2,4,8]{5,0,4,2,1,3:T(2,128)S(1)} %broadcast_select_fusion.2), channel_id=1, source_target_pairs={{0,2},{1,3},{2,0},{3,1},{4,6},{5,7},{6,4},{7,5},{8,10},{9,11},{10,... | collective-permute-start | bytes 24584 | tf_op jit(solution)/shard_map/ppermute | solution.py:303
  58.5 1.3 %collective-permute-start.12 = (f32[1,4,4,2,4,8]{5,0,4,2,1,3:T(1,128)S(1)}, f32[1,4,4,2,4,8]{5,0,4,2,1,3:T(1,128)S(1)}, u32[]{:S(2)}, u32[]{:S(2)}) collective-permute-start(f32[1,4,4,2,4,8]{5,0,4,2,1,3:T(1,128)S(1)} %broadcast_select_fusion.3), channel_id=1, source_target_pairs={{0,1},{1,0},{2,3},{3,2},{4,5},{5,4},{6,7},{7,6},{8,9},{9,8},{10,11... | collective-permute-start | bytes 12296 | tf_op jit(solution)/shard_map/ppermute | solution.py:303

commit v8 on v7

--- a/solution.py
+++ b/solution.py
@@ -50,7 +50,7 @@
         psi_ref, tlo_ref, thi_ref, zlo_ref, zhi_ref = rest[:5]
         out_ref = rest[5]
         scratch = rest[6:]
-    pad_ref, src_ref, zlo_s, zhi_s, u8, ut8, uz8 = scratch
+    pad_ref, src_ref, zlo_s, zhi_s, u8, ut8, uz8, acc_ref = scratch
     S, C, RI, T, ROWS, L = src_ref.shape
     Z = ROWS // 2
     K = noise_ref.shape[3]
@@ -119,7 +119,14 @@
         return jnp.where(x_first, pltpu.roll(v, L - NX + 1, axis=1), pltpu.roll(v, 1, axis=1))
 
     def body(t, carry):
-        acc = [[[None, None] for _ in range(3)] for _ in range(4)]
+        started = [[[False, False] for _ in range(3)] for _ in range(4)]
+
+        def accumulate(row, a, ri, value):
+            if started[row][a][ri]:
+                acc_ref[row, a, ri] = acc_ref[row, a, ri] + value
+            else:
+                acc_ref[row, a, ri] = value
+                started[row][a][ri] = True
 
         def shifted(s, c, ri, mu, stride):
             if mu == 3:
@@ -183,16 +190,14 @@
                             sum_re = tre if sum_re is None else sum_re + tre
                             sum_im = tim if sum_im is None else sum_im + tim
                         for row, (vre, vim) in ((s, (sum_re, sum_im)), (p, times_phase(sum_re, sum_im, cpr, cpi))):
-                            if acc[row][a][0] is None:
-                                acc[row][a] = [vre, vim]
-                            else:
-                                acc[row][a] = [acc[row][a][0] + vre, acc[row][a][1] + vim]
+                            accumulate(row, a, 0, vre)
+                            accumulate(row, a, 1, vim)
         for s in range(4):
             for c in range(3):
                 for ri in range(2):
                     psi = pad_ref[s, c, ri, t + 1]
                     src = src_ref[s, c, ri, t]
-                    residual = src - (psi - kappa_hop * acc[s][c][ri])
+                    residual = src - (psi - kappa_hop * acc_ref[s, c, ri])
                     value = psi + residual
                     if first:
                         out_ref[s, c, ri, t] = value
@@ -274,6 +279,7 @@
         pltpu.VMEM((4, 3, 3, RI, T, ROWS, L), jnp.float32),
         pltpu.VMEM((3, 3, RI, T + 1, ROWS, L), jnp.float32),
         pltpu.VMEM((3, 3, RI, T, ROWS, L), jnp.float32),
+        pltpu.VMEM((S, C, RI, ROWS, L), jnp.float32),
     ]
     return pl.pallas_call(
         functools.partial(hop_kernel, first),
@@ -295,13 +301,14 @@
     width = partial_value.shape[-1] // n
     x = jnp.moveaxis(partial_value.reshape(lead + (n, width)), -2, 0)
     me = lax.axis_index("sa")
-    d = n // 2
-    while d >= 1:
-        upper_mine = (me // d) % 2 == 1
-        keep = jnp.where(upper_mine, x[d:], x[:d])
-        send = jnp.where(upper_mine, x[:d], x[d:])
+    d = 1
+    while d < n:
+        x = x.reshape((x.shape[0] // 2, 2) + x.shape[1:])
+        odd = (me // d) % 2 == 1
+        keep = jnp.where(odd, x[:, 1], x[:, 0])
+        send = jnp.where(odd, x[:, 0], x[:, 1])
         x = keep + lax.ppermute(send, "sa", [(j, j ^ d) for j in range(n)])
-        d //= 2
+        d *= 2
     return x[0]
 
 

time: 60.9 us -> 60.4 us (level)
  Pallas kernels: 20.2 us -> 21.1 us
  waiting for transfers between devices: 11.4 us -> 10.6 us
  local copies, waits for them, and re-layouts: 8.53 us -> 7.81 us
    ppermute x10, waiting for transfers between devices: 5.87 us -> 4.46 us  [passed_along(): return lax.ppermute(value, axis, pairs)]
    ppermute x1, waiting for transfers between devices: 0.01 us -> 1.08 us  [from_partner(): lax.ppermute(x, axis, [(i, i ^ 1 << stride) for i in range(lax.axis_size(...]
    pallas_call x2, Pallas kernels: 20.2 us -> 21.1 us  [hopping_step(): pl.pallas_call(functools.partial(hop_kernel, first), grid=(H,), in_specs=...]
    squeeze x0 -> x1, other arithmetic: none -> 0.66 us  [reduce_scatter_sa(): return x[0]]
    squeeze x1 -> x0, local copies, waits for them, and re-layouts: 0.64 us -> none  [reduce_scatter_sa(): return x[0]]
    unnamed x31 -> x27, local copies, waits for them, and re-layouts: 2.28 us -> 2.31 us
  transfers between devices with their start and end apart: 13 -> 13, of which waited for: 4 -> 6; matrix products, arithmetic and copies ran while one was open for 14% -> 14% of each run, Pallas kernels for 17% -> 17%
where the time goes in v8:
time: 60.4 us; the launch traced here: 60.1 us
  Pallas kernels  21.1 us (35%)
  starting transfers between devices  14.9 us (25%)
  waiting for transfers between devices  10.6 us (18%)
  local copies, waits for them, and re-layouts  7.81 us (13%)
  matrix products  3.73 us (6%)
  other arithmetic  1.65 us (3%)
    pallas_call x2, Pallas kernels, hopping_step(): pl.pallas_call(functools.partial(hop_kernel, first), grid=(H,), in_specs=...  21.1 us
    ppermute x10, starting transfers between devices, passed_along(): return lax.ppermute(value, axis, pairs)  12.6 us
    ppermute x2, waiting for transfers between devices, reduce_scatter_sa(): x = keep + lax.ppermute(send, 'sa', [(j, j ^ d) for j in range(n)])  5.11 us
    ppermute x10, waiting for transfers between devices, passed_along(): return lax.ppermute(value, axis, pairs)  4.46 us
    dot_general x2, matrix products, intersection_part(): jnp.einsum('tvcazs,hqcbtgzs->hgqabtv', vector_piece, rounded, preferred_e...  3.73 us
    unnamed x27, local copies, waits for them, and re-layouts  2.31 us
    ppermute x1, starting transfers between devices, from_partner(): lax.ppermute(x, axis, [(i, i ^ 1 << stride) for i in range(lax.axis_size(...  1.73 us
  transfers between devices with their start and end apart: 13, of which 6 were waited for; matrix products, arithmetic and copies ran while one was open for 14% of the time, Pallas kernels for 17%

profile of v8, /device:TPU:0, one launch (start us, length us, event | category | flops | bytes accessed | tf_op | source)
XLA Modules:
  0.0 60.1 jit_solution(3536935201179904080)
XLA Ops:
  0.0 3.1 %collective-permute-start = (f32[4,3,2,1,4,256]{5,4,3,2,1,0:T(4,128)}, f32[4,3,2,1,4,256]{5,4,3,2,1,0:T(4,128)S(1)}, u32[]{:S(2)}, u32[]{:S(2)}) collective-permute-start(f32[4,3,2,1,4,256]{5,4,3,2,1,0:T(4,128)} %refs_3_.3), channel_id=1, source_target_pairs={{0,4},{4,8},{8,12},{12,0},{1,5},{5,9},{9,13},{13,1},{2,6},{6,10},{... | collective-permute-start | bytes 294920 | tf_op jit(solution)/shard_map/ppermute | solution.py:25
  3.1 2.1 %collective-permute-start.1 = (f32[4,3,2,1,4,256]{5,4,3,2,1,0:T(4,128)}, f32[4,3,2,1,4,256]{5,4,3,2,1,0:T(4,128)S(1)}, u32[]{:S(2)}, u32[]{:S(2)}) collective-permute-start(f32[4,3,2,1,4,256]{5,4,3,2,1,0:T(4,128)} %refs_3_.3), channel_id=1, source_target_pairs={{0,12},{4,0},{8,4},{12,8},{1,13},{5,1},{9,5},{13,9},{2,14},{6,2},{... | collective-permute-start | bytes 294920 | tf_op jit(solution)/shard_map/ppermute | solution.py:25
  5.1 1.0 %fusion.11 = (f32[4,3,2,1,1,256]{5,4,3,2,1,0:T(1,128)S(1)}, f32[4,3,2,1,1,256]{5,4,3,2,1,0:T(1,128)S(1)}) fusion(f32[4,3,2,1,4,256]{5,4,3,2,1,0:T(4,128)} %refs_3_.3), kind=kLoop, calls=%fused_computation.39 | loop fusion | bytes 98304 | tf_op jit(solution)/shard_map/slice | solution.py:349
  6.1 0.1 collective-permute-start.2
  6.2 1.7 %collective-permute-start.3 = (f32[4,3,2,1,1,256]{5,4,3,2,1,0:T(1,128)S(1)}, f32[4,3,2,1,1,256]{5,4,3,2,1,0:T(1,128)S(1)}, u32[]{:S(2)}, u32[]{:S(2)}) collective-permute-start(f32[4,3,2,1,1,256]{5,4,3,2,1,0:T(1,128)S(1)} %get-tuple-element.21), channel_id=1, source_target_pairs={{0,3},{1,0},{2,1},{3,2},{4,7},{5,4},{6,5},{7,6},{8,11},{9,8},{10,9... | collective-permute-start | bytes 73736 | tf_op jit(solution)/shard_map/ppermute | solution.py:25
  7.9 0.9 %slice_bitcast_fusion.1 = f32[3,3,2,1,4,256]{5,4,3,2,1,0:T(4,128)S(1)} fusion(f32[4,3,3,2,4,4,256]{6,5,4,3,2,1,0:T(4,128)} %refs_8_.3), kind=kLoop, calls=%fused_computation.13 | loop fusion | bytes 147456 | tf_op jit(solution)/shard_map/squeeze | solution.py:353
  8.8 1.0 %slice_bitcast_fusion = f32[3,3,2,4,1,256]{5,4,3,2,1,0:T(1,128)S(1)} fusion(f32[4,3,3,2,4,4,256]{6,5,4,3,2,1,0:T(4,128)} %refs_8_.3), kind=kLoop, calls=%fused_computation.12 | loop fusion | bytes 147456 | tf_op jit(solution)/shard_map/squeeze | solution.py:354
  9.9 0.7 %dynamic_slice.3 = s32[4]{0:T(128)S(1)} dynamic-slice(s32[8]{0:T(128)} %param.6, s32[]{:T(128)S(6)} %select_n.122), dynamic_slice_sizes={4} | dynamic-slice | bytes 36 | tf_op jit(solution)/shard_map/dynamic_slice | solution.py:338
  10.7 0.1 compare_convert_fusion
  10.7 0.1 fusion.8
  10.8 0.1 collective-permute-start.5
  10.9 0.6 pad_maximum_fusion.1.refs_2_
  11.5 0.6 reshape.211.refs_1_
  12.0 0.6 %reshape.210.refs_0_ = f32[16]{0:T(128)} reshape(f32[4,4]{1,0:T(4,128)S(1)} %fusion.8) | data formatting | bytes 128 | tf_op jit(solution)/shard_map/convert_element_type | solution.py:340
  12.6 2.3 %collective-permute-done.4.refs_9_ = f32[3,3,2,1,4,256]{5,4,3,2,1,0:T(4,128)S(1)} collective-permute-done((f32[3,3,2,1,4,256]{5,4,3,2,1,0:T(4,128)S(1)}, f32[3,3,2,1,4,256]{5,4,3,2,1,0:T(4,128)S(1)}, u32[]{:S(2)}, u32[]{:S(2)}) %collective-permute-start.4) | collective-permute-done | bytes 73760 | tf_op jit(solution)/shard_map/ppermute | solution.py:25
  15.0 0.6 copy-done.4
  15.6 0.1 copy-done.2
  15.7 0.6 %copy-done.3 = f32[4,3,2,1,4,256]{5,4,3,2,1,0:T(4,128)} copy-done((f32[4,3,2,1,4,256]{5,4,3,2,1,0:T(4,128)}, f32[4,3,2,1,4,256]{5,4,3,2,1,0:T(4,128)S(1)}, u32[]{:S(2)}) %copy-start.3) | copy-done | bytes 98328
  16.3 10.6 %shard_map.46 = (f32[2,4,3,2,4,8,256]{6,5,4,3,2,1,0:T(8,128)}, bf16[2,2,3,2,1,8,256]{6,5,4,3,2,1,0:T(8,128)(2,1)}, bf16[2,2,3,2,1,8,256]{6,5,4,3,2,1,0:T(8,128)(...) custom-call(f32[16]{0:T(128)} %reshape.210.refs_0_, f32[24]{0:T(128)} %reshape.211.refs_1_, ...), custom_call_target="tpu_custom_call" | custom-call | tf_op jit(solution)/shard_map/pallas_call | solution.py:284
  27.0 0.1 collective-permute-start.8
  27.0 1.7 %collective-permute-start.9 = (f32[2,2,3,2,4,2,256]{6,5,4,3,2,1,0:T(2,128)}, f32[2,2,3,2,4,2,256]{6,5,4,3,2,1,0:T(2,128)S(1)}, u32[]{:S(2)}, u32[]{:S(2)}) collective-permute-start(f32[2,2,3,2,4,2,256]{6,5,4,3,2,1,0:T(2,128)} %get-tuple-element.14), channel_id=1, source_target_pairs={{0,3},{1,0},{2,1},{3,2},{4,7},{5,4},{6,5},{7,6},{8,11},{9,8},{10,9... | collective-permute-start | bytes 589832 | tf_op jit(solution)/shard_map/ppermute | solution.py:25
  28.8 1.1 %collective-permute-start.6 = (bf16[2,2,3,2,1,8,256]{6,5,4,3,2,1,0:T(8,128)(2,1)}, bf16[2,2,3,2,1,8,256]{6,5,4,3,2,1,0:T(8,128)(2,1)S(1)}, u32[]{:S(2)}, u32[]{:S(2)}) collective-permute-start(bf16[2,2,3,2,1,8,256]{6,5,4,3,2,1,0:T(8,128)(2,1)} %get-tuple-element.11), channel_id=1, source_target_pairs={{0,4},{4,8},{8,12},{12,0},{1,5},{5,9},{9,13},{13,1},{2,6},{6,10},{... | collective-permute-start | bytes 294920 | tf_op jit(solution)/shard_map/ppermute | solution.py:25
  29.9 2.7 %collective-permute-start.7 = (bf16[2,2,3,2,1,8,256]{6,5,4,3,2,1,0:T(8,128)(2,1)}, bf16[2,2,3,2,1,8,256]{6,5,4,3,2,1,0:T(8,128)(2,1)S(1)}, u32[]{:S(2)}, u32[]{:S(2)}) collective-permute-start(bf16[2,2,3,2,1,8,256]{6,5,4,3,2,1,0:T(8,128)(2,1)} %get-tuple-element.12), channel_id=1, source_target_pairs={{0,12},{4,0},{8,4},{12,8},{1,13},{5,1},{9,5},{13,9},{2,14},{6,2},{... | collective-permute-start | bytes 294920 | tf_op jit(solution)/shard_map/ppermute | solution.py:25
  32.6 0.2 copy.16
  32.8 1.7 %collective-permute-start.10 = (bf16[4,16,3,2,4,256]{5,1,4,2,3,0:T(8,128)(2,1)S(1)}, bf16[4,16,3,2,4,256]{5,1,4,2,3,0:T(8,128)(2,1)S(1)}, u32[]{:S(2)}, u32[]{:S(2)}) collective-permute-start(bf16[4,16,3,2,4,256]{5,1,4,2,3,0:T(8,128)(2,1)S(1)} %copy.16), channel_id=1, source_target_pairs={{0,16},{16,0},{1,17},{17,1},{2,18},{18,2},{3,19},{19,3},{4,20},{20... | collective-permute-start | bytes 2359304 | tf_op jit(solution)/shard_map/ppermute | solution.py:29
  34.5 1.8 %collective-permute-done.6.refs_12_ = bf16[2,2,3,2,1,8,256]{6,5,4,3,2,1,0:T(8,128)(2,1)S(1)} collective-permute-done((bf16[2,2,3,2,1,8,256]{6,5,4,3,2,1,0:T(8,128)(2,1)}, bf16[2,2,3,2,1,8,256]{6,5,4,3,2,1,0:T(8,128)(2,1)S(1)}, u32[]{:S(2)}, u32[]{:S(2)}) %collective-permute-start.6) | collective-permute-done | bytes 98336 | tf_op jit(solution)/shard_map/ppermute | solution.py:25
  36.3 0.3 collective-permute-done.7.refs_13_
  36.6 0.4 copy-done.10
  37.0 0.3 copy-done.11
  37.2 0.1 copy-done.6
  37.3 0.1 copy-done.7
  37.4 10.4 %shard_map.47 = bf16[2,4,3,2,4,2,4,256]{7,6,5,4,3,2,1,0:T(4,128)(2,1)} custom-call(f32[16]{0:T(128)} %reshape.210.refs_0_, f32[24]{0:T(128)} %reshape.211.refs_1_, f32[2]{0:T(128)} %pad_maximum_fusion.1.refs_2_, f32[4,3,2,1,4,256]{5,4,3,2,1,0:T(4,128)} %refs_3_.3, f32[4,3,2,1,4,256]{5,4,3,2,1,0:T(4,128)} %copy-done.2, f32[4,3,2,1,4,256]{5,4,3,2,1,0:T(4,128)} %copy-done.3, ...), custom_call_target="tpu_custom_call" | custom-call | tf_op jit(solution)/shard_map/pallas_call | solution.py:284
  47.9 2.5 %convolution_bitcast_fusion.1 = f32[2,2,4,2,2,4,16]{6,2,3,1,4,0,5:T(4,128)S(1)} fusion(bf16[4,16,3,2,4,256,1,1,1]{5,4,3,2,1,0,8,7,6:T(4,128)(2,1)S(1)} %bitcast.71, bf16[2,4,3,2,4,2,4,256,1]{7,6,5,4,3,2,1,0,8:T(4,128)(2,1)} %bitcast.72), kind=kOutput, calls=%fused_computation.1 | convolution fusion | flops 25165824 | bytes 1589248 | tf_op jit(solution)/shard_map/tvcazs,hqcbtgzs->hgqabtv/dot_general | solution.py:316
  50.3 0.1 copy.13
  50.4 0.1 add.99
  50.6 0.1 sub.39
  50.7 1.1 %collective-permute-done.10 = bf16[4,16,3,2,4,256]{5,1,4,2,3,0:T(8,128)(2,1)S(1)} collective-permute-done((bf16[4,16,3,2,4,256]{5,1,4,2,3,0:T(8,128)(2,1)S(1)}, bf16[4,16,3,2,4,256]{5,1,4,2,3,0:T(8,128)(2,1)S(1)}, u32[]{:S(2)}, u32[]{:S(2)}) %collective-permute-start.10) | collective-permute-done | bytes 786464 | tf_op jit(solution)/shard_map/ppermute | solution.py:29
  51.8 1.3 %convolution_bitcast_fusion = f32[2,2,4,2,2,4,16]{6,2,3,1,4,0,5:T(4,128)S(1)} fusion(bf16[4,16,3,2,4,256]{5,1,4,2,3,0:T(8,128)(2,1)S(1)} %collective-permute-done.10, bf16[2,4,3,2,4,2,4,256,1]{7,6,5,4,3,2,1,0,8:T(4,128)(2,1)S(1)} %bitcast.73), kind=kOutput, calls=%fused_computation | convolution fusion | flops 25165824 | bytes 1589248 | tf_op jit(solution)/shard_map/tvcazs,hqcbtgzs->hgqabtv/dot_general | solution.py:316
  53.0 0.1 copy.18
  53.2 0.1 add.101
  53.3 0.1 sub.41
  53.4 0.1 copy_dynamic-update-slice_fusion
  53.5 0.1 pad_maximum_fusion
  53.6 0.1 collective-permute-start.11
  53.7 1.3 %collective-permute-done.11 = f32[2,4,4,2,4,8]{5,4,3,2,1,0:T(4,128)S(1)} collective-permute-done((f32[2,4,4,2,4,8]{5,4,3,2,1,0:T(4,128)S(1)}, f32[2,4,4,2,4,8]{5,4,3,2,1,0:T(4,128)S(1)}, u32[]{:S(2)}, u32[]{:S(2)}) %collective-permute-start.11) | collective-permute-done | bytes 8224 | tf_op jit(solution)/shard_map/ppermute | solution.py:310
  55.1 0.5 collective-permute-start.12
  55.7 3.8 %collective-permute-done.12 = f32[1,4,4,2,4,8]{5,4,3,2,1,0:T(4,128)S(1)} collective-permute-done((f32[1,4,4,2,4,8]{5,4,3,2,1,0:T(4,128)S(1)}, f32[1,4,4,2,4,8]{5,4,3,2,1,0:T(4,128)S(1)}, u32[]{:S(2)}, u32[]{:S(2)}) %collective-permute-start.12) | collective-permute-done | bytes 4128 | tf_op jit(solution)/shard_map/ppermute | solution.py:310
  59.5 0.7 %fusion.7 = f32[4,4,2,4,8]{4,3,2,1,0:T(4,128)} fusion(f32[1,4,4,2,4,8]{5,4,3,2,1,0:T(4,128)S(1)} %collective-permute-done.12, f32[1,2,4,4,2,4,8]{6,5,4,3,2,1,0:T(4,128)S(1)} %fusion.6, pred[]{:T(512)S(6)} %eq.53), kind=kLoop, calls=%fused_computation.15 | loop fusion | flops 2048 | bytes 16385 | tf_op jit(solution)/shard_map/squeeze | solution.py:312
  (35 shorter events, 0.3 us)
Async XLA Ops:
  0.0 32.6 %copy-start = (bf16[4,16,3,2,4,256]{5,4,3,2,1,0:T(4,128)(2,1)S(1)}, bf16[4,16,3,2,4,256]{5,4,3,2,1,0:T(4,128)(2,1)}, u32[]{:S(2)}) copy-start(bf16[4,16,3,2,4,256]{5,4,3,2,1,0:T(4,128)(2,1)} %param.7) | copy-start | bytes 2359300
  0.0 15.0 %collective-permute-start = (f32[4,3,2,1,4,256]{5,4,3,2,1,0:T(4,128)}, f32[4,3,2,1,4,256]{5,4,3,2,1,0:T(4,128)S(1)}, u32[]{:S(2)}, u32[]{:S(2)}) collective-permute-start(f32[4,3,2,1,4,256]{5,4,3,2,1,0:T(4,128)} %refs_3_.3), channel_id=1, source_target_pairs={{0,4},{4,8},{8,12},{12,0},{1,5},{5,9},{9,13},{13,1},{2,6},{6,10},{... | collective-permute-start | bytes 294920 | tf_op jit(solution)/shard_map/ppermute | solution.py:25
  3.1 12.0 %collective-permute-start.1 = (f32[4,3,2,1,4,256]{5,4,3,2,1,0:T(4,128)}, f32[4,3,2,1,4,256]{5,4,3,2,1,0:T(4,128)S(1)}, u32[]{:S(2)}, u32[]{:S(2)}) collective-permute-start(f32[4,3,2,1,4,256]{5,4,3,2,1,0:T(4,128)} %refs_3_.3), channel_id=1, source_target_pairs={{0,12},{4,0},{8,4},{12,8},{1,13},{5,1},{9,5},{13,9},{2,14},{6,2},{... | collective-permute-start | bytes 294920 | tf_op jit(solution)/shard_map/ppermute | solution.py:25
  6.1 4.7 %collective-permute-start.2 = (f32[4,3,2,1,1,256]{5,4,3,2,1,0:T(1,128)S(1)}, f32[4,3,2,1,1,256]{5,4,3,2,1,0:T(1,128)S(1)}, u32[]{:S(2)}, u32[]{:S(2)}) collective-permute-start(f32[4,3,2,1,1,256]{5,4,3,2,1,0:T(1,128)S(1)} %get-tuple-element.22), channel_id=1, source_target_pairs={{0,1},{1,2},{2,3},{3,0},{4,5},{5,6},{6,7},{7,4},{8,9},{9,10},{10,1... | collective-permute-start | bytes 73736 | tf_op jit(solution)/shard_map/ppermute | solution.py:25
  6.2 6.4 %collective-permute-start.3 = (f32[4,3,2,1,1,256]{5,4,3,2,1,0:T(1,128)S(1)}, f32[4,3,2,1,1,256]{5,4,3,2,1,0:T(1,128)S(1)}, u32[]{:S(2)}, u32[]{:S(2)}) collective-permute-start(f32[4,3,2,1,1,256]{5,4,3,2,1,0:T(1,128)S(1)} %get-tuple-element.21), channel_id=1, source_target_pairs={{0,3},{1,0},{2,1},{3,2},{4,7},{5,4},{6,5},{7,6},{8,11},{9,8},{10,9... | collective-permute-start | bytes 73736 | tf_op jit(solution)/shard_map/ppermute | solution.py:25
  8.8 6.2 %collective-permute-start.4 = (f32[3,3,2,1,4,256]{5,4,3,2,1,0:T(4,128)S(1)}, f32[3,3,2,1,4,256]{5,4,3,2,1,0:T(4,128)S(1)}, u32[]{:S(2)}, u32[]{:S(2)}) collective-permute-start(f32[3,3,2,1,4,256]{5,4,3,2,1,0:T(4,128)S(1)} %slice_bitcast_fusion.1), channel_id=1, source_target_pairs={{0,4},{4,8},{8,12},{12,0},{1,5},{5,9},{9,13},{13,1},{2,6},{6,10},{... | collective-permute-start | bytes 221192 | tf_op jit(solution)/shard_map/ppermute | solution.py:25
  10.8 4.2 %copy-start.8 = (f32[4,3,2,1,1,256]{5,4,3,2,1,0:T(1,128)}, f32[4,3,2,1,1,256]{5,4,3,2,1,0:T(1,128)S(1)}, u32[]{:S(2)}) copy-start(f32[4,3,2,1,1,256]{5,4,3,2,1,0:T(1,128)S(1)} %collective-permute-done.2.refs_6_) | copy-start | bytes 73732
  10.8 4.2 %collective-permute-start.5 = (f32[3,3,2,4,1,256]{5,4,3,2,1,0:T(1,128)S(1)}, f32[3,3,2,4,1,256]{5,4,3,2,1,0:T(1,128)S(1)}, u32[]{:S(2)}, u32[]{:S(2)}) collective-permute-start(f32[3,3,2,4,1,256]{5,4,3,2,1,0:T(1,128)S(1)} %slice_bitcast_fusion), channel_id=1, source_target_pairs={{0,1},{1,2},{2,3},{3,0},{4,5},{5,6},{6,7},{7,4},{8,9},{9,10},{10,1... | collective-permute-start | bytes 221192 | tf_op jit(solution)/shard_map/ppermute | solution.py:25
  12.6 2.4 %copy-start.9 = (f32[4,3,2,1,1,256]{5,4,3,2,1,0:T(1,128)}, f32[4,3,2,1,1,256]{5,4,3,2,1,0:T(1,128)S(1)}, u32[]{:S(2)}) copy-start(f32[4,3,2,1,1,256]{5,4,3,2,1,0:T(1,128)S(1)} %collective-permute-done.3.refs_7_) | copy-start | bytes 73732
  15.0 0.6 %copy-start.4 = (f32[3,3,2,1,4,256]{5,4,3,2,1,0:T(4,128)}, f32[3,3,2,1,4,256]{5,4,3,2,1,0:T(4,128)S(1)}, u32[]{:S(2)}) copy-start(f32[3,3,2,1,4,256]{5,4,3,2,1,0:T(4,128)S(1)} %collective-permute-done.4.refs_9_) | copy-start | bytes 221188
  15.0 0.6 %copy-start.5 = (f32[3,3,2,4,1,256]{5,4,3,2,1,0:T(1,128)}, f32[3,3,2,4,1,256]{5,4,3,2,1,0:T(1,128)S(1)}, u32[]{:S(2)}) copy-start(f32[3,3,2,4,1,256]{5,4,3,2,1,0:T(1,128)S(1)} %collective-permute-done.5.refs_10_) | copy-start | bytes 221188
  15.0 0.7 %copy-start.2 = (f32[4,3,2,1,4,256]{5,4,3,2,1,0:T(4,128)}, f32[4,3,2,1,4,256]{5,4,3,2,1,0:T(4,128)S(1)}, u32[]{:S(2)}) copy-start(f32[4,3,2,1,4,256]{5,4,3,2,1,0:T(4,128)S(1)} %collective-permute-done.refs_4_) | copy-start | bytes 294916
  15.7 0.6 %copy-start.3 = (f32[4,3,2,1,4,256]{5,4,3,2,1,0:T(4,128)}, f32[4,3,2,1,4,256]{5,4,3,2,1,0:T(4,128)S(1)}, u32[]{:S(2)}) copy-start(f32[4,3,2,1,4,256]{5,4,3,2,1,0:T(4,128)S(1)} %collective-permute-done.1.refs_5_) | copy-start | bytes 294916
  27.0 9.6 %collective-permute-start.8 = (f32[2,2,3,2,4,2,256]{6,5,4,3,2,1,0:T(2,128)}, f32[2,2,3,2,4,2,256]{6,5,4,3,2,1,0:T(2,128)S(1)}, u32[]{:S(2)}, u32[]{:S(2)}) collective-permute-start(f32[2,2,3,2,4,2,256]{6,5,4,3,2,1,0:T(2,128)} %get-tuple-element.13), channel_id=1, source_target_pairs={{0,1},{1,2},{2,3},{3,0},{4,5},{5,6},{6,7},{7,4},{8,9},{9,10},{10,1... | collective-permute-start | bytes 589832 | tf_op jit(solution)/shard_map/ppermute | solution.py:25
  27.0 9.6 %collective-permute-start.9 = (f32[2,2,3,2,4,2,256]{6,5,4,3,2,1,0:T(2,128)}, f32[2,2,3,2,4,2,256]{6,5,4,3,2,1,0:T(2,128)S(1)}, u32[]{:S(2)}, u32[]{:S(2)}) collective-permute-start(f32[2,2,3,2,4,2,256]{6,5,4,3,2,1,0:T(2,128)} %get-tuple-element.14), channel_id=1, source_target_pairs={{0,3},{1,0},{2,1},{3,2},{4,7},{5,4},{6,5},{7,6},{8,11},{9,8},{10,9... | collective-permute-start | bytes 589832 | tf_op jit(solution)/shard_map/ppermute | solution.py:25
  28.8 7.6 %collective-permute-start.6 = (bf16[2,2,3,2,1,8,256]{6,5,4,3,2,1,0:T(8,128)(2,1)}, bf16[2,2,3,2,1,8,256]{6,5,4,3,2,1,0:T(8,128)(2,1)S(1)}, u32[]{:S(2)}, u32[]{:S(2)}) collective-permute-start(bf16[2,2,3,2,1,8,256]{6,5,4,3,2,1,0:T(8,128)(2,1)} %get-tuple-element.11), channel_id=1, source_target_pairs={{0,4},{4,8},{8,12},{12,0},{1,5},{5,9},{9,13},{13,1},{2,6},{6,10},{... | collective-permute-start | bytes 294920 | tf_op jit(solution)/shard_map/ppermute | solution.py:25
  29.9 6.7 %collective-permute-start.7 = (bf16[2,2,3,2,1,8,256]{6,5,4,3,2,1,0:T(8,128)(2,1)}, bf16[2,2,3,2,1,8,256]{6,5,4,3,2,1,0:T(8,128)(2,1)S(1)}, u32[]{:S(2)}, u32[]{:S(2)}) collective-permute-start(bf16[2,2,3,2,1,8,256]{6,5,4,3,2,1,0:T(8,128)(2,1)} %get-tuple-element.12), channel_id=1, source_target_pairs={{0,12},{4,0},{8,4},{12,8},{1,13},{5,1},{9,5},{13,9},{2,14},{6,2},{... | collective-permute-start | bytes 294920 | tf_op jit(solution)/shard_map/ppermute | solution.py:25
  32.8 19.0 %collective-permute-start.10 = (bf16[4,16,3,2,4,256]{5,1,4,2,3,0:T(8,128)(2,1)S(1)}, bf16[4,16,3,2,4,256]{5,1,4,2,3,0:T(8,128)(2,1)S(1)}, u32[]{:S(2)}, u32[]{:S(2)}) collective-permute-start(bf16[4,16,3,2,4,256]{5,1,4,2,3,0:T(8,128)(2,1)S(1)} %copy.16), channel_id=1, source_target_pairs={{0,16},{16,0},{1,17},{17,1},{2,18},{18,2},{3,19},{19,3},{4,20},{20... | collective-permute-start | bytes 2359304 | tf_op jit(solution)/shard_map/ppermute | solution.py:29
  36.3 0.7 %copy-start.10 = (bf16[2,2,3,2,1,8,256]{6,5,4,3,2,1,0:T(8,128)(2,1)}, bf16[2,2,3,2,1,8,256]{6,5,4,3,2,1,0:T(8,128)(2,1)S(1)}, u32[]{:S(2)}) copy-start(bf16[2,2,3,2,1,8,256]{6,5,4,3,2,1,0:T(8,128)(2,1)S(1)} %collective-permute-done.6.refs_12_) | copy-start | bytes 294916
  36.6 0.6 %copy-start.11 = (bf16[2,2,3,2,1,8,256]{6,5,4,3,2,1,0:T(8,128)(2,1)}, bf16[2,2,3,2,1,8,256]{6,5,4,3,2,1,0:T(8,128)(2,1)S(1)}, u32[]{:S(2)}) copy-start(bf16[2,2,3,2,1,8,256]{6,5,4,3,2,1,0:T(8,128)(2,1)S(1)} %collective-permute-done.7.refs_13_) | copy-start | bytes 294916
  36.6 0.7 %copy-start.6 = (f32[2,2,3,2,4,2,256]{6,5,4,3,2,1,0:T(2,128)}, f32[2,2,3,2,4,2,256]{6,5,4,3,2,1,0:T(2,128)S(1)}, u32[]{:S(2)}) copy-start(f32[2,2,3,2,4,2,256]{6,5,4,3,2,1,0:T(2,128)S(1)} %collective-permute-done.8.refs_14_) | copy-start | bytes 589828
  36.6 0.8 %copy-start.7 = (f32[2,2,3,2,4,2,256]{6,5,4,3,2,1,0:T(2,128)}, f32[2,2,3,2,4,2,256]{6,5,4,3,2,1,0:T(2,128)S(1)}, u32[]{:S(2)}) copy-start(f32[2,2,3,2,4,2,256]{6,5,4,3,2,1,0:T(2,128)S(1)} %collective-permute-done.9.refs_15_) | copy-start | bytes 589828
  47.8 3.9 %copy-start.1 = (bf16[2,4,3,2,4,2,4,256]{7,6,5,4,3,2,1,0:T(4,128)(2,1)S(1)}, bf16[2,4,3,2,4,2,4,256]{7,6,5,4,3,2,1,0:T(4,128)(2,1)}, u32[]{:S(2)}) copy-start(bf16[2,4,3,2,4,2,4,256]{7,6,5,4,3,2,1,0:T(4,128)(2,1)} %shard_map.47) | copy-start | bytes 2359300
  53.6 1.4 %collective-permute-start.11 = (f32[2,4,4,2,4,8]{5,4,3,2,1,0:T(4,128)S(1)}, f32[2,4,4,2,4,8]{5,4,3,2,1,0:T(4,128)S(1)}, u32[]{:S(2)}, u32[]{:S(2)}) collective-permute-start(f32[2,4,4,2,4,8]{5,4,3,2,1,0:T(4,128)S(1)} %select_bitcast_fusion), channel_id=1, source_target_pairs={{0,1},{1,0},{2,3},{3,2},{4,5},{5,4},{6,7},{7,6},{8,9},{9,8},{10,11... | collective-permute-start | bytes 24584 | tf_op jit(solution)/shard_map/ppermute | solution.py:310
  55.1 4.3 %collective-permute-start.12 = (f32[1,4,4,2,4,8]{5,4,3,2,1,0:T(4,128)S(1)}, f32[1,4,4,2,4,8]{5,4,3,2,1,0:T(4,128)S(1)}, u32[]{:S(2)}, u32[]{:S(2)}) collective-permute-start(f32[1,4,4,2,4,8]{5,4,3,2,1,0:T(4,128)S(1)} %select_bitcast_fusion.1), channel_id=1, source_target_pairs={{0,2},{1,3},{2,0},{3,1},{4,6},{5,7},{6,4},{7,5},{8,10},{9,11},{10,... | collective-permute-start | bytes 12296 | tf_op jit(solution)/shard_map/ppermute | solution.py:310

commit v9 on v7

--- a/solution.py
+++ b/solution.py
@@ -40,9 +40,8 @@
 
 
 def hop_kernel(first, *refs):
-    (smask_ref, tmask_ref, sign_ref, noise_ref, ntlo_ref, nthi_ref, nzlo_ref, nzhi_ref,
-     u_ref, utedge_ref, uzedge_ref) = refs[:11]
-    rest = refs[11:]
+    (scal_ref, noise_ref, ntlo_ref, nthi_ref, nzlo_ref, nzhi_ref, u_ref, utedge_ref, uzedge_ref) = refs[:9]
+    rest = refs[9:]
     if first:
         out_ref, tfirst_ref, tlast_ref, zfirst_ref, zlast_ref = rest[:5]
         scratch = rest[5:]
@@ -56,6 +55,10 @@
     K = noise_ref.shape[3]
     span = T // K
     h = pl.program_id(0)
+    R = 2 * pl.num_programs(0)
+    smask = lambda i: scal_ref[i]
+    tmask = lambda i: scal_ref[R * S + i]
+    sign = lambda i: scal_ref[R * S + R * (T + 2) + i]
     lower = pl.ds(0, Z)
     upper = pl.ds(Z, Z)
 
@@ -77,17 +80,17 @@
             for ri in range(RI):
                 for g, half in ((0, lower), (1, upper)):
                     r = 2 * h + g
-                    fs = smask_ref[r * S + s]
+                    fs = smask(r * S + s)
                     for t in range(T):
                         src_ref[s, c, ri, t, half] = noise_ref[g, c, ri, t // span] * (
-                            fs * tmask_ref[r * (T + 2) + t + 1])
+                            fs * tmask(r * (T + 2) + t + 1))
                     if first:
                         pad_ref[s, c, ri, 0, half] = ntlo_ref[g, c, ri, 0] * (
-                            fs * tmask_ref[r * (T + 2)] * sign_ref[0])
+                            fs * tmask(r * (T + 2)) * sign(0))
                         pad_ref[s, c, ri, T + 1, half] = nthi_ref[g, c, ri, 0] * (
-                            fs * tmask_ref[r * (T + 2) + T + 1] * sign_ref[1])
+                            fs * tmask(r * (T + 2) + T + 1) * sign(1))
                         for t in range(T):
-                            f = fs * tmask_ref[r * (T + 2) + t + 1]
+                            f = fs * tmask(r * (T + 2) + t + 1)
                             zlo_s[s, c, ri, t, half] = jnp.broadcast_to(nzlo_ref[g, c, ri, t // span] * f, (Z, L))
                             zhi_s[s, c, ri, t, half] = jnp.broadcast_to(nzhi_ref[g, c, ri, t // span] * f, (Z, L))
                     else:
@@ -103,8 +106,8 @@
                 else:
                     pad_ref[s, c, ri, pl.ds(1, T)] = psi_ref[s, c, ri]
                     if s < 2:
-                        pad_ref[s, c, ri, pl.ds(0, 1)] = tlo_ref[s, c, ri].astype(jnp.float32) * sign_ref[0]
-                        pad_ref[s, c, ri, pl.ds(T + 1, 1)] = thi_ref[s, c, ri].astype(jnp.float32) * sign_ref[1]
+                        pad_ref[s, c, ri, pl.ds(0, 1)] = tlo_ref[s, c, ri].astype(jnp.float32) * sign(0)
+                        pad_ref[s, c, ri, pl.ds(T + 1, 1)] = thi_ref[s, c, ri].astype(jnp.float32) * sign(1)
                     else:
                         pad_ref[s, c, ri, pl.ds(0, 1)] = jnp.zeros((1, ROWS, L), jnp.float32)
                         pad_ref[s, c, ri, pl.ds(T + 1, 1)] = jnp.zeros((1, ROWS, L), jnp.float32)
@@ -255,7 +258,7 @@
         pl.BlockSpec((2, C, RI, K, 1, L), index6),
         pl.BlockSpec((2, C, RI, K, 1, L), index6),
     ]
-    in_specs = [smem, smem, smem] + noise_specs + [whole(x) for x in link_parts]
+    in_specs = [smem] + noise_specs + [whole(x) for x in link_parts]
     site_shape = (H, S, C, RI, T, ROWS, L)
     if first:
         t_shape = jax.ShapeDtypeStruct((H, 2, C, RI, 1, ROWS, L), jnp.bfloat16)
@@ -295,13 +298,14 @@
     width = partial_value.shape[-1] // n
     x = jnp.moveaxis(partial_value.reshape(lead + (n, width)), -2, 0)
     me = lax.axis_index("sa")
-    d = n // 2
-    while d >= 1:
-        upper_mine = (me // d) % 2 == 1
-        keep = jnp.where(upper_mine, x[d:], x[:d])
-        send = jnp.where(upper_mine, x[:d], x[d:])
+    d = 1
+    while d < n:
+        x = x.reshape((x.shape[0] // 2, 2) + x.shape[1:])
+        odd = (me // d) % 2 == 1
+        keep = jnp.where(odd, x[:, 1], x[:, 0])
+        send = jnp.where(odd, x[:, 0], x[:, 1])
         x = keep + lax.ppermute(send, "sa", [(j, j ^ d) for j in range(n)])
-        d //= 2
+        d *= 2
     return x[0]
 
 
@@ -333,7 +337,7 @@
     spin_mask = (jnp.arange(4)[None, :] == rhs_index[:, None] % 4).astype(jnp.float32)
     times = t_start - 1 + jnp.arange(slab_length + 2)
     time_mask = (times[None, :] % TDIL == own_offsets[:, None]).astype(jnp.float32)
-    scalars = (spin_mask.reshape(-1), time_mask.reshape(-1), signs)
+    scalars = (jnp.concatenate([spin_mask.reshape(-1), time_mask.reshape(-1), signs]),)
     noise_parts = (
         noise_slabs,
         passed_along(noise_slabs[:, :, :, K - 1:], "ta", 1),

time: 60.9 us -> 60 us (0.985)
  local copies, waits for them, and re-layouts: 8.53 us -> 6.8 us
  waiting for transfers between devices: 11.4 us -> 12.1 us
    ppermute x1, waiting for transfers between devices: 0.01 us -> 1.47 us  [from_partner(): lax.ppermute(x, axis, [(i, i ^ 1 << stride) for i in range(lax.axis_size(...]
    concatenate x0 -> x2, other arithmetic: none -> 0.66 us  [the longest x1 0.59 us: local_body(): jnp.concatenate([spin_mask.reshape(-1), time_mask.reshape(-1), signs])]
    squeeze x0 -> x1, other arithmetic: none -> 0.66 us  [reduce_scatter_sa(): return x[0]]
    squeeze x1 -> x0, local copies, waits for them, and re-layouts: 0.64 us -> none  [reduce_scatter_sa(): return x[0]]
    unnamed x31 -> x27, local copies, waits for them, and re-layouts: 2.28 us -> 2.31 us
  transfers between devices with their start and end apart: 13 -> 13, of which waited for: 4 -> 6; matrix products, arithmetic and copies ran while one was open for 14% -> 13% of each run, Pallas kernels for 17% -> 17%
where the time goes in v9:
time: 60 us; the launch traced here: 59.7 us
  Pallas kernels  20.2 us (34%)
  starting transfers between devices  14.9 us (25%)
  waiting for transfers between devices  12.1 us (20%)
  local copies, waits for them, and re-layouts  6.8 us (11%)
  matrix products  3.73 us (6%)
  other arithmetic  1.66 us (3%)
    pallas_call x2, Pallas kernels, hopping_step(): pl.pallas_call(functools.partial(hop_kernel, first), grid=(H,), in_specs=...  20.2 us
    ppermute x10, starting transfers between devices, passed_along(): return lax.ppermute(value, axis, pairs)  12.6 us
    ppermute x10, waiting for transfers between devices, passed_along(): return lax.ppermute(value, axis, pairs)  5.53 us
    ppermute x2, waiting for transfers between devices, reduce_scatter_sa(): x = keep + lax.ppermute(send, 'sa', [(j, j ^ d) for j in range(n)])  5.11 us
    dot_general x2, matrix products, intersection_part(): jnp.einsum('tvcazs,hqcbtgzs->hgqabtv', vector_piece, rounded, preferred_e...  3.73 us
    unnamed x27, local copies, waits for them, and re-layouts  2.31 us
    ppermute x1, starting transfers between devices, from_partner(): lax.ppermute(x, axis, [(i, i ^ 1 << stride) for i in range(lax.axis_size(...  1.73 us
    ppermute x1, waiting for transfers between devices, from_partner(): lax.ppermute(x, axis, [(i, i ^ 1 << stride) for i in range(lax.axis_size(...  1.47 us
  transfers between devices with their start and end apart: 13, of which 6 were waited for; matrix products, arithmetic and copies ran while one was open for 13% of the time, Pallas kernels for 17%

profile of v9, /device:TPU:0, one launch (start us, length us, event | category | flops | bytes accessed | tf_op | source)
XLA Modules:
  0.0 59.7 jit_solution(15254966967157259108)
XLA Ops:
  0.0 3.1 %collective-permute-start = (f32[4,3,2,1,4,256]{5,4,3,2,1,0:T(4,128)}, f32[4,3,2,1,4,256]{5,4,3,2,1,0:T(4,128)S(1)}, u32[]{:S(2)}, u32[]{:S(2)}) collective-permute-start(f32[4,3,2,1,4,256]{5,4,3,2,1,0:T(4,128)} %refs_1_.3), channel_id=1, source_target_pairs={{0,4},{4,8},{8,12},{12,0},{1,5},{5,9},{9,13},{13,1},{2,6},{6,10},{... | collective-permute-start | bytes 294920 | tf_op jit(solution)/shard_map/ppermute | solution.py:25
  3.1 2.1 %collective-permute-start.1 = (f32[4,3,2,1,4,256]{5,4,3,2,1,0:T(4,128)}, f32[4,3,2,1,4,256]{5,4,3,2,1,0:T(4,128)S(1)}, u32[]{:S(2)}, u32[]{:S(2)}) collective-permute-start(f32[4,3,2,1,4,256]{5,4,3,2,1,0:T(4,128)} %refs_1_.3), channel_id=1, source_target_pairs={{0,12},{4,0},{8,4},{12,8},{1,13},{5,1},{9,5},{13,9},{2,14},{6,2},{... | collective-permute-start | bytes 294920 | tf_op jit(solution)/shard_map/ppermute | solution.py:25
  5.1 1.0 %fusion.11 = (f32[4,3,2,1,1,256]{5,4,3,2,1,0:T(1,128)S(1)}, f32[4,3,2,1,1,256]{5,4,3,2,1,0:T(1,128)S(1)}) fusion(f32[4,3,2,1,4,256]{5,4,3,2,1,0:T(4,128)} %refs_1_.3), kind=kLoop, calls=%fused_computation.39 | loop fusion | bytes 98304 | tf_op jit(solution)/shard_map/slice | solution.py:346
  6.1 0.1 collective-permute-start.2
  6.2 1.7 %collective-permute-start.3 = (f32[4,3,2,1,1,256]{5,4,3,2,1,0:T(1,128)S(1)}, f32[4,3,2,1,1,256]{5,4,3,2,1,0:T(1,128)S(1)}, u32[]{:S(2)}, u32[]{:S(2)}) collective-permute-start(f32[4,3,2,1,1,256]{5,4,3,2,1,0:T(1,128)S(1)} %get-tuple-element.21), channel_id=1, source_target_pairs={{0,3},{1,0},{2,1},{3,2},{4,7},{5,4},{6,5},{7,6},{8,11},{9,8},{10,9... | collective-permute-start | bytes 73736 | tf_op jit(solution)/shard_map/ppermute | solution.py:25
  7.9 0.9 %slice_bitcast_fusion.1 = f32[3,3,2,1,4,256]{5,4,3,2,1,0:T(4,128)S(1)} fusion(f32[4,3,3,2,4,4,256]{6,5,4,3,2,1,0:T(4,128)} %refs_6_.3), kind=kLoop, calls=%fused_computation.13 | loop fusion | bytes 147456 | tf_op jit(solution)/shard_map/squeeze | solution.py:350
  8.8 1.0 %slice_bitcast_fusion = f32[3,3,2,4,1,256]{5,4,3,2,1,0:T(1,128)S(1)} fusion(f32[4,3,3,2,4,4,256]{6,5,4,3,2,1,0:T(4,128)} %refs_6_.3), kind=kLoop, calls=%fused_computation.12 | loop fusion | bytes 147456 | tf_op jit(solution)/shard_map/squeeze | solution.py:351
  9.9 0.7 %dynamic_slice.3 = s32[4]{0:T(128)S(1)} dynamic-slice(s32[8]{0:T(128)} %param.6, s32[]{:T(128)S(6)} %select_n.122), dynamic_slice_sizes={4} | dynamic-slice | bytes 36 | tf_op jit(solution)/shard_map/dynamic_slice | solution.py:335
  10.7 0.1 compare_convert_fusion
  10.7 0.1 fusion.8
  10.8 0.1 reshape.211
  10.9 0.1 reshape.210
  11.0 0.1 collective-permute-start.5
  11.1 0.6 pad_maximum_fusion.1.refs_0_
  11.7 3.3 %collective-permute-done.4.refs_7_ = f32[3,3,2,1,4,256]{5,4,3,2,1,0:T(4,128)S(1)} collective-permute-done((f32[3,3,2,1,4,256]{5,4,3,2,1,0:T(4,128)S(1)}, f32[3,3,2,1,4,256]{5,4,3,2,1,0:T(4,128)S(1)}, u32[]{:S(2)}, u32[]{:S(2)}) %collective-permute-start.4) | collective-permute-done | bytes 73760 | tf_op jit(solution)/shard_map/ppermute | solution.py:25
  15.0 0.6 copy-done.4
  15.6 0.1 copy-done.2
  15.7 0.6 %copy-done.3 = f32[4,3,2,1,4,256]{5,4,3,2,1,0:T(4,128)} copy-done((f32[4,3,2,1,4,256]{5,4,3,2,1,0:T(4,128)}, f32[4,3,2,1,4,256]{5,4,3,2,1,0:T(4,128)S(1)}, u32[]{:S(2)}) %copy-start.3) | copy-done | bytes 98328
  16.3 10.2 %shard_map.46 = (f32[2,4,3,2,4,8,256]{6,5,4,3,2,1,0:T(8,128)}, bf16[2,2,3,2,1,8,256]{6,5,4,3,2,1,0:T(8,128)(2,1)}, bf16[2,2,3,2,1,8,256]{6,5,4,3,2,1,0:T(8,128)(...) custom-call(f32[42]{0:T(128)} %pad_maximum_fusion.1.refs_0_, f32[4,3,2,1,4,256]{5,4,3,2,1,0:T(4,128)} %refs_1_.3, ...), custom_call_target="tpu_custom_call" | custom-call | tf_op jit(solution)/shard_map/pallas_call | solution.py:281
  26.6 1.7 %collective-permute-start.9 = (f32[2,2,3,2,4,2,256]{6,5,4,3,2,1,0:T(2,128)}, f32[2,2,3,2,4,2,256]{6,5,4,3,2,1,0:T(2,128)S(1)}, u32[]{:S(2)}, u32[]{:S(2)}) collective-permute-start(f32[2,2,3,2,4,2,256]{6,5,4,3,2,1,0:T(2,128)} %get-tuple-element.14), channel_id=1, source_target_pairs={{0,3},{1,0},{2,1},{3,2},{4,7},{5,4},{6,5},{7,6},{8,11},{9,8},{10,9... | collective-permute-start | bytes 589832 | tf_op jit(solution)/shard_map/ppermute | solution.py:25
  28.3 1.3 %collective-permute-start.6 = (bf16[2,2,3,2,1,8,256]{6,5,4,3,2,1,0:T(8,128)(2,1)}, bf16[2,2,3,2,1,8,256]{6,5,4,3,2,1,0:T(8,128)(2,1)S(1)}, u32[]{:S(2)}, u32[]{:S(2)}) collective-permute-start(bf16[2,2,3,2,1,8,256]{6,5,4,3,2,1,0:T(8,128)(2,1)} %get-tuple-element.11), channel_id=1, source_target_pairs={{0,4},{4,8},{8,12},{12,0},{1,5},{5,9},{9,13},{13,1},{2,6},{6,10},{... | collective-permute-start | bytes 294920 | tf_op jit(solution)/shard_map/ppermute | solution.py:25
  29.6 2.5 %collective-permute-start.7 = (bf16[2,2,3,2,1,8,256]{6,5,4,3,2,1,0:T(8,128)(2,1)}, bf16[2,2,3,2,1,8,256]{6,5,4,3,2,1,0:T(8,128)(2,1)S(1)}, u32[]{:S(2)}, u32[]{:S(2)}) collective-permute-start(bf16[2,2,3,2,1,8,256]{6,5,4,3,2,1,0:T(8,128)(2,1)} %get-tuple-element.12), channel_id=1, source_target_pairs={{0,12},{4,0},{8,4},{12,8},{1,13},{5,1},{9,5},{13,9},{2,14},{6,2},{... | collective-permute-start | bytes 294920 | tf_op jit(solution)/shard_map/ppermute | solution.py:25
  32.2 0.2 copy.16
  32.3 1.7 %collective-permute-start.10 = (bf16[4,16,3,2,4,256]{5,1,4,2,3,0:T(8,128)(2,1)S(1)}, bf16[4,16,3,2,4,256]{5,1,4,2,3,0:T(8,128)(2,1)S(1)}, u32[]{:S(2)}, u32[]{:S(2)}) collective-permute-start(bf16[4,16,3,2,4,256]{5,1,4,2,3,0:T(8,128)(2,1)S(1)} %copy.16), channel_id=1, source_target_pairs={{0,16},{16,0},{1,17},{17,1},{2,18},{18,2},{3,19},{19,3},{4,20},{20... | collective-permute-start | bytes 2359304 | tf_op jit(solution)/shard_map/ppermute | solution.py:29
  34.1 1.7 %collective-permute-done.6.refs_10_ = bf16[2,2,3,2,1,8,256]{6,5,4,3,2,1,0:T(8,128)(2,1)S(1)} collective-permute-done((bf16[2,2,3,2,1,8,256]{6,5,4,3,2,1,0:T(8,128)(2,1)}, bf16[2,2,3,2,1,8,256]{6,5,4,3,2,1,0:T(8,128)(2,1)S(1)}, u32[]{:S(2)}, u32[]{:S(2)}) %collective-permute-start.6) | collective-permute-done | bytes 98336 | tf_op jit(solution)/shard_map/ppermute | solution.py:25
  35.8 0.5 collective-permute-done.7.refs_11_
  36.3 0.2 copy-done.10
  36.5 0.4 copy-done.11
  36.9 0.1 copy-done.6
  37.0 0.1 copy-done.7
  37.1 10.0 %shard_map.47 = bf16[2,4,3,2,4,2,4,256]{7,6,5,4,3,2,1,0:T(4,128)(2,1)} custom-call(f32[42]{0:T(128)} %pad_maximum_fusion.1.refs_0_, f32[4,3,2,1,4,256]{5,4,3,2,1,0:T(4,128)} %refs_1_.3, f32[4,3,2,1,4,256]{5,4,3,2,1,0:T(4,128)} %copy-done.2, f32[4,3,2,1,4,256]{5,4,3,2,1,0:T(4,128)} %copy-done.3, f32[4,3,2,1,1,256]{5,4,3,2,1,0:T(1,128)} %copy-done.8, ...), custom_call_target="tpu_custom_call" | custom-call | tf_op jit(solution)/shard_map/pallas_call | solution.py:281
  47.1 2.5 %convolution_bitcast_fusion.1 = f32[2,2,4,2,2,4,16]{6,2,3,1,4,0,5:T(4,128)S(1)} fusion(bf16[4,16,3,2,4,256,1,1,1]{5,4,3,2,1,0,8,7,6:T(4,128)(2,1)S(1)} %bitcast.73, bf16[2,4,3,2,4,2,4,256,1]{7,6,5,4,3,2,1,0,8:T(4,128)(2,1)} %bitcast.71), kind=kOutput, calls=%fused_computation.1 | convolution fusion | flops 25165824 | bytes 1589248 | tf_op jit(solution)/shard_map/tvcazs,hqcbtgzs->hgqabtv/dot_general | solution.py:313
  49.6 0.1 copy.13
  49.7 0.1 add.99
  49.8 0.1 sub.39
  49.9 1.5 %collective-permute-done.10 = bf16[4,16,3,2,4,256]{5,1,4,2,3,0:T(8,128)(2,1)S(1)} collective-permute-done((bf16[4,16,3,2,4,256]{5,1,4,2,3,0:T(8,128)(2,1)S(1)}, bf16[4,16,3,2,4,256]{5,1,4,2,3,0:T(8,128)(2,1)S(1)}, u32[]{:S(2)}, u32[]{:S(2)}) %collective-permute-start.10) | collective-permute-done | bytes 786464 | tf_op jit(solution)/shard_map/ppermute | solution.py:29
  51.4 1.3 %convolution_bitcast_fusion = f32[2,2,4,2,2,4,16]{6,2,3,1,4,0,5:T(4,128)S(1)} fusion(bf16[4,16,3,2,4,256]{5,1,4,2,3,0:T(8,128)(2,1)S(1)} %collective-permute-done.10, bf16[2,4,3,2,4,2,4,256,1]{7,6,5,4,3,2,1,0,8:T(4,128)(2,1)S(1)} %bitcast.72), kind=kOutput, calls=%fused_computation | convolution fusion | flops 25165824 | bytes 1589248 | tf_op jit(solution)/shard_map/tvcazs,hqcbtgzs->hgqabtv/dot_general | solution.py:313
  52.7 0.1 copy.18
  52.8 0.1 add.101
  52.9 0.1 sub.41
  53.0 0.1 copy_dynamic-update-slice_fusion
  53.1 0.1 pad_maximum_fusion
  53.3 0.1 collective-permute-start.11
  53.4 1.3 %collective-permute-done.11 = f32[2,4,4,2,4,8]{5,4,3,2,1,0:T(4,128)S(1)} collective-permute-done((f32[2,4,4,2,4,8]{5,4,3,2,1,0:T(4,128)S(1)}, f32[2,4,4,2,4,8]{5,4,3,2,1,0:T(4,128)S(1)}, u32[]{:S(2)}, u32[]{:S(2)}) %collective-permute-start.11) | collective-permute-done | bytes 8224 | tf_op jit(solution)/shard_map/ppermute | solution.py:307
  54.7 0.1 fusion.6
  54.8 0.5 collective-permute-start.12
  55.3 3.8 %collective-permute-done.12 = f32[1,4,4,2,4,8]{5,4,3,2,1,0:T(4,128)S(1)} collective-permute-done((f32[1,4,4,2,4,8]{5,4,3,2,1,0:T(4,128)S(1)}, f32[1,4,4,2,4,8]{5,4,3,2,1,0:T(4,128)S(1)}, u32[]{:S(2)}, u32[]{:S(2)}) %collective-permute-start.12) | collective-permute-done | bytes 4128 | tf_op jit(solution)/shard_map/ppermute | solution.py:307
  59.1 0.7 %fusion.7 = f32[4,4,2,4,8]{4,3,2,1,0:T(4,128)} fusion(f32[1,4,4,2,4,8]{5,4,3,2,1,0:T(4,128)S(1)} %collective-permute-done.12, f32[1,2,4,4,2,4,8]{6,5,4,3,2,1,0:T(4,128)S(1)} %fusion.6, pred[]{:T(512)S(6)} %eq.53), kind=kLoop, calls=%fused_computation.15 | loop fusion | flops 2048 | bytes 16385 | tf_op jit(solution)/shard_map/squeeze | solution.py:309
  (35 shorter events, 0.3 us)
Async XLA Ops:
  0.0 32.2 %copy-start.1 = (bf16[4,16,3,2,4,256]{5,4,3,2,1,0:T(4,128)(2,1)S(1)}, bf16[4,16,3,2,4,256]{5,4,3,2,1,0:T(4,128)(2,1)}, u32[]{:S(2)}) copy-start(bf16[4,16,3,2,4,256]{5,4,3,2,1,0:T(4,128)(2,1)} %param.7) | copy-start | bytes 2359300
  0.0 15.0 %collective-permute-start = (f32[4,3,2,1,4,256]{5,4,3,2,1,0:T(4,128)}, f32[4,3,2,1,4,256]{5,4,3,2,1,0:T(4,128)S(1)}, u32[]{:S(2)}, u32[]{:S(2)}) collective-permute-start(f32[4,3,2,1,4,256]{5,4,3,2,1,0:T(4,128)} %refs_1_.3), channel_id=1, source_target_pairs={{0,4},{4,8},{8,12},{12,0},{1,5},{5,9},{9,13},{13,1},{2,6},{6,10},{... | collective-permute-start | bytes 294920 | tf_op jit(solution)/shard_map/ppermute | solution.py:25
  3.1 12.0 %collective-permute-start.1 = (f32[4,3,2,1,4,256]{5,4,3,2,1,0:T(4,128)}, f32[4,3,2,1,4,256]{5,4,3,2,1,0:T(4,128)S(1)}, u32[]{:S(2)}, u32[]{:S(2)}) collective-permute-start(f32[4,3,2,1,4,256]{5,4,3,2,1,0:T(4,128)} %refs_1_.3), channel_id=1, source_target_pairs={{0,12},{4,0},{8,4},{12,8},{1,13},{5,1},{9,5},{13,9},{2,14},{6,2},{... | collective-permute-start | bytes 294920 | tf_op jit(solution)/shard_map/ppermute | solution.py:25
  6.1 4.8 %collective-permute-start.2 = (f32[4,3,2,1,1,256]{5,4,3,2,1,0:T(1,128)S(1)}, f32[4,3,2,1,1,256]{5,4,3,2,1,0:T(1,128)S(1)}, u32[]{:S(2)}, u32[]{:S(2)}) collective-permute-start(f32[4,3,2,1,1,256]{5,4,3,2,1,0:T(1,128)S(1)} %get-tuple-element.22), channel_id=1, source_target_pairs={{0,1},{1,2},{2,3},{3,0},{4,5},{5,6},{6,7},{7,4},{8,9},{9,10},{10,1... | collective-permute-start | bytes 73736 | tf_op jit(solution)/shard_map/ppermute | solution.py:25
  6.2 5.5 %collective-permute-start.3 = (f32[4,3,2,1,1,256]{5,4,3,2,1,0:T(1,128)S(1)}, f32[4,3,2,1,1,256]{5,4,3,2,1,0:T(1,128)S(1)}, u32[]{:S(2)}, u32[]{:S(2)}) collective-permute-start(f32[4,3,2,1,1,256]{5,4,3,2,1,0:T(1,128)S(1)} %get-tuple-element.21), channel_id=1, source_target_pairs={{0,3},{1,0},{2,1},{3,2},{4,7},{5,4},{6,5},{7,6},{8,11},{9,8},{10,9... | collective-permute-start | bytes 73736 | tf_op jit(solution)/shard_map/ppermute | solution.py:25
  8.8 6.2 %collective-permute-start.4 = (f32[3,3,2,1,4,256]{5,4,3,2,1,0:T(4,128)S(1)}, f32[3,3,2,1,4,256]{5,4,3,2,1,0:T(4,128)S(1)}, u32[]{:S(2)}, u32[]{:S(2)}) collective-permute-start(f32[3,3,2,1,4,256]{5,4,3,2,1,0:T(4,128)S(1)} %slice_bitcast_fusion.1), channel_id=1, source_target_pairs={{0,4},{4,8},{8,12},{12,0},{1,5},{5,9},{9,13},{13,1},{2,6},{6,10},{... | collective-permute-start | bytes 221192 | tf_op jit(solution)/shard_map/ppermute | solution.py:25
  11.0 4.1 %copy-start.8 = (f32[4,3,2,1,1,256]{5,4,3,2,1,0:T(1,128)}, f32[4,3,2,1,1,256]{5,4,3,2,1,0:T(1,128)S(1)}, u32[]{:S(2)}) copy-start(f32[4,3,2,1,1,256]{5,4,3,2,1,0:T(1,128)S(1)} %collective-permute-done.2.refs_4_) | copy-start | bytes 73732
  11.0 4.0 %collective-permute-start.5 = (f32[3,3,2,4,1,256]{5,4,3,2,1,0:T(1,128)S(1)}, f32[3,3,2,4,1,256]{5,4,3,2,1,0:T(1,128)S(1)}, u32[]{:S(2)}, u32[]{:S(2)}) collective-permute-start(f32[3,3,2,4,1,256]{5,4,3,2,1,0:T(1,128)S(1)} %slice_bitcast_fusion), channel_id=1, source_target_pairs={{0,1},{1,2},{2,3},{3,0},{4,5},{5,6},{6,7},{7,4},{8,9},{9,10},{10,1... | collective-permute-start | bytes 221192 | tf_op jit(solution)/shard_map/ppermute | solution.py:25
  11.7 3.4 %copy-start.9 = (f32[4,3,2,1,1,256]{5,4,3,2,1,0:T(1,128)}, f32[4,3,2,1,1,256]{5,4,3,2,1,0:T(1,128)S(1)}, u32[]{:S(2)}) copy-start(f32[4,3,2,1,1,256]{5,4,3,2,1,0:T(1,128)S(1)} %collective-permute-done.3.refs_5_) | copy-start | bytes 73732
  15.0 0.6 %copy-start.4 = (f32[3,3,2,1,4,256]{5,4,3,2,1,0:T(4,128)}, f32[3,3,2,1,4,256]{5,4,3,2,1,0:T(4,128)S(1)}, u32[]{:S(2)}) copy-start(f32[3,3,2,1,4,256]{5,4,3,2,1,0:T(4,128)S(1)} %collective-permute-done.4.refs_7_) | copy-start | bytes 221188
  15.0 0.6 %copy-start.5 = (f32[3,3,2,4,1,256]{5,4,3,2,1,0:T(1,128)}, f32[3,3,2,4,1,256]{5,4,3,2,1,0:T(1,128)S(1)}, u32[]{:S(2)}) copy-start(f32[3,3,2,4,1,256]{5,4,3,2,1,0:T(1,128)S(1)} %collective-permute-done.5.refs_8_) | copy-start | bytes 221188
  15.0 0.7 %copy-start.2 = (f32[4,3,2,1,4,256]{5,4,3,2,1,0:T(4,128)}, f32[4,3,2,1,4,256]{5,4,3,2,1,0:T(4,128)S(1)}, u32[]{:S(2)}) copy-start(f32[4,3,2,1,4,256]{5,4,3,2,1,0:T(4,128)S(1)} %collective-permute-done.refs_2_) | copy-start | bytes 294916
  15.7 0.6 %copy-start.3 = (f32[4,3,2,1,4,256]{5,4,3,2,1,0:T(4,128)}, f32[4,3,2,1,4,256]{5,4,3,2,1,0:T(4,128)S(1)}, u32[]{:S(2)}) copy-start(f32[4,3,2,1,4,256]{5,4,3,2,1,0:T(4,128)S(1)} %collective-permute-done.1.refs_3_) | copy-start | bytes 294916
  26.5 9.7 %collective-permute-start.8 = (f32[2,2,3,2,4,2,256]{6,5,4,3,2,1,0:T(2,128)}, f32[2,2,3,2,4,2,256]{6,5,4,3,2,1,0:T(2,128)S(1)}, u32[]{:S(2)}, u32[]{:S(2)}) collective-permute-start(f32[2,2,3,2,4,2,256]{6,5,4,3,2,1,0:T(2,128)} %get-tuple-element.13), channel_id=1, source_target_pairs={{0,1},{1,2},{2,3},{3,0},{4,5},{5,6},{6,7},{7,4},{8,9},{9,10},{10,1... | collective-permute-start | bytes 589832 | tf_op jit(solution)/shard_map/ppermute | solution.py:25
  26.6 9.7 %collective-permute-start.9 = (f32[2,2,3,2,4,2,256]{6,5,4,3,2,1,0:T(2,128)}, f32[2,2,3,2,4,2,256]{6,5,4,3,2,1,0:T(2,128)S(1)}, u32[]{:S(2)}, u32[]{:S(2)}) collective-permute-start(f32[2,2,3,2,4,2,256]{6,5,4,3,2,1,0:T(2,128)} %get-tuple-element.14), channel_id=1, source_target_pairs={{0,3},{1,0},{2,1},{3,2},{4,7},{5,4},{6,5},{7,6},{8,11},{9,8},{10,9... | collective-permute-start | bytes 589832 | tf_op jit(solution)/shard_map/ppermute | solution.py:25
  28.3 7.5 %collective-permute-start.6 = (bf16[2,2,3,2,1,8,256]{6,5,4,3,2,1,0:T(8,128)(2,1)}, bf16[2,2,3,2,1,8,256]{6,5,4,3,2,1,0:T(8,128)(2,1)S(1)}, u32[]{:S(2)}, u32[]{:S(2)}) collective-permute-start(bf16[2,2,3,2,1,8,256]{6,5,4,3,2,1,0:T(8,128)(2,1)} %get-tuple-element.11), channel_id=1, source_target_pairs={{0,4},{4,8},{8,12},{12,0},{1,5},{5,9},{9,13},{13,1},{2,6},{6,10},{... | collective-permute-start | bytes 294920 | tf_op jit(solution)/shard_map/ppermute | solution.py:25
  29.6 6.6 %collective-permute-start.7 = (bf16[2,2,3,2,1,8,256]{6,5,4,3,2,1,0:T(8,128)(2,1)}, bf16[2,2,3,2,1,8,256]{6,5,4,3,2,1,0:T(8,128)(2,1)S(1)}, u32[]{:S(2)}, u32[]{:S(2)}) collective-permute-start(bf16[2,2,3,2,1,8,256]{6,5,4,3,2,1,0:T(8,128)(2,1)} %get-tuple-element.12), channel_id=1, source_target_pairs={{0,12},{4,0},{8,4},{12,8},{1,13},{5,1},{9,5},{13,9},{2,14},{6,2},{... | collective-permute-start | bytes 294920 | tf_op jit(solution)/shard_map/ppermute | solution.py:25
  32.3 19.1 %collective-permute-start.10 = (bf16[4,16,3,2,4,256]{5,1,4,2,3,0:T(8,128)(2,1)S(1)}, bf16[4,16,3,2,4,256]{5,1,4,2,3,0:T(8,128)(2,1)S(1)}, u32[]{:S(2)}, u32[]{:S(2)}) collective-permute-start(bf16[4,16,3,2,4,256]{5,1,4,2,3,0:T(8,128)(2,1)S(1)} %copy.16), channel_id=1, source_target_pairs={{0,16},{16,0},{1,17},{17,1},{2,18},{18,2},{3,19},{19,3},{4,20},{20... | collective-permute-start | bytes 2359304 | tf_op jit(solution)/shard_map/ppermute | solution.py:29
  35.8 0.7 %copy-start.10 = (bf16[2,2,3,2,1,8,256]{6,5,4,3,2,1,0:T(8,128)(2,1)}, bf16[2,2,3,2,1,8,256]{6,5,4,3,2,1,0:T(8,128)(2,1)S(1)}, u32[]{:S(2)}) copy-start(bf16[2,2,3,2,1,8,256]{6,5,4,3,2,1,0:T(8,128)(2,1)S(1)} %collective-permute-done.6.refs_10_) | copy-start | bytes 294916
  36.3 0.6 %copy-start.11 = (bf16[2,2,3,2,1,8,256]{6,5,4,3,2,1,0:T(8,128)(2,1)}, bf16[2,2,3,2,1,8,256]{6,5,4,3,2,1,0:T(8,128)(2,1)S(1)}, u32[]{:S(2)}) copy-start(bf16[2,2,3,2,1,8,256]{6,5,4,3,2,1,0:T(8,128)(2,1)S(1)} %collective-permute-done.7.refs_11_) | copy-start | bytes 294916
  36.3 0.7 %copy-start.6 = (f32[2,2,3,2,4,2,256]{6,5,4,3,2,1,0:T(2,128)}, f32[2,2,3,2,4,2,256]{6,5,4,3,2,1,0:T(2,128)S(1)}, u32[]{:S(2)}) copy-start(f32[2,2,3,2,4,2,256]{6,5,4,3,2,1,0:T(2,128)S(1)} %collective-permute-done.8.refs_12_) | copy-start | bytes 589828
  36.3 0.8 %copy-start.7 = (f32[2,2,3,2,4,2,256]{6,5,4,3,2,1,0:T(2,128)}, f32[2,2,3,2,4,2,256]{6,5,4,3,2,1,0:T(2,128)S(1)}, u32[]{:S(2)}) copy-start(f32[2,2,3,2,4,2,256]{6,5,4,3,2,1,0:T(2,128)S(1)} %collective-permute-done.9.refs_13_) | copy-start | bytes 589828
  47.1 4.3 %copy-start = (bf16[2,4,3,2,4,2,4,256]{7,6,5,4,3,2,1,0:T(4,128)(2,1)S(1)}, bf16[2,4,3,2,4,2,4,256]{7,6,5,4,3,2,1,0:T(4,128)(2,1)}, u32[]{:S(2)}) copy-start(bf16[2,4,3,2,4,2,4,256]{7,6,5,4,3,2,1,0:T(4,128)(2,1)} %shard_map.47) | copy-start | bytes 2359300
  53.3 1.4 %collective-permute-start.11 = (f32[2,4,4,2,4,8]{5,4,3,2,1,0:T(4,128)S(1)}, f32[2,4,4,2,4,8]{5,4,3,2,1,0:T(4,128)S(1)}, u32[]{:S(2)}, u32[]{:S(2)}) collective-permute-start(f32[2,4,4,2,4,8]{5,4,3,2,1,0:T(4,128)S(1)} %select_bitcast_fusion), channel_id=1, source_target_pairs={{0,1},{1,0},{2,3},{3,2},{4,5},{5,4},{6,7},{7,6},{8,9},{9,8},{10,11... | collective-permute-start | bytes 24584 | tf_op jit(solution)/shard_map/ppermute | solution.py:307
  54.8 4.3 %collective-permute-start.12 = (f32[1,4,4,2,4,8]{5,4,3,2,1,0:T(4,128)S(1)}, f32[1,4,4,2,4,8]{5,4,3,2,1,0:T(4,128)S(1)}, u32[]{:S(2)}, u32[]{:S(2)}) collective-permute-start(f32[1,4,4,2,4,8]{5,4,3,2,1,0:T(4,128)S(1)} %select_bitcast_fusion.1), channel_id=1, source_target_pairs={{0,2},{1,3},{2,0},{3,1},{4,6},{5,7},{6,4},{7,5},{8,10},{9,11},{10,... | collective-permute-start | bytes 12296 | tf_op jit(solution)/shard_map/ppermute | solution.py:307

commit v10 on v9

--- a/solution.py
+++ b/solution.py
@@ -68,7 +68,7 @@
             for b in range(3):
                 for ri in range(RI):
                     for half in (lower, upper):
-                        ut8[a, b, ri, pl.ds(0, 1), half] = utedge_ref[a, b, ri]
+                        ut8[a, b, ri, pl.ds(0, 1), half] = utedge_ref[a, b, ri].astype(jnp.float32)
                         ut8[a, b, ri, pl.ds(1, T), half] = u_ref[3, a, b, ri]
                         for t in range(T):
                             uz8[a, b, ri, t, half] = jnp.broadcast_to(uzedge_ref[a, b, ri, t], (Z, L))
@@ -85,9 +85,9 @@
                         src_ref[s, c, ri, t, half] = noise_ref[g, c, ri, t // span] * (
                             fs * tmask(r * (T + 2) + t + 1))
                     if first:
-                        pad_ref[s, c, ri, 0, half] = ntlo_ref[g, c, ri, 0] * (
+                        pad_ref[s, c, ri, 0, half] = ntlo_ref[g, c, ri, 0].astype(jnp.float32) * (
                             fs * tmask(r * (T + 2)) * sign(0))
-                        pad_ref[s, c, ri, T + 1, half] = nthi_ref[g, c, ri, 0] * (
+                        pad_ref[s, c, ri, T + 1, half] = nthi_ref[g, c, ri, 0].astype(jnp.float32) * (
                             fs * tmask(r * (T + 2) + T + 1) * sign(1))
                         for t in range(T):
                             f = fs * tmask(r * (T + 2) + t + 1)
@@ -340,14 +340,14 @@
     scalars = (jnp.concatenate([spin_mask.reshape(-1), time_mask.reshape(-1), signs]),)
     noise_parts = (
         noise_slabs,
-        passed_along(noise_slabs[:, :, :, K - 1:], "ta", 1),
-        passed_along(noise_slabs[:, :, :, :1], "ta", -1),
+        passed_along(noise_slabs[:, :, :, K - 1:].astype(jnp.bfloat16), "ta", 1),
+        passed_along(noise_slabs[:, :, :, :1].astype(jnp.bfloat16), "ta", -1),
         passed_along(noise_slabs[:, :, :, :, Z - 1:], "sa", 1),
         passed_along(noise_slabs[:, :, :, :, :1], "sa", -1),
     )
     link_parts = (
         gauge_links,
-        passed_along(gauge_links[3, :, :, :, -1:, :, :], "ta", 1),
+        passed_along(gauge_links[3, :, :, :, -1:, :, :].astype(jnp.bfloat16), "ta", 1),
         passed_along(gauge_links[2, :, :, :, :, -1:, :], "sa", 1),
     )
     spinor, t_first, t_last, z_first, z_last = hopping_step(True, scalars, noise_parts, link_parts, ())

time: 60 us -> 62.8 us (1.047)
  waiting for transfers between devices: 12.1 us -> 13.8 us
  other arithmetic: 1.66 us -> 2.71 us
    ppermute x10, waiting for transfers between devices: 5.53 us -> 7.09 us  [passed_along(): return lax.ppermute(value, axis, pairs)]
    convert_element_type x0 -> x1, other arithmetic: none -> 0.98 us  [local_body(): noise_slabs[:, :, :, K - 1:].astype(jnp.bfloat16)]
    convert_element_type x0 -> x1, local copies, waits for them, and re-layouts: none -> 0.9 us  [local_body(): gauge_links[3, :, :, :, -1:, :, :].astype(jnp.bfloat16)]
    squeeze x1 -> x0, local copies, waits for them, and re-layouts: 0.89 us -> none  [local_body(): gauge_links[3, :, :, :, -1:, :, :]]
  transfers between devices with their start and end apart: 13 -> 13, of which waited for: 6 -> 5; matrix products, arithmetic and copies ran while one was open for 13% -> 12% of each run, Pallas kernels for 17% -> 16%
where the time goes in v10:
time: 62.8 us; the launch traced here: 62.5 us
  Pallas kernels  20.1 us (32%)
  starting transfers between devices  15 us (24%)
  waiting for transfers between devices  13.8 us (22%)
  local copies, waits for them, and re-layouts  6.75 us (11%)
  matrix products  3.73 us (6%)
  other arithmetic  2.71 us (4%)
    pallas_call x2, Pallas kernels, hopping_step(): pl.pallas_call(functools.partial(hop_kernel, first), grid=(H,), in_specs=...  20.1 us
    ppermute x10, starting transfers between devices, passed_along(): return lax.ppermute(value, axis, pairs)  12.7 us
    ppermute x10, waiting for transfers between devices, passed_along(): return lax.ppermute(value, axis, pairs)  7.09 us
    ppermute x2, waiting for transfers between devices, reduce_scatter_sa(): x = keep + lax.ppermute(send, 'sa', [(j, j ^ d) for j in range(n)])  5.11 us
    dot_general x2, matrix products, intersection_part(): jnp.einsum('tvcazs,hqcbtgzs->hgqabtv', vector_piece, rounded, preferred_e...  3.73 us
    unnamed x27, local copies, waits for them, and re-layouts  2.25 us
    ppermute x1, starting transfers between devices, from_partner(): lax.ppermute(x, axis, [(i, i ^ 1 << stride) for i in range(lax.axis_size(...  1.69 us
    ppermute x1, waiting for transfers between devices, from_partner(): lax.ppermute(x, axis, [(i, i ^ 1 << stride) for i in range(lax.axis_size(...  1.64 us
  transfers between devices with their start and end apart: 13, of which 5 were waited for; matrix products, arithmetic and copies ran while one was open for 12% of the time, Pallas kernels for 16%

profile of v10, /device:TPU:0, one launch (start us, length us, event | category | flops | bytes accessed | tf_op | source)
XLA Modules:
  0.0 62.5 jit_solution(12625415863006353537)
XLA Ops:
  0.0 1.0 %convert_element_type.34 = bf16[4,3,2,1,4,256]{5,4,3,2,1,0:T(4,128)(2,1)S(1)} convert(f32[4,3,2,1,4,256]{5,4,3,2,1,0:T(4,128)} %refs_1_.3) | non-fusion elementwise | flops 24576 | bytes 147456 | tf_op jit(solution)/shard_map/convert_element_type | solution.py:343
  1.0 3.1 %collective-permute-start = (bf16[4,3,2,1,4,256]{5,4,3,2,1,0:T(4,128)(2,1)S(1)}, bf16[4,3,2,1,4,256]{5,4,3,2,1,0:T(4,128)(2,1)S(1)}, u32[]{:S(2)}, u32[]{:S(2)}) collective-permute-start(bf16[4,3,2,1,4,256]{5,4,3,2,1,0:T(4,128)(2,1)S(1)} %convert_element_type.34), channel_id=1, source_target_pairs={{0,4},{4,8},{8,12},{12,0},{1,5},{5,9},{9,13},{13,1},{2,6},{6,10},{... | collective-permute-start | bytes 147464 | tf_op jit(solution)/shard_map/ppermute | solution.py:25
  4.1 2.1 %collective-permute-start.1 = (bf16[4,3,2,1,4,256]{5,4,3,2,1,0:T(4,128)(2,1)S(1)}, bf16[4,3,2,1,4,256]{5,4,3,2,1,0:T(4,128)(2,1)S(1)}, u32[]{:S(2)}, u32[]{:S(2)}) collective-permute-start(bf16[4,3,2,1,4,256]{5,4,3,2,1,0:T(4,128)(2,1)S(1)} %convert_element_type.34), channel_id=1, source_target_pairs={{0,12},{4,0},{8,4},{12,8},{1,13},{5,1},{9,5},{13,9},{2,14},{6,2},{... | collective-permute-start | bytes 147464 | tf_op jit(solution)/shard_map/ppermute | solution.py:25
  6.2 1.0 %fusion.12 = (f32[4,3,2,1,1,256]{5,4,3,2,1,0:T(1,128)S(1)}, f32[4,3,2,1,1,256]{5,4,3,2,1,0:T(1,128)S(1)}) fusion(f32[4,3,2,1,4,256]{5,4,3,2,1,0:T(4,128)} %refs_1_.3), kind=kLoop, calls=%fused_computation.40 | loop fusion | bytes 98304 | tf_op jit(solution)/shard_map/slice | solution.py:346
  7.2 0.1 collective-permute-start.2
  7.3 1.7 %collective-permute-start.3 = (f32[4,3,2,1,1,256]{5,4,3,2,1,0:T(1,128)S(1)}, f32[4,3,2,1,1,256]{5,4,3,2,1,0:T(1,128)S(1)}, u32[]{:S(2)}, u32[]{:S(2)}) collective-permute-start(f32[4,3,2,1,1,256]{5,4,3,2,1,0:T(1,128)S(1)} %get-tuple-element.21), channel_id=1, source_target_pairs={{0,3},{1,0},{2,1},{3,2},{4,7},{5,4},{6,5},{7,6},{8,11},{9,8},{10,9... | collective-permute-start | bytes 73736 | tf_op jit(solution)/shard_map/ppermute | solution.py:25
  9.0 1.0 %slice_bitcast_fusion = f32[3,3,2,4,1,256]{5,4,3,2,1,0:T(1,128)S(1)} fusion(f32[4,3,3,2,4,4,256]{6,5,4,3,2,1,0:T(4,128)} %refs_6_.3), kind=kLoop, calls=%fused_computation.13 | loop fusion | bytes 147456 | tf_op jit(solution)/shard_map/squeeze | solution.py:351
  10.0 0.1 collective-permute-start.5
  10.1 0.9 %fusion.8 = bf16[3,3,2,1,4,256]{5,4,3,2,1,0:T(4,128)(2,1)S(1)} fusion(f32[4,3,3,2,4,4,256]{6,5,4,3,2,1,0:T(4,128)} %refs_6_.3), kind=kLoop, calls=%fused_computation.23 | loop fusion | bytes 73728 | tf_op jit(solution)/shard_map/convert_element_type | solution.py:350
  11.1 0.7 %dynamic_slice.3 = s32[4]{0:T(128)S(1)} dynamic-slice(s32[8]{0:T(128)} %param.6, s32[]{:T(128)S(6)} %select_n.122), dynamic_slice_sizes={4} | dynamic-slice | bytes 36 | tf_op jit(solution)/shard_map/dynamic_slice | solution.py:335
  11.8 0.1 compare_convert_fusion
  11.9 0.1 fusion.9
  12.0 0.1 reshape.224
  12.0 0.1 reshape.223
  12.1 0.0 collective-permute-start.4
  12.2 0.7 %pad_maximum_fusion.1.refs_0_ = f32[42]{0:T(128)} fusion(f32[1]{0:T(128)} %bitcast.1, f32[1]{0:T(128)} %bitcast, f32[24]{0:T(128)S(1)} %reshape.224, f32[16]{0:T(128)S(1)} %reshape.223), kind=kLoop, calls=%fused_computation.39 | loop fusion | flops 126 | bytes 336 | tf_op jit(solution)/shard_map/concatenate | solution.py:340
  12.8 5.1 %collective-permute-done.4.refs_7_ = bf16[3,3,2,1,4,256]{5,4,3,2,1,0:T(4,128)(2,1)S(1)} collective-permute-done((bf16[3,3,2,1,4,256]{5,4,3,2,1,0:T(4,128)(2,1)S(1)}, bf16[3,3,2,1,4,256]{5,4,3,2,1,0:T(4,128)(2,1)S(1)}, u32[]{:S(2)}, u32[]{:S(2)}) %collective-permute-start.4) | collective-permute-done | bytes 36896 | tf_op jit(solution)/shard_map/ppermute | solution.py:25
  18.0 0.6 copy-done.7
  18.6 0.6 %copy-done.2 = f32[3,3,2,4,1,256]{5,4,3,2,1,0:T(1,128)} copy-done((f32[3,3,2,4,1,256]{5,4,3,2,1,0:T(1,128)}, f32[3,3,2,4,1,256]{5,4,3,2,1,0:T(1,128)S(1)}, u32[]{:S(2)}) %copy-start.2) | copy-done | bytes 73752
  19.2 10.2 %shard_map.46 = (f32[2,4,3,2,4,8,256]{6,5,4,3,2,1,0:T(8,128)}, bf16[2,2,3,2,1,8,256]{6,5,4,3,2,1,0:T(8,128)(2,1)}, bf16[2,2,3,2,1,8,256]{6,5,4,3,2,1,0:T(8,128)(...) custom-call(f32[42]{0:T(128)} %pad_maximum_fusion.1.refs_0_, f32[4,3,2,1,4,256]{5,4,3,2,1,0:T(4,128)} %refs_1_.3, ...), custom_call_target="tpu_custom_call" | custom-call | tf_op jit(solution)/shard_map/pallas_call | solution.py:281
  29.4 0.6 %collective-permute-start.8 = (f32[2,2,3,2,4,2,256]{6,5,4,3,2,1,0:T(2,128)}, f32[2,2,3,2,4,2,256]{6,5,4,3,2,1,0:T(2,128)S(1)}, u32[]{:S(2)}, u32[]{:S(2)}) collective-permute-start(f32[2,2,3,2,4,2,256]{6,5,4,3,2,1,0:T(2,128)} %get-tuple-element.13), channel_id=1, source_target_pairs={{0,1},{1,2},{2,3},{3,0},{4,5},{5,6},{6,7},{7,4},{8,9},{9,10},{10,1... | collective-permute-start | bytes 589832 | tf_op jit(solution)/shard_map/ppermute | solution.py:25
  30.0 1.2 %collective-permute-start.9 = (f32[2,2,3,2,4,2,256]{6,5,4,3,2,1,0:T(2,128)}, f32[2,2,3,2,4,2,256]{6,5,4,3,2,1,0:T(2,128)S(1)}, u32[]{:S(2)}, u32[]{:S(2)}) collective-permute-start(f32[2,2,3,2,4,2,256]{6,5,4,3,2,1,0:T(2,128)} %get-tuple-element.14), channel_id=1, source_target_pairs={{0,3},{1,0},{2,1},{3,2},{4,7},{5,4},{6,5},{7,6},{8,11},{9,8},{10,9... | collective-permute-start | bytes 589832 | tf_op jit(solution)/shard_map/ppermute | solution.py:25
  31.2 3.8 %collective-permute-start.7 = (bf16[2,2,3,2,1,8,256]{6,5,4,3,2,1,0:T(8,128)(2,1)}, bf16[2,2,3,2,1,8,256]{6,5,4,3,2,1,0:T(8,128)(2,1)S(1)}, u32[]{:S(2)}, u32[]{:S(2)}) collective-permute-start(bf16[2,2,3,2,1,8,256]{6,5,4,3,2,1,0:T(8,128)(2,1)} %get-tuple-element.12), channel_id=1, source_target_pairs={{0,12},{4,0},{8,4},{12,8},{1,13},{5,1},{9,5},{13,9},{2,14},{6,2},{... | collective-permute-start | bytes 294920 | tf_op jit(solution)/shard_map/ppermute | solution.py:25
  35.0 0.2 copy.16
  35.2 1.7 %collective-permute-start.10 = (bf16[4,16,3,2,4,256]{5,1,4,2,3,0:T(8,128)(2,1)S(1)}, bf16[4,16,3,2,4,256]{5,1,4,2,3,0:T(8,128)(2,1)S(1)}, u32[]{:S(2)}, u32[]{:S(2)}) collective-permute-start(bf16[4,16,3,2,4,256]{5,1,4,2,3,0:T(8,128)(2,1)S(1)} %copy.16), channel_id=1, source_target_pairs={{0,16},{16,0},{1,17},{17,1},{2,18},{18,2},{3,19},{19,3},{4,20},{20... | collective-permute-start | bytes 2359304 | tf_op jit(solution)/shard_map/ppermute | solution.py:29
  36.9 2.0 %collective-permute-done.6.refs_10_ = bf16[2,2,3,2,1,8,256]{6,5,4,3,2,1,0:T(8,128)(2,1)S(1)} collective-permute-done((bf16[2,2,3,2,1,8,256]{6,5,4,3,2,1,0:T(8,128)(2,1)}, bf16[2,2,3,2,1,8,256]{6,5,4,3,2,1,0:T(8,128)(2,1)S(1)}, u32[]{:S(2)}, u32[]{:S(2)}) %collective-permute-start.6) | collective-permute-done | bytes 98336 | tf_op jit(solution)/shard_map/ppermute | solution.py:25
  38.9 0.6 copy-done.10
  39.5 0.0 copy-done.11
  39.5 0.1 copy-done.5
  39.6 0.1 copy-done.6
  39.7 10.0 %shard_map.47 = bf16[2,4,3,2,4,2,4,256]{7,6,5,4,3,2,1,0:T(4,128)(2,1)} custom-call(f32[42]{0:T(128)} %pad_maximum_fusion.1.refs_0_, f32[4,3,2,1,4,256]{5,4,3,2,1,0:T(4,128)} %refs_1_.3, bf16[4,3,2,1,4,256]{5,4,3,2,1,0:T(4,128)(2,1)} %copy-done.3, bf16[4,3,2,1,4,256]{5,4,3,2,1,0:T(4,128)(2,1)} %copy-done.4, f32[4,3,2,1,1,256]{5,4,3,2,1,0:T(1,128)} %copy-done.8, ...), custom_call_target="tpu_custom_call" | custom-call | tf_op jit(solution)/shard_map/pallas_call | solution.py:281
  49.7 2.5 %convolution_bitcast_fusion.1 = f32[2,2,4,2,2,4,16]{6,2,3,1,4,0,5:T(4,128)S(1)} fusion(bf16[4,16,3,2,4,256,1,1,1]{5,4,3,2,1,0,8,7,6:T(4,128)(2,1)S(1)} %bitcast.69, bf16[2,4,3,2,4,2,4,256,1]{7,6,5,4,3,2,1,0,8:T(4,128)(2,1)} %bitcast.70), kind=kOutput, calls=%fused_computation.1 | convolution fusion | flops 25165824 | bytes 1589248 | tf_op jit(solution)/shard_map/tvcazs,hqcbtgzs->hgqabtv/dot_general | solution.py:313
  52.1 0.1 copy.13
  52.3 0.1 add.99
  52.4 0.1 sub.39
  52.5 1.6 %collective-permute-done.10 = bf16[4,16,3,2,4,256]{5,1,4,2,3,0:T(8,128)(2,1)S(1)} collective-permute-done((bf16[4,16,3,2,4,256]{5,1,4,2,3,0:T(8,128)(2,1)S(1)}, bf16[4,16,3,2,4,256]{5,1,4,2,3,0:T(8,128)(2,1)S(1)}, u32[]{:S(2)}, u32[]{:S(2)}) %collective-permute-start.10) | collective-permute-done | bytes 786464 | tf_op jit(solution)/shard_map/ppermute | solution.py:29
  54.1 1.3 %convolution_bitcast_fusion = f32[2,2,4,2,2,4,16]{6,2,3,1,4,0,5:T(4,128)S(1)} fusion(bf16[4,16,3,2,4,256]{5,1,4,2,3,0:T(8,128)(2,1)S(1)} %collective-permute-done.10, bf16[2,4,3,2,4,2,4,256,1]{7,6,5,4,3,2,1,0,8:T(4,128)(2,1)S(1)} %bitcast.71), kind=kOutput, calls=%fused_computation | convolution fusion | flops 25165824 | bytes 1589248 | tf_op jit(solution)/shard_map/tvcazs,hqcbtgzs->hgqabtv/dot_general | solution.py:313
  55.4 0.1 copy.18
  55.5 0.1 add.101
  55.7 0.1 sub.41
  55.8 0.1 copy_dynamic-update-slice_fusion
  55.9 0.1 pad_maximum_fusion
  56.0 0.1 collective-permute-start.11
  56.1 1.3 %collective-permute-done.11 = f32[2,4,4,2,4,8]{5,4,3,2,1,0:T(4,128)S(1)} collective-permute-done((f32[2,4,4,2,4,8]{5,4,3,2,1,0:T(4,128)S(1)}, f32[2,4,4,2,4,8]{5,4,3,2,1,0:T(4,128)S(1)}, u32[]{:S(2)}, u32[]{:S(2)}) %collective-permute-start.11) | collective-permute-done | bytes 8224 | tf_op jit(solution)/shard_map/ppermute | solution.py:307
  57.4 0.1 fusion.6
  57.5 0.5 collective-permute-start.12
  58.0 3.8 %collective-permute-done.12 = f32[1,4,4,2,4,8]{5,4,3,2,1,0:T(4,128)S(1)} collective-permute-done((f32[1,4,4,2,4,8]{5,4,3,2,1,0:T(4,128)S(1)}, f32[1,4,4,2,4,8]{5,4,3,2,1,0:T(4,128)S(1)}, u32[]{:S(2)}, u32[]{:S(2)}) %collective-permute-start.12) | collective-permute-done | bytes 4128 | tf_op jit(solution)/shard_map/ppermute | solution.py:307
  61.8 0.7 %fusion.7 = f32[4,4,2,4,8]{4,3,2,1,0:T(4,128)} fusion(f32[1,4,4,2,4,8]{5,4,3,2,1,0:T(4,128)S(1)} %collective-permute-done.12, f32[1,2,4,4,2,4,8]{6,5,4,3,2,1,0:T(4,128)S(1)} %fusion.6, pred[]{:T(512)S(6)} %eq.53), kind=kLoop, calls=%fused_computation.15 | loop fusion | flops 2048 | bytes 16385 | tf_op jit(solution)/shard_map/squeeze | solution.py:309
  (36 shorter events, 0.3 us)
Async XLA Ops:
  0.0 35.0 %copy-start = (bf16[4,16,3,2,4,256]{5,4,3,2,1,0:T(4,128)(2,1)S(1)}, bf16[4,16,3,2,4,256]{5,4,3,2,1,0:T(4,128)(2,1)}, u32[]{:S(2)}) copy-start(bf16[4,16,3,2,4,256]{5,4,3,2,1,0:T(4,128)(2,1)} %param.7) | copy-start | bytes 2359300
  1.0 16.9 %collective-permute-start = (bf16[4,3,2,1,4,256]{5,4,3,2,1,0:T(4,128)(2,1)S(1)}, bf16[4,3,2,1,4,256]{5,4,3,2,1,0:T(4,128)(2,1)S(1)}, u32[]{:S(2)}, u32[]{:S(2)}) collective-permute-start(bf16[4,3,2,1,4,256]{5,4,3,2,1,0:T(4,128)(2,1)S(1)} %convert_element_type.34), channel_id=1, source_target_pairs={{0,4},{4,8},{8,12},{12,0},{1,5},{5,9},{9,13},{13,1},{2,6},{6,10},{... | collective-permute-start | bytes 147464 | tf_op jit(solution)/shard_map/ppermute | solution.py:25
  4.1 13.8 %collective-permute-start.1 = (bf16[4,3,2,1,4,256]{5,4,3,2,1,0:T(4,128)(2,1)S(1)}, bf16[4,3,2,1,4,256]{5,4,3,2,1,0:T(4,128)(2,1)S(1)}, u32[]{:S(2)}, u32[]{:S(2)}) collective-permute-start(bf16[4,3,2,1,4,256]{5,4,3,2,1,0:T(4,128)(2,1)S(1)} %convert_element_type.34), channel_id=1, source_target_pairs={{0,12},{4,0},{8,4},{12,8},{1,13},{5,1},{9,5},{13,9},{2,14},{6,2},{... | collective-permute-start | bytes 147464 | tf_op jit(solution)/shard_map/ppermute | solution.py:25
  7.2 4.9 %collective-permute-start.2 = (f32[4,3,2,1,1,256]{5,4,3,2,1,0:T(1,128)S(1)}, f32[4,3,2,1,1,256]{5,4,3,2,1,0:T(1,128)S(1)}, u32[]{:S(2)}, u32[]{:S(2)}) collective-permute-start(f32[4,3,2,1,1,256]{5,4,3,2,1,0:T(1,128)S(1)} %get-tuple-element.22), channel_id=1, source_target_pairs={{0,1},{1,2},{2,3},{3,0},{4,5},{5,6},{6,7},{7,4},{8,9},{9,10},{10,1... | collective-permute-start | bytes 73736 | tf_op jit(solution)/shard_map/ppermute | solution.py:25
  7.3 5.6 %collective-permute-start.3 = (f32[4,3,2,1,1,256]{5,4,3,2,1,0:T(1,128)S(1)}, f32[4,3,2,1,1,256]{5,4,3,2,1,0:T(1,128)S(1)}, u32[]{:S(2)}, u32[]{:S(2)}) collective-permute-start(f32[4,3,2,1,1,256]{5,4,3,2,1,0:T(1,128)S(1)} %get-tuple-element.21), channel_id=1, source_target_pairs={{0,3},{1,0},{2,1},{3,2},{4,7},{5,4},{6,5},{7,6},{8,11},{9,8},{10,9... | collective-permute-start | bytes 73736 | tf_op jit(solution)/shard_map/ppermute | solution.py:25
  10.0 7.9 %collective-permute-start.5 = (f32[3,3,2,4,1,256]{5,4,3,2,1,0:T(1,128)S(1)}, f32[3,3,2,4,1,256]{5,4,3,2,1,0:T(1,128)S(1)}, u32[]{:S(2)}, u32[]{:S(2)}) collective-permute-start(f32[3,3,2,4,1,256]{5,4,3,2,1,0:T(1,128)S(1)} %slice_bitcast_fusion), channel_id=1, source_target_pairs={{0,1},{1,2},{2,3},{3,0},{4,5},{5,6},{6,7},{7,4},{8,9},{9,10},{10,1... | collective-permute-start | bytes 221192 | tf_op jit(solution)/shard_map/ppermute | solution.py:25
  12.1 5.8 %copy-start.8 = (f32[4,3,2,1,1,256]{5,4,3,2,1,0:T(1,128)}, f32[4,3,2,1,1,256]{5,4,3,2,1,0:T(1,128)S(1)}, u32[]{:S(2)}) copy-start(f32[4,3,2,1,1,256]{5,4,3,2,1,0:T(1,128)S(1)} %collective-permute-done.2.refs_4_) | copy-start | bytes 73732
  12.1 5.8 %collective-permute-start.4 = (bf16[3,3,2,1,4,256]{5,4,3,2,1,0:T(4,128)(2,1)S(1)}, bf16[3,3,2,1,4,256]{5,4,3,2,1,0:T(4,128)(2,1)S(1)}, u32[]{:S(2)}, u32[]{:S(2)}) collective-permute-start(bf16[3,3,2,1,4,256]{5,4,3,2,1,0:T(4,128)(2,1)S(1)} %fusion.8), channel_id=1, source_target_pairs={{0,4},{4,8},{8,12},{12,0},{1,5},{5,9},{9,13},{13,1},{2,6},{6,10},{... | collective-permute-start | bytes 110600 | tf_op jit(solution)/shard_map/ppermute | solution.py:25
  12.8 5.1 %copy-start.9 = (f32[4,3,2,1,1,256]{5,4,3,2,1,0:T(1,128)}, f32[4,3,2,1,1,256]{5,4,3,2,1,0:T(1,128)S(1)}, u32[]{:S(2)}) copy-start(f32[4,3,2,1,1,256]{5,4,3,2,1,0:T(1,128)S(1)} %collective-permute-done.3.refs_5_) | copy-start | bytes 73732
  17.9 0.6 copy-start.7
  17.9 0.6 %copy-start.3 = (bf16[4,3,2,1,4,256]{5,4,3,2,1,0:T(4,128)(2,1)}, bf16[4,3,2,1,4,256]{5,4,3,2,1,0:T(4,128)(2,1)S(1)}, u32[]{:S(2)}) copy-start(bf16[4,3,2,1,4,256]{5,4,3,2,1,0:T(4,128)(2,1)S(1)} %collective-permute-done.refs_2_) | copy-start | bytes 147460
  17.9 0.6 %copy-start.4 = (bf16[4,3,2,1,4,256]{5,4,3,2,1,0:T(4,128)(2,1)}, bf16[4,3,2,1,4,256]{5,4,3,2,1,0:T(4,128)(2,1)S(1)}, u32[]{:S(2)}) copy-start(bf16[4,3,2,1,4,256]{5,4,3,2,1,0:T(4,128)(2,1)S(1)} %collective-permute-done.1.refs_3_) | copy-start | bytes 147460
  18.6 0.6 %copy-start.2 = (f32[3,3,2,4,1,256]{5,4,3,2,1,0:T(1,128)}, f32[3,3,2,4,1,256]{5,4,3,2,1,0:T(1,128)S(1)}, u32[]{:S(2)}) copy-start(f32[3,3,2,4,1,256]{5,4,3,2,1,0:T(1,128)S(1)} %collective-permute-done.5.refs_8_) | copy-start | bytes 221188
  29.4 9.5 %collective-permute-start.8 = (f32[2,2,3,2,4,2,256]{6,5,4,3,2,1,0:T(2,128)}, f32[2,2,3,2,4,2,256]{6,5,4,3,2,1,0:T(2,128)S(1)}, u32[]{:S(2)}, u32[]{:S(2)}) collective-permute-start(f32[2,2,3,2,4,2,256]{6,5,4,3,2,1,0:T(2,128)} %get-tuple-element.13), channel_id=1, source_target_pairs={{0,1},{1,2},{2,3},{3,0},{4,5},{5,6},{6,7},{7,4},{8,9},{9,10},{10,1... | collective-permute-start | bytes 589832 | tf_op jit(solution)/shard_map/ppermute | solution.py:25
  30.0 8.9 %collective-permute-start.9 = (f32[2,2,3,2,4,2,256]{6,5,4,3,2,1,0:T(2,128)}, f32[2,2,3,2,4,2,256]{6,5,4,3,2,1,0:T(2,128)S(1)}, u32[]{:S(2)}, u32[]{:S(2)}) collective-permute-start(f32[2,2,3,2,4,2,256]{6,5,4,3,2,1,0:T(2,128)} %get-tuple-element.14), channel_id=1, source_target_pairs={{0,3},{1,0},{2,1},{3,2},{4,7},{5,4},{6,5},{7,6},{8,11},{9,8},{10,9... | collective-permute-start | bytes 589832 | tf_op jit(solution)/shard_map/ppermute | solution.py:25
  31.2 7.7 %collective-permute-start.6 = (bf16[2,2,3,2,1,8,256]{6,5,4,3,2,1,0:T(8,128)(2,1)}, bf16[2,2,3,2,1,8,256]{6,5,4,3,2,1,0:T(8,128)(2,1)S(1)}, u32[]{:S(2)}, u32[]{:S(2)}) collective-permute-start(bf16[2,2,3,2,1,8,256]{6,5,4,3,2,1,0:T(8,128)(2,1)} %get-tuple-element.11), channel_id=1, source_target_pairs={{0,4},{4,8},{8,12},{12,0},{1,5},{5,9},{9,13},{13,1},{2,6},{6,10},{... | collective-permute-start | bytes 294920 | tf_op jit(solution)/shard_map/ppermute | solution.py:25
  31.2 7.7 %collective-permute-start.7 = (bf16[2,2,3,2,1,8,256]{6,5,4,3,2,1,0:T(8,128)(2,1)}, bf16[2,2,3,2,1,8,256]{6,5,4,3,2,1,0:T(8,128)(2,1)S(1)}, u32[]{:S(2)}, u32[]{:S(2)}) collective-permute-start(bf16[2,2,3,2,1,8,256]{6,5,4,3,2,1,0:T(8,128)(2,1)} %get-tuple-element.12), channel_id=1, source_target_pairs={{0,12},{4,0},{8,4},{12,8},{1,13},{5,1},{9,5},{13,9},{2,14},{6,2},{... | collective-permute-start | bytes 294920 | tf_op jit(solution)/shard_map/ppermute | solution.py:25
  35.2 19.0 %collective-permute-start.10 = (bf16[4,16,3,2,4,256]{5,1,4,2,3,0:T(8,128)(2,1)S(1)}, bf16[4,16,3,2,4,256]{5,1,4,2,3,0:T(8,128)(2,1)S(1)}, u32[]{:S(2)}, u32[]{:S(2)}) collective-permute-start(bf16[4,16,3,2,4,256]{5,1,4,2,3,0:T(8,128)(2,1)S(1)} %copy.16), channel_id=1, source_target_pairs={{0,16},{16,0},{1,17},{17,1},{2,18},{18,2},{3,19},{19,3},{4,20},{20... | collective-permute-start | bytes 2359304 | tf_op jit(solution)/shard_map/ppermute | solution.py:29
  38.8 0.6 %copy-start.10 = (bf16[2,2,3,2,1,8,256]{6,5,4,3,2,1,0:T(8,128)(2,1)}, bf16[2,2,3,2,1,8,256]{6,5,4,3,2,1,0:T(8,128)(2,1)S(1)}, u32[]{:S(2)}) copy-start(bf16[2,2,3,2,1,8,256]{6,5,4,3,2,1,0:T(8,128)(2,1)S(1)} %collective-permute-done.6.refs_10_) | copy-start | bytes 294916
  38.9 0.7 %copy-start.11 = (bf16[2,2,3,2,1,8,256]{6,5,4,3,2,1,0:T(8,128)(2,1)}, bf16[2,2,3,2,1,8,256]{6,5,4,3,2,1,0:T(8,128)(2,1)S(1)}, u32[]{:S(2)}) copy-start(bf16[2,2,3,2,1,8,256]{6,5,4,3,2,1,0:T(8,128)(2,1)S(1)} %collective-permute-done.7.refs_11_) | copy-start | bytes 294916
  38.9 0.8 %copy-start.5 = (f32[2,2,3,2,4,2,256]{6,5,4,3,2,1,0:T(2,128)}, f32[2,2,3,2,4,2,256]{6,5,4,3,2,1,0:T(2,128)S(1)}, u32[]{:S(2)}) copy-start(f32[2,2,3,2,4,2,256]{6,5,4,3,2,1,0:T(2,128)S(1)} %collective-permute-done.8.refs_12_) | copy-start | bytes 589828
  38.9 0.8 %copy-start.6 = (f32[2,2,3,2,4,2,256]{6,5,4,3,2,1,0:T(2,128)}, f32[2,2,3,2,4,2,256]{6,5,4,3,2,1,0:T(2,128)S(1)}, u32[]{:S(2)}) copy-start(f32[2,2,3,2,4,2,256]{6,5,4,3,2,1,0:T(2,128)S(1)} %collective-permute-done.9.refs_13_) | copy-start | bytes 589828
  49.6 4.5 %copy-start.1 = (bf16[2,4,3,2,4,2,4,256]{7,6,5,4,3,2,1,0:T(4,128)(2,1)S(1)}, bf16[2,4,3,2,4,2,4,256]{7,6,5,4,3,2,1,0:T(4,128)(2,1)}, u32[]{:S(2)}) copy-start(bf16[2,4,3,2,4,2,4,256]{7,6,5,4,3,2,1,0:T(4,128)(2,1)} %shard_map.47) | copy-start | bytes 2359300
  56.0 1.4 %collective-permute-start.11 = (f32[2,4,4,2,4,8]{5,4,3,2,1,0:T(4,128)S(1)}, f32[2,4,4,2,4,8]{5,4,3,2,1,0:T(4,128)S(1)}, u32[]{:S(2)}, u32[]{:S(2)}) collective-permute-start(f32[2,4,4,2,4,8]{5,4,3,2,1,0:T(4,128)S(1)} %select_bitcast_fusion), channel_id=1, source_target_pairs={{0,1},{1,0},{2,3},{3,2},{4,5},{5,4},{6,7},{7,6},{8,9},{9,8},{10,11... | collective-permute-start | bytes 24584 | tf_op jit(solution)/shard_map/ppermute | solution.py:307
  57.5 4.3 %collective-permute-start.12 = (f32[1,4,4,2,4,8]{5,4,3,2,1,0:T(4,128)S(1)}, f32[1,4,4,2,4,8]{5,4,3,2,1,0:T(4,128)S(1)}, u32[]{:S(2)}, u32[]{:S(2)}) collective-permute-start(f32[1,4,4,2,4,8]{5,4,3,2,1,0:T(4,128)S(1)} %select_bitcast_fusion.1), channel_id=1, source_target_pairs={{0,2},{1,3},{2,0},{3,1},{4,6},{5,7},{6,4},{7,5},{8,10},{9,11},{10,... | collective-permute-start | bytes 12296 | tf_op jit(solution)/shard_map/ppermute | solution.py:307

commit v11 on v9

--- a/solution.py
+++ b/solution.py
@@ -37,6 +37,16 @@
     if ci == 1:
         return -im, re
     return im, -re
+
+
+def add_phase(are, aim, re, im, cr, ci):
+    if ci == 0:
+        if cr == 1:
+            return are + re, aim + im
+        return are - re, aim - im
+    if ci == 1:
+        return are - im, aim + re
+    return are + im, aim - re
 
 
 def hop_kernel(first, *refs):
@@ -161,8 +171,7 @@
                     for c in range(3):
                         sre = shifted(s, c, 0, mu, stride)
                         sim = shifted(s, c, 1, mu, stride)
-                        pre, pim = times_phase(shifted(p, c, 0, mu, stride), shifted(p, c, 1, mu, stride), cr, ci)
-                        colours.append((sre + pre, sim + pim))
+                        colours.append(add_phase(sre, sim, shifted(p, c, 0, mu, stride), shifted(p, c, 1, mu, stride), cr, ci))
                     half.append(colours)
                 if stride == 1:
                     links = [[(u8[mu, a, b, 0, t], u8[mu, a, b, 1, t]) for b in range(3)] for a in range(3)]
@@ -185,11 +194,14 @@
                                 tim = lre * him - lim * hre
                             sum_re = tre if sum_re is None else sum_re + tre
                             sum_im = tim if sum_im is None else sum_im + tim
-                        for row, (vre, vim) in ((s, (sum_re, sum_im)), (p, times_phase(sum_re, sum_im, cpr, cpi))):
-                            if acc[row][a][0] is None:
-                                acc[row][a] = [vre, vim]
-                            else:
-                                acc[row][a] = [acc[row][a][0] + vre, acc[row][a][1] + vim]
+                        if acc[s][a][0] is None:
+                            acc[s][a] = [sum_re, sum_im]
+                        else:
+                            acc[s][a] = [acc[s][a][0] + sum_re, acc[s][a][1] + sum_im]
+                        if acc[p][a][0] is None:
+                            acc[p][a] = list(times_phase(sum_re, sum_im, cpr, cpi))
+                        else:
+                            acc[p][a] = list(add_phase(acc[p][a][0], acc[p][a][1], sum_re, sum_im, cpr, cpi))
         for s in range(4):
             for c in range(3):
                 for ri in range(2):

time: 60 us -> 60.1 us (level)
  no operation moved by 1% of the time
where the time goes in v11:
time: 60.1 us; the launch traced here: 59.8 us
  Pallas kernels  20.2 us (34%)
  starting transfers between devices  14.9 us (25%)
  waiting for transfers between devices  12.1 us (20%)
  local copies, waits for them, and re-layouts  6.8 us (11%)
  matrix products  3.73 us (6%)
  other arithmetic  1.66 us (3%)
    pallas_call x2, Pallas kernels, hopping_step(): pl.pallas_call(functools.partial(hop_kernel, first), grid=(H,), in_specs=...  20.2 us
    ppermute x10, starting transfers between devices, passed_along(): return lax.ppermute(value, axis, pairs)  12.6 us
    ppermute x10, waiting for transfers between devices, passed_along(): return lax.ppermute(value, axis, pairs)  5.53 us
    ppermute x2, waiting for transfers between devices, reduce_scatter_sa(): x = keep + lax.ppermute(send, 'sa', [(j, j ^ d) for j in range(n)])  5.11 us
    dot_general x2, matrix products, intersection_part(): jnp.einsum('tvcazs,hqcbtgzs->hgqabtv', vector_piece, rounded, preferred_e...  3.73 us
    unnamed x27, local copies, waits for them, and re-layouts  2.31 us
    ppermute x1, starting transfers between devices, from_partner(): lax.ppermute(x, axis, [(i, i ^ 1 << stride) for i in range(lax.axis_size(...  1.73 us
    ppermute x1, waiting for transfers between devices, from_partner(): lax.ppermute(x, axis, [(i, i ^ 1 << stride) for i in range(lax.axis_size(...  1.44 us
  transfers between devices with their start and end apart: 13, of which 6 were waited for; matrix products, arithmetic and copies ran while one was open for 13% of the time, Pallas kernels for 17%

profile of v11, /device:TPU:0, one launch (start us, length us, event | category | flops | bytes accessed | tf_op | source)
XLA Modules:
  0.0 59.8 jit_solution(4087968242939346318)
XLA Ops:
  0.0 3.1 %collective-permute-start = (f32[4,3,2,1,4,256]{5,4,3,2,1,0:T(4,128)}, f32[4,3,2,1,4,256]{5,4,3,2,1,0:T(4,128)S(1)}, u32[]{:S(2)}, u32[]{:S(2)}) collective-permute-start(f32[4,3,2,1,4,256]{5,4,3,2,1,0:T(4,128)} %refs_1_.3), channel_id=1, source_target_pairs={{0,4},{4,8},{8,12},{12,0},{1,5},{5,9},{9,13},{13,1},{2,6},{6,10},{... | collective-permute-start | bytes 294920 | tf_op jit(solution)/shard_map/ppermute | solution.py:25
  3.1 2.1 %collective-permute-start.1 = (f32[4,3,2,1,4,256]{5,4,3,2,1,0:T(4,128)}, f32[4,3,2,1,4,256]{5,4,3,2,1,0:T(4,128)S(1)}, u32[]{:S(2)}, u32[]{:S(2)}) collective-permute-start(f32[4,3,2,1,4,256]{5,4,3,2,1,0:T(4,128)} %refs_1_.3), channel_id=1, source_target_pairs={{0,12},{4,0},{8,4},{12,8},{1,13},{5,1},{9,5},{13,9},{2,14},{6,2},{... | collective-permute-start | bytes 294920 | tf_op jit(solution)/shard_map/ppermute | solution.py:25
  5.1 1.0 %fusion.11 = (f32[4,3,2,1,1,256]{5,4,3,2,1,0:T(1,128)S(1)}, f32[4,3,2,1,1,256]{5,4,3,2,1,0:T(1,128)S(1)}) fusion(f32[4,3,2,1,4,256]{5,4,3,2,1,0:T(4,128)} %refs_1_.3), kind=kLoop, calls=%fused_computation.39 | loop fusion | bytes 98304 | tf_op jit(solution)/shard_map/slice | solution.py:358
  6.1 0.1 collective-permute-start.2
  6.2 1.7 %collective-permute-start.3 = (f32[4,3,2,1,1,256]{5,4,3,2,1,0:T(1,128)S(1)}, f32[4,3,2,1,1,256]{5,4,3,2,1,0:T(1,128)S(1)}, u32[]{:S(2)}, u32[]{:S(2)}) collective-permute-start(f32[4,3,2,1,1,256]{5,4,3,2,1,0:T(1,128)S(1)} %get-tuple-element.21), channel_id=1, source_target_pairs={{0,3},{1,0},{2,1},{3,2},{4,7},{5,4},{6,5},{7,6},{8,11},{9,8},{10,9... | collective-permute-start | bytes 73736 | tf_op jit(solution)/shard_map/ppermute | solution.py:25
  7.9 0.9 %slice_bitcast_fusion.1 = f32[3,3,2,1,4,256]{5,4,3,2,1,0:T(4,128)S(1)} fusion(f32[4,3,3,2,4,4,256]{6,5,4,3,2,1,0:T(4,128)} %refs_6_.3), kind=kLoop, calls=%fused_computation.13 | loop fusion | bytes 147456 | tf_op jit(solution)/shard_map/squeeze | solution.py:362
  8.8 1.0 %slice_bitcast_fusion = f32[3,3,2,4,1,256]{5,4,3,2,1,0:T(1,128)S(1)} fusion(f32[4,3,3,2,4,4,256]{6,5,4,3,2,1,0:T(4,128)} %refs_6_.3), kind=kLoop, calls=%fused_computation.12 | loop fusion | bytes 147456 | tf_op jit(solution)/shard_map/squeeze | solution.py:363
  9.9 0.7 %dynamic_slice.3 = s32[4]{0:T(128)S(1)} dynamic-slice(s32[8]{0:T(128)} %param.6, s32[]{:T(128)S(6)} %select_n.122), dynamic_slice_sizes={4} | dynamic-slice | bytes 36 | tf_op jit(solution)/shard_map/dynamic_slice | solution.py:347
  10.7 0.1 compare_convert_fusion
  10.7 0.1 fusion.8
  10.8 0.1 reshape.211
  10.9 0.1 reshape.210
  11.0 0.1 collective-permute-start.5
  11.1 0.6 pad_maximum_fusion.1.refs_0_
  11.7 3.3 %collective-permute-done.4.refs_7_ = f32[3,3,2,1,4,256]{5,4,3,2,1,0:T(4,128)S(1)} collective-permute-done((f32[3,3,2,1,4,256]{5,4,3,2,1,0:T(4,128)S(1)}, f32[3,3,2,1,4,256]{5,4,3,2,1,0:T(4,128)S(1)}, u32[]{:S(2)}, u32[]{:S(2)}) %collective-permute-start.4) | collective-permute-done | bytes 73760 | tf_op jit(solution)/shard_map/ppermute | solution.py:25
  15.0 0.6 copy-done.4
  15.6 0.1 copy-done.2
  15.7 0.6 %copy-done.3 = f32[4,3,2,1,4,256]{5,4,3,2,1,0:T(4,128)} copy-done((f32[4,3,2,1,4,256]{5,4,3,2,1,0:T(4,128)}, f32[4,3,2,1,4,256]{5,4,3,2,1,0:T(4,128)S(1)}, u32[]{:S(2)}) %copy-start.3) | copy-done | bytes 98328
  16.3 10.2 %shard_map.46 = (f32[2,4,3,2,4,8,256]{6,5,4,3,2,1,0:T(8,128)}, bf16[2,2,3,2,1,8,256]{6,5,4,3,2,1,0:T(8,128)(2,1)}, bf16[2,2,3,2,1,8,256]{6,5,4,3,2,1,0:T(8,128)(...) custom-call(f32[42]{0:T(128)} %pad_maximum_fusion.1.refs_0_, f32[4,3,2,1,4,256]{5,4,3,2,1,0:T(4,128)} %refs_1_.3, ...), custom_call_target="tpu_custom_call" | custom-call | tf_op jit(solution)/shard_map/pallas_call | solution.py:293
  26.6 1.7 %collective-permute-start.9 = (f32[2,2,3,2,4,2,256]{6,5,4,3,2,1,0:T(2,128)}, f32[2,2,3,2,4,2,256]{6,5,4,3,2,1,0:T(2,128)S(1)}, u32[]{:S(2)}, u32[]{:S(2)}) collective-permute-start(f32[2,2,3,2,4,2,256]{6,5,4,3,2,1,0:T(2,128)} %get-tuple-element.14), channel_id=1, source_target_pairs={{0,3},{1,0},{2,1},{3,2},{4,7},{5,4},{6,5},{7,6},{8,11},{9,8},{10,9... | collective-permute-start | bytes 589832 | tf_op jit(solution)/shard_map/ppermute | solution.py:25
  28.3 1.3 %collective-permute-start.6 = (bf16[2,2,3,2,1,8,256]{6,5,4,3,2,1,0:T(8,128)(2,1)}, bf16[2,2,3,2,1,8,256]{6,5,4,3,2,1,0:T(8,128)(2,1)S(1)}, u32[]{:S(2)}, u32[]{:S(2)}) collective-permute-start(bf16[2,2,3,2,1,8,256]{6,5,4,3,2,1,0:T(8,128)(2,1)} %get-tuple-element.11), channel_id=1, source_target_pairs={{0,4},{4,8},{8,12},{12,0},{1,5},{5,9},{9,13},{13,1},{2,6},{6,10},{... | collective-permute-start | bytes 294920 | tf_op jit(solution)/shard_map/ppermute | solution.py:25
  29.6 2.5 %collective-permute-start.7 = (bf16[2,2,3,2,1,8,256]{6,5,4,3,2,1,0:T(8,128)(2,1)}, bf16[2,2,3,2,1,8,256]{6,5,4,3,2,1,0:T(8,128)(2,1)S(1)}, u32[]{:S(2)}, u32[]{:S(2)}) collective-permute-start(bf16[2,2,3,2,1,8,256]{6,5,4,3,2,1,0:T(8,128)(2,1)} %get-tuple-element.12), channel_id=1, source_target_pairs={{0,12},{4,0},{8,4},{12,8},{1,13},{5,1},{9,5},{13,9},{2,14},{6,2},{... | collective-permute-start | bytes 294920 | tf_op jit(solution)/shard_map/ppermute | solution.py:25
  32.2 0.2 copy.16
  32.3 1.7 %collective-permute-start.10 = (bf16[4,16,3,2,4,256]{5,1,4,2,3,0:T(8,128)(2,1)S(1)}, bf16[4,16,3,2,4,256]{5,1,4,2,3,0:T(8,128)(2,1)S(1)}, u32[]{:S(2)}, u32[]{:S(2)}) collective-permute-start(bf16[4,16,3,2,4,256]{5,1,4,2,3,0:T(8,128)(2,1)S(1)} %copy.16), channel_id=1, source_target_pairs={{0,16},{16,0},{1,17},{17,1},{2,18},{18,2},{3,19},{19,3},{4,20},{20... | collective-permute-start | bytes 2359304 | tf_op jit(solution)/shard_map/ppermute | solution.py:29
  34.1 1.7 %collective-permute-done.6.refs_10_ = bf16[2,2,3,2,1,8,256]{6,5,4,3,2,1,0:T(8,128)(2,1)S(1)} collective-permute-done((bf16[2,2,3,2,1,8,256]{6,5,4,3,2,1,0:T(8,128)(2,1)}, bf16[2,2,3,2,1,8,256]{6,5,4,3,2,1,0:T(8,128)(2,1)S(1)}, u32[]{:S(2)}, u32[]{:S(2)}) %collective-permute-start.6) | collective-permute-done | bytes 98336 | tf_op jit(solution)/shard_map/ppermute | solution.py:25
  35.8 0.5 collective-permute-done.7.refs_11_
  36.3 0.2 copy-done.10
  36.5 0.4 copy-done.11
  36.9 0.1 copy-done.6
  37.0 0.1 copy-done.7
  37.1 10.0 %shard_map.47 = bf16[2,4,3,2,4,2,4,256]{7,6,5,4,3,2,1,0:T(4,128)(2,1)} custom-call(f32[42]{0:T(128)} %pad_maximum_fusion.1.refs_0_, f32[4,3,2,1,4,256]{5,4,3,2,1,0:T(4,128)} %refs_1_.3, f32[4,3,2,1,4,256]{5,4,3,2,1,0:T(4,128)} %copy-done.2, f32[4,3,2,1,4,256]{5,4,3,2,1,0:T(4,128)} %copy-done.3, f32[4,3,2,1,1,256]{5,4,3,2,1,0:T(1,128)} %copy-done.8, ...), custom_call_target="tpu_custom_call" | custom-call | tf_op jit(solution)/shard_map/pallas_call | solution.py:293
  47.1 2.5 %convolution_bitcast_fusion.1 = f32[2,2,4,2,2,4,16]{6,2,3,1,4,0,5:T(4,128)S(1)} fusion(bf16[4,16,3,2,4,256,1,1,1]{5,4,3,2,1,0,8,7,6:T(4,128)(2,1)S(1)} %bitcast.73, bf16[2,4,3,2,4,2,4,256,1]{7,6,5,4,3,2,1,0,8:T(4,128)(2,1)} %bitcast.71), kind=kOutput, calls=%fused_computation.1 | convolution fusion | flops 25165824 | bytes 1589248 | tf_op jit(solution)/shard_map/tvcazs,hqcbtgzs->hgqabtv/dot_general | solution.py:325
  49.6 0.1 copy.13
  49.7 0.1 add.99
  49.8 0.1 sub.39
  50.0 1.4 %collective-permute-done.10 = bf16[4,16,3,2,4,256]{5,1,4,2,3,0:T(8,128)(2,1)S(1)} collective-permute-done((bf16[4,16,3,2,4,256]{5,1,4,2,3,0:T(8,128)(2,1)S(1)}, bf16[4,16,3,2,4,256]{5,1,4,2,3,0:T(8,128)(2,1)S(1)}, u32[]{:S(2)}, u32[]{:S(2)}) %collective-permute-start.10) | collective-permute-done | bytes 786464 | tf_op jit(solution)/shard_map/ppermute | solution.py:29
  51.4 1.3 %convolution_bitcast_fusion = f32[2,2,4,2,2,4,16]{6,2,3,1,4,0,5:T(4,128)S(1)} fusion(bf16[4,16,3,2,4,256]{5,1,4,2,3,0:T(8,128)(2,1)S(1)} %collective-permute-done.10, bf16[2,4,3,2,4,2,4,256,1]{7,6,5,4,3,2,1,0,8:T(4,128)(2,1)S(1)} %bitcast.72), kind=kOutput, calls=%fused_computation | convolution fusion | flops 25165824 | bytes 1589248 | tf_op jit(solution)/shard_map/tvcazs,hqcbtgzs->hgqabtv/dot_general | solution.py:325
  52.7 0.1 copy.18
  52.8 0.1 add.101
  52.9 0.1 sub.41
  53.1 0.1 copy_dynamic-update-slice_fusion
  53.2 0.1 pad_maximum_fusion
  53.3 0.1 collective-permute-start.11
  53.4 1.3 %collective-permute-done.11 = f32[2,4,4,2,4,8]{5,4,3,2,1,0:T(4,128)S(1)} collective-permute-done((f32[2,4,4,2,4,8]{5,4,3,2,1,0:T(4,128)S(1)}, f32[2,4,4,2,4,8]{5,4,3,2,1,0:T(4,128)S(1)}, u32[]{:S(2)}, u32[]{:S(2)}) %collective-permute-start.11) | collective-permute-done | bytes 8224 | tf_op jit(solution)/shard_map/ppermute | solution.py:319
  54.7 0.1 fusion.6
  54.8 0.5 collective-permute-start.12
  55.3 3.8 %collective-permute-done.12 = f32[1,4,4,2,4,8]{5,4,3,2,1,0:T(4,128)S(1)} collective-permute-done((f32[1,4,4,2,4,8]{5,4,3,2,1,0:T(4,128)S(1)}, f32[1,4,4,2,4,8]{5,4,3,2,1,0:T(4,128)S(1)}, u32[]{:S(2)}, u32[]{:S(2)}) %collective-permute-start.12) | collective-permute-done | bytes 4128 | tf_op jit(solution)/shard_map/ppermute | solution.py:319
  59.1 0.7 %fusion.7 = f32[4,4,2,4,8]{4,3,2,1,0:T(4,128)} fusion(f32[1,4,4,2,4,8]{5,4,3,2,1,0:T(4,128)S(1)} %collective-permute-done.12, f32[1,2,4,4,2,4,8]{6,5,4,3,2,1,0:T(4,128)S(1)} %fusion.6, pred[]{:T(512)S(6)} %eq.53), kind=kLoop, calls=%fused_computation.15 | loop fusion | flops 2048 | bytes 16385 | tf_op jit(solution)/shard_map/squeeze | solution.py:321
  (35 shorter events, 0.3 us)
Async XLA Ops:
  0.0 32.2 %copy-start.1 = (bf16[4,16,3,2,4,256]{5,4,3,2,1,0:T(4,128)(2,1)S(1)}, bf16[4,16,3,2,4,256]{5,4,3,2,1,0:T(4,128)(2,1)}, u32[]{:S(2)}) copy-start(bf16[4,16,3,2,4,256]{5,4,3,2,1,0:T(4,128)(2,1)} %param.7) | copy-start | bytes 2359300
  0.0 15.0 %collective-permute-start = (f32[4,3,2,1,4,256]{5,4,3,2,1,0:T(4,128)}, f32[4,3,2,1,4,256]{5,4,3,2,1,0:T(4,128)S(1)}, u32[]{:S(2)}, u32[]{:S(2)}) collective-permute-start(f32[4,3,2,1,4,256]{5,4,3,2,1,0:T(4,128)} %refs_1_.3), channel_id=1, source_target_pairs={{0,4},{4,8},{8,12},{12,0},{1,5},{5,9},{9,13},{13,1},{2,6},{6,10},{... | collective-permute-start | bytes 294920 | tf_op jit(solution)/shard_map/ppermute | solution.py:25
  3.1 12.0 %collective-permute-start.1 = (f32[4,3,2,1,4,256]{5,4,3,2,1,0:T(4,128)}, f32[4,3,2,1,4,256]{5,4,3,2,1,0:T(4,128)S(1)}, u32[]{:S(2)}, u32[]{:S(2)}) collective-permute-start(f32[4,3,2,1,4,256]{5,4,3,2,1,0:T(4,128)} %refs_1_.3), channel_id=1, source_target_pairs={{0,12},{4,0},{8,4},{12,8},{1,13},{5,1},{9,5},{13,9},{2,14},{6,2},{... | collective-permute-start | bytes 294920 | tf_op jit(solution)/shard_map/ppermute | solution.py:25
  6.1 4.8 %collective-permute-start.2 = (f32[4,3,2,1,1,256]{5,4,3,2,1,0:T(1,128)S(1)}, f32[4,3,2,1,1,256]{5,4,3,2,1,0:T(1,128)S(1)}, u32[]{:S(2)}, u32[]{:S(2)}) collective-permute-start(f32[4,3,2,1,1,256]{5,4,3,2,1,0:T(1,128)S(1)} %get-tuple-element.22), channel_id=1, source_target_pairs={{0,1},{1,2},{2,3},{3,0},{4,5},{5,6},{6,7},{7,4},{8,9},{9,10},{10,1... | collective-permute-start | bytes 73736 | tf_op jit(solution)/shard_map/ppermute | solution.py:25
  6.2 5.5 %collective-permute-start.3 = (f32[4,3,2,1,1,256]{5,4,3,2,1,0:T(1,128)S(1)}, f32[4,3,2,1,1,256]{5,4,3,2,1,0:T(1,128)S(1)}, u32[]{:S(2)}, u32[]{:S(2)}) collective-permute-start(f32[4,3,2,1,1,256]{5,4,3,2,1,0:T(1,128)S(1)} %get-tuple-element.21), channel_id=1, source_target_pairs={{0,3},{1,0},{2,1},{3,2},{4,7},{5,4},{6,5},{7,6},{8,11},{9,8},{10,9... | collective-permute-start | bytes 73736 | tf_op jit(solution)/shard_map/ppermute | solution.py:25
  8.8 6.2 %collective-permute-start.4 = (f32[3,3,2,1,4,256]{5,4,3,2,1,0:T(4,128)S(1)}, f32[3,3,2,1,4,256]{5,4,3,2,1,0:T(4,128)S(1)}, u32[]{:S(2)}, u32[]{:S(2)}) collective-permute-start(f32[3,3,2,1,4,256]{5,4,3,2,1,0:T(4,128)S(1)} %slice_bitcast_fusion.1), channel_id=1, source_target_pairs={{0,4},{4,8},{8,12},{12,0},{1,5},{5,9},{9,13},{13,1},{2,6},{6,10},{... | collective-permute-start | bytes 221192 | tf_op jit(solution)/shard_map/ppermute | solution.py:25
  11.0 4.1 %copy-start.8 = (f32[4,3,2,1,1,256]{5,4,3,2,1,0:T(1,128)}, f32[4,3,2,1,1,256]{5,4,3,2,1,0:T(1,128)S(1)}, u32[]{:S(2)}) copy-start(f32[4,3,2,1,1,256]{5,4,3,2,1,0:T(1,128)S(1)} %collective-permute-done.2.refs_4_) | copy-start | bytes 73732
  11.0 4.0 %collective-permute-start.5 = (f32[3,3,2,4,1,256]{5,4,3,2,1,0:T(1,128)S(1)}, f32[3,3,2,4,1,256]{5,4,3,2,1,0:T(1,128)S(1)}, u32[]{:S(2)}, u32[]{:S(2)}) collective-permute-start(f32[3,3,2,4,1,256]{5,4,3,2,1,0:T(1,128)S(1)} %slice_bitcast_fusion), channel_id=1, source_target_pairs={{0,1},{1,2},{2,3},{3,0},{4,5},{5,6},{6,7},{7,4},{8,9},{9,10},{10,1... | collective-permute-start | bytes 221192 | tf_op jit(solution)/shard_map/ppermute | solution.py:25
  11.7 3.4 %copy-start.9 = (f32[4,3,2,1,1,256]{5,4,3,2,1,0:T(1,128)}, f32[4,3,2,1,1,256]{5,4,3,2,1,0:T(1,128)S(1)}, u32[]{:S(2)}) copy-start(f32[4,3,2,1,1,256]{5,4,3,2,1,0:T(1,128)S(1)} %collective-permute-done.3.refs_5_) | copy-start | bytes 73732
  15.0 0.6 %copy-start.4 = (f32[3,3,2,1,4,256]{5,4,3,2,1,0:T(4,128)}, f32[3,3,2,1,4,256]{5,4,3,2,1,0:T(4,128)S(1)}, u32[]{:S(2)}) copy-start(f32[3,3,2,1,4,256]{5,4,3,2,1,0:T(4,128)S(1)} %collective-permute-done.4.refs_7_) | copy-start | bytes 221188
  15.0 0.6 %copy-start.5 = (f32[3,3,2,4,1,256]{5,4,3,2,1,0:T(1,128)}, f32[3,3,2,4,1,256]{5,4,3,2,1,0:T(1,128)S(1)}, u32[]{:S(2)}) copy-start(f32[3,3,2,4,1,256]{5,4,3,2,1,0:T(1,128)S(1)} %collective-permute-done.5.refs_8_) | copy-start | bytes 221188
  15.0 0.7 %copy-start.2 = (f32[4,3,2,1,4,256]{5,4,3,2,1,0:T(4,128)}, f32[4,3,2,1,4,256]{5,4,3,2,1,0:T(4,128)S(1)}, u32[]{:S(2)}) copy-start(f32[4,3,2,1,4,256]{5,4,3,2,1,0:T(4,128)S(1)} %collective-permute-done.refs_2_) | copy-start | bytes 294916
  15.7 0.6 %copy-start.3 = (f32[4,3,2,1,4,256]{5,4,3,2,1,0:T(4,128)}, f32[4,3,2,1,4,256]{5,4,3,2,1,0:T(4,128)S(1)}, u32[]{:S(2)}) copy-start(f32[4,3,2,1,4,256]{5,4,3,2,1,0:T(4,128)S(1)} %collective-permute-done.1.refs_3_) | copy-start | bytes 294916
  26.6 9.7 %collective-permute-start.8 = (f32[2,2,3,2,4,2,256]{6,5,4,3,2,1,0:T(2,128)}, f32[2,2,3,2,4,2,256]{6,5,4,3,2,1,0:T(2,128)S(1)}, u32[]{:S(2)}, u32[]{:S(2)}) collective-permute-start(f32[2,2,3,2,4,2,256]{6,5,4,3,2,1,0:T(2,128)} %get-tuple-element.13), channel_id=1, source_target_pairs={{0,1},{1,2},{2,3},{3,0},{4,5},{5,6},{6,7},{7,4},{8,9},{9,10},{10,1... | collective-permute-start | bytes 589832 | tf_op jit(solution)/shard_map/ppermute | solution.py:25
  26.6 9.7 %collective-permute-start.9 = (f32[2,2,3,2,4,2,256]{6,5,4,3,2,1,0:T(2,128)}, f32[2,2,3,2,4,2,256]{6,5,4,3,2,1,0:T(2,128)S(1)}, u32[]{:S(2)}, u32[]{:S(2)}) collective-permute-start(f32[2,2,3,2,4,2,256]{6,5,4,3,2,1,0:T(2,128)} %get-tuple-element.14), channel_id=1, source_target_pairs={{0,3},{1,0},{2,1},{3,2},{4,7},{5,4},{6,5},{7,6},{8,11},{9,8},{10,9... | collective-permute-start | bytes 589832 | tf_op jit(solution)/shard_map/ppermute | solution.py:25
  28.3 7.5 %collective-permute-start.6 = (bf16[2,2,3,2,1,8,256]{6,5,4,3,2,1,0:T(8,128)(2,1)}, bf16[2,2,3,2,1,8,256]{6,5,4,3,2,1,0:T(8,128)(2,1)S(1)}, u32[]{:S(2)}, u32[]{:S(2)}) collective-permute-start(bf16[2,2,3,2,1,8,256]{6,5,4,3,2,1,0:T(8,128)(2,1)} %get-tuple-element.11), channel_id=1, source_target_pairs={{0,4},{4,8},{8,12},{12,0},{1,5},{5,9},{9,13},{13,1},{2,6},{6,10},{... | collective-permute-start | bytes 294920 | tf_op jit(solution)/shard_map/ppermute | solution.py:25
  29.6 6.6 %collective-permute-start.7 = (bf16[2,2,3,2,1,8,256]{6,5,4,3,2,1,0:T(8,128)(2,1)}, bf16[2,2,3,2,1,8,256]{6,5,4,3,2,1,0:T(8,128)(2,1)S(1)}, u32[]{:S(2)}, u32[]{:S(2)}) collective-permute-start(bf16[2,2,3,2,1,8,256]{6,5,4,3,2,1,0:T(8,128)(2,1)} %get-tuple-element.12), channel_id=1, source_target_pairs={{0,12},{4,0},{8,4},{12,8},{1,13},{5,1},{9,5},{13,9},{2,14},{6,2},{... | collective-permute-start | bytes 294920 | tf_op jit(solution)/shard_map/ppermute | solution.py:25
  32.3 19.1 %collective-permute-start.10 = (bf16[4,16,3,2,4,256]{5,1,4,2,3,0:T(8,128)(2,1)S(1)}, bf16[4,16,3,2,4,256]{5,1,4,2,3,0:T(8,128)(2,1)S(1)}, u32[]{:S(2)}, u32[]{:S(2)}) collective-permute-start(bf16[4,16,3,2,4,256]{5,1,4,2,3,0:T(8,128)(2,1)S(1)} %copy.16), channel_id=1, source_target_pairs={{0,16},{16,0},{1,17},{17,1},{2,18},{18,2},{3,19},{19,3},{4,20},{20... | collective-permute-start | bytes 2359304 | tf_op jit(solution)/shard_map/ppermute | solution.py:29
  35.8 0.7 %copy-start.10 = (bf16[2,2,3,2,1,8,256]{6,5,4,3,2,1,0:T(8,128)(2,1)}, bf16[2,2,3,2,1,8,256]{6,5,4,3,2,1,0:T(8,128)(2,1)S(1)}, u32[]{:S(2)}) copy-start(bf16[2,2,3,2,1,8,256]{6,5,4,3,2,1,0:T(8,128)(2,1)S(1)} %collective-permute-done.6.refs_10_) | copy-start | bytes 294916
  36.3 0.6 %copy-start.11 = (bf16[2,2,3,2,1,8,256]{6,5,4,3,2,1,0:T(8,128)(2,1)}, bf16[2,2,3,2,1,8,256]{6,5,4,3,2,1,0:T(8,128)(2,1)S(1)}, u32[]{:S(2)}) copy-start(bf16[2,2,3,2,1,8,256]{6,5,4,3,2,1,0:T(8,128)(2,1)S(1)} %collective-permute-done.7.refs_11_) | copy-start | bytes 294916
  36.3 0.7 %copy-start.6 = (f32[2,2,3,2,4,2,256]{6,5,4,3,2,1,0:T(2,128)}, f32[2,2,3,2,4,2,256]{6,5,4,3,2,1,0:T(2,128)S(1)}, u32[]{:S(2)}) copy-start(f32[2,2,3,2,4,2,256]{6,5,4,3,2,1,0:T(2,128)S(1)} %collective-permute-done.8.refs_12_) | copy-start | bytes 589828
  36.3 0.8 %copy-start.7 = (f32[2,2,3,2,4,2,256]{6,5,4,3,2,1,0:T(2,128)}, f32[2,2,3,2,4,2,256]{6,5,4,3,2,1,0:T(2,128)S(1)}, u32[]{:S(2)}) copy-start(f32[2,2,3,2,4,2,256]{6,5,4,3,2,1,0:T(2,128)S(1)} %collective-permute-done.9.refs_13_) | copy-start | bytes 589828
  47.1 4.3 %copy-start = (bf16[2,4,3,2,4,2,4,256]{7,6,5,4,3,2,1,0:T(4,128)(2,1)S(1)}, bf16[2,4,3,2,4,2,4,256]{7,6,5,4,3,2,1,0:T(4,128)(2,1)}, u32[]{:S(2)}) copy-start(bf16[2,4,3,2,4,2,4,256]{7,6,5,4,3,2,1,0:T(4,128)(2,1)} %shard_map.47) | copy-start | bytes 2359300
  53.3 1.4 %collective-permute-start.11 = (f32[2,4,4,2,4,8]{5,4,3,2,1,0:T(4,128)S(1)}, f32[2,4,4,2,4,8]{5,4,3,2,1,0:T(4,128)S(1)}, u32[]{:S(2)}, u32[]{:S(2)}) collective-permute-start(f32[2,4,4,2,4,8]{5,4,3,2,1,0:T(4,128)S(1)} %select_bitcast_fusion), channel_id=1, source_target_pairs={{0,1},{1,0},{2,3},{3,2},{4,5},{5,4},{6,7},{7,6},{8,9},{9,8},{10,11... | collective-permute-start | bytes 24584 | tf_op jit(solution)/shard_map/ppermute | solution.py:319
  54.8 4.3 %collective-permute-start.12 = (f32[1,4,4,2,4,8]{5,4,3,2,1,0:T(4,128)S(1)}, f32[1,4,4,2,4,8]{5,4,3,2,1,0:T(4,128)S(1)}, u32[]{:S(2)}, u32[]{:S(2)}) collective-permute-start(f32[1,4,4,2,4,8]{5,4,3,2,1,0:T(4,128)S(1)} %select_bitcast_fusion.1), channel_id=1, source_target_pairs={{0,2},{1,3},{2,0},{3,1},{4,6},{5,7},{6,4},{7,5},{8,10},{9,11},{10,... | collective-permute-start | bytes 12296 | tf_op jit(solution)/shard_map/ppermute | solution.py:319

commit v12 on v11

--- a/solution.py
+++ b/solution.py
@@ -370,11 +370,9 @@
         passed_along(z_first, "sa", -1),
     )
     rounded = hopping_step(False, scalars, noise_parts, link_parts, (spinor,) + halos)
-    own_part = intersection_part(rounded, vectors)
-    partner_part = intersection_part(rounded, partner_vectors)
-    lower_half = jnp.where(section_index == 0, own_part, partner_part)
-    upper_half = jnp.where(section_index == 0, partner_part, own_part)
-    partial_value = jnp.concatenate([lower_half, upper_half], axis=4)
+    first_half = jnp.where(section_index == 0, vectors, partner_vectors)
+    second_half = jnp.where(section_index == 0, partner_vectors, vectors)
+    partial_value = intersection_part(rounded, jnp.concatenate([first_half, second_half], axis=1))
     return reduce_scatter_sa(partial_value)
 
 

time: 60.1 us -> 61.4 us (1.022)
  matrix products: 3.73 us -> 1.47 us
  waiting for transfers between devices: 12.1 us -> 14.3 us
  local copies, waits for them, and re-layouts: 6.8 us -> 7.86 us
    ppermute x10, waiting for transfers between devices: 5.53 us -> 9.25 us  [passed_along(): return lax.ppermute(value, axis, pairs)]
    dot_general x2 -> x1, matrix products: 3.73 us -> 1.47 us  [intersection_part(): jnp.einsum('tvcazs,hqcbtgzs->hgqabtv', vector_piece, rounded, preferred_e...]
    unnamed x27, local copies, waits for them, and re-layouts: 2.31 us -> 4.28 us
    ppermute x1, waiting for transfers between devices: 1.44 us -> 0.01 us  [from_partner(): lax.ppermute(x, axis, [(i, i ^ 1 << stride) for i in range(lax.axis_size(...]
    dynamic_slice x1, local copies, waits for them, and re-layouts: 0.74 us -> 0.07 us  [local_body(): lax.dynamic_slice_in_dim(offsets, section_index * batch_rows, batch_rows)]
  transfers between devices with their start and end apart: 13 -> 13, of which waited for: 6 -> 4; matrix products, arithmetic and copies ran while one was open for 13% -> 9% of each run, Pallas kernels for 17% -> 33%
where the time goes in v12:
time: 61.4 us; the launch traced here: 61.1 us
  Pallas kernels  20.3 us (33%)
  starting transfers between devices  15 us (24%)
  waiting for transfers between devices  14.3 us (23%)
  local copies, waits for them, and re-layouts  7.86 us (13%)
  other arithmetic  1.88 us (3%)
  matrix products  1.47 us (2%)
    pallas_call x2, Pallas kernels, hopping_step(): pl.pallas_call(functools.partial(hop_kernel, first), grid=(H,), in_specs=...  20.3 us
    ppermute x10, starting transfers between devices, passed_along(): return lax.ppermute(value, axis, pairs)  12.6 us
    ppermute x10, waiting for transfers between devices, passed_along(): return lax.ppermute(value, axis, pairs)  9.25 us
    ppermute x2, waiting for transfers between devices, reduce_scatter_sa(): x = keep + lax.ppermute(send, 'sa', [(j, j ^ d) for j in range(n)])  5.08 us
    unnamed x27, local copies, waits for them, and re-layouts  4.28 us
    ppermute x1, starting transfers between devices, from_partner(): lax.ppermute(x, axis, [(i, i ^ 1 << stride) for i in range(lax.axis_size(...  1.73 us
    dot_general x1, matrix products, intersection_part(): jnp.einsum('tvcazs,hqcbtgzs->hgqabtv', vector_piece, rounded, preferred_e...  1.47 us
  transfers between devices with their start and end apart: 13, of which 4 were waited for; matrix products, arithmetic and copies ran while one was open for 9% of the time, Pallas kernels for 33%

profile of v12, /device:TPU:0, one launch (start us, length us, event | category | flops | bytes accessed | tf_op | source)
XLA Modules:
  0.0 61.1 jit_solution(479094710989822131)
XLA Ops:
  0.0 3.1 %collective-permute-start = (f32[4,3,2,1,4,256]{5,4,3,2,1,0:T(4,128)}, f32[4,3,2,1,4,256]{5,4,3,2,1,0:T(4,128)S(1)}, u32[]{:S(2)}, u32[]{:S(2)}) collective-permute-start(f32[4,3,2,1,4,256]{5,4,3,2,1,0:T(4,128)} %refs_1_.3), channel_id=1, source_target_pairs={{0,4},{4,8},{8,12},{12,0},{1,5},{5,9},{9,13},{13,1},{2,6},{6,10},{... | collective-permute-start | bytes 294920 | tf_op jit(solution)/shard_map/ppermute | solution.py:25
  3.1 2.1 %collective-permute-start.1 = (f32[4,3,2,1,4,256]{5,4,3,2,1,0:T(4,128)}, f32[4,3,2,1,4,256]{5,4,3,2,1,0:T(4,128)S(1)}, u32[]{:S(2)}, u32[]{:S(2)}) collective-permute-start(f32[4,3,2,1,4,256]{5,4,3,2,1,0:T(4,128)} %refs_1_.3), channel_id=1, source_target_pairs={{0,12},{4,0},{8,4},{12,8},{1,13},{5,1},{9,5},{13,9},{2,14},{6,2},{... | collective-permute-start | bytes 294920 | tf_op jit(solution)/shard_map/ppermute | solution.py:25
  5.1 1.0 %fusion.11 = (f32[4,3,2,1,1,256]{5,4,3,2,1,0:T(1,128)S(1)}, f32[4,3,2,1,1,256]{5,4,3,2,1,0:T(1,128)S(1)}) fusion(f32[4,3,2,1,4,256]{5,4,3,2,1,0:T(4,128)} %refs_1_.3), kind=kLoop, calls=%fused_computation.32 | loop fusion | bytes 98304 | tf_op jit(solution)/shard_map/slice | solution.py:358
  6.1 0.1 collective-permute-start.2
  6.2 1.7 %collective-permute-start.3 = (f32[4,3,2,1,1,256]{5,4,3,2,1,0:T(1,128)S(1)}, f32[4,3,2,1,1,256]{5,4,3,2,1,0:T(1,128)S(1)}, u32[]{:S(2)}, u32[]{:S(2)}) collective-permute-start(f32[4,3,2,1,1,256]{5,4,3,2,1,0:T(1,128)S(1)} %get-tuple-element.19), channel_id=1, source_target_pairs={{0,3},{1,0},{2,1},{3,2},{4,7},{5,4},{6,5},{7,6},{8,11},{9,8},{10,9... | collective-permute-start | bytes 73736 | tf_op jit(solution)/shard_map/ppermute | solution.py:25
  7.9 1.3 %copy.12 = bf16[4,16,3,2,4,256]{5,1,4,2,3,0:T(8,128)(2,1)S(1)} copy(bf16[4,16,3,2,4,256]{5,4,3,2,1,0:T(4,128)(2,1)} %param.7) | data formatting | bytes 1572864 | tf_op args[3]
  9.2 1.7 %collective-permute-start.10 = (bf16[4,16,3,2,4,256]{5,1,4,2,3,0:T(8,128)(2,1)S(1)}, bf16[4,16,3,2,4,256]{5,1,4,2,3,0:T(8,128)(2,1)S(1)}, u32[]{:S(2)}, u32[]{:S(2)}) collective-permute-start(bf16[4,16,3,2,4,256]{5,1,4,2,3,0:T(8,128)(2,1)S(1)} %copy.12), channel_id=1, source_target_pairs={{0,16},{16,0},{1,17},{17,1},{2,18},{18,2},{3,19},{19,3},{4,20},{20... | collective-permute-start | bytes 2359304 | tf_op jit(solution)/shard_map/ppermute | solution.py:29
  11.0 0.9 %slice_bitcast_fusion.1 = f32[3,3,2,1,4,256]{5,4,3,2,1,0:T(4,128)S(1)} fusion(f32[4,3,3,2,4,4,256]{6,5,4,3,2,1,0:T(4,128)} %refs_6_.3), kind=kLoop, calls=%fused_computation.13 | loop fusion | bytes 147456 | tf_op jit(solution)/shard_map/squeeze | solution.py:362
  11.9 0.1 dynamic_slice.3
  11.9 0.1 compare_convert_fusion
  12.0 1.0 %slice_bitcast_fusion = f32[3,3,2,4,1,256]{5,4,3,2,1,0:T(1,128)S(1)} fusion(f32[4,3,3,2,4,4,256]{6,5,4,3,2,1,0:T(4,128)} %refs_6_.3), kind=kLoop, calls=%fused_computation.12 | loop fusion | bytes 147456 | tf_op jit(solution)/shard_map/squeeze | solution.py:363
  13.1 0.1 fusion.7
  13.1 0.1 reshape.159
  13.2 0.1 reshape.158
  13.3 0.0 collective-permute-done.2.refs_4_
  13.3 0.0 collective-permute-start.4
  13.4 0.0 collective-permute-done.3.refs_5_
  13.4 0.1 collective-permute-start.5
  13.5 0.7 %pad_maximum_fusion.1.refs_0_ = f32[42]{0:T(128)} fusion(f32[1]{0:T(128)} %bitcast.1, f32[1]{0:T(128)} %bitcast, f32[24]{0:T(128)S(1)} %reshape.159, f32[16]{0:T(128)S(1)} %reshape.158), kind=kLoop, calls=%fused_computation.30 | loop fusion | flops 126 | bytes 336 | tf_op jit(solution)/shard_map/concatenate | solution.py:352
  14.1 5.4 %collective-permute-done.4.refs_7_ = f32[3,3,2,1,4,256]{5,4,3,2,1,0:T(4,128)S(1)} collective-permute-done((f32[3,3,2,1,4,256]{5,4,3,2,1,0:T(4,128)S(1)}, f32[3,3,2,1,4,256]{5,4,3,2,1,0:T(4,128)S(1)}, u32[]{:S(2)}, u32[]{:S(2)}) %collective-permute-start.4) | collective-permute-done | bytes 73760 | tf_op jit(solution)/shard_map/ppermute | solution.py:25
  19.5 0.0 collective-permute-done.5.refs_8_
  19.6 0.6 copy-done.4
  20.1 0.0 copy-done.5
  20.1 0.0 copy-done.2
  20.2 0.6 %copy-done.3 = f32[4,3,2,1,4,256]{5,4,3,2,1,0:T(4,128)} copy-done((f32[4,3,2,1,4,256]{5,4,3,2,1,0:T(4,128)}, f32[4,3,2,1,4,256]{5,4,3,2,1,0:T(4,128)S(1)}, u32[]{:S(2)}) %copy-start.3) | copy-done | bytes 98328
  20.8 10.2 %shard_map.46 = (f32[2,4,3,2,4,8,256]{6,5,4,3,2,1,0:T(8,128)}, bf16[2,2,3,2,1,8,256]{6,5,4,3,2,1,0:T(8,128)(2,1)}, bf16[2,2,3,2,1,8,256]{6,5,4,3,2,1,0:T(8,128)(...) custom-call(f32[42]{0:T(128)} %pad_maximum_fusion.1.refs_0_, f32[4,3,2,1,4,256]{5,4,3,2,1,0:T(4,128)} %refs_1_.3, ...), custom_call_target="tpu_custom_call" | custom-call | tf_op jit(solution)/shard_map/pallas_call | solution.py:293
  31.0 0.0 collective-permute-start.8
  31.1 1.7 %collective-permute-start.9 = (f32[2,2,3,2,4,2,256]{6,5,4,3,2,1,0:T(2,128)}, f32[2,2,3,2,4,2,256]{6,5,4,3,2,1,0:T(2,128)S(1)}, u32[]{:S(2)}, u32[]{:S(2)}) collective-permute-start(f32[2,2,3,2,4,2,256]{6,5,4,3,2,1,0:T(2,128)} %get-tuple-element.14), channel_id=1, source_target_pairs={{0,3},{1,0},{2,1},{3,2},{4,7},{5,4},{6,5},{7,6},{8,11},{9,8},{10,9... | collective-permute-start | bytes 589832 | tf_op jit(solution)/shard_map/ppermute | solution.py:25
  32.8 3.8 %collective-permute-start.7 = (bf16[2,2,3,2,1,8,256]{6,5,4,3,2,1,0:T(8,128)(2,1)}, bf16[2,2,3,2,1,8,256]{6,5,4,3,2,1,0:T(8,128)(2,1)S(1)}, u32[]{:S(2)}, u32[]{:S(2)}) collective-permute-start(bf16[2,2,3,2,1,8,256]{6,5,4,3,2,1,0:T(8,128)(2,1)} %get-tuple-element.12), channel_id=1, source_target_pairs={{0,12},{4,0},{8,4},{12,8},{1,13},{5,1},{9,5},{13,9},{2,14},{6,2},{... | collective-permute-start | bytes 294920 | tf_op jit(solution)/shard_map/ppermute | solution.py:25
  36.6 3.9 %collective-permute-done.6.refs_10_ = bf16[2,2,3,2,1,8,256]{6,5,4,3,2,1,0:T(8,128)(2,1)S(1)} collective-permute-done((bf16[2,2,3,2,1,8,256]{6,5,4,3,2,1,0:T(8,128)(2,1)}, bf16[2,2,3,2,1,8,256]{6,5,4,3,2,1,0:T(8,128)(2,1)S(1)}, u32[]{:S(2)}, u32[]{:S(2)}) %collective-permute-start.6) | collective-permute-done | bytes 98336 | tf_op jit(solution)/shard_map/ppermute | solution.py:25
  40.5 0.6 copy-done.10
  41.1 0.0 copy-done.11
  41.2 0.1 copy-done.6
  41.2 0.1 copy-done.7
  41.3 10.1 %shard_map.47 = bf16[2,4,3,2,4,2,4,256]{7,6,5,4,3,2,1,0:T(4,128)(2,1)} custom-call(f32[42]{0:T(128)} %pad_maximum_fusion.1.refs_0_, f32[4,3,2,1,4,256]{5,4,3,2,1,0:T(4,128)} %refs_1_.3, f32[4,3,2,1,4,256]{5,4,3,2,1,0:T(4,128)} %copy-done.2, f32[4,3,2,1,4,256]{5,4,3,2,1,0:T(4,128)} %copy-done.3, f32[4,3,2,1,1,256]{5,4,3,2,1,0:T(1,128)} %copy-done.8, ...), custom_call_target="tpu_custom_call" | custom-call | tf_op jit(solution)/shard_map/pallas_call | solution.py:293
  51.4 0.2 broadcast_select_fusion.1
  51.6 0.9 %copy-done.1 = bf16[2,4,3,2,4,2,4,256]{7,6,5,4,3,2,1,0:T(4,128)(2,1)S(1)} copy-done((bf16[2,4,3,2,4,2,4,256]{7,6,5,4,3,2,1,0:T(4,128)(2,1)S(1)}, bf16[2,4,3,2,4,2,4,256]{7,6,5,4,3,2,1,0:T(4,128)(2,1)}, u32[]{:S(2)}) %copy-start.1) | copy-done | bytes 786456
  52.6 1.5 %fusion.1 = f32[2,2,4,2,2,4,32]{6,2,3,1,4,0,5:T(4,128)S(1)} fusion(bf16[4,16,3,2,4,256]{5,1,4,2,3,0:T(8,128)(2,1)S(1)} %get-tuple-element.16, bf16[4,16,3,2,4,256]{5,1,4,2,3,0:T(8,128)(2,1)S(1)} %get-tuple-element.15, bf16[2,4,3,2,4,2,4,256,1]{7,6,5,4,3,2,1,0,8:T(4,128)(2,1)S(1)} %bitcast.60), kind=kOutput, calls=%fused_computation.2 | convolution fusion | flops 53477376 | bytes 2392064 | tf_op jit(solution)/shard_map/tvcazs,hqcbtgzs->hgqabtv/dot_general | solution.py:325
  54.0 0.1 copy.15
  54.1 0.1 add.85
  54.3 0.1 sub.25
  54.5 0.1 pad_maximum_fusion
  54.6 0.1 collective-permute-start.11
  54.7 1.3 %collective-permute-done.11 = f32[2,4,4,2,4,8]{5,4,3,2,1,0:T(4,128)S(1)} collective-permute-done((f32[2,4,4,2,4,8]{5,4,3,2,1,0:T(4,128)S(1)}, f32[2,4,4,2,4,8]{5,4,3,2,1,0:T(4,128)S(1)}, u32[]{:S(2)}, u32[]{:S(2)}) %collective-permute-start.11) | collective-permute-done | bytes 8224 | tf_op jit(solution)/shard_map/ppermute | solution.py:319
  56.0 0.1 fusion.5
  56.1 0.6 collective-permute-start.12
  56.7 3.8 %collective-permute-done.12 = f32[1,4,4,2,4,8]{5,4,3,2,1,0:T(4,128)S(1)} collective-permute-done((f32[1,4,4,2,4,8]{5,4,3,2,1,0:T(4,128)S(1)}, f32[1,4,4,2,4,8]{5,4,3,2,1,0:T(4,128)S(1)}, u32[]{:S(2)}, u32[]{:S(2)}) %collective-permute-start.12) | collective-permute-done | bytes 4128 | tf_op jit(solution)/shard_map/ppermute | solution.py:319
  60.4 0.7 %fusion.6 = f32[4,4,2,4,8]{4,3,2,1,0:T(4,128)} fusion(f32[1,4,4,2,4,8]{5,4,3,2,1,0:T(4,128)S(1)} %collective-permute-done.12, f32[1,2,4,4,2,4,8]{6,5,4,3,2,1,0:T(4,128)S(1)} %fusion.5, pred[]{:T(512)S(6)} %eq.53), kind=kLoop, calls=%fused_computation.15 | loop fusion | flops 2048 | bytes 16385 | tf_op jit(solution)/shard_map/squeeze | solution.py:321
  (31 shorter events, 0.2 us)
Async XLA Ops:
  0.0 11.9 %copy-start.12 = (s32[8]{0:T(128)S(1)}, s32[8]{0:T(128)}, u32[]{:S(2)}) copy-start(s32[8]{0:T(128)} %param.6) | copy-start | bytes 100
  0.0 19.5 %collective-permute-start = (f32[4,3,2,1,4,256]{5,4,3,2,1,0:T(4,128)}, f32[4,3,2,1,4,256]{5,4,3,2,1,0:T(4,128)S(1)}, u32[]{:S(2)}, u32[]{:S(2)}) collective-permute-start(f32[4,3,2,1,4,256]{5,4,3,2,1,0:T(4,128)} %refs_1_.3), channel_id=1, source_target_pairs={{0,4},{4,8},{8,12},{12,0},{1,5},{5,9},{9,13},{13,1},{2,6},{6,10},{... | collective-permute-start | bytes 294920 | tf_op jit(solution)/shard_map/ppermute | solution.py:25
  3.1 16.5 %collective-permute-start.1 = (f32[4,3,2,1,4,256]{5,4,3,2,1,0:T(4,128)}, f32[4,3,2,1,4,256]{5,4,3,2,1,0:T(4,128)S(1)}, u32[]{:S(2)}, u32[]{:S(2)}) collective-permute-start(f32[4,3,2,1,4,256]{5,4,3,2,1,0:T(4,128)} %refs_1_.3), channel_id=1, source_target_pairs={{0,12},{4,0},{8,4},{12,8},{1,13},{5,1},{9,5},{13,9},{2,14},{6,2},{... | collective-permute-start | bytes 294920 | tf_op jit(solution)/shard_map/ppermute | solution.py:25
  6.1 7.2 %collective-permute-start.2 = (f32[4,3,2,1,1,256]{5,4,3,2,1,0:T(1,128)S(1)}, f32[4,3,2,1,1,256]{5,4,3,2,1,0:T(1,128)S(1)}, u32[]{:S(2)}, u32[]{:S(2)}) collective-permute-start(f32[4,3,2,1,1,256]{5,4,3,2,1,0:T(1,128)S(1)} %get-tuple-element.20), channel_id=1, source_target_pairs={{0,1},{1,2},{2,3},{3,0},{4,5},{5,6},{6,7},{7,4},{8,9},{9,10},{10,1... | collective-permute-start | bytes 73736 | tf_op jit(solution)/shard_map/ppermute | solution.py:25
  6.2 7.2 %collective-permute-start.3 = (f32[4,3,2,1,1,256]{5,4,3,2,1,0:T(1,128)S(1)}, f32[4,3,2,1,1,256]{5,4,3,2,1,0:T(1,128)S(1)}, u32[]{:S(2)}, u32[]{:S(2)}) collective-permute-start(f32[4,3,2,1,1,256]{5,4,3,2,1,0:T(1,128)S(1)} %get-tuple-element.19), channel_id=1, source_target_pairs={{0,3},{1,0},{2,1},{3,2},{4,7},{5,4},{6,5},{7,6},{8,11},{9,8},{10,9... | collective-permute-start | bytes 73736 | tf_op jit(solution)/shard_map/ppermute | solution.py:25
  9.2 42.2 %collective-permute-start.10 = (bf16[4,16,3,2,4,256]{5,1,4,2,3,0:T(8,128)(2,1)S(1)}, bf16[4,16,3,2,4,256]{5,1,4,2,3,0:T(8,128)(2,1)S(1)}, u32[]{:S(2)}, u32[]{:S(2)}) collective-permute-start(bf16[4,16,3,2,4,256]{5,1,4,2,3,0:T(8,128)(2,1)S(1)} %copy.12), channel_id=1, source_target_pairs={{0,16},{16,0},{1,17},{17,1},{2,18},{18,2},{3,19},{19,3},{4,20},{20... | collective-permute-start | bytes 2359304 | tf_op jit(solution)/shard_map/ppermute | solution.py:29
  13.3 6.2 %copy-start.8 = (f32[4,3,2,1,1,256]{5,4,3,2,1,0:T(1,128)}, f32[4,3,2,1,1,256]{5,4,3,2,1,0:T(1,128)S(1)}, u32[]{:S(2)}) copy-start(f32[4,3,2,1,1,256]{5,4,3,2,1,0:T(1,128)S(1)} %collective-permute-done.2.refs_4_) | copy-start | bytes 73732
  13.3 6.2 %collective-permute-start.4 = (f32[3,3,2,1,4,256]{5,4,3,2,1,0:T(4,128)S(1)}, f32[3,3,2,1,4,256]{5,4,3,2,1,0:T(4,128)S(1)}, u32[]{:S(2)}, u32[]{:S(2)}) collective-permute-start(f32[3,3,2,1,4,256]{5,4,3,2,1,0:T(4,128)S(1)} %slice_bitcast_fusion.1), channel_id=1, source_target_pairs={{0,4},{4,8},{8,12},{12,0},{1,5},{5,9},{9,13},{13,1},{2,6},{6,10},{... | collective-permute-start | bytes 221192 | tf_op jit(solution)/shard_map/ppermute | solution.py:25
  13.4 6.2 %copy-start.9 = (f32[4,3,2,1,1,256]{5,4,3,2,1,0:T(1,128)}, f32[4,3,2,1,1,256]{5,4,3,2,1,0:T(1,128)S(1)}, u32[]{:S(2)}) copy-start(f32[4,3,2,1,1,256]{5,4,3,2,1,0:T(1,128)S(1)} %collective-permute-done.3.refs_5_) | copy-start | bytes 73732
  13.4 6.1 %collective-permute-start.5 = (f32[3,3,2,4,1,256]{5,4,3,2,1,0:T(1,128)S(1)}, f32[3,3,2,4,1,256]{5,4,3,2,1,0:T(1,128)S(1)}, u32[]{:S(2)}, u32[]{:S(2)}) collective-permute-start(f32[3,3,2,4,1,256]{5,4,3,2,1,0:T(1,128)S(1)} %slice_bitcast_fusion), channel_id=1, source_target_pairs={{0,1},{1,2},{2,3},{3,0},{4,5},{5,6},{6,7},{7,4},{8,9},{9,10},{10,1... | collective-permute-start | bytes 221192 | tf_op jit(solution)/shard_map/ppermute | solution.py:25
  19.5 0.6 %copy-start.4 = (f32[3,3,2,1,4,256]{5,4,3,2,1,0:T(4,128)}, f32[3,3,2,1,4,256]{5,4,3,2,1,0:T(4,128)S(1)}, u32[]{:S(2)}) copy-start(f32[3,3,2,1,4,256]{5,4,3,2,1,0:T(4,128)S(1)} %collective-permute-done.4.refs_7_) | copy-start | bytes 221188
  19.5 0.6 %copy-start.5 = (f32[3,3,2,4,1,256]{5,4,3,2,1,0:T(1,128)}, f32[3,3,2,4,1,256]{5,4,3,2,1,0:T(1,128)S(1)}, u32[]{:S(2)}) copy-start(f32[3,3,2,4,1,256]{5,4,3,2,1,0:T(1,128)S(1)} %collective-permute-done.5.refs_8_) | copy-start | bytes 221188
  19.5 0.7 %copy-start.2 = (f32[4,3,2,1,4,256]{5,4,3,2,1,0:T(4,128)}, f32[4,3,2,1,4,256]{5,4,3,2,1,0:T(4,128)S(1)}, u32[]{:S(2)}) copy-start(f32[4,3,2,1,4,256]{5,4,3,2,1,0:T(4,128)S(1)} %collective-permute-done.refs_2_) | copy-start | bytes 294916
  20.2 0.6 %copy-start.3 = (f32[4,3,2,1,4,256]{5,4,3,2,1,0:T(4,128)}, f32[4,3,2,1,4,256]{5,4,3,2,1,0:T(4,128)S(1)}, u32[]{:S(2)}) copy-start(f32[4,3,2,1,4,256]{5,4,3,2,1,0:T(4,128)S(1)} %collective-permute-done.1.refs_3_) | copy-start | bytes 294916
  31.0 9.5 %collective-permute-start.8 = (f32[2,2,3,2,4,2,256]{6,5,4,3,2,1,0:T(2,128)}, f32[2,2,3,2,4,2,256]{6,5,4,3,2,1,0:T(2,128)S(1)}, u32[]{:S(2)}, u32[]{:S(2)}) collective-permute-start(f32[2,2,3,2,4,2,256]{6,5,4,3,2,1,0:T(2,128)} %get-tuple-element.13), channel_id=1, source_target_pairs={{0,1},{1,2},{2,3},{3,0},{4,5},{5,6},{6,7},{7,4},{8,9},{9,10},{10,1... | collective-permute-start | bytes 589832 | tf_op jit(solution)/shard_map/ppermute | solution.py:25
  31.1 9.4 %collective-permute-start.9 = (f32[2,2,3,2,4,2,256]{6,5,4,3,2,1,0:T(2,128)}, f32[2,2,3,2,4,2,256]{6,5,4,3,2,1,0:T(2,128)S(1)}, u32[]{:S(2)}, u32[]{:S(2)}) collective-permute-start(f32[2,2,3,2,4,2,256]{6,5,4,3,2,1,0:T(2,128)} %get-tuple-element.14), channel_id=1, source_target_pairs={{0,3},{1,0},{2,1},{3,2},{4,7},{5,4},{6,5},{7,6},{8,11},{9,8},{10,9... | collective-permute-start | bytes 589832 | tf_op jit(solution)/shard_map/ppermute | solution.py:25
  32.8 7.7 %collective-permute-start.6 = (bf16[2,2,3,2,1,8,256]{6,5,4,3,2,1,0:T(8,128)(2,1)}, bf16[2,2,3,2,1,8,256]{6,5,4,3,2,1,0:T(8,128)(2,1)S(1)}, u32[]{:S(2)}, u32[]{:S(2)}) collective-permute-start(bf16[2,2,3,2,1,8,256]{6,5,4,3,2,1,0:T(8,128)(2,1)} %get-tuple-element.11), channel_id=1, source_target_pairs={{0,4},{4,8},{8,12},{12,0},{1,5},{5,9},{9,13},{13,1},{2,6},{6,10},{... | collective-permute-start | bytes 294920 | tf_op jit(solution)/shard_map/ppermute | solution.py:25
  32.8 7.7 %collective-permute-start.7 = (bf16[2,2,3,2,1,8,256]{6,5,4,3,2,1,0:T(8,128)(2,1)}, bf16[2,2,3,2,1,8,256]{6,5,4,3,2,1,0:T(8,128)(2,1)S(1)}, u32[]{:S(2)}, u32[]{:S(2)}) collective-permute-start(bf16[2,2,3,2,1,8,256]{6,5,4,3,2,1,0:T(8,128)(2,1)} %get-tuple-element.12), channel_id=1, source_target_pairs={{0,12},{4,0},{8,4},{12,8},{1,13},{5,1},{9,5},{13,9},{2,14},{6,2},{... | collective-permute-start | bytes 294920 | tf_op jit(solution)/shard_map/ppermute | solution.py:25
  40.5 0.6 %copy-start.10 = (bf16[2,2,3,2,1,8,256]{6,5,4,3,2,1,0:T(8,128)(2,1)}, bf16[2,2,3,2,1,8,256]{6,5,4,3,2,1,0:T(8,128)(2,1)S(1)}, u32[]{:S(2)}) copy-start(bf16[2,2,3,2,1,8,256]{6,5,4,3,2,1,0:T(8,128)(2,1)S(1)} %collective-permute-done.6.refs_10_) | copy-start | bytes 294916
  40.5 0.7 %copy-start.11 = (bf16[2,2,3,2,1,8,256]{6,5,4,3,2,1,0:T(8,128)(2,1)}, bf16[2,2,3,2,1,8,256]{6,5,4,3,2,1,0:T(8,128)(2,1)S(1)}, u32[]{:S(2)}) copy-start(bf16[2,2,3,2,1,8,256]{6,5,4,3,2,1,0:T(8,128)(2,1)S(1)} %collective-permute-done.7.refs_11_) | copy-start | bytes 294916
  40.5 0.7 %copy-start.6 = (f32[2,2,3,2,4,2,256]{6,5,4,3,2,1,0:T(2,128)}, f32[2,2,3,2,4,2,256]{6,5,4,3,2,1,0:T(2,128)S(1)}, u32[]{:S(2)}) copy-start(f32[2,2,3,2,4,2,256]{6,5,4,3,2,1,0:T(2,128)S(1)} %collective-permute-done.8.refs_12_) | copy-start | bytes 589828
  40.5 0.8 %copy-start.7 = (f32[2,2,3,2,4,2,256]{6,5,4,3,2,1,0:T(2,128)}, f32[2,2,3,2,4,2,256]{6,5,4,3,2,1,0:T(2,128)S(1)}, u32[]{:S(2)}) copy-start(f32[2,2,3,2,4,2,256]{6,5,4,3,2,1,0:T(2,128)S(1)} %collective-permute-done.9.refs_13_) | copy-start | bytes 589828
  41.3 10.1 %copy-start = (bf16[4,16,3,2,4,256]{5,4,3,2,1,0:T(4,128)(2,1)S(1)}, bf16[4,16,3,2,4,256]{5,4,3,2,1,0:T(4,128)(2,1)}, u32[]{:S(2)}) copy-start(bf16[4,16,3,2,4,256]{5,4,3,2,1,0:T(4,128)(2,1)} %param.7) | copy-start | bytes 2359300
  51.4 1.1 %copy-start.1 = (bf16[2,4,3,2,4,2,4,256]{7,6,5,4,3,2,1,0:T(4,128)(2,1)S(1)}, bf16[2,4,3,2,4,2,4,256]{7,6,5,4,3,2,1,0:T(4,128)(2,1)}, u32[]{:S(2)}) copy-start(bf16[2,4,3,2,4,2,4,256]{7,6,5,4,3,2,1,0:T(4,128)(2,1)} %shard_map.47) | copy-start | bytes 2359300
  54.6 1.4 %collective-permute-start.11 = (f32[2,4,4,2,4,8]{5,4,3,2,1,0:T(4,128)S(1)}, f32[2,4,4,2,4,8]{5,4,3,2,1,0:T(4,128)S(1)}, u32[]{:S(2)}, u32[]{:S(2)}) collective-permute-start(f32[2,4,4,2,4,8]{5,4,3,2,1,0:T(4,128)S(1)} %select_bitcast_fusion), channel_id=1, source_target_pairs={{0,1},{1,0},{2,3},{3,2},{4,5},{5,4},{6,7},{7,6},{8,9},{9,8},{10,11... | collective-permute-start | bytes 24584 | tf_op jit(solution)/shard_map/ppermute | solution.py:319
  56.1 4.3 %collective-permute-start.12 = (f32[1,4,4,2,4,8]{5,4,3,2,1,0:T(4,128)S(1)}, f32[1,4,4,2,4,8]{5,4,3,2,1,0:T(4,128)S(1)}, u32[]{:S(2)}, u32[]{:S(2)}) collective-permute-start(f32[1,4,4,2,4,8]{5,4,3,2,1,0:T(4,128)S(1)} %select_bitcast_fusion.1), channel_id=1, source_target_pairs={{0,2},{1,3},{2,0},{3,1},{4,6},{5,7},{6,4},{7,5},{8,10},{9,11},{10,... | collective-permute-start | bytes 12296 | tf_op jit(solution)/shard_map/ppermute | solution.py:319

commit v13 on v12

--- a/solution.py
+++ b/solution.py
@@ -370,9 +370,9 @@
         passed_along(z_first, "sa", -1),
     )
     rounded = hopping_step(False, scalars, noise_parts, link_parts, (spinor,) + halos)
-    first_half = jnp.where(section_index == 0, vectors, partner_vectors)
-    second_half = jnp.where(section_index == 0, partner_vectors, vectors)
-    partial_value = intersection_part(rounded, jnp.concatenate([first_half, second_half], axis=1))
+    own_first = intersection_part(rounded, jnp.concatenate([vectors, partner_vectors], axis=1))
+    half = vectors.shape[1]
+    partial_value = jnp.where(section_index == 0, own_first, jnp.roll(own_first, half, axis=4))
     return reduce_scatter_sa(partial_value)
 
 

time: 61.4 us -> 62 us (level)
  matrix products: 1.47 us -> 2.52 us
    dot_general x1, matrix products: 1.47 us -> 2.52 us  [intersection_part(): jnp.einsum('tvcazs,hqcbtgzs->hgqabtv', vector_piece, rounded, preferred_e...]
    unnamed x27 -> x23, local copies, waits for them, and re-layouts: 4.28 us -> 3.39 us
  transfers between devices with their start and end apart: 13 -> 13, of which waited for: 4 -> 4; matrix products, arithmetic and copies ran while one was open for 9% -> 8% of each run, Pallas kernels for 33% -> 33%
where the time goes in v13:
time: 62 us; the launch traced here: 61.6 us
  Pallas kernels  20.3 us (33%)
  starting transfers between devices  15 us (24%)
  waiting for transfers between devices  14.4 us (23%)
  local copies, waits for them, and re-layouts  7.3 us (12%)
  matrix products  2.52 us (4%)
  other arithmetic  1.79 us (3%)
    pallas_call x2, Pallas kernels, hopping_step(): pl.pallas_call(functools.partial(hop_kernel, first), grid=(H,), in_specs=...  20.3 us
    ppermute x10, starting transfers between devices, passed_along(): return lax.ppermute(value, axis, pairs)  12.6 us
    ppermute x10, waiting for transfers between devices, passed_along(): return lax.ppermute(value, axis, pairs)  9.33 us
    ppermute x2, waiting for transfers between devices, reduce_scatter_sa(): x = keep + lax.ppermute(send, 'sa', [(j, j ^ d) for j in range(n)])  5.08 us
    unnamed x23, local copies, waits for them, and re-layouts  3.39 us
    dot_general x1, matrix products, intersection_part(): jnp.einsum('tvcazs,hqcbtgzs->hgqabtv', vector_piece, rounded, preferred_e...  2.52 us
    ppermute x1, starting transfers between devices, from_partner(): lax.ppermute(x, axis, [(i, i ^ 1 << stride) for i in range(lax.axis_size(...  1.73 us
  transfers between devices with their start and end apart: 13, of which 4 were waited for; matrix products, arithmetic and copies ran while one was open for 8% of the time, Pallas kernels for 33%

profile of v13, /device:TPU:0, one launch (start us, length us, event | category | flops | bytes accessed | tf_op | source)
XLA Modules:
  0.0 61.6 jit_solution(14833716767853372135)
XLA Ops:
  0.0 3.1 %collective-permute-start = (f32[4,3,2,1,4,256]{5,4,3,2,1,0:T(4,128)}, f32[4,3,2,1,4,256]{5,4,3,2,1,0:T(4,128)S(1)}, u32[]{:S(2)}, u32[]{:S(2)}) collective-permute-start(f32[4,3,2,1,4,256]{5,4,3,2,1,0:T(4,128)} %refs_1_.3), channel_id=1, source_target_pairs={{0,4},{4,8},{8,12},{12,0},{1,5},{5,9},{9,13},{13,1},{2,6},{6,10},{... | collective-permute-start | bytes 294920 | tf_op jit(solution)/shard_map/ppermute | solution.py:25
  3.1 2.1 %collective-permute-start.1 = (f32[4,3,2,1,4,256]{5,4,3,2,1,0:T(4,128)}, f32[4,3,2,1,4,256]{5,4,3,2,1,0:T(4,128)S(1)}, u32[]{:S(2)}, u32[]{:S(2)}) collective-permute-start(f32[4,3,2,1,4,256]{5,4,3,2,1,0:T(4,128)} %refs_1_.3), channel_id=1, source_target_pairs={{0,12},{4,0},{8,4},{12,8},{1,13},{5,1},{9,5},{13,9},{2,14},{6,2},{... | collective-permute-start | bytes 294920 | tf_op jit(solution)/shard_map/ppermute | solution.py:25
  5.1 1.0 %fusion.12 = (f32[4,3,2,1,1,256]{5,4,3,2,1,0:T(1,128)S(1)}, f32[4,3,2,1,1,256]{5,4,3,2,1,0:T(1,128)S(1)}) fusion(f32[4,3,2,1,4,256]{5,4,3,2,1,0:T(4,128)} %refs_1_.3), kind=kLoop, calls=%fused_computation.34 | loop fusion | bytes 98304 | tf_op jit(solution)/shard_map/slice | solution.py:358
  6.1 0.1 collective-permute-start.2
  6.2 1.7 %collective-permute-start.3 = (f32[4,3,2,1,1,256]{5,4,3,2,1,0:T(1,128)S(1)}, f32[4,3,2,1,1,256]{5,4,3,2,1,0:T(1,128)S(1)}, u32[]{:S(2)}, u32[]{:S(2)}) collective-permute-start(f32[4,3,2,1,1,256]{5,4,3,2,1,0:T(1,128)S(1)} %get-tuple-element.15), channel_id=1, source_target_pairs={{0,3},{1,0},{2,1},{3,2},{4,7},{5,4},{6,5},{7,6},{8,11},{9,8},{10,9... | collective-permute-start | bytes 73736 | tf_op jit(solution)/shard_map/ppermute | solution.py:25
  7.9 1.3 %copy.12 = bf16[4,16,3,2,4,256]{5,1,4,2,3,0:T(8,128)(2,1)S(1)} copy(bf16[4,16,3,2,4,256]{5,4,3,2,1,0:T(4,128)(2,1)} %param.7) | data formatting | bytes 1572864 | tf_op args[3]
  9.2 1.7 %collective-permute-start.10 = (bf16[4,16,3,2,4,256]{5,1,4,2,3,0:T(8,128)(2,1)S(1)}, bf16[4,16,3,2,4,256]{5,1,4,2,3,0:T(8,128)(2,1)S(1)}, u32[]{:S(2)}, u32[]{:S(2)}) collective-permute-start(bf16[4,16,3,2,4,256]{5,1,4,2,3,0:T(8,128)(2,1)S(1)} %copy.12), channel_id=1, source_target_pairs={{0,16},{16,0},{1,17},{17,1},{2,18},{18,2},{3,19},{19,3},{4,20},{20... | collective-permute-start | bytes 2359304 | tf_op jit(solution)/shard_map/ppermute | solution.py:29
  11.0 0.9 %slice_bitcast_fusion.1 = f32[3,3,2,1,4,256]{5,4,3,2,1,0:T(4,128)S(1)} fusion(f32[4,3,3,2,4,4,256]{6,5,4,3,2,1,0:T(4,128)} %refs_6_.3), kind=kLoop, calls=%fused_computation.11 | loop fusion | bytes 147456 | tf_op jit(solution)/shard_map/squeeze | solution.py:362
  11.9 0.1 dynamic_slice.3
  11.9 0.1 compare_convert_fusion
  12.0 1.0 %slice_bitcast_fusion = f32[3,3,2,4,1,256]{5,4,3,2,1,0:T(1,128)S(1)} fusion(f32[4,3,3,2,4,4,256]{6,5,4,3,2,1,0:T(4,128)} %refs_6_.3), kind=kLoop, calls=%fused_computation.10 | loop fusion | bytes 147456 | tf_op jit(solution)/shard_map/squeeze | solution.py:363
  13.1 0.1 fusion.8
  13.1 0.1 reshape.183
  13.2 0.1 reshape.182
  13.3 0.0 collective-permute-done.2.refs_4_
  13.3 0.0 collective-permute-start.4
  13.4 0.0 collective-permute-done.3.refs_5_
  13.4 0.1 collective-permute-start.5
  13.5 0.6 pad_maximum_fusion.1.refs_0_
  14.0 5.5 %collective-permute-done.4.refs_7_ = f32[3,3,2,1,4,256]{5,4,3,2,1,0:T(4,128)S(1)} collective-permute-done((f32[3,3,2,1,4,256]{5,4,3,2,1,0:T(4,128)S(1)}, f32[3,3,2,1,4,256]{5,4,3,2,1,0:T(4,128)S(1)}, u32[]{:S(2)}, u32[]{:S(2)}) %collective-permute-start.4) | collective-permute-done | bytes 73760 | tf_op jit(solution)/shard_map/ppermute | solution.py:25
  19.6 0.6 copy-done.2
  20.1 0.0 copy-done.3
  20.2 0.0 copy-done
  20.2 0.6 %copy-done.1 = f32[4,3,2,1,4,256]{5,4,3,2,1,0:T(4,128)} copy-done((f32[4,3,2,1,4,256]{5,4,3,2,1,0:T(4,128)}, f32[4,3,2,1,4,256]{5,4,3,2,1,0:T(4,128)S(1)}, u32[]{:S(2)}) %copy-start.1) | copy-done | bytes 98328
  20.8 10.3 %shard_map.46 = (f32[2,4,3,2,4,8,256]{6,5,4,3,2,1,0:T(8,128)}, bf16[2,2,3,2,1,8,256]{6,5,4,3,2,1,0:T(8,128)(2,1)}, bf16[2,2,3,2,1,8,256]{6,5,4,3,2,1,0:T(8,128)(...) custom-call(f32[42]{0:T(128)} %pad_maximum_fusion.1.refs_0_, f32[4,3,2,1,4,256]{5,4,3,2,1,0:T(4,128)} %refs_1_.3, ...), custom_call_target="tpu_custom_call" | custom-call | tf_op jit(solution)/shard_map/pallas_call | solution.py:293
  31.1 0.0 collective-permute-start.8
  31.1 1.7 %collective-permute-start.9 = (f32[2,2,3,2,4,2,256]{6,5,4,3,2,1,0:T(2,128)}, f32[2,2,3,2,4,2,256]{6,5,4,3,2,1,0:T(2,128)S(1)}, u32[]{:S(2)}, u32[]{:S(2)}) collective-permute-start(f32[2,2,3,2,4,2,256]{6,5,4,3,2,1,0:T(2,128)} %get-tuple-element.14), channel_id=1, source_target_pairs={{0,3},{1,0},{2,1},{3,2},{4,7},{5,4},{6,5},{7,6},{8,11},{9,8},{10,9... | collective-permute-start | bytes 589832 | tf_op jit(solution)/shard_map/ppermute | solution.py:25
  32.9 3.8 %collective-permute-start.7 = (bf16[2,2,3,2,1,8,256]{6,5,4,3,2,1,0:T(8,128)(2,1)}, bf16[2,2,3,2,1,8,256]{6,5,4,3,2,1,0:T(8,128)(2,1)S(1)}, u32[]{:S(2)}, u32[]{:S(2)}) collective-permute-start(bf16[2,2,3,2,1,8,256]{6,5,4,3,2,1,0:T(8,128)(2,1)} %get-tuple-element.12), channel_id=1, source_target_pairs={{0,12},{4,0},{8,4},{12,8},{1,13},{5,1},{9,5},{13,9},{2,14},{6,2},{... | collective-permute-start | bytes 294920 | tf_op jit(solution)/shard_map/ppermute | solution.py:25
  36.7 3.9 %collective-permute-done.6.refs_10_ = bf16[2,2,3,2,1,8,256]{6,5,4,3,2,1,0:T(8,128)(2,1)S(1)} collective-permute-done((bf16[2,2,3,2,1,8,256]{6,5,4,3,2,1,0:T(8,128)(2,1)}, bf16[2,2,3,2,1,8,256]{6,5,4,3,2,1,0:T(8,128)(2,1)S(1)}, u32[]{:S(2)}, u32[]{:S(2)}) %collective-permute-start.6) | collective-permute-done | bytes 98336 | tf_op jit(solution)/shard_map/ppermute | solution.py:25
  40.6 0.6 copy-done.8
  41.2 0.0 copy-done.9
  41.2 0.1 copy-done.4
  41.3 0.1 copy-done.5
  41.4 10.0 %shard_map.47 = bf16[2,4,3,2,4,2,4,256]{7,6,5,4,3,2,1,0:T(4,128)(2,1)} custom-call(f32[42]{0:T(128)} %pad_maximum_fusion.1.refs_0_, f32[4,3,2,1,4,256]{5,4,3,2,1,0:T(4,128)} %refs_1_.3, f32[4,3,2,1,4,256]{5,4,3,2,1,0:T(4,128)} %copy-done, f32[4,3,2,1,4,256]{5,4,3,2,1,0:T(4,128)} %copy-done.1, f32[4,3,2,1,1,256]{5,4,3,2,1,0:T(1,128)} %copy-done.6, ...), custom_call_target="tpu_custom_call" | custom-call | tf_op jit(solution)/shard_map/pallas_call | solution.py:293
  51.4 2.5 %fusion.1 = f32[2,2,4,2,2,4,32]{6,2,3,1,4,0,5:T(4,128)S(1)} fusion(bf16[4,16,3,2,4,256]{5,1,4,2,3,0:T(8,128)(2,1)S(1)} %collective-permute-done.10, bf16[4,16,3,2,4,256]{5,1,4,2,3,0:T(8,128)(2,1)S(1)} %copy.12, bf16[2,4,3,2,4,2,4,256,1]{7,6,5,4,3,2,1,0,8:T(4,128)(2,1)} %bitcast.86), kind=kOutput, calls=%fused_computation.2 | convolution fusion | flops 53477376 | bytes 2392064 | tf_op jit(solution)/shard_map/tvcazs,hqcbtgzs->hgqabtv/dot_general | solution.py:325
  54.0 0.1 copy.14
  54.1 0.1 slice_maximum_fusion
  54.2 0.1 concatenate.18
  54.4 0.1 concatenate.19
  54.6 0.1 add.92
  54.8 0.1 sub.32
  55.0 0.1 maximum_select_fusion
  55.1 0.1 collective-permute-start.11
  55.2 1.3 %collective-permute-done.11 = f32[2,4,4,2,4,8]{5,4,3,2,1,0:T(4,128)S(1)} collective-permute-done((f32[2,4,4,2,4,8]{5,4,3,2,1,0:T(4,128)S(1)}, f32[2,4,4,2,4,8]{5,4,3,2,1,0:T(4,128)S(1)}, u32[]{:S(2)}, u32[]{:S(2)}) %collective-permute-start.11) | collective-permute-done | bytes 8224 | tf_op jit(solution)/shard_map/ppermute | solution.py:319
  56.6 0.1 fusion.5
  56.6 0.6 collective-permute-start.12
  57.2 3.8 %collective-permute-done.12 = f32[1,4,4,2,4,8]{5,4,3,2,1,0:T(4,128)S(1)} collective-permute-done((f32[1,4,4,2,4,8]{5,4,3,2,1,0:T(4,128)S(1)}, f32[1,4,4,2,4,8]{5,4,3,2,1,0:T(4,128)S(1)}, u32[]{:S(2)}, u32[]{:S(2)}) %collective-permute-start.12) | collective-permute-done | bytes 4128 | tf_op jit(solution)/shard_map/ppermute | solution.py:319
  61.0 0.7 %fusion.6 = f32[4,4,2,4,8]{4,3,2,1,0:T(4,128)} fusion(f32[1,4,4,2,4,8]{5,4,3,2,1,0:T(4,128)S(1)} %collective-permute-done.12, f32[1,2,4,4,2,4,8]{6,5,4,3,2,1,0:T(4,128)S(1)} %fusion.5, pred[]{:T(512)S(6)} %eq.52), kind=kLoop, calls=%fused_computation.15 | loop fusion | flops 2048 | bytes 16385 | tf_op jit(solution)/shard_map/squeeze | solution.py:321
  (34 shorter events, 0.3 us)
Async XLA Ops:
  0.0 11.9 %copy-start.10 = (s32[8]{0:T(128)S(1)}, s32[8]{0:T(128)}, u32[]{:S(2)}) copy-start(s32[8]{0:T(128)} %param.6) | copy-start | bytes 100
  0.0 19.5 %collective-permute-start = (f32[4,3,2,1,4,256]{5,4,3,2,1,0:T(4,128)}, f32[4,3,2,1,4,256]{5,4,3,2,1,0:T(4,128)S(1)}, u32[]{:S(2)}, u32[]{:S(2)}) collective-permute-start(f32[4,3,2,1,4,256]{5,4,3,2,1,0:T(4,128)} %refs_1_.3), channel_id=1, source_target_pairs={{0,4},{4,8},{8,12},{12,0},{1,5},{5,9},{9,13},{13,1},{2,6},{6,10},{... | collective-permute-start | bytes 294920 | tf_op jit(solution)/shard_map/ppermute | solution.py:25
  3.1 16.5 %collective-permute-start.1 = (f32[4,3,2,1,4,256]{5,4,3,2,1,0:T(4,128)}, f32[4,3,2,1,4,256]{5,4,3,2,1,0:T(4,128)S(1)}, u32[]{:S(2)}, u32[]{:S(2)}) collective-permute-start(f32[4,3,2,1,4,256]{5,4,3,2,1,0:T(4,128)} %refs_1_.3), channel_id=1, source_target_pairs={{0,12},{4,0},{8,4},{12,8},{1,13},{5,1},{9,5},{13,9},{2,14},{6,2},{... | collective-permute-start | bytes 294920 | tf_op jit(solution)/shard_map/ppermute | solution.py:25
  6.1 7.2 %collective-permute-start.2 = (f32[4,3,2,1,1,256]{5,4,3,2,1,0:T(1,128)S(1)}, f32[4,3,2,1,1,256]{5,4,3,2,1,0:T(1,128)S(1)}, u32[]{:S(2)}, u32[]{:S(2)}) collective-permute-start(f32[4,3,2,1,1,256]{5,4,3,2,1,0:T(1,128)S(1)} %get-tuple-element.16), channel_id=1, source_target_pairs={{0,1},{1,2},{2,3},{3,0},{4,5},{5,6},{6,7},{7,4},{8,9},{9,10},{10,1... | collective-permute-start | bytes 73736 | tf_op jit(solution)/shard_map/ppermute | solution.py:25
  6.2 7.2 %collective-permute-start.3 = (f32[4,3,2,1,1,256]{5,4,3,2,1,0:T(1,128)S(1)}, f32[4,3,2,1,1,256]{5,4,3,2,1,0:T(1,128)S(1)}, u32[]{:S(2)}, u32[]{:S(2)}) collective-permute-start(f32[4,3,2,1,1,256]{5,4,3,2,1,0:T(1,128)S(1)} %get-tuple-element.15), channel_id=1, source_target_pairs={{0,3},{1,0},{2,1},{3,2},{4,7},{5,4},{6,5},{7,6},{8,11},{9,8},{10,9... | collective-permute-start | bytes 73736 | tf_op jit(solution)/shard_map/ppermute | solution.py:25
  9.2 42.2 %collective-permute-start.10 = (bf16[4,16,3,2,4,256]{5,1,4,2,3,0:T(8,128)(2,1)S(1)}, bf16[4,16,3,2,4,256]{5,1,4,2,3,0:T(8,128)(2,1)S(1)}, u32[]{:S(2)}, u32[]{:S(2)}) collective-permute-start(bf16[4,16,3,2,4,256]{5,1,4,2,3,0:T(8,128)(2,1)S(1)} %copy.12), channel_id=1, source_target_pairs={{0,16},{16,0},{1,17},{17,1},{2,18},{18,2},{3,19},{19,3},{4,20},{20... | collective-permute-start | bytes 2359304 | tf_op jit(solution)/shard_map/ppermute | solution.py:29
  13.3 6.2 %copy-start.6 = (f32[4,3,2,1,1,256]{5,4,3,2,1,0:T(1,128)}, f32[4,3,2,1,1,256]{5,4,3,2,1,0:T(1,128)S(1)}, u32[]{:S(2)}) copy-start(f32[4,3,2,1,1,256]{5,4,3,2,1,0:T(1,128)S(1)} %collective-permute-done.2.refs_4_) | copy-start | bytes 73732
  13.3 6.2 %collective-permute-start.4 = (f32[3,3,2,1,4,256]{5,4,3,2,1,0:T(4,128)S(1)}, f32[3,3,2,1,4,256]{5,4,3,2,1,0:T(4,128)S(1)}, u32[]{:S(2)}, u32[]{:S(2)}) collective-permute-start(f32[3,3,2,1,4,256]{5,4,3,2,1,0:T(4,128)S(1)} %slice_bitcast_fusion.1), channel_id=1, source_target_pairs={{0,4},{4,8},{8,12},{12,0},{1,5},{5,9},{9,13},{13,1},{2,6},{6,10},{... | collective-permute-start | bytes 221192 | tf_op jit(solution)/shard_map/ppermute | solution.py:25
  13.4 6.2 %copy-start.7 = (f32[4,3,2,1,1,256]{5,4,3,2,1,0:T(1,128)}, f32[4,3,2,1,1,256]{5,4,3,2,1,0:T(1,128)S(1)}, u32[]{:S(2)}) copy-start(f32[4,3,2,1,1,256]{5,4,3,2,1,0:T(1,128)S(1)} %collective-permute-done.3.refs_5_) | copy-start | bytes 73732
  13.4 6.1 %collective-permute-start.5 = (f32[3,3,2,4,1,256]{5,4,3,2,1,0:T(1,128)S(1)}, f32[3,3,2,4,1,256]{5,4,3,2,1,0:T(1,128)S(1)}, u32[]{:S(2)}, u32[]{:S(2)}) collective-permute-start(f32[3,3,2,4,1,256]{5,4,3,2,1,0:T(1,128)S(1)} %slice_bitcast_fusion), channel_id=1, source_target_pairs={{0,1},{1,2},{2,3},{3,0},{4,5},{5,6},{6,7},{7,4},{8,9},{9,10},{10,1... | collective-permute-start | bytes 221192 | tf_op jit(solution)/shard_map/ppermute | solution.py:25
  19.5 0.6 %copy-start.2 = (f32[3,3,2,1,4,256]{5,4,3,2,1,0:T(4,128)}, f32[3,3,2,1,4,256]{5,4,3,2,1,0:T(4,128)S(1)}, u32[]{:S(2)}) copy-start(f32[3,3,2,1,4,256]{5,4,3,2,1,0:T(4,128)S(1)} %collective-permute-done.4.refs_7_) | copy-start | bytes 221188
  19.5 0.6 %copy-start.3 = (f32[3,3,2,4,1,256]{5,4,3,2,1,0:T(1,128)}, f32[3,3,2,4,1,256]{5,4,3,2,1,0:T(1,128)S(1)}, u32[]{:S(2)}) copy-start(f32[3,3,2,4,1,256]{5,4,3,2,1,0:T(1,128)S(1)} %collective-permute-done.5.refs_8_) | copy-start | bytes 221188
  19.5 0.7 %copy-start = (f32[4,3,2,1,4,256]{5,4,3,2,1,0:T(4,128)}, f32[4,3,2,1,4,256]{5,4,3,2,1,0:T(4,128)S(1)}, u32[]{:S(2)}) copy-start(f32[4,3,2,1,4,256]{5,4,3,2,1,0:T(4,128)S(1)} %collective-permute-done.refs_2_) | copy-start | bytes 294916
  20.2 0.6 %copy-start.1 = (f32[4,3,2,1,4,256]{5,4,3,2,1,0:T(4,128)}, f32[4,3,2,1,4,256]{5,4,3,2,1,0:T(4,128)S(1)}, u32[]{:S(2)}) copy-start(f32[4,3,2,1,4,256]{5,4,3,2,1,0:T(4,128)S(1)} %collective-permute-done.1.refs_3_) | copy-start | bytes 294916
  31.1 9.5 %collective-permute-start.8 = (f32[2,2,3,2,4,2,256]{6,5,4,3,2,1,0:T(2,128)}, f32[2,2,3,2,4,2,256]{6,5,4,3,2,1,0:T(2,128)S(1)}, u32[]{:S(2)}, u32[]{:S(2)}) collective-permute-start(f32[2,2,3,2,4,2,256]{6,5,4,3,2,1,0:T(2,128)} %get-tuple-element.13), channel_id=1, source_target_pairs={{0,1},{1,2},{2,3},{3,0},{4,5},{5,6},{6,7},{7,4},{8,9},{9,10},{10,1... | collective-permute-start | bytes 589832 | tf_op jit(solution)/shard_map/ppermute | solution.py:25
  31.1 9.4 %collective-permute-start.9 = (f32[2,2,3,2,4,2,256]{6,5,4,3,2,1,0:T(2,128)}, f32[2,2,3,2,4,2,256]{6,5,4,3,2,1,0:T(2,128)S(1)}, u32[]{:S(2)}, u32[]{:S(2)}) collective-permute-start(f32[2,2,3,2,4,2,256]{6,5,4,3,2,1,0:T(2,128)} %get-tuple-element.14), channel_id=1, source_target_pairs={{0,3},{1,0},{2,1},{3,2},{4,7},{5,4},{6,5},{7,6},{8,11},{9,8},{10,9... | collective-permute-start | bytes 589832 | tf_op jit(solution)/shard_map/ppermute | solution.py:25
  32.9 7.7 %collective-permute-start.6 = (bf16[2,2,3,2,1,8,256]{6,5,4,3,2,1,0:T(8,128)(2,1)}, bf16[2,2,3,2,1,8,256]{6,5,4,3,2,1,0:T(8,128)(2,1)S(1)}, u32[]{:S(2)}, u32[]{:S(2)}) collective-permute-start(bf16[2,2,3,2,1,8,256]{6,5,4,3,2,1,0:T(8,128)(2,1)} %get-tuple-element.11), channel_id=1, source_target_pairs={{0,4},{4,8},{8,12},{12,0},{1,5},{5,9},{9,13},{13,1},{2,6},{6,10},{... | collective-permute-start | bytes 294920 | tf_op jit(solution)/shard_map/ppermute | solution.py:25
  32.9 7.7 %collective-permute-start.7 = (bf16[2,2,3,2,1,8,256]{6,5,4,3,2,1,0:T(8,128)(2,1)}, bf16[2,2,3,2,1,8,256]{6,5,4,3,2,1,0:T(8,128)(2,1)S(1)}, u32[]{:S(2)}, u32[]{:S(2)}) collective-permute-start(bf16[2,2,3,2,1,8,256]{6,5,4,3,2,1,0:T(8,128)(2,1)} %get-tuple-element.12), channel_id=1, source_target_pairs={{0,12},{4,0},{8,4},{12,8},{1,13},{5,1},{9,5},{13,9},{2,14},{6,2},{... | collective-permute-start | bytes 294920 | tf_op jit(solution)/shard_map/ppermute | solution.py:25
  40.6 0.6 %copy-start.8 = (bf16[2,2,3,2,1,8,256]{6,5,4,3,2,1,0:T(8,128)(2,1)}, bf16[2,2,3,2,1,8,256]{6,5,4,3,2,1,0:T(8,128)(2,1)S(1)}, u32[]{:S(2)}) copy-start(bf16[2,2,3,2,1,8,256]{6,5,4,3,2,1,0:T(8,128)(2,1)S(1)} %collective-permute-done.6.refs_10_) | copy-start | bytes 294916
  40.6 0.7 %copy-start.9 = (bf16[2,2,3,2,1,8,256]{6,5,4,3,2,1,0:T(8,128)(2,1)}, bf16[2,2,3,2,1,8,256]{6,5,4,3,2,1,0:T(8,128)(2,1)S(1)}, u32[]{:S(2)}) copy-start(bf16[2,2,3,2,1,8,256]{6,5,4,3,2,1,0:T(8,128)(2,1)S(1)} %collective-permute-done.7.refs_11_) | copy-start | bytes 294916
  40.6 0.8 %copy-start.4 = (f32[2,2,3,2,4,2,256]{6,5,4,3,2,1,0:T(2,128)}, f32[2,2,3,2,4,2,256]{6,5,4,3,2,1,0:T(2,128)S(1)}, u32[]{:S(2)}) copy-start(f32[2,2,3,2,4,2,256]{6,5,4,3,2,1,0:T(2,128)S(1)} %collective-permute-done.8.refs_12_) | copy-start | bytes 589828
  40.6 0.8 %copy-start.5 = (f32[2,2,3,2,4,2,256]{6,5,4,3,2,1,0:T(2,128)}, f32[2,2,3,2,4,2,256]{6,5,4,3,2,1,0:T(2,128)S(1)}, u32[]{:S(2)}) copy-start(f32[2,2,3,2,4,2,256]{6,5,4,3,2,1,0:T(2,128)S(1)} %collective-permute-done.9.refs_13_) | copy-start | bytes 589828
  55.1 1.4 %collective-permute-start.11 = (f32[2,4,4,2,4,8]{5,4,3,2,1,0:T(4,128)S(1)}, f32[2,4,4,2,4,8]{5,4,3,2,1,0:T(4,128)S(1)}, u32[]{:S(2)}, u32[]{:S(2)}) collective-permute-start(f32[2,4,4,2,4,8]{5,4,3,2,1,0:T(4,128)S(1)} %select_bitcast_fusion), channel_id=1, source_target_pairs={{0,1},{1,0},{2,3},{3,2},{4,5},{5,4},{6,7},{7,6},{8,9},{9,8},{10,11... | collective-permute-start | bytes 24584 | tf_op jit(solution)/shard_map/ppermute | solution.py:319
  56.6 4.3 %collective-permute-start.12 = (f32[1,4,4,2,4,8]{5,4,3,2,1,0:T(4,128)S(1)}, f32[1,4,4,2,4,8]{5,4,3,2,1,0:T(4,128)S(1)}, u32[]{:S(2)}, u32[]{:S(2)}) collective-permute-start(f32[1,4,4,2,4,8]{5,4,3,2,1,0:T(4,128)S(1)} %select_bitcast_fusion.1), channel_id=1, source_target_pairs={{0,2},{1,3},{2,0},{3,1},{4,6},{5,7},{6,4},{7,5},{8,10},{9,11},{10,... | collective-permute-start | bytes 12296 | tf_op jit(solution)/shard_map/ppermute | solution.py:319
